TPU v7x, 32 devices: a whole 2x2x4 slice. The times are simulated.
32 devices in a mesh: seq: 8 (over z, x), tp: 4 (over y, core).
Axes of the slice: x: 2, y: 2, z: 4, core: 2. Of those that a mesh axis runs over, the one named last changes fastest.
Arguments:
- queries: bfloat16 [1024, 4096], P('seq', 'tp'), may hold values from -600 to 600
- suffix_keys: bfloat16 [1024, 1024], P('seq', 'tp'), may hold values from -6 to 6
- suffix_values: bfloat16 [1024, 1024], P('seq', 'tp'), may hold values from -6 to 6
- prefix_keys: bfloat16 [512, 1024], P('seq', 'tp'), may hold values from -6 to 6
- prefix_values: bfloat16 [512, 1024], P('seq', 'tp'), may hold values from -6 to 6
- suffix_lengths: int32 [24], replicated, may hold values from 1 to 128, 1024 in all
- request_group: int32 [24], replicated, may hold values from 0 to 3
- block_group: int32 [8], replicated, may hold values from 0 to 3, as said below
Outputs:
- attended: bfloat16 [1024, 4096], P('seq', 'tp')
- cache_keys: bfloat16 [1024, 1024], P(('seq', 'tp'))
- cache_values: bfloat16 [1024, 1024], P(('seq', 'tp'))
Inputs may be any that keep to these rules, and one draw needn't show every extreme that they name: `suffix_lengths`: the suffixes fill the 1024 packed tokens end to end in order; the longest has exactly 128 tokens. `block_group`: each prefix is held by exactly 2 blocks, in any order.
All inputs are finite; a program needn't handle non-finite values.
Results may differ from a plain program's by a relative error of at most 0.009.
The roundings to bfloat16 on the way count: a program that leaves them out, or rounds other values in their place, can miss the bound.
Values may be sent and summed in bfloat16 or wider, within the bound.
No kernel may reach another device: no remote copies, remote signals or barrier semaphores. Data moves between devices by JAX's collectives and lax.ppermute only.
A program may use at most 64 MiB of HBM per device.

v0:
```python
import math

import jax
import jax.numpy as jnp
from jax import lax
from jax.sharding import PartitionSpec as P

HD = 128
GROUPS = 4


BIG_NEGATIVE = -1e30


def from_behind(array, axis, by):
    length = lax.axis_size(axis)
    pairs = [(i, i + by) for i in range(length) if 0 <= i + by < length]
    return lax.ppermute(array, axis, pairs)


def rotate(values, position):
    half = values.shape[-1] // 2
    freq = jnp.exp(
        jnp.arange(half, dtype=jnp.float32) * (-2.0 * math.log(500000.0) / values.shape[-1])
    )
    angle = position.astype(jnp.float32)[:, None] * freq[None, :]
    cosine = jnp.cos(angle)[:, None, :]
    sine = jnp.sin(angle)[:, None, :]
    floats = values.astype(jnp.float32)
    lower = floats[..., :half]
    upper = floats[..., half:]
    return jnp.concatenate(
        [lower * cosine - upper * sine, upper * cosine + lower * sine], axis=-1
    ).astype(jnp.bfloat16)


def token_info(index, suffix_lengths, request_group):
    ends = jnp.cumsum(suffix_lengths)
    request = jnp.sum((index[:, None] >= ends[None, :]).astype(jnp.int32), axis=1)
    onehot = request[:, None] == jnp.arange(suffix_lengths.shape[0], dtype=jnp.int32)[None, :]
    first = jnp.sum(jnp.where(onehot, (ends - suffix_lengths)[None, :], 0), axis=1)
    group = jnp.sum(jnp.where(onehot, request_group[None, :], 0), axis=1)
    return (request, index - first, group)


def body(
    queries,
    suffix_keys,
    suffix_values,
    prefix_keys,
    prefix_values,
    suffix_lengths,
    request_group,
    block_group,
):
    rows = queries.shape[0]
    kv_cols = suffix_keys.shape[1]
    kv_heads = kv_cols // HD
    q_heads = queries.shape[1] // HD
    repeat = q_heads // kv_heads
    devices = lax.axis_size("seq")
    me = lax.axis_index("seq")
    block_rows = prefix_keys.shape[0]
    prefix_len = block_rows * devices // GROUPS
    span = max(1, min(2048 // rows, devices // 8))
    scale = HD ** (-0.5)
    index = me * rows + jnp.arange(rows, dtype=jnp.int32)
    request, offset, group = token_info(index, suffix_lengths, request_group)
    position = offset + prefix_len
    q_rot = rotate(queries.reshape(rows, q_heads, HD), position).reshape(rows, kv_heads, repeat, HD)
    k_rot = rotate(suffix_keys.reshape(rows, kv_heads, HD), position).reshape(rows, kv_cols)

    def update(carry, keys, values, visible):
        high, total, accum = carry
        keys_split = keys.reshape(keys.shape[0], kv_heads, HD)
        values_split = values.reshape(values.shape[0], kv_heads, HD)
        scores = (
            jnp.einsum("bgrd,kgd->bgrk", q_rot, keys_split, preferred_element_type=jnp.float32)
            * scale
        )
        mask = visible[:, None, None, :]
        scores = jnp.where(mask, scores, BIG_NEGATIVE)
        new_high = jnp.maximum(high, jnp.max(scores, axis=-1))
        weights = jnp.where(mask, jnp.exp(scores - new_high[..., None]), 0.0)
        factor = jnp.exp(high - new_high)
        total = total * factor + jnp.sum(weights, axis=-1)
        accum = accum * factor[..., None] + jnp.einsum(
            "bgrk,kgd->bgrd",
            weights.astype(jnp.bfloat16),
            values_split,
            preferred_element_type=jnp.float32,
        )
        return (new_high, total, accum)

    def guarded(carry, keys, values, visible):
        return update(carry, keys, values, visible)

    def suffix_visible(back):
        key_index = (me - back) * rows + jnp.arange(rows, dtype=jnp.int32)
        key_request, _, _ = token_info(key_index, suffix_lengths, request_group)
        return (
            (key_index[None, :] >= 0)
            & (key_request[None, :] == request[:, None])
            & (key_index[None, :] <= index[:, None])
        )

    start_state = (
        jnp.full((rows, kv_heads, repeat), BIG_NEGATIVE, jnp.float32),
        jnp.zeros((rows, kv_heads, repeat), jnp.float32),
        jnp.zeros((rows, kv_heads, repeat, HD), jnp.float32),
    )
    carry = start_state
    keys = lax.all_gather(prefix_keys, "seq", axis=0, tiled=True)
    values = lax.all_gather(prefix_values, "seq", axis=0, tiled=True)
    count = keys.shape[0]
    width = 512

    def one_step(state, step):
        first = step * width
        keys_part = lax.dynamic_slice_in_dim(keys, first, width, 0)
        values_part = lax.dynamic_slice_in_dim(values, first, width, 0)
        row_index = first + jnp.arange(width, dtype=jnp.int32)
        holder = row_index // block_rows
        matches = holder[:, None] == jnp.arange(block_group.shape[0], dtype=jnp.int32)[None, :]
        row_group = jnp.sum(jnp.where(matches, block_group[None, :], 0), axis=1)
        visible = row_group[None, :] == group[:, None]
        return (guarded(state, keys_part, values_part, visible), None)

    carry, _ = lax.scan(one_step, carry, jnp.arange(count // width, dtype=jnp.int32))
    carry = guarded(carry, k_rot, suffix_values, suffix_visible(0))
    for back in range(1, span + 1):
        earlier_keys, earlier_values = from_behind((k_rot, suffix_values), "seq", back)
        carry = guarded(carry, earlier_keys, earlier_values, suffix_visible(back))
    high, total, accum = carry
    attended = (accum / total[..., None]).reshape(rows, q_heads * HD).astype(jnp.bfloat16)
    cache_keys, cache_values = (
        lax.all_to_all(k_rot, "tp", split_axis=0, concat_axis=1, tiled=True),
        lax.all_to_all(suffix_values, "tp", split_axis=0, concat_axis=1, tiled=True),
    )
    return (attended, cache_keys, cache_values)


def solution(mesh):
    return jax.shard_map(
        body,
        mesh=mesh,
        in_specs=(
            P("seq", "tp"),
            P("seq", "tp"),
            P("seq", "tp"),
            P("seq", "tp"),
            P("seq", "tp"),
            P(),
            P(),
            P(),
        ),
        out_specs=(P("seq", "tp"), P(("seq", "tp"), None), P(("seq", "tp"), None)),
        check_vma=False,
    )
```

profile of v0, /device:TPU:0, one launch (start us, length us, event | category | flops | bytes accessed | tf_op | source)
XLA Modules:
  0.0 101.6 jit_solution(3033059807300362979)
XLA Ops:
  0.7 0.8 copy.95
  2.4 0.7 select_reduce_fusion.2
  3.1 0.9 copy.101
  4.7 0.7 copy.106
  5.5 5.5 %collective-permute-start = (bf16[128,256]{0,1:T(8,128)(2,1)}, bf16[128,256]{0,1:T(8,128)(2,1)}, u32[]{:S(2)}, u32[]{:S(2)}) collective-permute-start(bf16[128,256]{0,1:T(8,128)(2,1)} %bitcast.19), channel_id=1, source_target_pairs={{0,4},{4,8},{8,12},{12,16},{16,20},{20,24},{24,28},{1,5},{5,9},{9,... | collective-permute-start | bytes 196616 | tf_op jit(solution)/shard_map/ppermute | solution.py:18
  10.9 3.5 %collective-permute-start.1 = (bf16[128,256]{1,0:T(8,128)(2,1)}, bf16[128,256]{1,0:T(8,128)(2,1)}, u32[]{:S(2)}, u32[]{:S(2)}) collective-permute-start(bf16[128,256]{1,0:T(8,128)(2,1)} %param.10), channel_id=1, source_target_pairs={{0,4},{4,8},{8,12},{12,16},{16,20},{20,24},{24,28},{1,5},{5,9},{9,... | collective-permute-start | bytes 196616 | tf_op jit(solution)/shard_map/ppermute | solution.py:18
  15.2 3.3 %all-to-all-start = ((bf16[4,32,256]{2,1,0:T(8,128)(2,1)}), bf16[4,32,256]{2,1,0:T(8,128)(2,1)S(1)}, u32[]{:S(2)}, u32[]{:S(2)}) async-start(bf16[4,32,256]{2,1,0:T(8,128)(2,1)} %convert_element_type.70), calls=%async_computation | async-start | bytes 131072 | tf_op jit(solution)/shard_map/all_to_all | solution.py:137
  18.9 31.0 %all_gather.6 = bf16[512,256]{1,0:T(8,128)(2,1)S(1)} all-gather(bf16[64,256]{1,0:T(8,128)(2,1)S(1)} %copy-done.7), channel_id=1, replica_groups=mesh['seq'=8,'tp'=4] {'seq'}, dimensions={0}, use_global_device_ids=true | all-gather | bytes 294912 | tf_op jit(solution)/shard_map/all_gather | solution.py:113
  50.4 0.8 compare_and_fusion
  51.2 1.2 %bitcast_reduce_fusion = (f32[128,2,4]{0,2,1:T(4,128)}, f32[2,128,4,512]{3,1,2,0:T(8,128)S(1)}) fusion(pred[128,512]{1,0:T(8,128)(4,1)S(1)} %broadcast_compare_fusion, bf16[512,2,128,1]{0,2,3,1:T(8,128)(2,1)S(1)} %bitcast.101, bf16[128,2,4,64]{3,0,2,1:T(8,128)(2,1)S(1)} %bitcast.98, bf16[128,2,4,64]{3,0,2,1:T(8,128)(2,1)S(1)} %bitcast.95), kind=kOutput, calls=%fused_computation.1 | convolution fusion | flops 136313856 | bytes 2691072 | tf_op jit(solution)/shard_map/while/body/eval_jaxpr/bgrd,kgd->bgrk/dot_general | solution.py:78
  52.4 0.9 fusion.49
  53.9 3.9 %all-to-all-start.1 = ((bf16[4,32,256]{2,1,0:T(8,128)(2,1)}), bf16[4,32,256]{2,1,0:T(8,128)(2,1)}, u32[]{:S(2)}, u32[]{:S(2)}) async-start(bf16[4,32,256]{2,1,0:T(8,128)(2,1)} %bitcast.29), calls=%async_computation.1 | async-start | bytes 131072 | tf_op jit(solution)/shard_map/all_to_all | solution.py:138
  57.8 31.0 %all_gather.7 = bf16[512,256]{1,0:T(8,128)(2,1)S(1)} all-gather(bf16[64,256]{1,0:T(8,128)(2,1)} %param.12), channel_id=1, replica_groups=mesh['seq'=8,'tp'=4] {'seq'}, dimensions={0}, use_global_device_ids=true | all-gather | bytes 294912 | tf_op jit(solution)/shard_map/all_gather | solution.py:114
  88.9 0.9 copy.124
  89.8 0.8 copy.100
  90.7 1.5 %copy.131 = bf16[4,4,8,256]{3,2,0,1:T(8,128)(2,1)} copy(bf16[4,4,8,256]{3,2,1,0:T(8,128)(2,1)} %bitcast.106) | data formatting | bytes 131072 | tf_op jit(solution)/shard_map/all_to_all | solution.py:137
  92.2 1.5 %copy.132 = bf16[4,4,8,256]{3,2,0,1:T(8,128)(2,1)} copy(bf16[4,4,8,256]{3,2,1,0:T(8,128)(2,1)} %bitcast.46) | data formatting | bytes 131072 | tf_op jit(solution)/shard_map/all_to_all | solution.py:138
  93.6 1.2 %fusion.48 = (f32[128,2,4]{0,2,1:T(4,128)S(1)}, f32[128,2,4,128]{0,3,2,1:T(8,128)S(1)}) fusion(bf16[128,2,128,1]{0,2,3,1:T(8,128)(2,1)} %bitcast.39, bf16[128,2,4,64]{3,0,2,1:T(8,128)(2,1)S(1)} %bitcast.100, bf16[128,2,4,64]{3,0,2,1:T(8,128)(2,1)S(1)} %bitcast.97, pred[128,128]{0,1:T(8,128)(4,1)} %get-tuple-element.67), kind=kOutput, calls=%fused_computation.88 | convolution fusion | flops 34470912 | bytes 872448 | tf_op jit(solution)/shard_map/bgrd,kgd->bgrk/dot_general | solution.py:78
  94.9 0.7 fusion.44
  96.0 0.7 fusion.2
  96.9 1.6 %fusion.7 = f32[128,2,4,128]{0,3,2,1:T(8,128)} fusion(f32[128,2,4,128]{0,3,2,1:T(8,128)S(1)} %convolution_bitcast_fusion.1, bf16[512,2,128,1]{0,2,3,1:T(8,128)(2,1)S(1)} %bitcast.104, f32[2,128,4,512]{3,1,2,0:T(8,128)S(1)} %get-tuple-element.76, f32[128,2,4]{0,2,1:T(4,128)S(1)} %get-tuple-element.66, pred[128,512]{1,0:T(8,128)(4,1)S(1)} %broadcast_compare_fusion, ...), kind=kOutput, calls=%fused_computation.13 | convolution fusion | flops 137363456 | bytes 3489792 | tf_op jit(solution)/shard_map/while/body/eval_jaxpr/bgrk,kgd->bgrd/dot_general | solution.py:87
  98.5 0.9 copy.108
  99.4 1.3 %fusion.14 = bf16[128,2,4,128]{0,3,2,1:T(8,128)(2,1)S(1)} fusion(f32[128,2,4,128]{0,3,2,1:T(8,128)} %fusion.7, bf16[128,2,128,1]{0,2,3,1:T(8,128)(2,1)S(1)} %bitcast.109, f32[128,2,4,128]{0,3,2,1:T(8,128)S(1)} %copy-done.1, f32[128,2,4]{0,2,1:T(4,128)S(1)} %get-tuple-element.52, f32[128,2,4]{0,2,1:T(4,128)S(1)} %get-tuple-element.55, ...), kind=kOutput, calls=%fused_computation.22 | convolution fusion | flops 34340864 | bytes 1400832 | tf_op jit(solution)/shard_map/bgrk,kgd->bgrd/dot_general | solution.py:87
  100.7 0.9 copy.113
  (50 shorter events, 4.4 us)
Async XLA Ops:
  0.6 17.9 %copy-start.2 = (bf16[128,1024]{1,0:T(8,128)(2,1)S(1)}, bf16[128,1024]{1,0:T(8,128)(2,1)}, u32[]{:S(2)}) copy-start(bf16[128,1024]{1,0:T(8,128)(2,1)} %param.8) | copy-start | bytes 786436
  5.5 88.2 %collective-permute-start = (bf16[128,256]{0,1:T(8,128)(2,1)}, bf16[128,256]{0,1:T(8,128)(2,1)}, u32[]{:S(2)}, u32[]{:S(2)}) collective-permute-start(bf16[128,256]{0,1:T(8,128)(2,1)} %bitcast.19), channel_id=1, source_target_pairs={{0,4},{4,8},{8,12},{12,16},{16,20},{20,24},{24,28},{1,5},{5,9},{9,... | collective-permute-start | bytes 196616 | tf_op jit(solution)/shard_map/ppermute | solution.py:18
  10.9 87.5 %collective-permute-start.1 = (bf16[128,256]{1,0:T(8,128)(2,1)}, bf16[128,256]{1,0:T(8,128)(2,1)}, u32[]{:S(2)}, u32[]{:S(2)}) collective-permute-start(bf16[128,256]{1,0:T(8,128)(2,1)} %param.10), channel_id=1, source_target_pairs={{0,4},{4,8},{8,12},{12,16},{16,20},{20,24},{24,28},{1,5},{5,9},{9,... | collective-permute-start | bytes 196616 | tf_op jit(solution)/shard_map/ppermute | solution.py:18
  14.5 4.4 %copy-start.7 = (bf16[64,256]{1,0:T(8,128)(2,1)S(1)}, bf16[64,256]{1,0:T(8,128)(2,1)}, u32[]{:S(2)}) copy-start(bf16[64,256]{1,0:T(8,128)(2,1)} %param.11) | copy-start | bytes 98308
  15.2 38.1 %all-to-all-start = ((bf16[4,32,256]{2,1,0:T(8,128)(2,1)}), bf16[4,32,256]{2,1,0:T(8,128)(2,1)S(1)}, u32[]{:S(2)}, u32[]{:S(2)}) async-start(bf16[4,32,256]{2,1,0:T(8,128)(2,1)} %convert_element_type.70), calls=%async_computation | async-start | bytes 131072 | tf_op jit(solution)/shard_map/all_to_all | solution.py:137
  18.6 31.6 %copy-start.8 = (s32[8]{0:T(128)S(1)}, s32[8]{0:T(128)}, u32[]{:S(2)}) copy-start(s32[8]{0:T(128)} %param.15) | copy-start | bytes 100
  53.3 0.6 copy-start.4
  53.9 38.2 %all-to-all-start.1 = ((bf16[4,32,256]{2,1,0:T(8,128)(2,1)}), bf16[4,32,256]{2,1,0:T(8,128)(2,1)}, u32[]{:S(2)}, u32[]{:S(2)}) async-start(bf16[4,32,256]{2,1,0:T(8,128)(2,1)} %bitcast.29), calls=%async_computation.1 | async-start | bytes 131072 | tf_op jit(solution)/shard_map/all_to_all | solution.py:138
  94.9 2.0 %copy-start = (f32[128,2,4,128]{0,3,2,1:T(8,128)}, f32[128,2,4,128]{0,3,2,1:T(8,128)S(1)}, u32[]{:S(2)}) copy-start(f32[128,2,4,128]{0,3,2,1:T(8,128)S(1)} %get-tuple-element.72) | copy-start | bytes 1572868
  94.9 1.8 %copy-start.5 = (pred[128,128]{0,1:T(8,128)(4,1)S(1)}, pred[128,128]{0,1:T(8,128)(4,1)}, u32[]{:S(2)}) copy-start(pred[128,128]{0,1:T(8,128)(4,1)} %get-tuple-element.67) | copy-start | bytes 49156
  95.7 1.1 %copy-start.6 = (f32[128,2,4]{0,2,1:T(4,128)S(1)}, f32[128,2,4]{0,2,1:T(4,128)}, u32[]{:S(2)}) copy-start(f32[128,2,4]{0,2,1:T(4,128)} %get-tuple-element.75) | copy-start | bytes 12292
  95.7 1.1 %copy-start.3 = (bf16[512,256]{0,1:T(8,128)(2,1)S(1)}, bf16[512,256]{0,1:T(8,128)(2,1)}, u32[]{:S(2)}) copy-start(bf16[512,256]{0,1:T(8,128)(2,1)} %copy.100) | copy-start | bytes 786436
  96.9 2.6 %copy-start.1 = (f32[128,2,4,128]{0,3,2,1:T(8,128)S(1)}, f32[128,2,4,128]{0,3,2,1:T(8,128)}, u32[]{:S(2)}) copy-start(f32[128,2,4,128]{0,3,2,1:T(8,128)} %copy-done) | copy-start | bytes 1572868
where the time goes:
time: 102 us
  blocking collectives  62 us (61%)
  starting transfers between devices  16.1 us (16%)
  local copies, waits for them, and re-layouts  11.1 us (11%)
  matrix products  6.46 us (6%)
  other arithmetic  5.01 us (5%)
    all_gather x1, blocking collectives, body(): values = lax.all_gather(prefix_values, 'seq', axis=0, tiled=True)  31 us
    all_gather x1, blocking collectives, body(): keys = lax.all_gather(prefix_keys, 'seq', axis=0, tiled=True)  31 us
    ppermute x2, starting transfers between devices, from_behind(): return lax.ppermute(array, axis, pairs)  8.92 us
    all_to_all x1, starting transfers between devices, body(): lax.all_to_all(suffix_values, 'tp', split_axis=0, concat_axis=1, tiled=True)  3.89 us
    dot_general x3, matrix products, update(): jnp.einsum('bgrd,kgd->bgrk', q_rot, keys_split, preferred_element_type=jn...  3.34 us
    all_to_all x1, starting transfers between devices, body(): lax.all_to_all(k_rot, 'tp', split_axis=0, concat_axis=1, tiled=True)  3.28 us
    dot_general x3, matrix products, update(): jnp.einsum('bgrk,kgd->bgrd', weights.astype(jnp.bfloat16), values_split,...  3.12 us
    unnamed x23, local copies, waits for them, and re-layouts  2.76 us
  transfers between devices with their start and end apart: 4, of which 0 were waited for; matrix products, arithmetic and copies ran while one was open for 14% of the time, Pallas kernels for 0%

commit v1 on v0

v1 whole, which is shorter than its diff:
```python
import math

import jax
import jax.numpy as jnp
from jax import lax
from jax.sharding import PartitionSpec as P

HD = 128
GROUPS = 4


BIG_NEGATIVE = -1e30


def rotate(values, position):
    half = values.shape[-1] // 2
    freq = jnp.exp(
        jnp.arange(half, dtype=jnp.float32) * (-2.0 * math.log(500000.0) / values.shape[-1])
    )
    angle = position.astype(jnp.float32)[:, None] * freq[None, :]
    cosine = jnp.cos(angle)[:, None, :]
    sine = jnp.sin(angle)[:, None, :]
    floats = values.astype(jnp.float32)
    lower = floats[..., :half]
    upper = floats[..., half:]
    return jnp.concatenate(
        [lower * cosine - upper * sine, upper * cosine + lower * sine], axis=-1
    ).astype(jnp.bfloat16)


def token_info(index, suffix_lengths, request_group):
    ends = jnp.cumsum(suffix_lengths)
    request = jnp.sum((index[:, None] >= ends[None, :]).astype(jnp.int32), axis=1)
    onehot = request[:, None] == jnp.arange(suffix_lengths.shape[0], dtype=jnp.int32)[None, :]
    first = jnp.sum(jnp.where(onehot, (ends - suffix_lengths)[None, :], 0), axis=1)
    group = jnp.sum(jnp.where(onehot, request_group[None, :], 0), axis=1)
    return (request, index - first, group)


def shifted(array, axis, by, wrap):
    length = lax.axis_size(axis)
    pairs = [(i, (i + by) % length) for i in range(length) if wrap or i + by < length]
    return lax.ppermute(array, axis, pairs)


def body(
    queries,
    suffix_keys,
    suffix_values,
    prefix_keys,
    prefix_values,
    suffix_lengths,
    request_group,
    block_group,
):
    rows = queries.shape[0]
    kv_cols = suffix_keys.shape[1]
    kv_heads = kv_cols // HD
    q_heads = queries.shape[1] // HD
    repeat = q_heads // kv_heads
    devices = lax.axis_size("seq")
    me = lax.axis_index("seq")
    block_rows = prefix_keys.shape[0]
    prefix_len = block_rows * devices // GROUPS
    span = max(1, min(2048 // rows, devices // 8))
    scale = HD ** (-0.5)
    index = me * rows + jnp.arange(rows, dtype=jnp.int32)
    request, offset, group = token_info(index, suffix_lengths, request_group)

    prefix_kv = jnp.concatenate([prefix_keys, prefix_values], axis=1)
    suffix_kv = jnp.concatenate([suffix_keys, suffix_values], axis=1)

    prefix_parts = []
    suffix_parts = [(0, suffix_kv)]
    if devices <= 16:
        prefix_parts.append((me, prefix_kv))
        for by in range(1, devices):
            if by <= span:
                both = shifted(jnp.concatenate([prefix_kv, suffix_kv], axis=0), "seq", by, True)
                prefix_parts.append(((me - by) % devices, both[:block_rows]))
                suffix_parts.append((by, both[block_rows:]))
            else:
                part = shifted(prefix_kv, "seq", by, True)
                prefix_parts.append(((me - by) % devices, part))
    else:
        gathered = lax.all_gather(prefix_kv, "seq", axis=0, tiled=True)
        prefix_parts.append((None, gathered))
        for by in range(1, span + 1):
            suffix_parts.append((by, shifted(suffix_kv, "seq", by, False)))

    position = offset + prefix_len
    q_rot = rotate(queries.reshape(rows, q_heads, HD), position).reshape(rows, kv_heads, repeat, HD)

    key_chunks, value_chunks, visible_chunks = [], [], []
    for holder, kv in prefix_parts:
        count = kv.shape[0]
        if holder is None:
            holder_index = jnp.arange(count, dtype=jnp.int32) // block_rows
            row_group = jnp.take(block_group, holder_index)
            visible = row_group[None, :] == group[:, None]
        else:
            row_group = lax.dynamic_index_in_dim(block_group, holder, keepdims=False)
            visible = jnp.broadcast_to((group == row_group)[:, None], (rows, count))
        key_chunks.append(kv[:, :kv_cols])
        value_chunks.append(kv[:, kv_cols:])
        visible_chunks.append(visible)

    own_k_rot = None
    for back, kv in suffix_parts:
        key_index = (me - back) * rows + jnp.arange(rows, dtype=jnp.int32)
        key_request, key_offset, _ = token_info(key_index, suffix_lengths, request_group)
        k_rot = rotate(kv[:, :kv_cols].reshape(rows, kv_heads, HD), key_offset + prefix_len).reshape(
            rows, kv_cols
        )
        if back == 0:
            own_k_rot = k_rot
        visible = (
            (key_index[None, :] >= 0)
            & (key_request[None, :] == request[:, None])
            & (key_index[None, :] <= index[:, None])
        )
        key_chunks.append(k_rot)
        value_chunks.append(kv[:, kv_cols:])
        visible_chunks.append(visible)

    cache = lax.all_to_all(
        jnp.stack([own_k_rot, suffix_values], axis=0), "tp", split_axis=1, concat_axis=2, tiled=True
    )

    def scores_of(keys, visible):
        keys_split = keys.reshape(keys.shape[0], kv_heads, HD)
        scores = (
            jnp.einsum("bgrd,kgd->bgrk", q_rot, keys_split, preferred_element_type=jnp.float32)
            * scale
        )
        return jnp.where(visible[:, None, None, :], scores, BIG_NEGATIVE)

    def summed_of(scores, high, values, visible):
        weights = jnp.where(visible[:, None, None, :], jnp.exp(scores - high[..., None]), 0.0)
        summed = jnp.einsum(
            "bgrk,kgd->bgrd",
            weights.astype(jnp.bfloat16),
            values.reshape(values.shape[0], kv_heads, HD),
            preferred_element_type=jnp.float32,
        )
        return jnp.sum(weights, axis=-1), summed

    keys = jnp.concatenate(key_chunks, axis=0)
    values = jnp.concatenate(value_chunks, axis=0)
    visible = jnp.concatenate(visible_chunks, axis=1)
    count = keys.shape[0]
    if count * rows * q_heads * 4 <= (8 << 20):
        scores = scores_of(keys, visible)
        high = jnp.max(scores, axis=-1)
        total, summed = summed_of(scores, high, values, visible)
    else:
        width = 512
        steps = count // width
        tail = steps * width
        piece_k = keys[:tail].reshape(steps, width, kv_cols)
        piece_v = values[:tail].reshape(steps, width, kv_cols)
        piece_m = jnp.moveaxis(visible[:, :tail].reshape(rows, steps, width), 1, 0)

        def high_step(high, piece):
            k, m = piece
            return jnp.maximum(high, jnp.max(scores_of(k, m), axis=-1)), None

        high = jnp.max(scores_of(keys[tail:], visible[:, tail:]), axis=-1)
        high, _ = lax.scan(high_step, high, (piece_k, piece_m))

        def sum_step(carry, piece):
            k, v, m = piece
            total, summed = summed_of(scores_of(k, m), high, v, m)
            return (carry[0] + total, carry[1] + summed), None

        start = summed_of(scores_of(keys[tail:], visible[:, tail:]), high, values[tail:], visible[:, tail:])
        (total, summed), _ = lax.scan(sum_step, start, (piece_k, piece_v, piece_m))
    attended = (summed / total[..., None]).reshape(rows, q_heads * HD).astype(jnp.bfloat16)
    return (attended, cache[0], cache[1])


def solution(mesh):
    return jax.shard_map(
        body,
        mesh=mesh,
        in_specs=(
            P("seq", "tp"),
            P("seq", "tp"),
            P("seq", "tp"),
            P("seq", "tp"),
            P("seq", "tp"),
            P(),
            P(),
            P(),
        ),
        out_specs=(P("seq", "tp"), P(("seq", "tp"), None), P(("seq", "tp"), None)),
        check_vma=False,
    )
```

time: 102 us -> 54 us (0.53)
  blocking collectives: 62 us -> 0 us
  waiting for transfers between devices: 0.01 us -> 8.59 us
  other arithmetic: 5.01 us -> 12.1 us
  matrix products: 6.46 us -> 2.44 us
    all_gather x2 -> x0, blocking collectives: 62 us -> none  [the longest x1 31 us: body(): values = lax.all_gather(prefix_values, 'seq', axis=0, tiled=True)]
    ppermute x2 -> x7, waiting for transfers between devices: 0.01 us -> 8.58 us  [shifted(): return lax.ppermute(array, axis, pairs)]
    eq x1, other arithmetic: 0.11 us -> 5.06 us  [body(): visible = jnp.broadcast_to((group == row_group)[:, None], (rows, count))]
    ppermute x2 -> x7, starting transfers between devices: 8.92 us -> 13.8 us  [shifted(): return lax.ppermute(array, axis, pairs)]
    unnamed x23 -> x28, local copies, waits for them, and re-layouts: 2.76 us -> 7.21 us
    dot_general x6 -> x2, matrix products: 6.46 us -> 2.44 us  [the longest x1 1.79 us: summed_of(): jnp.einsum('bgrk,kgd->bgrd', weights.astype(jnp.bfloat16), values.reshape...]
    all_to_all x2 -> x1, starting transfers between devices: 7.18 us -> 3.32 us  [body(): lax.all_to_all(jnp.stack([own_k_rot, suffix_values], axis=0), 'tp', split...]
    all_to_all x2 -> x1, local copies, waits for them, and re-layouts: 2.95 us -> 0.02 us  [body(): lax.all_to_all(jnp.stack([own_k_rot, suffix_values], axis=0), 'tp', split...]
  transfers between devices with their start and end apart: 4 -> 8, of which waited for: 0 -> 2; matrix products, arithmetic and copies ran while one was open for 14% -> 41% of each run, Pallas kernels for 0% -> 0%
where the time goes in v1:
time: 54 us; the launch traced here: 53.3 us
  starting transfers between devices  17.1 us (32%)
  other arithmetic  12.1 us (22%)
  local copies, waits for them, and re-layouts  11.9 us (22%)
  waiting for transfers between devices  8.59 us (16%)
  matrix products  2.44 us (5%)
  between operations  1.1 us (2%)
    ppermute x7, starting transfers between devices, shifted(): return lax.ppermute(array, axis, pairs)  13.8 us
    ppermute x7, waiting for transfers between devices, shifted(): return lax.ppermute(array, axis, pairs)  8.58 us
    unnamed x28, local copies, waits for them, and re-layouts  7.21 us
    eq x1, other arithmetic, body(): visible = jnp.broadcast_to((group == row_group)[:, None], (rows, count))  5.06 us
    all_to_all x1, starting transfers between devices, body(): lax.all_to_all(jnp.stack([own_k_rot, suffix_values], axis=0), 'tp', split...  3.32 us
    sub x1, other arithmetic, summed_of(): scores - high[..., None]  2.87 us
    dot_general x1, matrix products, summed_of(): jnp.einsum('bgrk,kgd->bgrd', weights.astype(jnp.bfloat16), values.reshape...  1.79 us
    dynamic_slice x1, local copies, waits for them, and re-layouts, body(): row_group = lax.dynamic_index_in_dim(block_group, holder, keepdims=False)  1.65 us
  transfers between devices with their start and end apart: 8, of which 2 were waited for; matrix products, arithmetic and copies ran while one was open for 41% of the time, Pallas kernels for 0%

profile of v1, /device:TPU:0, one launch (start us, length us, event | category | flops | bytes accessed | tf_op | source)
XLA Modules:
  0.0 53.3 jit_solution(17495478784341974166)
XLA Ops:
  0.6 0.9 %copy.164 = bf16[64,256]{0,1:T(8,128)(2,1)S(1)} copy(bf16[64,256]{1,0:T(8,128)(2,1)} %param.12) | data formatting | bytes 65536 | tf_op args[4]
  1.5 0.9 %copy.160 = bf16[64,256]{0,1:T(8,128)(2,1)S(1)} copy(bf16[64,256]{1,0:T(8,128)(2,1)} %param.11) | data formatting | bytes 65536 | tf_op args[3]
  2.4 5.1 %collective-permute-start.5 = (bf16[64,512]{0,1:T(8,128)(2,1)S(1)}, bf16[64,512]{0,1:T(8,128)(2,1)S(1)}, u32[]{:S(2)}, u32[]{:S(2)}) collective-permute-start(bf16[64,512]{0,1:T(8,128)(2,1)S(1)} %pad_maximum_fusion), channel_id=1, source_target_pairs={{0,24},{4,28},{8,0},{12,4},{16,8},{20,12},{24,16},{28,20},{1,25},{... | collective-permute-start | bytes 196616 | tf_op jit(solution)/shard_map/ppermute | solution.py:43
  7.9 3.5 %collective-permute-start.3 = (bf16[64,512]{0,1:T(8,128)(2,1)S(1)}, bf16[64,512]{0,1:T(8,128)(2,1)S(1)}, u32[]{:S(2)}, u32[]{:S(2)}) collective-permute-start(bf16[64,512]{0,1:T(8,128)(2,1)S(1)} %pad_maximum_fusion), channel_id=1, source_target_pairs={{0,16},{4,20},{8,24},{12,28},{16,0},{20,4},{24,8},{28,12},{1,17},{... | collective-permute-start | bytes 196616 | tf_op jit(solution)/shard_map/ppermute | solution.py:43
  11.4 1.0 %collective-permute-start.1 = (bf16[64,512]{0,1:T(8,128)(2,1)S(1)}, bf16[64,512]{0,1:T(8,128)(2,1)S(1)}, u32[]{:S(2)}, u32[]{:S(2)}) collective-permute-start(bf16[64,512]{0,1:T(8,128)(2,1)S(1)} %pad_maximum_fusion), channel_id=1, source_target_pairs={{0,8},{4,12},{8,16},{12,20},{16,24},{20,28},{24,0},{28,4},{1,9},{5... | collective-permute-start | bytes 196616 | tf_op jit(solution)/shard_map/ppermute | solution.py:43
  12.4 0.8 %constant_dynamic-update-slice_fusion.16 = bf16[768,2,128]{2,0,1:T(8,128)(2,1)S(1)} fusion(bf16[64,256]{1,0:T(8,128)(2,1)} %param.11), kind=kLoop, calls=%fused_computation.51 | loop fusion | bytes 65536
  13.2 0.7 %copy.166 = s32[24,1]{1,0:T(8,128)S(1)} copy(s32[24,1]{0,1:T(1,128)} %bitcast.92) | data formatting | bytes 192 | tf_op jit(solution)/shard_map/reshape.225
  14.1 0.7 %sub.66 = s32[24]{0:T(128)S(1)} subtract(s32[24]{0:T(128)S(1)} %reduce, s32[24]{0:T(128)} %param.13) | non-fusion elementwise | flops 24 | bytes 288 | tf_op jit(solution)/shard_map/sub | solution.py:35
  14.8 0.7 %select_reduce_fusion.2 = (s32[128]{0:T(128)S(1)}, s32[128]{0:T(128)S(1)}, s32[128]{0:T(128)S(1)}) fusion(s32[24]{0:T(128)} %param.14, s32[128]{0:T(128)S(1)} %get-tuple-element.25, s32[24]{0:T(128)S(1)} %sub.66, s32[128]{0:T(128)S(1)} %get-tuple-element.24), kind=kLoop, calls=%fused_computation.56 | loop fusion | flops 24192 | bytes 2752 | tf_op jit(solution)/shard_map/reduce_sum | solution.py:36
  15.6 1.0 %copy.163 = bf16[128,256]{0,1:T(8,128)(2,1)S(1)} copy(bf16[128,256]{1,0:T(8,128)(2,1)} %param.10) | data formatting | bytes 131072 | tf_op args[2]
  16.5 1.0 %copy.162 = bf16[128,256]{0,1:T(8,128)(2,1)S(1)} copy(bf16[128,256]{1,0:T(8,128)(2,1)} %param.9) | data formatting | bytes 131072 | tf_op args[1]
  17.5 1.7 %fusion.36 = (s32[1]{0:T(128)}, s32[1]{0:T(128)}, s32[1]{0:T(128)}, s32[1]{0:T(128)}, s32[1]{0:T(128)}, /*index=5*/s32[1]{0:T(128)}, s32[1]{0:T(128)}, s32[1]{0:T(128)}) fusion(s32[8]{0:T(128)} %param.15, s32[]{:T(128)S(6)} %select_n.89, s32[]{:T(128)S(6)} %select_n.85, s32[]{:T(128)S(6)} %select_n.83, s32[]{:T(128)S(6)} %select_n.81, s32[]{:T(128)S(6)} %select_n.79, ...), kind=kLoop, calls=%fused_computation.89 | loop fusion | bytes 96 | tf_op jit(solution)/shard_map/jit(dynamic_index_in_dim)/dynamic_slice | solution.py:102
  19.2 5.1 %broadcast_compare_fusion.2 = (pred[128]{0:T(512)(128)(4,1)S(1)}, pred[128]{0:T(512)(128)(4,1)S(1)}, pred[128]{0:T(512)(128)(4,1)S(1)}, pred[128]{0:T(512)(128)(...) fusion(s32[128]{0:T(128)S(1)} %get-tuple-element.21, ...), kind=kLoop, calls=%fused_computation.66 | loop fusion | flops 1024 | bytes 1568 | tf_op jit(solution)/shard_map/eq | solution.py:103
  24.5 1.0 %convert_bitcast_fusion = f32[16,8,8,128]{3,1,2,0:T(8,128)S(1)} fusion(bf16[128,1024]{1,0:T(8,128)(2,1)} %param.8), kind=kLoop, calls=%fused_computation.12 | loop fusion | flops 131072 | bytes 786432
  27.2 3.8 %collective-permute-start.6 = (bf16[64,512]{0,1:T(8,128)(2,1)S(1)}, bf16[64,512]{0,1:T(8,128)(2,1)S(1)}, u32[]{:S(2)}, u32[]{:S(2)}) collective-permute-start(bf16[64,512]{0,1:T(8,128)(2,1)S(1)} %pad_maximum_fusion), channel_id=1, source_target_pairs={{0,28},{4,0},{8,4},{12,8},{16,12},{20,16},{24,20},{28,24},{1,29},{... | collective-permute-start | bytes 196616 | tf_op jit(solution)/shard_map/ppermute | solution.py:43
  31.7 1.8 %collective-permute-done.6 = bf16[64,512]{0,1:T(8,128)(2,1)S(1)} collective-permute-done((bf16[64,512]{0,1:T(8,128)(2,1)S(1)}, bf16[64,512]{0,1:T(8,128)(2,1)S(1)}, u32[]{:S(2)}, u32[]{:S(2)}) %collective-permute-start.6) | collective-permute-done | bytes 65568 | tf_op jit(solution)/shard_map/ppermute | solution.py:43
  33.6 6.8 %collective-permute-done = bf16[192,512]{0,1:T(8,128)(2,1)S(1)} collective-permute-done((bf16[192,512]{0,1:T(8,128)(2,1)S(1)}, bf16[192,512]{0,1:T(8,128)(2,1)S(1)}, u32[]{:S(2)}, u32[]{:S(2)}) %collective-permute-start) | collective-permute-done | bytes 196640 | tf_op jit(solution)/shard_map/ppermute | solution.py:43
  41.2 0.8 %copy.192 = bf16[2,128,256]{2,0,1:T(2,128)(2,1)} copy(bf16[2,128,256]{1,2,0:T(8,128)(2,1)S(1)} %pad_maximum_fusion.1) | data formatting | bytes 262144 | tf_op jit(solution)/shard_map/stack | solution.py:127
  42.0 3.3 %all-to-all-start = ((bf16[2,128,256]{2,0,1:T(2,128)(2,1)}), bf16[2,128,256]{2,0,1:T(2,128)(2,1)S(1)}, u32[]{:S(2)}, u32[]{:S(2)}) async-start(bf16[2,128,256]{2,0,1:T(2,128)(2,1)} %copy.192), calls=%async_computation | async-start | bytes 262144 | tf_op jit(solution)/shard_map/all_to_all | solution.py:126
  45.5 0.7 %fusion.16 = f32[2,768,128,4]{2,1,3,0:T(8,128)S(1)} fusion(bf16[768,2,128]{2,0,1:T(8,128)(2,1)S(1)} %maximum_dynamic-update-slice_fusion, bf16[128,2,4,64]{3,0,2,1:T(8,128)(2,1)S(1)} %bitcast.73, bf16[128,2,4,64]{3,0,2,1:T(8,128)(2,1)S(1)} %bitcast.72), kind=kOutput, calls=%fused_computation.15 | convolution fusion | flops 201850880 | bytes 3801088 | tf_op jit(solution)/shard_map/bgrd,kgd->bgrk/dot_general | solution.py:133
  46.1 2.9 %fusion.37 = (f32[128,2,4]{0,2,1:T(4,128)S(1)}, bf16[128,2,4,768]{0,3,2,1:T(8,128)(2,1)}) fusion(f32[2,768,128,4]{2,1,3,0:T(8,128)S(1)} %fusion.16, pred[128,768]{0,1:T(8,128)(4,1)S(1)} %and_dynamic-update-slice_fusion), kind=kOutput, calls=%fused_computation.90 | output fusion | flops 6292223 | bytes 4820992 | tf_op jit(solution)/shard_map/sub | solution.py:139
  49.2 1.8 %fusion.13 = bf16[128,2,4,128]{0,3,2,1:T(8,128)(2,1)S(1)} fusion(bf16[768,2,128,1]{0,2,3,1:T(8,128)(2,1)S(1)} %bitcast.78, bf16[128,2,4,768]{0,3,2,1:T(8,128)(2,1)} %get-tuple-element.81, f32[128,2,4]{0,2,1:T(4,128)S(1)} %get-tuple-element.80), kind=kOutput, calls=%fused_computation.11 | convolution fusion | flops 201588736 | bytes 2232320 | tf_op jit(solution)/shard_map/bgrk,kgd->bgrd/dot_general | solution.py:140
  51.0 0.8 %copy.196 = bf16[128,1024]{1,0:T(8,128)(2,1)} copy(bf16[128,1024]{0,1:T(8,128)(2,1)S(1)} %bitcast.79) | data formatting | bytes 524288
  52.0 0.6 %copy.223 = bf16[4,8,4,256]{3,1,2,0:T(8,128)(2,1)} copy(bf16[4,8,4,256]{3,2,1,0:T(4,128)(2,1)S(1)} %bitcast.80) | data formatting | bytes 131072
  (74 shorter events, 5.1 us)
Async XLA Ops:
  2.4 24.7 %collective-permute-start.5 = (bf16[64,512]{0,1:T(8,128)(2,1)S(1)}, bf16[64,512]{0,1:T(8,128)(2,1)S(1)}, u32[]{:S(2)}, u32[]{:S(2)}) collective-permute-start(bf16[64,512]{0,1:T(8,128)(2,1)S(1)} %pad_maximum_fusion), channel_id=1, source_target_pairs={{0,24},{4,28},{8,0},{12,4},{16,8},{20,12},{24,16},{28,20},{1,25},{... | collective-permute-start | bytes 196616 | tf_op jit(solution)/shard_map/ppermute | solution.py:43
  7.5 23.4 %collective-permute-start.4 = (bf16[64,512]{0,1:T(8,128)(2,1)S(1)}, bf16[64,512]{0,1:T(8,128)(2,1)S(1)}, u32[]{:S(2)}, u32[]{:S(2)}) collective-permute-start(bf16[64,512]{0,1:T(8,128)(2,1)S(1)} %pad_maximum_fusion), channel_id=1, source_target_pairs={{0,20},{4,24},{8,28},{12,0},{16,4},{20,8},{24,12},{28,16},{1,21},{... | collective-permute-start | bytes 196616 | tf_op jit(solution)/shard_map/ppermute | solution.py:43
  7.9 23.2 %collective-permute-start.3 = (bf16[64,512]{0,1:T(8,128)(2,1)S(1)}, bf16[64,512]{0,1:T(8,128)(2,1)S(1)}, u32[]{:S(2)}, u32[]{:S(2)}) collective-permute-start(bf16[64,512]{0,1:T(8,128)(2,1)S(1)} %pad_maximum_fusion), channel_id=1, source_target_pairs={{0,16},{4,20},{8,24},{12,28},{16,0},{20,4},{24,8},{28,12},{1,17},{... | collective-permute-start | bytes 196616 | tf_op jit(solution)/shard_map/ppermute | solution.py:43
  11.4 19.7 %collective-permute-start.2 = (bf16[64,512]{0,1:T(8,128)(2,1)S(1)}, bf16[64,512]{0,1:T(8,128)(2,1)S(1)}, u32[]{:S(2)}, u32[]{:S(2)}) collective-permute-start(bf16[64,512]{0,1:T(8,128)(2,1)S(1)} %pad_maximum_fusion), channel_id=1, source_target_pairs={{0,12},{4,16},{8,20},{12,24},{16,28},{20,0},{24,4},{28,8},{1,13},{... | collective-permute-start | bytes 196616 | tf_op jit(solution)/shard_map/ppermute | solution.py:43
  11.4 19.7 %collective-permute-start.1 = (bf16[64,512]{0,1:T(8,128)(2,1)S(1)}, bf16[64,512]{0,1:T(8,128)(2,1)S(1)}, u32[]{:S(2)}, u32[]{:S(2)}) collective-permute-start(bf16[64,512]{0,1:T(8,128)(2,1)S(1)} %pad_maximum_fusion), channel_id=1, source_target_pairs={{0,8},{4,12},{8,16},{12,20},{16,24},{20,28},{24,0},{28,4},{1,9},{5... | collective-permute-start | bytes 196616 | tf_op jit(solution)/shard_map/ppermute | solution.py:43
  27.2 6.3 %collective-permute-start.6 = (bf16[64,512]{0,1:T(8,128)(2,1)S(1)}, bf16[64,512]{0,1:T(8,128)(2,1)S(1)}, u32[]{:S(2)}, u32[]{:S(2)}) collective-permute-start(bf16[64,512]{0,1:T(8,128)(2,1)S(1)} %pad_maximum_fusion), channel_id=1, source_target_pairs={{0,28},{4,0},{8,4},{12,8},{16,12},{20,16},{24,20},{28,24},{1,29},{... | collective-permute-start | bytes 196616 | tf_op jit(solution)/shard_map/ppermute | solution.py:43
  31.0 9.4 %collective-permute-start = (bf16[192,512]{0,1:T(8,128)(2,1)S(1)}, bf16[192,512]{0,1:T(8,128)(2,1)S(1)}, u32[]{:S(2)}, u32[]{:S(2)}) collective-permute-start(bf16[192,512]{0,1:T(8,128)(2,1)S(1)} %maximum_maximum_fusion), channel_id=1, source_target_pairs={{0,4},{4,8},{8,12},{12,16},{16,20},{20,24},{24,28},{28,0},{1,5},{5... | collective-permute-start | bytes 589832 | tf_op jit(solution)/shard_map/ppermute | solution.py:43
  42.0 9.9 %all-to-all-start = ((bf16[2,128,256]{2,0,1:T(2,128)(2,1)}), bf16[2,128,256]{2,0,1:T(2,128)(2,1)S(1)}, u32[]{:S(2)}, u32[]{:S(2)}) async-start(bf16[2,128,256]{2,0,1:T(2,128)(2,1)} %copy.192), calls=%async_computation | async-start | bytes 262144 | tf_op jit(solution)/shard_map/all_to_all | solution.py:126

commit v2 on v1

--- a/solution.py
+++ b/solution.py
@@ -1,8 +1,11 @@
+import functools
 import math
 
 import jax
 import jax.numpy as jnp
 from jax import lax
+from jax.experimental import pallas as pl
+from jax.experimental.pallas import tpu as pltpu
 from jax.sharding import PartitionSpec as P
 
 HD = 128
@@ -26,6 +29,60 @@
     return jnp.concatenate(
         [lower * cosine - upper * sine, upper * cosine + lower * sine], axis=-1
     ).astype(jnp.bfloat16)
+
+
+def attend_kernel(pieces, q_heads, repeat, scale, *refs):
+    q_ref, cq_ref, sq_ref, tok_ref, key_ref = refs[:5]
+    data = refs[5 : len(refs) - 3]
+    out_ref, kscr, vscr = refs[len(refs) - 3 :]
+    at = 0
+    for k_at, k_row, k_col, v_at, v_row, v_col, count in pieces:
+        kscr[at : at + count, :] = data[k_at][k_row : k_row + count, k_col : k_col + kscr.shape[1]]
+        vscr[at : at + count, :] = data[v_at][v_row : v_row + count, v_col : v_col + vscr.shape[1]]
+        at += count
+    tok = tok_ref[...]
+    keym = key_ref[...]
+    visible = (keym[0:1, :] == tok[:, 1:2]) | (
+        (keym[1:2, :] == tok[:, 0:1]) & (keym[2:3, :] <= tok[:, 2:3])
+    )
+    cq = cq_ref[...]
+    sq = sq_ref[...]
+    for h in range(q_heads):
+        g = h // repeat
+        x = q_ref[:, h * HD : (h + 1) * HD].astype(jnp.float32)
+        q = (x * cq + pltpu.roll(x, HD // 2, 1) * sq).astype(jnp.bfloat16)
+        k = kscr[:, g * HD : (g + 1) * HD]
+        scores = lax.dot_general(
+            q, k, (((1,), (1,)), ((), ())), preferred_element_type=jnp.float32
+        ) * scale
+        scores = jnp.where(visible, scores, BIG_NEGATIVE)
+        high = jnp.max(scores, axis=1, keepdims=True)
+        weights = jnp.where(visible, jnp.exp(scores - high), 0.0)
+        total = jnp.sum(weights, axis=1, keepdims=True)
+        v = vscr[:, g * HD : (g + 1) * HD]
+        summed = jnp.dot(weights.astype(jnp.bfloat16), v, preferred_element_type=jnp.float32)
+        out_ref[:, h * HD : (h + 1) * HD] = (summed / total).astype(out_ref.dtype)
+
+
+def attend(queries, cq, sq, tok, keym, data, pieces, kv_cols, repeat, scale):
+    rows = queries.shape[0]
+    q_heads = queries.shape[1] // HD
+    count = keym.shape[1]
+    flops = 4 * rows * count * HD * q_heads
+    nbytes = sum(a.size * a.dtype.itemsize for a in [queries, cq, sq, tok, keym, *data])
+    return pl.pallas_call(
+        functools.partial(attend_kernel, tuple(pieces), q_heads, repeat, scale),
+        out_shape=jax.ShapeDtypeStruct(queries.shape, jnp.bfloat16),
+        scratch_shapes=[
+            pltpu.VMEM((count, kv_cols), jnp.bfloat16),
+            pltpu.VMEM((count, kv_cols), jnp.bfloat16),
+        ],
+        cost_estimate=pl.CostEstimate(
+            flops=flops,
+            transcendentals=rows * count * q_heads,
+            bytes_accessed=nbytes + queries.size * 2,
+        ),
+    )(queries, cq, sq, tok, keym, *data)
 
 
 def token_info(index, suffix_lengths, request_group):
@@ -70,23 +127,67 @@
     prefix_kv = jnp.concatenate([prefix_keys, prefix_values], axis=1)
     suffix_kv = jnp.concatenate([suffix_keys, suffix_values], axis=1)
 
+    def rotated_keys(raw, back):
+        key_index = (me - back) * rows + jnp.arange(rows, dtype=jnp.int32)
+        key_request, key_offset, _ = token_info(key_index, suffix_lengths, request_group)
+        k_rot = rotate(raw.reshape(rows, kv_heads, HD), key_offset + prefix_len).reshape(rows, kv_cols)
+        return key_index, key_request, k_rot
+
+    if devices <= 16:
+        own_index, own_request, own_k_rot = rotated_keys(suffix_keys, 0)
+        cache = lax.all_to_all(
+            jnp.stack([own_k_rot, suffix_values], axis=0), "tp", split_axis=1, concat_axis=2, tiled=True
+        )
+        data = [prefix_kv]
+        pieces = [(0, 0, 0, 0, 0, kv_cols, block_rows)]
+        groups = [jnp.broadcast_to(lax.dynamic_index_in_dim(block_group, me, keepdims=False), (block_rows,))]
+        tails = []
+        for by in range(1, devices):
+            if by <= span:
+                part = shifted(jnp.concatenate([prefix_kv, suffix_kv], axis=0), "seq", by, True)
+                key_index, key_request, k_rot = rotated_keys(part[block_rows:, :kv_cols], by)
+                tails.append((len(data), k_rot, key_index, key_request))
+            else:
+                part = shifted(prefix_kv, "seq", by, True)
+            data.append(part)
+            pieces.append((len(data) - 1, 0, 0, len(data) - 1, 0, kv_cols, block_rows))
+            holder = (me - by) % devices
+            groups.append(jnp.broadcast_to(lax.dynamic_index_in_dim(block_group, holder, keepdims=False), (block_rows,)))
+        data.append(own_k_rot)
+        data.append(suffix_values)
+        pieces.append((len(data) - 2, 0, 0, len(data) - 1, 0, 0, rows))
+        requests = [jnp.full((block_rows * devices,), -2, jnp.int32), own_request]
+        indices = [jnp.zeros((block_rows * devices,), jnp.int32), own_index]
+        for at, k_rot, key_index, key_request in tails:
+            data.append(k_rot)
+            pieces.append((len(data) - 1, 0, 0, at, block_rows, kv_cols, rows))
+            requests.append(jnp.where(key_index >= 0, key_request, -2))
+            indices.append(key_index)
+        suffix_count = rows * (1 + len(tails))
+        groups.append(jnp.full((suffix_count,), -1, jnp.int32))
+        keym = jnp.stack(
+            [jnp.concatenate(groups), jnp.concatenate(requests), jnp.concatenate(indices)], axis=0
+        )
+        keym = jnp.pad(keym, ((0, 5), (0, 0)))
+        tok = jnp.pad(jnp.stack([request, group, index], axis=1), ((0, 0), (0, 125)))
+        half = HD // 2
+        freq = jnp.exp(
+            jnp.arange(half, dtype=jnp.float32) * (-2.0 * math.log(500000.0) / HD)
+        )
+        angle = (offset + prefix_len).astype(jnp.float32)[:, None] * freq[None, :]
+        cosine = jnp.cos(angle)
+        sine = jnp.sin(angle)
+        cq = jnp.concatenate([cosine, cosine], axis=1)
+        sq = jnp.concatenate([-sine, sine], axis=1)
+        attended = attend(queries, cq, sq, tok, keym, data, pieces, kv_cols, repeat, scale)
+        return (attended, cache[0], cache[1])
+
     prefix_parts = []
     suffix_parts = [(0, suffix_kv)]
-    if devices <= 16:
-        prefix_parts.append((me, prefix_kv))
-        for by in range(1, devices):
-            if by <= span:
-                both = shifted(jnp.concatenate([prefix_kv, suffix_kv], axis=0), "seq", by, True)
-                prefix_parts.append(((me - by) % devices, both[:block_rows]))
-                suffix_parts.append((by, both[block_rows:]))
-            else:
-                part = shifted(prefix_kv, "seq", by, True)
-                prefix_parts.append(((me - by) % devices, part))
-    else:
-        gathered = lax.all_gather(prefix_kv, "seq", axis=0, tiled=True)
-        prefix_parts.append((None, gathered))
-        for by in range(1, span + 1):
-            suffix_parts.append((by, shifted(suffix_kv, "seq", by, False)))
+    gathered = lax.all_gather(prefix_kv, "seq", axis=0, tiled=True)
+    prefix_parts.append((None, gathered))
+    for by in range(1, span + 1):
+        suffix_parts.append((by, shifted(suffix_kv, "seq", by, False)))
 
     position = offset + prefix_len
     q_rot = rotate(queries.reshape(rows, q_heads, HD), position).reshape(rows, kv_heads, repeat, HD)

time: 54 us -> 44.8 us (0.83)
  other arithmetic: 12.1 us -> 2.91 us
  waiting for transfers between devices: 8.59 us -> 1.42 us
  Pallas kernels: 0 us -> 4.85 us
  local copies, waits for them, and re-layouts: 11.9 us -> 15.7 us
  matrix products: 2.44 us -> 0 us
  starting transfers between devices: 17.1 us -> 18 us
    ppermute x7, waiting for transfers between devices: 8.58 us -> 1.42 us  [shifted(): return lax.ppermute(array, axis, pairs)]
    eq x1 -> x0, other arithmetic: 5.06 us -> none  [body(): visible = jnp.broadcast_to((group == row_group)[:, None], (rows, count))]
    broadcast_in_dim x0 -> x11, local copies, waits for them, and re-layouts: none -> 5.01 us  [the longest x7 4.44 us: body(): jnp.broadcast_to(lax.dynamic_index_in_dim(block_group, holder, keepdims=F...]
    pallas_call x0 -> x1, Pallas kernels: none -> 4.85 us  [attend(): pl.pallas_call(functools.partial(attend_kernel, tuple(pieces), q_heads, r...]
    sub x1 -> x0, other arithmetic: 2.87 us -> none  [summed_of(): scores - high[..., None]]
    dot_general x2 -> x0, matrix products: 2.44 us -> none  [the longest x1 1.79 us: summed_of(): jnp.einsum('bgrk,kgd->bgrd', weights.astype(jnp.bfloat16), values.reshape...]
    unnamed x28 -> x30, local copies, waits for them, and re-layouts: 7.21 us -> 5.43 us
    concatenate x3 -> x5, other arithmetic: 0.28 us -> 1.62 us  [the longest x1 0.71 us: body(): cq = jnp.concatenate([cosine, cosine], axis=1)]
  transfers between devices with their start and end apart: 8 -> 8, of which waited for: 2 -> 1; matrix products, arithmetic and copies ran while one was open for 41% -> 33% of each run, Pallas kernels for 0% -> 0%
where the time goes in v2:
time: 44.8 us; the launch traced here: 44.1 us
  starting transfers between devices  18 us (40%)
  local copies, waits for them, and re-layouts  15.7 us (35%)
  Pallas kernels  4.85 us (11%)
  other arithmetic  2.91 us (6%)
  waiting for transfers between devices  1.42 us (3%)
  between operations  1.14 us (3%)
    ppermute x7, starting transfers between devices, shifted(): return lax.ppermute(array, axis, pairs)  14.7 us
    unnamed x30, local copies, waits for them, and re-layouts  5.43 us
    pallas_call x1, Pallas kernels, attend(): pl.pallas_call(functools.partial(attend_kernel, tuple(pieces), q_heads, r...  4.85 us
    broadcast_in_dim x7, local copies, waits for them, and re-layouts, body(): jnp.broadcast_to(lax.dynamic_index_in_dim(block_group, holder, keepdims=F...  4.44 us
    all_to_all x1, starting transfers between devices, body(): lax.all_to_all(jnp.stack([own_k_rot, suffix_values], axis=0), 'tp', split...  3.33 us
    ppermute x7, waiting for transfers between devices, shifted(): return lax.ppermute(array, axis, pairs)  1.42 us
    another operation x2, local copies, waits for them, and re-layouts, body(): jnp.stack([own_k_rot, suffix_values], axis=0)  0.93 us
  transfers between devices with their start and end apart: 8, of which 1 were waited for; matrix products, arithmetic and copies ran while one was open for 33% of the time, Pallas kernels for 0%

profile of v2, /device:TPU:0, one launch (start us, length us, event | category | flops | bytes accessed | tf_op | source)
XLA Modules:
  0.0 44.1 jit_solution(5122047069549435421)
XLA Ops:
  0.7 0.8 %constant_dynamic-update-slice_fusion.1 = bf16[64,512]{1,0:T(8,128)(2,1)S(1)} fusion(bf16[64,256]{1,0:T(8,128)(2,1)} %param.11), kind=kLoop, calls=%fused_computation.26 | loop fusion | bytes 65536
  1.4 0.8 %constant_dynamic-update-slice_fusion.refs_5_ = bf16[64,512]{1,0:T(8,128)(2,1)S(1)} fusion(bf16[64,512]{1,0:T(8,128)(2,1)S(1)} %constant_dynamic-update-slice_fusion.1, bf16[64,256]{1,0:T(8,128)(2,1)} %param.12), kind=kLoop, calls=%fused_computation.25 | loop fusion | bytes 65536 | tf_op jit(solution)/shard_map/concatenate | solution.py:127
  2.2 3.0 %collective-permute-start.1 = (bf16[64,512]{1,0:T(8,128)(2,1)S(1)}, bf16[64,512]{1,0:T(8,128)(2,1)S(1)}, u32[]{:S(2)}, u32[]{:S(2)}) collective-permute-start(bf16[64,512]{1,0:T(8,128)(2,1)S(1)} %constant_dynamic-update-slice_fusion.refs_5_), channel_id=1, source_target_pairs={{0,8},{4,12},{8,16},{12,20},{16,24},{20,28},{24,0},{28,4},{1,9},{5... | collective-permute-start | bytes 196616 | tf_op jit(solution)/shard_map/ppermute | solution.py:100
  5.2 2.5 %collective-permute-start.2 = (bf16[64,512]{1,0:T(8,128)(2,1)S(1)}, bf16[64,512]{1,0:T(8,128)(2,1)S(1)}, u32[]{:S(2)}, u32[]{:S(2)}) collective-permute-start(bf16[64,512]{1,0:T(8,128)(2,1)S(1)} %constant_dynamic-update-slice_fusion.refs_5_), channel_id=1, source_target_pairs={{0,12},{4,16},{8,20},{12,24},{16,28},{20,0},{24,4},{28,8},{1,13},{... | collective-permute-start | bytes 196616 | tf_op jit(solution)/shard_map/ppermute | solution.py:100
  7.7 1.2 %collective-permute-start.3 = (bf16[64,512]{1,0:T(8,128)(2,1)S(1)}, bf16[64,512]{1,0:T(8,128)(2,1)S(1)}, u32[]{:S(2)}, u32[]{:S(2)}) collective-permute-start(bf16[64,512]{1,0:T(8,128)(2,1)S(1)} %constant_dynamic-update-slice_fusion.refs_5_), channel_id=1, source_target_pairs={{0,16},{4,20},{8,24},{12,28},{16,0},{20,4},{24,8},{28,12},{1,17},{... | collective-permute-start | bytes 196616 | tf_op jit(solution)/shard_map/ppermute | solution.py:100
  9.0 2.7 %collective-permute-start.4 = (bf16[64,512]{1,0:T(8,128)(2,1)S(1)}, bf16[64,512]{1,0:T(8,128)(2,1)S(1)}, u32[]{:S(2)}, u32[]{:S(2)}) collective-permute-start(bf16[64,512]{1,0:T(8,128)(2,1)S(1)} %constant_dynamic-update-slice_fusion.refs_5_), channel_id=1, source_target_pairs={{0,20},{4,24},{8,28},{12,0},{16,4},{20,8},{24,12},{28,16},{1,21},{... | collective-permute-start | bytes 196616 | tf_op jit(solution)/shard_map/ppermute | solution.py:100
  11.7 1.5 %collective-permute-start = (bf16[192,512]{1,0:T(8,128)(2,1)S(1)}, bf16[192,512]{1,0:T(8,128)(2,1)S(1)}, u32[]{:S(2)}, u32[]{:S(2)}) collective-permute-start(bf16[192,512]{1,0:T(8,128)(2,1)S(1)} %maximum_maximum_fusion), channel_id=1, source_target_pairs={{0,4},{4,8},{8,12},{12,16},{16,20},{20,24},{24,28},{28,0},{1,5},{5... | collective-permute-start | bytes 589832 | tf_op jit(solution)/shard_map/ppermute | solution.py:100
  13.4 0.6 %copy-done.11 = s32[24]{0:T(128)S(1)} copy-done((s32[24]{0:T(128)S(1)}, s32[24]{0:T(128)}, u32[]{:S(2)}) %copy-start.11) | copy-done | bytes 120
  14.4 0.7 %copy-done.12 = s32[24]{0:T(128)S(1)} copy-done((s32[24]{0:T(128)S(1)}, s32[24]{0:T(128)}, u32[]{:S(2)}) %copy-start.12) | copy-done | bytes 120
  16.0 0.8 %copy.51 = bf16[2,128,256]{2,0,1:T(2,128)(2,1)} copy(bf16[2,128,256]{1,2,0:T(8,128)(2,1)S(1)} %pad_maximum_fusion) | data formatting | bytes 262144 | tf_op jit(solution)/shard_map/stack | solution.py:139
  16.8 3.3 %all-to-all-start = ((bf16[2,128,256]{2,0,1:T(2,128)(2,1)}), bf16[2,128,256]{2,0,1:T(2,128)(2,1)S(1)}, u32[]{:S(2)}, u32[]{:S(2)}) async-start(bf16[2,128,256]{2,0,1:T(2,128)(2,1)} %copy.51), calls=%async_computation | async-start | bytes 262144 | tf_op jit(solution)/shard_map/all_to_all | solution.py:138
  20.3 0.7 %pad_maximum_fusion.1.refs_1_ = f32[128,128]{1,0:T(8,128)} fusion(f32[128,64]{1,0:T(8,128)S(1)} %get-tuple-element.19), kind=kLoop, calls=%fused_computation.11 | loop fusion | flops 16384 | bytes 98304 | tf_op jit(solution)/shard_map/concatenate | solution.py:180
  21.0 0.7 %copy.54.refs_13_ = bf16[128,256]{1,0:T(8,128)(2,1)} copy(bf16[128,256]{0,1:T(8,128)(2,1)S(1)} %bitcast.31) | data formatting | bytes 131072 | tf_op jit(solution)/shard_map/convert_element_type | solution.py:31
  21.8 0.7 %copy-done.10 = s32[8]{0:T(128)S(1)} copy-done((s32[8]{0:T(128)S(1)}, s32[8]{0:T(128)}, u32[]{:S(2)}) %copy-start.10) | copy-done | bytes 56
  22.4 0.7 %fusion.2 = (s32[1]{0:T(128)}, s32[1]{0:T(128)}, s32[1]{0:T(128)}, s32[1]{0:T(128)}, s32[1]{0:T(128)}, /*index=5*/s32[1]{0:T(128)}, s32[1]{0:T(128)}, s32[1]{0:T(128)}) fusion(s32[8]{0:T(128)S(1)} %copy-done.10, s32[]{:T(128)S(6)} %select_n.87, s32[]{:T(128)S(6)} %select_n.83, s32[]{:T(128)S(6)} %select_n.81, s32[]{:T(128)S(6)} %select_n.79, ...), kind=kLoop, calls=%fused_computation.38 | loop fusion | bytes 96 | tf_op jit(solution)/shard_map/jit(dynamic_index_in_dim)/dynamic_slice | solution.py:155
  23.1 0.6 %broadcast_in_dim.100 = s32[64]{0:T(128)S(1)} broadcast(s32[]{:T(128)} %bitcast.8), dimensions={} | broadcast | bytes 260 | tf_op jit(solution)/shard_map/broadcast_in_dim | solution.py:155
  24.4 0.6 %broadcast_in_dim.102 = s32[64]{0:T(128)S(1)} broadcast(s32[]{:T(128)} %bitcast.10), dimensions={} | broadcast | bytes 260 | tf_op jit(solution)/shard_map/broadcast_in_dim | solution.py:155
  29.7 0.7 %pad_maximum_fusion.2.refs_2_ = f32[128,128]{1,0:T(8,128)} fusion(f32[128,64]{1,0:T(8,128)S(1)} %get-tuple-element.20, f32[128,64]{1,0:T(8,128)S(1)} %get-tuple-element.21), kind=kLoop, calls=%fused_computation.12 | loop fusion | flops 16384 | bytes 131072 | tf_op jit(solution)/shard_map/concatenate | solution.py:181
  30.7 0.6 %copy.56 = bf16[4,8,4,256]{3,1,2,0:T(8,128)(2,1)} copy(bf16[4,8,4,256]{3,2,1,0:T(4,128)(2,1)S(1)} %bitcast.35) | data formatting | bytes 131072
  31.4 0.6 %copy.57 = bf16[4,8,4,256]{3,1,2,0:T(8,128)(2,1)} copy(bf16[4,8,4,256]{3,2,1,0:T(4,128)(2,1)S(1)} %bitcast.36) | data formatting | bytes 131072
  33.0 3.3 %collective-permute-start.6 = (bf16[64,512]{1,0:T(8,128)(2,1)S(1)}, bf16[64,512]{1,0:T(8,128)(2,1)S(1)}, u32[]{:S(2)}, u32[]{:S(2)}) collective-permute-start(bf16[64,512]{1,0:T(8,128)(2,1)S(1)} %constant_dynamic-update-slice_fusion.refs_5_), channel_id=1, source_target_pairs={{0,28},{4,0},{8,4},{12,8},{16,12},{20,16},{24,20},{28,24},{1,29},{... | collective-permute-start | bytes 196616 | tf_op jit(solution)/shard_map/ppermute | solution.py:100
  36.5 0.6 %copy.59 = bf16[16,8,2,128]{3,1,2,0:T(8,128)(2,1)} copy(bf16[16,8,2,128]{3,2,1,0:T(2,128)(2,1)S(1)} %bitcast.34) | data formatting | bytes 131072
  37.2 1.4 %collective-permute-done.6.refs_12_ = bf16[64,512]{1,0:T(8,128)(2,1)S(1)} collective-permute-done((bf16[64,512]{1,0:T(8,128)(2,1)S(1)}, bf16[64,512]{1,0:T(8,128)(2,1)S(1)}, u32[]{:S(2)}, u32[]{:S(2)}) %collective-permute-start.6) | collective-permute-done | bytes 65568 | tf_op jit(solution)/shard_map/ppermute | solution.py:100
  39.2 4.9 %shard_map.103 = bf16[128,1024]{1,0:T(8,128)(2,1)} custom-call(bf16[128,1024]{1,0:T(8,128)(2,1)} %refs_0_.1, f32[128,128]{1,0:T(8,128)} %pad_maximum_fusion.1.refs_1_, f32[128,128]{1,0:T(8,128)} %pad_maximum_fusion.2.refs_2_, s32[128,128]{1,0:T(8,128)} %pad.8.refs_3_, s32[8,768]{1,0:T(8,128)} %pad.9.refs_4_, bf16[64,512]{1,0:T(8,128)(2,1)} %copy-done.1, ...), custom_call_target="tpu_custom_call" | custom-call | flops 402653184 | bytes 1597440 | tf_op jit(solution)/shard_map/pallas_call | solution.py:73
  (79 shorter events, 8.8 us)
Async XLA Ops:
  0.6 11.0 %copy-start = (bf16[128,256]{1,0:T(8,128)(2,1)S(1)}, bf16[128,256]{1,0:T(8,128)(2,1)}, u32[]{:S(2)}) copy-start(bf16[128,256]{1,0:T(8,128)(2,1)} %refs_14_.1) | copy-start | bytes 196612
  0.6 11.0 %copy-start.3 = (bf16[128,256]{1,0:T(8,128)(2,1)S(1)}, bf16[128,256]{1,0:T(8,128)(2,1)}, u32[]{:S(2)}) copy-start(bf16[128,256]{1,0:T(8,128)(2,1)} %param.9) | copy-start | bytes 196612
  2.2 30.8 %copy-start.1 = (bf16[64,512]{1,0:T(8,128)(2,1)}, bf16[64,512]{1,0:T(8,128)(2,1)S(1)}, u32[]{:S(2)}) copy-start(bf16[64,512]{1,0:T(8,128)(2,1)S(1)} %constant_dynamic-update-slice_fusion.refs_5_) | copy-start | bytes 196612
  2.2 30.8 %collective-permute-start.1 = (bf16[64,512]{1,0:T(8,128)(2,1)S(1)}, bf16[64,512]{1,0:T(8,128)(2,1)S(1)}, u32[]{:S(2)}, u32[]{:S(2)}) collective-permute-start(bf16[64,512]{1,0:T(8,128)(2,1)S(1)} %constant_dynamic-update-slice_fusion.refs_5_), channel_id=1, source_target_pairs={{0,8},{4,12},{8,16},{12,20},{16,24},{20,28},{24,0},{28,4},{1,9},{5... | collective-permute-start | bytes 196616 | tf_op jit(solution)/shard_map/ppermute | solution.py:100
  5.2 31.9 %collective-permute-start.2 = (bf16[64,512]{1,0:T(8,128)(2,1)S(1)}, bf16[64,512]{1,0:T(8,128)(2,1)S(1)}, u32[]{:S(2)}, u32[]{:S(2)}) collective-permute-start(bf16[64,512]{1,0:T(8,128)(2,1)S(1)} %constant_dynamic-update-slice_fusion.refs_5_), channel_id=1, source_target_pairs={{0,12},{4,16},{8,20},{12,24},{16,28},{20,0},{24,4},{28,8},{1,13},{... | collective-permute-start | bytes 196616 | tf_op jit(solution)/shard_map/ppermute | solution.py:100
  7.7 29.4 %collective-permute-start.3 = (bf16[64,512]{1,0:T(8,128)(2,1)S(1)}, bf16[64,512]{1,0:T(8,128)(2,1)S(1)}, u32[]{:S(2)}, u32[]{:S(2)}) collective-permute-start(bf16[64,512]{1,0:T(8,128)(2,1)S(1)} %constant_dynamic-update-slice_fusion.refs_5_), channel_id=1, source_target_pairs={{0,16},{4,20},{8,24},{12,28},{16,0},{20,4},{24,8},{28,12},{1,17},{... | collective-permute-start | bytes 196616 | tf_op jit(solution)/shard_map/ppermute | solution.py:100
  9.0 28.2 %collective-permute-start.4 = (bf16[64,512]{1,0:T(8,128)(2,1)S(1)}, bf16[64,512]{1,0:T(8,128)(2,1)S(1)}, u32[]{:S(2)}, u32[]{:S(2)}) collective-permute-start(bf16[64,512]{1,0:T(8,128)(2,1)S(1)} %constant_dynamic-update-slice_fusion.refs_5_), channel_id=1, source_target_pairs={{0,20},{4,24},{8,28},{12,0},{16,4},{20,8},{24,12},{28,16},{1,21},{... | collective-permute-start | bytes 196616 | tf_op jit(solution)/shard_map/ppermute | solution.py:100
  11.7 20.4 %collective-permute-start = (bf16[192,512]{1,0:T(8,128)(2,1)S(1)}, bf16[192,512]{1,0:T(8,128)(2,1)S(1)}, u32[]{:S(2)}, u32[]{:S(2)}) collective-permute-start(bf16[192,512]{1,0:T(8,128)(2,1)S(1)} %maximum_maximum_fusion), channel_id=1, source_target_pairs={{0,4},{4,8},{8,12},{12,16},{16,20},{20,24},{24,28},{28,0},{1,5},{5... | collective-permute-start | bytes 589832 | tf_op jit(solution)/shard_map/ppermute | solution.py:100
  13.4 0.7 %copy-start.11 = (s32[24]{0:T(128)S(1)}, s32[24]{0:T(128)}, u32[]{:S(2)}) copy-start(s32[24]{0:T(128)} %param.13) | copy-start | bytes 292
  14.4 0.7 %copy-start.12 = (s32[24]{0:T(128)S(1)}, s32[24]{0:T(128)}, u32[]{:S(2)}) copy-start(s32[24]{0:T(128)} %param.14) | copy-start | bytes 292
  16.8 13.6 %all-to-all-start = ((bf16[2,128,256]{2,0,1:T(2,128)(2,1)}), bf16[2,128,256]{2,0,1:T(2,128)(2,1)S(1)}, u32[]{:S(2)}, u32[]{:S(2)}) async-start(bf16[2,128,256]{2,0,1:T(2,128)(2,1)} %copy.51), calls=%async_computation | async-start | bytes 262144 | tf_op jit(solution)/shard_map/all_to_all | solution.py:138
  21.8 0.7 %copy-start.10 = (s32[8]{0:T(128)S(1)}, s32[8]{0:T(128)}, u32[]{:S(2)}) copy-start(s32[8]{0:T(128)} %param.15) | copy-start | bytes 100
  32.1 0.7 %copy-start.2 = (bf16[192,512]{1,0:T(8,128)(2,1)}, bf16[192,512]{1,0:T(8,128)(2,1)S(1)}, u32[]{:S(2)}) copy-start(bf16[192,512]{1,0:T(8,128)(2,1)S(1)} %collective-permute-done.refs_6_) | copy-start | bytes 589828
  32.1 5.2 %collective-permute-start.5 = (bf16[64,512]{1,0:T(8,128)(2,1)S(1)}, bf16[64,512]{1,0:T(8,128)(2,1)S(1)}, u32[]{:S(2)}, u32[]{:S(2)}) collective-permute-start(bf16[64,512]{1,0:T(8,128)(2,1)S(1)} %constant_dynamic-update-slice_fusion.refs_5_), channel_id=1, source_target_pairs={{0,24},{4,28},{8,0},{12,4},{16,8},{20,12},{24,16},{28,20},{1,25},{... | collective-permute-start | bytes 196616 | tf_op jit(solution)/shard_map/ppermute | solution.py:100
  33.0 3.5 %copy-start.4 = (bf16[64,512]{1,0:T(8,128)(2,1)}, bf16[64,512]{1,0:T(8,128)(2,1)S(1)}, u32[]{:S(2)}) copy-start(bf16[64,512]{1,0:T(8,128)(2,1)S(1)} %collective-permute-done.1.refs_7_) | copy-start | bytes 196612
  33.0 5.6 %collective-permute-start.6 = (bf16[64,512]{1,0:T(8,128)(2,1)S(1)}, bf16[64,512]{1,0:T(8,128)(2,1)S(1)}, u32[]{:S(2)}, u32[]{:S(2)}) collective-permute-start(bf16[64,512]{1,0:T(8,128)(2,1)S(1)} %constant_dynamic-update-slice_fusion.refs_5_), channel_id=1, source_target_pairs={{0,28},{4,0},{8,4},{12,8},{16,12},{20,16},{24,20},{28,24},{1,29},{... | collective-permute-start | bytes 196616 | tf_op jit(solution)/shard_map/ppermute | solution.py:100
  37.2 1.5 %copy-start.5 = (bf16[64,512]{1,0:T(8,128)(2,1)}, bf16[64,512]{1,0:T(8,128)(2,1)S(1)}, u32[]{:S(2)}) copy-start(bf16[64,512]{1,0:T(8,128)(2,1)S(1)} %collective-permute-done.2.refs_8_) | copy-start | bytes 196612
  37.2 1.5 %copy-start.6 = (bf16[64,512]{1,0:T(8,128)(2,1)}, bf16[64,512]{1,0:T(8,128)(2,1)S(1)}, u32[]{:S(2)}) copy-start(bf16[64,512]{1,0:T(8,128)(2,1)S(1)} %collective-permute-done.3.refs_9_) | copy-start | bytes 196612
  37.2 1.4 %copy-start.7 = (bf16[64,512]{1,0:T(8,128)(2,1)}, bf16[64,512]{1,0:T(8,128)(2,1)S(1)}, u32[]{:S(2)}) copy-start(bf16[64,512]{1,0:T(8,128)(2,1)S(1)} %collective-permute-done.4.refs_10_) | copy-start | bytes 196612
  37.2 1.4 %copy-start.8 = (bf16[64,512]{1,0:T(8,128)(2,1)}, bf16[64,512]{1,0:T(8,128)(2,1)S(1)}, u32[]{:S(2)}) copy-start(bf16[64,512]{1,0:T(8,128)(2,1)S(1)} %collective-permute-done.5.refs_11_) | copy-start | bytes 196612
  38.6 0.6 %copy-start.9 = (bf16[64,512]{1,0:T(8,128)(2,1)}, bf16[64,512]{1,0:T(8,128)(2,1)S(1)}, u32[]{:S(2)}) copy-start(bf16[64,512]{1,0:T(8,128)(2,1)S(1)} %collective-permute-done.6.refs_12_) | copy-start | bytes 196612

commit v3 on v2

--- a/solution.py
+++ b/solution.py
@@ -31,26 +31,77 @@
     ).astype(jnp.bfloat16)
 
 
-def attend_kernel(pieces, q_heads, repeat, scale, *refs):
-    q_ref, cq_ref, sq_ref, tok_ref, key_ref = refs[:5]
-    data = refs[5 : len(refs) - 3]
-    out_ref, kscr, vscr = refs[len(refs) - 3 :]
-    at = 0
-    for k_at, k_row, k_col, v_at, v_row, v_col, count in pieces:
-        kscr[at : at + count, :] = data[k_at][k_row : k_row + count, k_col : k_col + kscr.shape[1]]
-        vscr[at : at + count, :] = data[v_at][v_row : v_row + count, v_col : v_col + vscr.shape[1]]
-        at += count
-    tok = tok_ref[...]
-    keym = key_ref[...]
-    visible = (keym[0:1, :] == tok[:, 1:2]) | (
-        (keym[1:2, :] == tok[:, 0:1]) & (keym[2:3, :] <= tok[:, 2:3])
+def attend_kernel(meta, *refs):
+    devices, block_rows, rows, tails, prefix_len, repeat, scale = meta
+    me_ref, lens_ref, rg_ref, bg_ref, freq_ref, q_ref, own_k_ref, own_v_ref = refs[:8]
+    data = refs[8 : 8 + devices]
+    out_ref, kscr, vscr = refs[8 + devices :]
+    kv_cols = kscr.shape[1]
+    count = kscr.shape[0]
+    base = devices * block_rows
+    q_heads = q_ref.shape[1] // HD
+    me = me_ref[0]
+    starts, at = [], 0
+    for j in range(lens_ref.shape[0]):
+        starts.append(at)
+        at = at + lens_ref[j]
+
+    def info(index):
+        request = jnp.full(index.shape, -2, jnp.int32)
+        first = jnp.zeros(index.shape, jnp.int32)
+        group = jnp.full(index.shape, -1, jnp.int32)
+        for j, start in enumerate(starts):
+            after = index >= start
+            request = jnp.where(after, j, request)
+            first = jnp.where(after, start, first)
+            group = jnp.where(after, rg_ref[j], group)
+        return request, index - first, group
+
+    freq = freq_ref[...]
+    lane = lax.broadcasted_iota(jnp.int32, (1, HD), 1)
+    sign = jnp.where(lane < HD // 2, -1.0, 1.0).astype(jnp.float32)
+
+    def tables(offset):
+        angle = (offset + prefix_len).astype(jnp.float32) * freq
+        return jnp.cos(angle), jnp.sin(angle) * sign
+
+    def rotated(x, cosine, sine):
+        return (x * cosine + pltpu.roll(x, HD // 2, 1) * sine).astype(jnp.bfloat16)
+
+    for c in range(devices):
+        kscr[c * block_rows : (c + 1) * block_rows, :] = data[c][0:block_rows, 0:kv_cols]
+        vscr[c * block_rows : (c + 1) * block_rows, :] = data[c][0:block_rows, kv_cols : 2 * kv_cols]
+    kscr[base : base + rows, :] = own_k_ref[...]
+    vscr[base : base + rows, :] = own_v_ref[...]
+    for b in range(1, tails + 1):
+        low = base + b * rows
+        index = (me - b) * rows + lax.broadcasted_iota(jnp.int32, (rows, 1), 0)
+        _, offset, _ = info(index)
+        cosine, sine = tables(offset)
+        for g in range(kv_cols // HD):
+            x = data[b][block_rows : block_rows + rows, g * HD : (g + 1) * HD].astype(jnp.float32)
+            kscr[low : low + rows, g * HD : (g + 1) * HD] = rotated(x, cosine, sine)
+        vscr[low : low + rows, :] = data[b][block_rows : block_rows + rows, kv_cols : 2 * kv_cols]
+
+    token = me * rows + lax.broadcasted_iota(jnp.int32, (rows, 1), 0)
+    request, offset, group = info(token)
+    col = lax.broadcasted_iota(jnp.int32, (1, count), 1)
+    key_group = jnp.full((1, count), -1, jnp.int32)
+    for c in range(devices):
+        holder = lax.rem(me - c + devices, devices)
+        key_group = jnp.where(col >= c * block_rows, bg_ref[holder], key_group)
+    key_index = jnp.full((1, count), -1, jnp.int32)
+    for b in range(tails + 1):
+        low = base + b * rows
+        key_index = jnp.where(col >= low, (me - b) * rows + col - low, key_index)
+    key_request, _, _ = info(key_index)
+    visible = ((col < base) & (key_group == group)) | (
+        (key_request == request) & (key_index <= token)
     )
-    cq = cq_ref[...]
-    sq = sq_ref[...]
+    cosine, sine = tables(offset)
     for h in range(q_heads):
         g = h // repeat
-        x = q_ref[:, h * HD : (h + 1) * HD].astype(jnp.float32)
-        q = (x * cq + pltpu.roll(x, HD // 2, 1) * sq).astype(jnp.bfloat16)
+        q = rotated(q_ref[:, h * HD : (h + 1) * HD].astype(jnp.float32), cosine, sine)
         k = kscr[:, g * HD : (g + 1) * HD]
         scores = lax.dot_general(
             q, k, (((1,), (1,)), ((), ())), preferred_element_type=jnp.float32
@@ -64,15 +115,21 @@
         out_ref[:, h * HD : (h + 1) * HD] = (summed / total).astype(out_ref.dtype)
 
 
-def attend(queries, cq, sq, tok, keym, data, pieces, kv_cols, repeat, scale):
-    rows = queries.shape[0]
+def attend(meta, scalars, freq, queries, own_k, own_v, data):
+    devices, block_rows, rows, tails = meta[:4]
+    kv_cols = own_k.shape[1]
     q_heads = queries.shape[1] // HD
-    count = keym.shape[1]
+    count = devices * block_rows + rows * (1 + tails)
     flops = 4 * rows * count * HD * q_heads
-    nbytes = sum(a.size * a.dtype.itemsize for a in [queries, cq, sq, tok, keym, *data])
+    arrays = [queries, own_k, own_v, *data]
+    nbytes = sum(a.size * a.dtype.itemsize for a in arrays)
+    smem = pl.BlockSpec(memory_space=pltpu.SMEM)
+    vmem = pl.BlockSpec(memory_space=pltpu.VMEM)
     return pl.pallas_call(
-        functools.partial(attend_kernel, tuple(pieces), q_heads, repeat, scale),
+        functools.partial(attend_kernel, meta),
         out_shape=jax.ShapeDtypeStruct(queries.shape, jnp.bfloat16),
+        in_specs=[smem] * len(scalars) + [vmem] * (1 + len(arrays)),
+        out_specs=vmem,
         scratch_shapes=[
             pltpu.VMEM((count, kv_cols), jnp.bfloat16),
             pltpu.VMEM((count, kv_cols), jnp.bfloat16),
@@ -82,7 +139,7 @@
             transcendentals=rows * count * q_heads,
             bytes_accessed=nbytes + queries.size * 2,
         ),
-    )(queries, cq, sq, tok, keym, *data)
+    )(*scalars, freq, *arrays)
 
 
 def token_info(index, suffix_lengths, request_group):
@@ -134,52 +191,25 @@
         return key_index, key_request, k_rot
 
     if devices <= 16:
-        own_index, own_request, own_k_rot = rotated_keys(suffix_keys, 0)
+        _, own_offset, _ = token_info(index, suffix_lengths, request_group)
+        own_k_rot = rotate(suffix_keys.reshape(rows, kv_heads, HD), own_offset + prefix_len).reshape(
+            rows, kv_cols
+        )
         cache = lax.all_to_all(
             jnp.stack([own_k_rot, suffix_values], axis=0), "tp", split_axis=1, concat_axis=2, tiled=True
         )
         data = [prefix_kv]
-        pieces = [(0, 0, 0, 0, 0, kv_cols, block_rows)]
-        groups = [jnp.broadcast_to(lax.dynamic_index_in_dim(block_group, me, keepdims=False), (block_rows,))]
-        tails = []
         for by in range(1, devices):
             if by <= span:
-                part = shifted(jnp.concatenate([prefix_kv, suffix_kv], axis=0), "seq", by, True)
-                key_index, key_request, k_rot = rotated_keys(part[block_rows:, :kv_cols], by)
-                tails.append((len(data), k_rot, key_index, key_request))
+                data.append(shifted(jnp.concatenate([prefix_kv, suffix_kv], axis=0), "seq", by, True))
             else:
-                part = shifted(prefix_kv, "seq", by, True)
-            data.append(part)
-            pieces.append((len(data) - 1, 0, 0, len(data) - 1, 0, kv_cols, block_rows))
-            holder = (me - by) % devices
-            groups.append(jnp.broadcast_to(lax.dynamic_index_in_dim(block_group, holder, keepdims=False), (block_rows,)))
-        data.append(own_k_rot)
-        data.append(suffix_values)
-        pieces.append((len(data) - 2, 0, 0, len(data) - 1, 0, 0, rows))
-        requests = [jnp.full((block_rows * devices,), -2, jnp.int32), own_request]
-        indices = [jnp.zeros((block_rows * devices,), jnp.int32), own_index]
-        for at, k_rot, key_index, key_request in tails:
-            data.append(k_rot)
-            pieces.append((len(data) - 1, 0, 0, at, block_rows, kv_cols, rows))
-            requests.append(jnp.where(key_index >= 0, key_request, -2))
-            indices.append(key_index)
-        suffix_count = rows * (1 + len(tails))
-        groups.append(jnp.full((suffix_count,), -1, jnp.int32))
-        keym = jnp.stack(
-            [jnp.concatenate(groups), jnp.concatenate(requests), jnp.concatenate(indices)], axis=0
-        )
-        keym = jnp.pad(keym, ((0, 5), (0, 0)))
-        tok = jnp.pad(jnp.stack([request, group, index], axis=1), ((0, 0), (0, 125)))
+                data.append(shifted(prefix_kv, "seq", by, True))
         half = HD // 2
-        freq = jnp.exp(
-            jnp.arange(half, dtype=jnp.float32) * (-2.0 * math.log(500000.0) / HD)
-        )
-        angle = (offset + prefix_len).astype(jnp.float32)[:, None] * freq[None, :]
-        cosine = jnp.cos(angle)
-        sine = jnp.sin(angle)
-        cq = jnp.concatenate([cosine, cosine], axis=1)
-        sq = jnp.concatenate([-sine, sine], axis=1)
-        attended = attend(queries, cq, sq, tok, keym, data, pieces, kv_cols, repeat, scale)
+        freq = jnp.exp(jnp.arange(half, dtype=jnp.float32) * (-2.0 * math.log(500000.0) / HD))
+        freq = jnp.concatenate([freq, freq])[None, :]
+        scalars = [me.astype(jnp.int32).reshape(1), suffix_lengths, request_group, block_group]
+        meta = (devices, block_rows, rows, min(span, devices - 1), prefix_len, repeat, scale)
+        attended = attend(meta, scalars, freq, queries, own_k_rot, suffix_values, data)
         return (attended, cache[0], cache[1])
 
     prefix_parts = []

time: 44.8 us -> 37.9 us (0.85)
  local copies, waits for them, and re-layouts: 15.7 us -> 6.3 us
  waiting for transfers between devices: 1.42 us -> 7.32 us
  starting transfers between devices: 18 us -> 16.2 us
  other arithmetic: 2.91 us -> 1.28 us
  Pallas kernels: 4.85 us -> 5.53 us
    broadcast_in_dim x11 -> x0, local copies, waits for them, and re-layouts: 5.01 us -> none  [the longest x7 4.44 us: body(): jnp.broadcast_to(lax.dynamic_index_in_dim(block_group, holder, keepdims=F...]
    ppermute x7, waiting for transfers between devices: 1.42 us -> 6.21 us  [shifted(): return lax.ppermute(array, axis, pairs)]
    ppermute x7, starting transfers between devices: 14.7 us -> 12.9 us  [shifted(): return lax.ppermute(array, axis, pairs)]
    concatenate x5 -> x0, other arithmetic: 1.62 us -> none  [the longest x1 0.71 us: body(): cq = jnp.concatenate([cosine, cosine], axis=1)]
    unnamed x30 -> x27, local copies, waits for them, and re-layouts: 5.43 us -> 4.12 us
    pad x2 -> x0, local copies, waits for them, and re-layouts: 1.23 us -> none  [the longest x1 0.62 us: body(): jnp.pad(jnp.stack([request, group, index], axis=1), ((0, 0), (0, 125)))]
    all_to_all x1, waiting for transfers between devices: 0.01 us -> 1.1 us  [body(): lax.all_to_all(jnp.stack([own_k_rot, suffix_values], axis=0), 'tp', split...]
    concatenate x1, local copies, waits for them, and re-layouts: 0.76 us -> 0.01 us  [body(): prefix_kv = jnp.concatenate([prefix_keys, prefix_values], axis=1)]
  transfers between devices with their start and end apart: 8 -> 8, of which waited for: 1 -> 2; matrix products, arithmetic and copies ran while one was open for 33% -> 13% of each run, Pallas kernels for 0% -> 0%
where the time goes in v3:
time: 37.9 us; the launch traced here: 37.5 us
  starting transfers between devices  16.2 us (43%)
  waiting for transfers between devices  7.32 us (19%)
  local copies, waits for them, and re-layouts  6.3 us (17%)
  Pallas kernels  5.53 us (15%)
  other arithmetic  1.28 us (3%)
  between operations  0.83 us (2%)
    ppermute x7, starting transfers between devices, shifted(): return lax.ppermute(array, axis, pairs)  12.9 us
    ppermute x7, waiting for transfers between devices, shifted(): return lax.ppermute(array, axis, pairs)  6.21 us
    pallas_call x1, Pallas kernels, attend(): pl.pallas_call(functools.partial(attend_kernel, meta), out_shape=jax.Shap...  5.53 us
    unnamed x27, local copies, waits for them, and re-layouts  4.12 us
    all_to_all x1, starting transfers between devices, body(): lax.all_to_all(jnp.stack([own_k_rot, suffix_values], axis=0), 'tp', split...  3.33 us
    all_to_all x1, waiting for transfers between devices, body(): lax.all_to_all(jnp.stack([own_k_rot, suffix_values], axis=0), 'tp', split...  1.1 us
    another operation x2, local copies, waits for them, and re-layouts, body(): jnp.stack([own_k_rot, suffix_values], axis=0)  0.9 us
  transfers between devices with their start and end apart: 8, of which 2 were waited for; matrix products, arithmetic and copies ran while one was open for 13% of the time, Pallas kernels for 0%

profile of v3, /device:TPU:0, one launch (start us, length us, event | category | flops | bytes accessed | tf_op | source)
XLA Modules:
  0.0 37.5 jit_solution(10030097169236242706)
XLA Ops:
  0.6 0.8 %constant_dynamic-update-slice_fusion.1 = bf16[64,512]{1,0:T(8,128)(2,1)S(1)} fusion(bf16[64,256]{1,0:T(8,128)(2,1)} %param.11), kind=kLoop, calls=%fused_computation.11 | loop fusion | bytes 65536
  1.4 3.1 %collective-permute-start.1 = (bf16[64,512]{1,0:T(8,128)(2,1)S(1)}, bf16[64,512]{1,0:T(8,128)(2,1)S(1)}, u32[]{:S(2)}, u32[]{:S(2)}) collective-permute-start(bf16[64,512]{1,0:T(8,128)(2,1)S(1)} %constant_dynamic-update-slice_fusion.refs_8_), channel_id=1, source_target_pairs={{0,8},{4,12},{8,16},{12,20},{16,24},{20,28},{24,0},{28,4},{1,9},{5... | collective-permute-start | bytes 196616 | tf_op jit(solution)/shard_map/ppermute | solution.py:157
  4.5 2.5 %collective-permute-start.2 = (bf16[64,512]{1,0:T(8,128)(2,1)S(1)}, bf16[64,512]{1,0:T(8,128)(2,1)S(1)}, u32[]{:S(2)}, u32[]{:S(2)}) collective-permute-start(bf16[64,512]{1,0:T(8,128)(2,1)S(1)} %constant_dynamic-update-slice_fusion.refs_8_), channel_id=1, source_target_pairs={{0,12},{4,16},{8,20},{12,24},{16,28},{20,0},{24,4},{28,8},{1,13},{... | collective-permute-start | bytes 196616 | tf_op jit(solution)/shard_map/ppermute | solution.py:157
  7.0 1.2 %collective-permute-start.3 = (bf16[64,512]{1,0:T(8,128)(2,1)S(1)}, bf16[64,512]{1,0:T(8,128)(2,1)S(1)}, u32[]{:S(2)}, u32[]{:S(2)}) collective-permute-start(bf16[64,512]{1,0:T(8,128)(2,1)S(1)} %constant_dynamic-update-slice_fusion.refs_8_), channel_id=1, source_target_pairs={{0,16},{4,20},{8,24},{12,28},{16,0},{20,4},{24,8},{28,12},{1,17},{... | collective-permute-start | bytes 196616 | tf_op jit(solution)/shard_map/ppermute | solution.py:157
  8.2 2.7 %collective-permute-start.4 = (bf16[64,512]{1,0:T(8,128)(2,1)S(1)}, bf16[64,512]{1,0:T(8,128)(2,1)S(1)}, u32[]{:S(2)}, u32[]{:S(2)}) collective-permute-start(bf16[64,512]{1,0:T(8,128)(2,1)S(1)} %constant_dynamic-update-slice_fusion.refs_8_), channel_id=1, source_target_pairs={{0,20},{4,24},{8,28},{12,0},{16,4},{20,8},{24,12},{28,16},{1,21},{... | collective-permute-start | bytes 196616 | tf_op jit(solution)/shard_map/ppermute | solution.py:157
  10.9 1.3 %collective-permute-start.5 = (bf16[64,512]{1,0:T(8,128)(2,1)S(1)}, bf16[64,512]{1,0:T(8,128)(2,1)S(1)}, u32[]{:S(2)}, u32[]{:S(2)}) collective-permute-start(bf16[64,512]{1,0:T(8,128)(2,1)S(1)} %constant_dynamic-update-slice_fusion.refs_8_), channel_id=1, source_target_pairs={{0,24},{4,28},{8,0},{12,4},{16,8},{20,12},{24,16},{28,20},{1,25},{... | collective-permute-start | bytes 196616 | tf_op jit(solution)/shard_map/ppermute | solution.py:157
  12.3 0.6 %copy-done.4 = s32[24]{0:T(128)S(1)} copy-done((s32[24]{0:T(128)S(1)}, s32[24]{0:T(128)}, u32[]{:S(2)}) %copy-start.4) | copy-done | bytes 120
  13.1 0.1 reduce
  13.5 0.7 %copy-done.1 = bf16[128,256]{1,0:T(8,128)(2,1)S(1)} copy-done((bf16[128,256]{1,0:T(8,128)(2,1)S(1)}, bf16[128,256]{1,0:T(8,128)(2,1)}, u32[]{:S(2)}) %copy-start.1) | copy-done | bytes 65560
  14.2 0.1 copy.28
  14.4 0.2 multiply_cosine_fusion
  14.6 0.8 %copy.29 = bf16[2,128,256]{2,0,1:T(2,128)(2,1)} copy(bf16[2,128,256]{1,2,0:T(8,128)(2,1)S(1)} %pad_maximum_fusion) | data formatting | bytes 262144 | tf_op jit(solution)/shard_map/stack | solution.py:199
  15.4 3.3 %all-to-all-start = ((bf16[2,128,256]{2,0,1:T(2,128)(2,1)}), bf16[2,128,256]{2,0,1:T(2,128)(2,1)S(1)}, u32[]{:S(2)}, u32[]{:S(2)}) async-start(bf16[2,128,256]{2,0,1:T(2,128)(2,1)} %copy.29), calls=%async_computation | async-start | bytes 262144 | tf_op jit(solution)/shard_map/all_to_all | solution.py:198
  18.8 0.7 %copy.32.refs_6_ = bf16[128,256]{1,0:T(8,128)(2,1)} copy(bf16[128,256]{0,1:T(8,128)(2,1)S(1)} %bitcast.19) | data formatting | bytes 131072 | tf_op jit(solution)/shard_map/convert_element_type | solution.py:31
  19.5 0.6 %maximum_bitcast_fusion.refs_4_ = f32[1,128]{1,0:T(1,128)} fusion(f32[64]{0:T(128)S(1)} %multiply_exponential_fusion), kind=kLoop, calls=%fused_computation.12 | loop fusion | flops 128 | bytes 768 | tf_op jit(solution)/shard_map/broadcast_in_dim | solution.py:209
  20.2 1.4 %collective-permute-start.6 = (bf16[64,512]{1,0:T(8,128)(2,1)S(1)}, bf16[64,512]{1,0:T(8,128)(2,1)S(1)}, u32[]{:S(2)}, u32[]{:S(2)}) collective-permute-start(bf16[64,512]{1,0:T(8,128)(2,1)S(1)} %constant_dynamic-update-slice_fusion.refs_8_), channel_id=1, source_target_pairs={{0,28},{4,0},{8,4},{12,8},{16,12},{20,16},{24,20},{28,24},{1,29},{... | collective-permute-start | bytes 196616 | tf_op jit(solution)/shard_map/ppermute | solution.py:157
  21.6 0.6 %collective-permute-start = (bf16[192,512]{1,0:T(8,128)(2,1)S(1)}, bf16[192,512]{1,0:T(8,128)(2,1)S(1)}, u32[]{:S(2)}, u32[]{:S(2)}) collective-permute-start(bf16[192,512]{1,0:T(8,128)(2,1)S(1)} %maximum_maximum_fusion), channel_id=1, source_target_pairs={{0,4},{4,8},{8,12},{12,16},{16,20},{20,24},{24,28},{28,0},{1,5},{5... | collective-permute-start | bytes 589832 | tf_op jit(solution)/shard_map/ppermute | solution.py:157
  22.2 1.1 %all-to-all-done = bf16[2,128,256]{2,0,1:T(2,128)(2,1)S(1)} async-done(((bf16[2,128,256]{2,0,1:T(2,128)(2,1)}), bf16[2,128,256]{2,0,1:T(2,128)(2,1)S(1)}, u32[]{:S(2)}, u32[]{:S(2)}) %all-to-all-start) | async-done | bytes 131104 | tf_op jit(solution)/shard_map/all_to_all | solution.py:198
  23.3 0.2 fusion
  23.6 0.6 %copy.33 = bf16[4,8,4,256]{3,1,2,0:T(8,128)(2,1)} copy(bf16[4,8,4,256]{3,2,1,0:T(4,128)(2,1)S(1)} %bitcast.21) | data formatting | bytes 131072
  24.4 0.6 %copy.34 = bf16[4,8,4,256]{3,1,2,0:T(8,128)(2,1)} copy(bf16[4,8,4,256]{3,2,1,0:T(4,128)(2,1)S(1)} %bitcast.22) | data formatting | bytes 131072
  25.1 6.2 %collective-permute-done.refs_9_ = bf16[192,512]{1,0:T(8,128)(2,1)S(1)} collective-permute-done((bf16[192,512]{1,0:T(8,128)(2,1)S(1)}, bf16[192,512]{1,0:T(8,128)(2,1)S(1)}, u32[]{:S(2)}, u32[]{:S(2)}) %collective-permute-start) | collective-permute-done | bytes 196640 | tf_op jit(solution)/shard_map/ppermute | solution.py:157
  31.3 0.7 %copy-done.5 = bf16[192,512]{1,0:T(8,128)(2,1)} copy-done((bf16[192,512]{1,0:T(8,128)(2,1)}, bf16[192,512]{1,0:T(8,128)(2,1)S(1)}, u32[]{:S(2)}) %copy-start.5) | copy-done | bytes 196632
  32.0 5.5 %shard_map.103 = bf16[128,1024]{1,0:T(8,128)(2,1)} custom-call(s32[1]{0:T(128)} %bitcast.refs_0_, s32[24]{0:T(128)} %refs_1_.1, s32[24]{0:T(128)} %refs_2_.1, s32[8]{0:T(128)} %refs_3_.1, f32[1,128]{1,0:T(1,128)} %maximum_bitcast_fusion.refs_4_, bf16[128,1024]{1,0:T(8,128)(2,1)} %refs_5_.1, bf16[128,256]{1,0:T(8,128)(2,1)} %copy.32.refs_6_, ...), custom_call_target="tpu_custom_call" | custom-call | flops 402653184 | bytes 1310720 | tf_op jit(solution)/shard_map/pallas_call | solution.py:128
  (43 shorter events, 0.7 us)
Async XLA Ops:
  0.6 0.8 %copy-start.3 = (bf16[64,256]{1,0:T(8,128)(2,1)S(1)}, bf16[64,256]{1,0:T(8,128)(2,1)}, u32[]{:S(2)}) copy-start(bf16[64,256]{1,0:T(8,128)(2,1)} %param.12) | copy-start | bytes 98308
  1.4 12.0 %copy-start = (bf16[128,256]{1,0:T(8,128)(2,1)S(1)}, bf16[128,256]{1,0:T(8,128)(2,1)}, u32[]{:S(2)}) copy-start(bf16[128,256]{1,0:T(8,128)(2,1)} %param.9) | copy-start | bytes 196612
  1.4 18.7 %copy-start.2 = (bf16[64,512]{1,0:T(8,128)(2,1)}, bf16[64,512]{1,0:T(8,128)(2,1)S(1)}, u32[]{:S(2)}) copy-start(bf16[64,512]{1,0:T(8,128)(2,1)S(1)} %constant_dynamic-update-slice_fusion.refs_8_) | copy-start | bytes 196612
  1.4 18.7 %collective-permute-start.1 = (bf16[64,512]{1,0:T(8,128)(2,1)S(1)}, bf16[64,512]{1,0:T(8,128)(2,1)S(1)}, u32[]{:S(2)}, u32[]{:S(2)}) collective-permute-start(bf16[64,512]{1,0:T(8,128)(2,1)S(1)} %constant_dynamic-update-slice_fusion.refs_8_), channel_id=1, source_target_pairs={{0,8},{4,12},{8,16},{12,20},{16,24},{20,28},{24,0},{28,4},{1,9},{5... | collective-permute-start | bytes 196616 | tf_op jit(solution)/shard_map/ppermute | solution.py:157
  4.5 17.1 %collective-permute-start.2 = (bf16[64,512]{1,0:T(8,128)(2,1)S(1)}, bf16[64,512]{1,0:T(8,128)(2,1)S(1)}, u32[]{:S(2)}, u32[]{:S(2)}) collective-permute-start(bf16[64,512]{1,0:T(8,128)(2,1)S(1)} %constant_dynamic-update-slice_fusion.refs_8_), channel_id=1, source_target_pairs={{0,12},{4,16},{8,20},{12,24},{16,28},{20,0},{24,4},{28,8},{1,13},{... | collective-permute-start | bytes 196616 | tf_op jit(solution)/shard_map/ppermute | solution.py:157
  7.0 18.0 %collective-permute-start.3 = (bf16[64,512]{1,0:T(8,128)(2,1)S(1)}, bf16[64,512]{1,0:T(8,128)(2,1)S(1)}, u32[]{:S(2)}, u32[]{:S(2)}) collective-permute-start(bf16[64,512]{1,0:T(8,128)(2,1)S(1)} %constant_dynamic-update-slice_fusion.refs_8_), channel_id=1, source_target_pairs={{0,16},{4,20},{8,24},{12,28},{16,0},{20,4},{24,8},{28,12},{1,17},{... | collective-permute-start | bytes 196616 | tf_op jit(solution)/shard_map/ppermute | solution.py:157
  8.2 16.8 %collective-permute-start.4 = (bf16[64,512]{1,0:T(8,128)(2,1)S(1)}, bf16[64,512]{1,0:T(8,128)(2,1)S(1)}, u32[]{:S(2)}, u32[]{:S(2)}) collective-permute-start(bf16[64,512]{1,0:T(8,128)(2,1)S(1)} %constant_dynamic-update-slice_fusion.refs_8_), channel_id=1, source_target_pairs={{0,20},{4,24},{8,28},{12,0},{16,4},{20,8},{24,12},{28,16},{1,21},{... | collective-permute-start | bytes 196616 | tf_op jit(solution)/shard_map/ppermute | solution.py:157
  10.9 14.1 %collective-permute-start.5 = (bf16[64,512]{1,0:T(8,128)(2,1)S(1)}, bf16[64,512]{1,0:T(8,128)(2,1)S(1)}, u32[]{:S(2)}, u32[]{:S(2)}) collective-permute-start(bf16[64,512]{1,0:T(8,128)(2,1)S(1)} %constant_dynamic-update-slice_fusion.refs_8_), channel_id=1, source_target_pairs={{0,24},{4,28},{8,0},{12,4},{16,8},{20,12},{24,16},{28,20},{1,25},{... | collective-permute-start | bytes 196616 | tf_op jit(solution)/shard_map/ppermute | solution.py:157
  12.3 0.7 %copy-start.4 = (s32[24]{0:T(128)S(1)}, s32[24]{0:T(128)}, u32[]{:S(2)}) copy-start(s32[24]{0:T(128)} %refs_1_.1) | copy-start | bytes 292
  13.4 0.8 %copy-start.1 = (bf16[128,256]{1,0:T(8,128)(2,1)S(1)}, bf16[128,256]{1,0:T(8,128)(2,1)}, u32[]{:S(2)}) copy-start(bf16[128,256]{1,0:T(8,128)(2,1)} %refs_7_.1) | copy-start | bytes 196612
  15.4 7.9 %all-to-all-start = ((bf16[2,128,256]{2,0,1:T(2,128)(2,1)}), bf16[2,128,256]{2,0,1:T(2,128)(2,1)S(1)}, u32[]{:S(2)}, u32[]{:S(2)}) async-start(bf16[2,128,256]{2,0,1:T(2,128)(2,1)} %copy.29), calls=%async_computation | async-start | bytes 262144 | tf_op jit(solution)/shard_map/all_to_all | solution.py:198
  20.2 3.4 %copy-start.6 = (bf16[64,512]{1,0:T(8,128)(2,1)}, bf16[64,512]{1,0:T(8,128)(2,1)S(1)}, u32[]{:S(2)}) copy-start(bf16[64,512]{1,0:T(8,128)(2,1)S(1)} %collective-permute-done.1.refs_10_) | copy-start | bytes 196612
  20.2 4.9 %collective-permute-start.6 = (bf16[64,512]{1,0:T(8,128)(2,1)S(1)}, bf16[64,512]{1,0:T(8,128)(2,1)S(1)}, u32[]{:S(2)}, u32[]{:S(2)}) collective-permute-start(bf16[64,512]{1,0:T(8,128)(2,1)S(1)} %constant_dynamic-update-slice_fusion.refs_8_), channel_id=1, source_target_pairs={{0,28},{4,0},{8,4},{12,8},{16,12},{20,16},{24,20},{28,24},{1,29},{... | collective-permute-start | bytes 196616 | tf_op jit(solution)/shard_map/ppermute | solution.py:157
  21.6 2.0 %copy-start.7 = (bf16[64,512]{1,0:T(8,128)(2,1)}, bf16[64,512]{1,0:T(8,128)(2,1)S(1)}, u32[]{:S(2)}) copy-start(bf16[64,512]{1,0:T(8,128)(2,1)S(1)} %collective-permute-done.2.refs_11_) | copy-start | bytes 196612
  21.6 9.7 %collective-permute-start = (bf16[192,512]{1,0:T(8,128)(2,1)S(1)}, bf16[192,512]{1,0:T(8,128)(2,1)S(1)}, u32[]{:S(2)}, u32[]{:S(2)}) collective-permute-start(bf16[192,512]{1,0:T(8,128)(2,1)S(1)} %maximum_maximum_fusion), channel_id=1, source_target_pairs={{0,4},{4,8},{8,12},{12,16},{16,20},{20,24},{24,28},{28,0},{1,5},{5... | collective-permute-start | bytes 589832 | tf_op jit(solution)/shard_map/ppermute | solution.py:157
  25.0 6.3 %copy-start.8 = (bf16[64,512]{1,0:T(8,128)(2,1)}, bf16[64,512]{1,0:T(8,128)(2,1)S(1)}, u32[]{:S(2)}) copy-start(bf16[64,512]{1,0:T(8,128)(2,1)S(1)} %collective-permute-done.3.refs_12_) | copy-start | bytes 196612
  25.0 6.3 %copy-start.9 = (bf16[64,512]{1,0:T(8,128)(2,1)}, bf16[64,512]{1,0:T(8,128)(2,1)S(1)}, u32[]{:S(2)}) copy-start(bf16[64,512]{1,0:T(8,128)(2,1)S(1)} %collective-permute-done.4.refs_13_) | copy-start | bytes 196612
  25.1 6.2 %copy-start.10 = (bf16[64,512]{1,0:T(8,128)(2,1)}, bf16[64,512]{1,0:T(8,128)(2,1)S(1)}, u32[]{:S(2)}) copy-start(bf16[64,512]{1,0:T(8,128)(2,1)S(1)} %collective-permute-done.5.refs_14_) | copy-start | bytes 196612
  25.1 6.2 %copy-start.11 = (bf16[64,512]{1,0:T(8,128)(2,1)}, bf16[64,512]{1,0:T(8,128)(2,1)S(1)}, u32[]{:S(2)}) copy-start(bf16[64,512]{1,0:T(8,128)(2,1)S(1)} %collective-permute-done.6.refs_15_) | copy-start | bytes 196612
  31.3 0.7 %copy-start.5 = (bf16[192,512]{1,0:T(8,128)(2,1)}, bf16[192,512]{1,0:T(8,128)(2,1)S(1)}, u32[]{:S(2)}) copy-start(bf16[192,512]{1,0:T(8,128)(2,1)S(1)} %collective-permute-done.refs_9_) | copy-start | bytes 589828

commit v4 on v3

--- a/solution.py
+++ b/solution.py
@@ -198,12 +198,19 @@
         cache = lax.all_to_all(
             jnp.stack([own_k_rot, suffix_values], axis=0), "tp", split_axis=1, concat_axis=2, tiled=True
         )
-        data = [prefix_kv]
+        received = {}
+        late = list(range(span + 1, devices))[: max(0, devices - 1 - 5)]
         for by in range(1, devices):
             if by <= span:
-                data.append(shifted(jnp.concatenate([prefix_kv, suffix_kv], axis=0), "seq", by, True))
-            else:
-                data.append(shifted(prefix_kv, "seq", by, True))
+                received[by] = shifted(jnp.concatenate([prefix_kv, suffix_kv], axis=0), "seq", by, True)
+            elif by not in late:
+                received[by] = shifted(prefix_kv, "seq", by, True)
+        for i, by in enumerate(late):
+            gate = received[devices - 1 - i]
+            gate, payload = lax.optimization_barrier((gate, prefix_kv))
+            received[devices - 1 - i] = gate
+            received[by] = shifted(payload, "seq", by, True)
+        data = [prefix_kv] + [received[by] for by in range(1, devices)]
         half = HD // 2
         freq = jnp.exp(jnp.arange(half, dtype=jnp.float32) * (-2.0 * math.log(500000.0) / HD))
         freq = jnp.concatenate([freq, freq])[None, :]

time: 37.9 us -> 36.4 us (0.960)
  waiting for transfers between devices: 7.32 us -> 6.21 us
  starting transfers between devices: 16.2 us -> 15.8 us
    ppermute x7, waiting for transfers between devices: 6.21 us -> 3.63 us  [shifted(): return lax.ppermute(array, axis, pairs)]
    all_to_all x1, waiting for transfers between devices: 1.1 us -> 2.58 us  [body(): lax.all_to_all(jnp.stack([own_k_rot, suffix_values], axis=0), 'tp', split...]
    concatenate x1, local copies, waits for them, and re-layouts: 0.01 us -> 0.76 us  [body(): prefix_kv = jnp.concatenate([prefix_keys, prefix_values], axis=1)]
    unnamed x27 -> x25, local copies, waits for them, and re-layouts: 4.12 us -> 3.43 us
    ppermute x7, starting transfers between devices: 12.9 us -> 12.5 us  [shifted(): return lax.ppermute(array, axis, pairs)]
  transfers between devices with their start and end apart: 8 -> 8, of which waited for: 2 -> 3; matrix products, arithmetic and copies ran while one was open for 13% -> 13% of each run, Pallas kernels for 0% -> 0%
where the time goes in v4:
time: 36.4 us; the launch traced here: 36 us
  starting transfers between devices  15.8 us (43%)
  local copies, waits for them, and re-layouts  6.37 us (18%)
  waiting for transfers between devices  6.21 us (17%)
  Pallas kernels  5.53 us (15%)
  other arithmetic  1.28 us (4%)
  between operations  0.83 us (2%)
    ppermute x7, starting transfers between devices, shifted(): return lax.ppermute(array, axis, pairs)  12.5 us
    pallas_call x1, Pallas kernels, attend(): pl.pallas_call(functools.partial(attend_kernel, meta), out_shape=jax.Shap...  5.53 us
    ppermute x7, waiting for transfers between devices, shifted(): return lax.ppermute(array, axis, pairs)  3.63 us
    unnamed x25, local copies, waits for them, and re-layouts  3.43 us
    all_to_all x1, starting transfers between devices, body(): lax.all_to_all(jnp.stack([own_k_rot, suffix_values], axis=0), 'tp', split...  3.33 us
    all_to_all x1, waiting for transfers between devices, body(): lax.all_to_all(jnp.stack([own_k_rot, suffix_values], axis=0), 'tp', split...  2.58 us
    another operation x2, local copies, waits for them, and re-layouts, body(): jnp.stack([own_k_rot, suffix_values], axis=0)  0.9 us
    concatenate x1, local copies, waits for them, and re-layouts, body(): prefix_kv = jnp.concatenate([prefix_keys, prefix_values], axis=1)  0.76 us
  transfers between devices with their start and end apart: 8, of which 3 were waited for; matrix products, arithmetic and copies ran while one was open for 13% of the time, Pallas kernels for 0%

profile of v4, /device:TPU:0, one launch (start us, length us, event | category | flops | bytes accessed | tf_op | source)
XLA Modules:
  0.0 36.0 jit_solution(13451708518540686986)
XLA Ops:
  0.7 0.8 %constant_dynamic-update-slice_fusion.1 = bf16[64,512]{1,0:T(8,128)(2,1)S(1)} fusion(bf16[64,256]{1,0:T(8,128)(2,1)} %param.11), kind=kLoop, calls=%fused_computation.11 | loop fusion | bytes 65536
  1.4 0.8 %constant_dynamic-update-slice_fusion.refs_8_ = bf16[64,512]{1,0:T(8,128)(2,1)S(1)} fusion(bf16[64,512]{1,0:T(8,128)(2,1)S(1)} %constant_dynamic-update-slice_fusion.1, bf16[64,256]{1,0:T(8,128)(2,1)} %param.12), kind=kLoop, calls=%fused_computation.10 | loop fusion | bytes 65536 | tf_op jit(solution)/shard_map/concatenate | solution.py:184
  2.2 6.0 %collective-permute-start.1 = (bf16[64,512]{1,0:T(8,128)(2,1)S(1)}, bf16[64,512]{1,0:T(8,128)(2,1)S(1)}, u32[]{:S(2)}, u32[]{:S(2)}) collective-permute-start(bf16[64,512]{1,0:T(8,128)(2,1)S(1)} %constant_dynamic-update-slice_fusion.refs_8_), channel_id=1, source_target_pairs={{0,28},{4,0},{8,4},{12,8},{16,12},{20,16},{24,20},{28,24},{1,29},{... | collective-permute-start | bytes 196616 | tf_op jit(solution)/shard_map/ppermute | solution.py:157
  8.2 0.4 %collective-permute-start.3 = (bf16[64,512]{1,0:T(8,128)(2,1)S(1)}, bf16[64,512]{1,0:T(8,128)(2,1)S(1)}, u32[]{:S(2)}, u32[]{:S(2)}) collective-permute-start(bf16[64,512]{1,0:T(8,128)(2,1)S(1)} %constant_dynamic-update-slice_fusion.refs_8_), channel_id=1, source_target_pairs={{0,24},{4,28},{8,0},{12,4},{16,8},{20,12},{24,16},{28,20},{1,25},{... | collective-permute-start | bytes 196616 | tf_op jit(solution)/shard_map/ppermute | solution.py:157
  8.6 3.0 %collective-permute-start.6 = (bf16[64,512]{1,0:T(8,128)(2,1)S(1)}, bf16[64,512]{1,0:T(8,128)(2,1)S(1)}, u32[]{:S(2)}, u32[]{:S(2)}) collective-permute-start(bf16[64,512]{1,0:T(8,128)(2,1)S(1)} %constant_dynamic-update-slice_fusion.refs_8_), channel_id=1, source_target_pairs={{0,20},{4,24},{8,28},{12,0},{16,4},{20,8},{24,12},{28,16},{1,21},{... | collective-permute-start | bytes 196616 | tf_op jit(solution)/shard_map/ppermute | solution.py:157
  11.7 2.4 %collective-permute-start = (bf16[192,512]{1,0:T(8,128)(2,1)S(1)}, bf16[192,512]{1,0:T(8,128)(2,1)S(1)}, u32[]{:S(2)}, u32[]{:S(2)}) collective-permute-start(bf16[192,512]{1,0:T(8,128)(2,1)S(1)} %maximum_maximum_fusion), channel_id=1, source_target_pairs={{0,4},{4,8},{8,12},{12,16},{16,20},{20,24},{24,28},{28,0},{1,5},{5... | collective-permute-start | bytes 589832 | tf_op jit(solution)/shard_map/ppermute | solution.py:157
  14.1 0.1 copy.25
  14.3 0.6 %copy-done.3 = s32[24]{0:T(128)S(1)} copy-done((s32[24]{0:T(128)S(1)}, s32[24]{0:T(128)}, u32[]{:S(2)}) %copy-start.3) | copy-done | bytes 120
  15.0 0.1 reduce
  15.4 0.1 copy.28
  15.5 0.2 multiply_cosine_fusion
  15.7 0.8 %copy.29 = bf16[2,128,256]{2,0,1:T(2,128)(2,1)} copy(bf16[2,128,256]{1,2,0:T(8,128)(2,1)S(1)} %pad_maximum_fusion) | data formatting | bytes 262144 | tf_op jit(solution)/shard_map/stack | solution.py:199
  16.5 3.3 %all-to-all-start = ((bf16[2,128,256]{2,0,1:T(2,128)(2,1)}), bf16[2,128,256]{2,0,1:T(2,128)(2,1)S(1)}, u32[]{:S(2)}, u32[]{:S(2)}) async-start(bf16[2,128,256]{2,0,1:T(2,128)(2,1)} %copy.29), calls=%async_computation | async-start | bytes 262144 | tf_op jit(solution)/shard_map/all_to_all | solution.py:198
  19.9 0.7 %copy.32.refs_6_ = bf16[128,256]{1,0:T(8,128)(2,1)} copy(bf16[128,256]{0,1:T(8,128)(2,1)S(1)} %bitcast.19) | data formatting | bytes 131072 | tf_op jit(solution)/shard_map/convert_element_type | solution.py:31
  20.6 0.6 %maximum_bitcast_fusion.refs_4_ = f32[1,128]{1,0:T(1,128)} fusion(f32[64]{0:T(128)S(1)} %multiply_exponential_fusion), kind=kLoop, calls=%fused_computation.12 | loop fusion | flops 128 | bytes 768 | tf_op jit(solution)/shard_map/broadcast_in_dim | solution.py:216
  21.3 0.6 %collective-permute-start.4 = (bf16[64,512]{1,0:T(8,128)(2,1)S(1)}, bf16[64,512]{1,0:T(8,128)(2,1)S(1)}, u32[]{:S(2)}, u32[]{:S(2)}) collective-permute-start(bf16[64,512]{1,0:T(8,128)(2,1)S(1)} %constant_dynamic-update-slice_fusion.refs_8_), channel_id=1, source_target_pairs={{0,12},{4,16},{8,20},{12,24},{16,28},{20,0},{24,4},{28,8},{1,13},{... | collective-permute-start | bytes 196616 | tf_op jit(solution)/shard_map/ppermute | solution.py:157
  21.9 2.6 %all-to-all-done = bf16[2,128,256]{2,0,1:T(2,128)(2,1)S(1)} async-done(((bf16[2,128,256]{2,0,1:T(2,128)(2,1)}), bf16[2,128,256]{2,0,1:T(2,128)(2,1)S(1)}, u32[]{:S(2)}, u32[]{:S(2)}) %all-to-all-start) | async-done | bytes 131104 | tf_op jit(solution)/shard_map/all_to_all | solution.py:198
  24.5 0.2 fusion
  24.8 0.6 %copy.33 = bf16[4,8,4,256]{3,1,2,0:T(8,128)(2,1)} copy(bf16[4,8,4,256]{3,2,1,0:T(4,128)(2,1)S(1)} %bitcast.21) | data formatting | bytes 131072
  25.5 0.6 %copy.34 = bf16[4,8,4,256]{3,1,2,0:T(8,128)(2,1)} copy(bf16[4,8,4,256]{3,2,1,0:T(4,128)(2,1)S(1)} %bitcast.22) | data formatting | bytes 131072
  26.2 1.8 %collective-permute-done.2.refs_10_ = bf16[64,512]{1,0:T(8,128)(2,1)S(1)} collective-permute-done((bf16[64,512]{1,0:T(8,128)(2,1)S(1)}, bf16[64,512]{1,0:T(8,128)(2,1)S(1)}, u32[]{:S(2)}, u32[]{:S(2)}) %collective-permute-start.2) | collective-permute-done | bytes 65568 | tf_op jit(solution)/shard_map/ppermute | solution.py:157
  28.0 1.8 %collective-permute-done.4.refs_11_ = bf16[64,512]{1,0:T(8,128)(2,1)S(1)} collective-permute-done((bf16[64,512]{1,0:T(8,128)(2,1)S(1)}, bf16[64,512]{1,0:T(8,128)(2,1)S(1)}, u32[]{:S(2)}, u32[]{:S(2)}) %collective-permute-start.4) | collective-permute-done | bytes 65568 | tf_op jit(solution)/shard_map/ppermute | solution.py:157
  29.8 0.6 %copy-done.10 = bf16[64,512]{1,0:T(8,128)(2,1)} copy-done((bf16[64,512]{1,0:T(8,128)(2,1)}, bf16[64,512]{1,0:T(8,128)(2,1)S(1)}, u32[]{:S(2)}) %copy-start.10) | copy-done | bytes 65560
  30.5 5.5 %shard_map.103 = bf16[128,1024]{1,0:T(8,128)(2,1)} custom-call(s32[1]{0:T(128)} %bitcast.refs_0_, s32[24]{0:T(128)} %refs_1_.1, s32[24]{0:T(128)} %refs_2_.1, s32[8]{0:T(128)} %refs_3_.1, f32[1,128]{1,0:T(1,128)} %maximum_bitcast_fusion.refs_4_, bf16[128,1024]{1,0:T(8,128)(2,1)} %refs_5_.1, bf16[128,256]{1,0:T(8,128)(2,1)} %copy.32.refs_6_, ...), custom_call_target="tpu_custom_call" | custom-call | flops 402653184 | bytes 1310720 | tf_op jit(solution)/shard_map/pallas_call | solution.py:128
  (41 shorter events, 0.7 us)
Async XLA Ops:
  0.6 11.0 %copy-start = (bf16[128,256]{1,0:T(8,128)(2,1)S(1)}, bf16[128,256]{1,0:T(8,128)(2,1)}, u32[]{:S(2)}) copy-start(bf16[128,256]{1,0:T(8,128)(2,1)} %param.9) | copy-start | bytes 196612
  0.6 11.0 %copy-start.1 = (bf16[128,256]{1,0:T(8,128)(2,1)S(1)}, bf16[128,256]{1,0:T(8,128)(2,1)}, u32[]{:S(2)}) copy-start(bf16[128,256]{1,0:T(8,128)(2,1)} %refs_7_.1) | copy-start | bytes 196612
  2.2 19.1 %copy-start.2 = (bf16[64,512]{1,0:T(8,128)(2,1)}, bf16[64,512]{1,0:T(8,128)(2,1)S(1)}, u32[]{:S(2)}) copy-start(bf16[64,512]{1,0:T(8,128)(2,1)S(1)} %constant_dynamic-update-slice_fusion.refs_8_) | copy-start | bytes 196612
  2.2 19.0 %collective-permute-start.1 = (bf16[64,512]{1,0:T(8,128)(2,1)S(1)}, bf16[64,512]{1,0:T(8,128)(2,1)S(1)}, u32[]{:S(2)}, u32[]{:S(2)}) collective-permute-start(bf16[64,512]{1,0:T(8,128)(2,1)S(1)} %constant_dynamic-update-slice_fusion.refs_8_), channel_id=1, source_target_pairs={{0,28},{4,0},{8,4},{12,8},{16,12},{20,16},{24,20},{28,24},{1,29},{... | collective-permute-start | bytes 196616 | tf_op jit(solution)/shard_map/ppermute | solution.py:157
  8.2 13.1 %collective-permute-start.3 = (bf16[64,512]{1,0:T(8,128)(2,1)S(1)}, bf16[64,512]{1,0:T(8,128)(2,1)S(1)}, u32[]{:S(2)}, u32[]{:S(2)}) collective-permute-start(bf16[64,512]{1,0:T(8,128)(2,1)S(1)} %constant_dynamic-update-slice_fusion.refs_8_), channel_id=1, source_target_pairs={{0,24},{4,28},{8,0},{12,4},{16,8},{20,12},{24,16},{28,20},{1,25},{... | collective-permute-start | bytes 196616 | tf_op jit(solution)/shard_map/ppermute | solution.py:157
  8.6 17.5 %collective-permute-start.5 = (bf16[64,512]{1,0:T(8,128)(2,1)S(1)}, bf16[64,512]{1,0:T(8,128)(2,1)S(1)}, u32[]{:S(2)}, u32[]{:S(2)}) collective-permute-start(bf16[64,512]{1,0:T(8,128)(2,1)S(1)} %constant_dynamic-update-slice_fusion.refs_8_), channel_id=1, source_target_pairs={{0,16},{4,20},{8,24},{12,28},{16,0},{20,4},{24,8},{28,12},{1,17},{... | collective-permute-start | bytes 196616 | tf_op jit(solution)/shard_map/ppermute | solution.py:157
  8.6 17.5 %collective-permute-start.6 = (bf16[64,512]{1,0:T(8,128)(2,1)S(1)}, bf16[64,512]{1,0:T(8,128)(2,1)S(1)}, u32[]{:S(2)}, u32[]{:S(2)}) collective-permute-start(bf16[64,512]{1,0:T(8,128)(2,1)S(1)} %constant_dynamic-update-slice_fusion.refs_8_), channel_id=1, source_target_pairs={{0,20},{4,24},{8,28},{12,0},{16,4},{20,8},{24,12},{28,16},{1,21},{... | collective-permute-start | bytes 196616 | tf_op jit(solution)/shard_map/ppermute | solution.py:157
  11.7 18.1 %collective-permute-start = (bf16[192,512]{1,0:T(8,128)(2,1)S(1)}, bf16[192,512]{1,0:T(8,128)(2,1)S(1)}, u32[]{:S(2)}, u32[]{:S(2)}) collective-permute-start(bf16[192,512]{1,0:T(8,128)(2,1)S(1)} %maximum_maximum_fusion), channel_id=1, source_target_pairs={{0,4},{4,8},{8,12},{12,16},{16,20},{20,24},{24,28},{28,0},{1,5},{5... | collective-permute-start | bytes 589832 | tf_op jit(solution)/shard_map/ppermute | solution.py:157
  14.2 0.7 %copy-start.3 = (s32[24]{0:T(128)S(1)}, s32[24]{0:T(128)}, u32[]{:S(2)}) copy-start(s32[24]{0:T(128)} %refs_1_.1) | copy-start | bytes 292
  16.5 7.9 %all-to-all-start = ((bf16[2,128,256]{2,0,1:T(2,128)(2,1)}), bf16[2,128,256]{2,0,1:T(2,128)(2,1)S(1)}, u32[]{:S(2)}, u32[]{:S(2)}) async-start(bf16[2,128,256]{2,0,1:T(2,128)(2,1)} %copy.29), calls=%async_computation | async-start | bytes 262144 | tf_op jit(solution)/shard_map/all_to_all | solution.py:198
  21.3 3.4 %copy-start.5 = (bf16[64,512]{1,0:T(8,128)(2,1)}, bf16[64,512]{1,0:T(8,128)(2,1)S(1)}, u32[]{:S(2)}) copy-start(bf16[64,512]{1,0:T(8,128)(2,1)S(1)} %collective-permute-done.1.refs_15_) | copy-start | bytes 196612
  21.3 6.7 %collective-permute-start.2 = (bf16[64,512]{1,0:T(8,128)(2,1)S(1)}, bf16[64,512]{1,0:T(8,128)(2,1)S(1)}, u32[]{:S(2)}, u32[]{:S(2)}) collective-permute-start(bf16[64,512]{1,0:T(8,128)(2,1)S(1)} %constant_dynamic-update-slice_fusion.refs_8_), channel_id=1, source_target_pairs={{0,8},{4,12},{8,16},{12,20},{16,24},{20,28},{24,0},{28,4},{1,9},{5... | collective-permute-start | bytes 196616 | tf_op jit(solution)/shard_map/ppermute | solution.py:157
  21.3 3.4 %copy-start.6 = (bf16[64,512]{1,0:T(8,128)(2,1)}, bf16[64,512]{1,0:T(8,128)(2,1)S(1)}, u32[]{:S(2)}) copy-start(bf16[64,512]{1,0:T(8,128)(2,1)S(1)} %collective-permute-done.3.refs_14_) | copy-start | bytes 196612
  21.3 8.5 %collective-permute-start.4 = (bf16[64,512]{1,0:T(8,128)(2,1)S(1)}, bf16[64,512]{1,0:T(8,128)(2,1)S(1)}, u32[]{:S(2)}, u32[]{:S(2)}) collective-permute-start(bf16[64,512]{1,0:T(8,128)(2,1)S(1)} %constant_dynamic-update-slice_fusion.refs_8_), channel_id=1, source_target_pairs={{0,12},{4,16},{8,20},{12,24},{16,28},{20,0},{24,4},{28,8},{1,13},{... | collective-permute-start | bytes 196616 | tf_op jit(solution)/shard_map/ppermute | solution.py:157
  26.1 3.6 %copy-start.7 = (bf16[64,512]{1,0:T(8,128)(2,1)}, bf16[64,512]{1,0:T(8,128)(2,1)S(1)}, u32[]{:S(2)}) copy-start(bf16[64,512]{1,0:T(8,128)(2,1)S(1)} %collective-permute-done.5.refs_12_) | copy-start | bytes 196612
  26.2 3.6 %copy-start.8 = (bf16[64,512]{1,0:T(8,128)(2,1)}, bf16[64,512]{1,0:T(8,128)(2,1)S(1)}, u32[]{:S(2)}) copy-start(bf16[64,512]{1,0:T(8,128)(2,1)S(1)} %collective-permute-done.6.refs_13_) | copy-start | bytes 196612
  27.9 1.9 %copy-start.9 = (bf16[64,512]{1,0:T(8,128)(2,1)}, bf16[64,512]{1,0:T(8,128)(2,1)S(1)}, u32[]{:S(2)}) copy-start(bf16[64,512]{1,0:T(8,128)(2,1)S(1)} %collective-permute-done.2.refs_10_) | copy-start | bytes 196612
  29.8 0.6 %copy-start.10 = (bf16[64,512]{1,0:T(8,128)(2,1)}, bf16[64,512]{1,0:T(8,128)(2,1)S(1)}, u32[]{:S(2)}) copy-start(bf16[64,512]{1,0:T(8,128)(2,1)S(1)} %collective-permute-done.4.refs_11_) | copy-start | bytes 196612
  29.8 0.7 %copy-start.4 = (bf16[192,512]{1,0:T(8,128)(2,1)}, bf16[192,512]{1,0:T(8,128)(2,1)S(1)}, u32[]{:S(2)}) copy-start(bf16[192,512]{1,0:T(8,128)(2,1)S(1)} %collective-permute-done.refs_9_) | copy-start | bytes 589828

commit v5 on v4

--- a/solution.py
+++ b/solution.py
@@ -191,13 +191,6 @@
         return key_index, key_request, k_rot
 
     if devices <= 16:
-        _, own_offset, _ = token_info(index, suffix_lengths, request_group)
-        own_k_rot = rotate(suffix_keys.reshape(rows, kv_heads, HD), own_offset + prefix_len).reshape(
-            rows, kv_cols
-        )
-        cache = lax.all_to_all(
-            jnp.stack([own_k_rot, suffix_values], axis=0), "tp", split_axis=1, concat_axis=2, tiled=True
-        )
         received = {}
         late = list(range(span + 1, devices))[: max(0, devices - 1 - 5)]
         for by in range(1, devices):
@@ -205,12 +198,23 @@
                 received[by] = shifted(jnp.concatenate([prefix_kv, suffix_kv], axis=0), "seq", by, True)
             elif by not in late:
                 received[by] = shifted(prefix_kv, "seq", by, True)
+        gates = tuple(received[devices - 1 - i] for i in range(len(late)))
+        gates, payload, cache_keys_in, cache_values_in = lax.optimization_barrier(
+            (gates, prefix_kv, suffix_keys, suffix_values)
+        )
         for i, by in enumerate(late):
-            gate = received[devices - 1 - i]
-            gate, payload = lax.optimization_barrier((gate, prefix_kv))
-            received[devices - 1 - i] = gate
+            received[devices - 1 - i] = gates[i]
             received[by] = shifted(payload, "seq", by, True)
         data = [prefix_kv] + [received[by] for by in range(1, devices)]
+        if not late:
+            cache_keys_in, cache_values_in = suffix_keys, suffix_values
+        _, own_offset, _ = token_info(index, suffix_lengths, request_group)
+        own_k_rot = rotate(cache_keys_in.reshape(rows, kv_heads, HD), own_offset + prefix_len).reshape(
+            rows, kv_cols
+        )
+        cache = lax.all_to_all(
+            jnp.stack([own_k_rot, cache_values_in], axis=0), "tp", split_axis=1, concat_axis=2, tiled=True
+        )
         half = HD // 2
         freq = jnp.exp(jnp.arange(half, dtype=jnp.float32) * (-2.0 * math.log(500000.0) / HD))
         freq = jnp.concatenate([freq, freq])[None, :]

time: 36.4 us -> 36.2 us (level)
  waiting for transfers between devices: 6.21 us -> 5.57 us
  local copies, waits for them, and re-layouts: 6.37 us -> 6.87 us
    ppermute x7, waiting for transfers between devices: 3.63 us -> 2.93 us  [shifted(): return lax.ppermute(array, axis, pairs)]
    unnamed x25, local copies, waits for them, and re-layouts: 3.43 us -> 3.94 us
where the time goes in v5:
time: 36.2 us; the launch traced here: 35.8 us
  starting transfers between devices  15.8 us (44%)
  local copies, waits for them, and re-layouts  6.87 us (19%)
  waiting for transfers between devices  5.57 us (15%)
  Pallas kernels  5.54 us (15%)
  other arithmetic  1.28 us (4%)
  between operations  0.81 us (2%)
    ppermute x7, starting transfers between devices, shifted(): return lax.ppermute(array, axis, pairs)  12.5 us
    pallas_call x1, Pallas kernels, attend(): pl.pallas_call(functools.partial(attend_kernel, meta), out_shape=jax.Shap...  5.54 us
    unnamed x25, local copies, waits for them, and re-layouts  3.94 us
    all_to_all x1, starting transfers between devices, body(): lax.all_to_all(jnp.stack([own_k_rot, cache_values_in], axis=0), 'tp', spl...  3.33 us
    ppermute x7, waiting for transfers between devices, shifted(): return lax.ppermute(array, axis, pairs)  2.93 us
    all_to_all x1, waiting for transfers between devices, body(): lax.all_to_all(jnp.stack([own_k_rot, cache_values_in], axis=0), 'tp', spl...  2.64 us
    another operation x2, local copies, waits for them, and re-layouts, body(): jnp.stack([own_k_rot, cache_values_in], axis=0)  0.9 us
    concatenate x1, local copies, waits for them, and re-layouts, body(): prefix_kv = jnp.concatenate([prefix_keys, prefix_values], axis=1)  0.76 us
  transfers between devices with their start and end apart: 8, of which 3 were waited for; matrix products, arithmetic and copies ran while one was open for 13% of the time, Pallas kernels for 0%

profile of v5, /device:TPU:0, one launch (start us, length us, event | category | flops | bytes accessed | tf_op | source)
XLA Modules:
  0.0 35.8 jit_solution(15102470926071358190)
XLA Ops:
  0.7 0.8 %constant_dynamic-update-slice_fusion.1 = bf16[64,512]{1,0:T(8,128)(2,1)S(1)} fusion(bf16[64,256]{1,0:T(8,128)(2,1)} %param.11), kind=kLoop, calls=%fused_computation.11 | loop fusion | bytes 65536
  1.4 0.8 %constant_dynamic-update-slice_fusion.refs_8_ = bf16[64,512]{1,0:T(8,128)(2,1)S(1)} fusion(bf16[64,512]{1,0:T(8,128)(2,1)S(1)} %constant_dynamic-update-slice_fusion.1, bf16[64,256]{1,0:T(8,128)(2,1)} %param.12), kind=kLoop, calls=%fused_computation.10 | loop fusion | bytes 65536 | tf_op jit(solution)/shard_map/concatenate | solution.py:184
  2.2 6.0 %collective-permute-start = (bf16[64,512]{1,0:T(8,128)(2,1)S(1)}, bf16[64,512]{1,0:T(8,128)(2,1)S(1)}, u32[]{:S(2)}, u32[]{:S(2)}) collective-permute-start(bf16[64,512]{1,0:T(8,128)(2,1)S(1)} %constant_dynamic-update-slice_fusion.refs_8_), channel_id=1, source_target_pairs={{0,28},{4,0},{8,4},{12,8},{16,12},{20,16},{24,20},{28,24},{1,29},{... | collective-permute-start | bytes 196616 | tf_op jit(solution)/shard_map/ppermute | solution.py:157
  8.2 0.4 %collective-permute-start.1 = (bf16[64,512]{1,0:T(8,128)(2,1)S(1)}, bf16[64,512]{1,0:T(8,128)(2,1)S(1)}, u32[]{:S(2)}, u32[]{:S(2)}) collective-permute-start(bf16[64,512]{1,0:T(8,128)(2,1)S(1)} %constant_dynamic-update-slice_fusion.refs_8_), channel_id=1, source_target_pairs={{0,24},{4,28},{8,0},{12,4},{16,8},{20,12},{24,16},{28,20},{1,25},{... | collective-permute-start | bytes 196616 | tf_op jit(solution)/shard_map/ppermute | solution.py:157
  8.6 3.0 %collective-permute-start.6 = (bf16[64,512]{1,0:T(8,128)(2,1)S(1)}, bf16[64,512]{1,0:T(8,128)(2,1)S(1)}, u32[]{:S(2)}, u32[]{:S(2)}) collective-permute-start(bf16[64,512]{1,0:T(8,128)(2,1)S(1)} %constant_dynamic-update-slice_fusion.refs_8_), channel_id=1, source_target_pairs={{0,20},{4,24},{8,28},{12,0},{16,4},{20,8},{24,12},{28,16},{1,21},{... | collective-permute-start | bytes 196616 | tf_op jit(solution)/shard_map/ppermute | solution.py:157
  11.7 2.4 %collective-permute-start.2 = (bf16[192,512]{1,0:T(8,128)(2,1)S(1)}, bf16[192,512]{1,0:T(8,128)(2,1)S(1)}, u32[]{:S(2)}, u32[]{:S(2)}) collective-permute-start(bf16[192,512]{1,0:T(8,128)(2,1)S(1)} %maximum_maximum_fusion), channel_id=1, source_target_pairs={{0,4},{4,8},{8,12},{12,16},{16,20},{20,24},{24,28},{28,0},{1,5},{5... | collective-permute-start | bytes 589832 | tf_op jit(solution)/shard_map/ppermute | solution.py:157
  14.1 0.6 %copy-done.3 = s32[24]{0:T(128)S(1)} copy-done((s32[24]{0:T(128)S(1)}, s32[24]{0:T(128)}, u32[]{:S(2)}) %copy-start.3) | copy-done | bytes 120
  14.9 0.1 reduce
  15.2 0.2 multiply_cosine_fusion
  15.6 0.5 %copy-done.5 = bf16[64,512]{1,0:T(8,128)(2,1)} copy-done((bf16[64,512]{1,0:T(8,128)(2,1)}, bf16[64,512]{1,0:T(8,128)(2,1)S(1)}, u32[]{:S(2)}) %copy-start.5) | copy-done | bytes 65560
  16.1 0.1 copy.28
  16.3 0.8 %copy.29 = bf16[2,128,256]{2,0,1:T(2,128)(2,1)} copy(bf16[2,128,256]{1,2,0:T(8,128)(2,1)S(1)} %pad_maximum_fusion) | data formatting | bytes 262144 | tf_op jit(solution)/shard_map/stack | solution.py:216
  17.1 3.3 %all-to-all-start = ((bf16[2,128,256]{2,0,1:T(2,128)(2,1)}), bf16[2,128,256]{2,0,1:T(2,128)(2,1)S(1)}, u32[]{:S(2)}, u32[]{:S(2)}) async-start(bf16[2,128,256]{2,0,1:T(2,128)(2,1)} %copy.29), calls=%async_computation | async-start | bytes 262144 | tf_op jit(solution)/shard_map/all_to_all | solution.py:215
  20.4 0.6 %maximum_bitcast_fusion.refs_4_ = f32[1,128]{1,0:T(1,128)} fusion(f32[64]{0:T(128)S(1)} %multiply_exponential_fusion), kind=kLoop, calls=%fused_computation.12 | loop fusion | flops 128 | bytes 768 | tf_op jit(solution)/shard_map/broadcast_in_dim | solution.py:220
  21.1 0.6 %collective-permute-start.4 = (bf16[64,512]{1,0:T(8,128)(2,1)S(1)}, bf16[64,512]{1,0:T(8,128)(2,1)S(1)}, u32[]{:S(2)}, u32[]{:S(2)}) collective-permute-start(bf16[64,512]{1,0:T(8,128)(2,1)S(1)} %constant_dynamic-update-slice_fusion.refs_8_), channel_id=1, source_target_pairs={{0,12},{4,16},{8,20},{12,24},{16,28},{20,0},{24,4},{28,8},{1,13},{... | collective-permute-start | bytes 196616 | tf_op jit(solution)/shard_map/ppermute | solution.py:157
  21.6 0.7 %copy.32.refs_6_ = bf16[128,256]{1,0:T(8,128)(2,1)} copy(bf16[128,256]{0,1:T(8,128)(2,1)S(1)} %bitcast.19) | data formatting | bytes 131072 | tf_op jit(solution)/shard_map/convert_element_type | solution.py:31
  22.4 2.6 %all-to-all-done = bf16[2,128,256]{2,0,1:T(2,128)(2,1)S(1)} async-done(((bf16[2,128,256]{2,0,1:T(2,128)(2,1)}), bf16[2,128,256]{2,0,1:T(2,128)(2,1)S(1)}, u32[]{:S(2)}, u32[]{:S(2)}) %all-to-all-start) | async-done | bytes 131104 | tf_op jit(solution)/shard_map/all_to_all | solution.py:215
  25.0 0.2 fusion
  25.3 0.6 %copy.33 = bf16[4,8,4,256]{3,1,2,0:T(8,128)(2,1)} copy(bf16[4,8,4,256]{3,2,1,0:T(4,128)(2,1)S(1)} %bitcast.21) | data formatting | bytes 131072
  26.0 0.6 %copy.34 = bf16[4,8,4,256]{3,1,2,0:T(8,128)(2,1)} copy(bf16[4,8,4,256]{3,2,1,0:T(4,128)(2,1)S(1)} %bitcast.22) | data formatting | bytes 131072
  26.7 1.1 %collective-permute-done.3.refs_10_ = bf16[64,512]{1,0:T(8,128)(2,1)S(1)} collective-permute-done((bf16[64,512]{1,0:T(8,128)(2,1)S(1)}, bf16[64,512]{1,0:T(8,128)(2,1)S(1)}, u32[]{:S(2)}, u32[]{:S(2)}) %collective-permute-start.3) | collective-permute-done | bytes 65568 | tf_op jit(solution)/shard_map/ppermute | solution.py:157
  27.8 1.8 %collective-permute-done.4.refs_11_ = bf16[64,512]{1,0:T(8,128)(2,1)S(1)} collective-permute-done((bf16[64,512]{1,0:T(8,128)(2,1)S(1)}, bf16[64,512]{1,0:T(8,128)(2,1)S(1)}, u32[]{:S(2)}, u32[]{:S(2)}) %collective-permute-start.4) | collective-permute-done | bytes 65568 | tf_op jit(solution)/shard_map/ppermute | solution.py:157
  29.6 0.6 %copy-done.10 = bf16[64,512]{1,0:T(8,128)(2,1)} copy-done((bf16[64,512]{1,0:T(8,128)(2,1)}, bf16[64,512]{1,0:T(8,128)(2,1)S(1)}, u32[]{:S(2)}) %copy-start.10) | copy-done | bytes 65560
  30.3 5.5 %shard_map.103 = bf16[128,1024]{1,0:T(8,128)(2,1)} custom-call(s32[1]{0:T(128)} %bitcast.refs_0_, s32[24]{0:T(128)} %refs_1_.1, s32[24]{0:T(128)} %refs_2_.1, s32[8]{0:T(128)} %refs_3_.1, f32[1,128]{1,0:T(1,128)} %maximum_bitcast_fusion.refs_4_, bf16[128,1024]{1,0:T(8,128)(2,1)} %refs_5_.1, bf16[128,256]{1,0:T(8,128)(2,1)} %copy.32.refs_6_, ...), custom_call_target="tpu_custom_call" | custom-call | flops 402653184 | bytes 1310720 | tf_op jit(solution)/shard_map/pallas_call | solution.py:128
  (41 shorter events, 0.8 us)
Async XLA Ops:
  0.6 11.0 %copy-start.1 = (bf16[128,256]{1,0:T(8,128)(2,1)S(1)}, bf16[128,256]{1,0:T(8,128)(2,1)}, u32[]{:S(2)}) copy-start(bf16[128,256]{1,0:T(8,128)(2,1)} %refs_7_.1) | copy-start | bytes 196612
  0.6 11.0 %copy-start = (bf16[128,256]{1,0:T(8,128)(2,1)S(1)}, bf16[128,256]{1,0:T(8,128)(2,1)}, u32[]{:S(2)}) copy-start(bf16[128,256]{1,0:T(8,128)(2,1)} %param.9) | copy-start | bytes 196612
  2.2 18.9 %copy-start.2 = (bf16[64,512]{1,0:T(8,128)(2,1)}, bf16[64,512]{1,0:T(8,128)(2,1)S(1)}, u32[]{:S(2)}) copy-start(bf16[64,512]{1,0:T(8,128)(2,1)S(1)} %constant_dynamic-update-slice_fusion.refs_8_) | copy-start | bytes 196612
  2.2 13.2 %collective-permute-start = (bf16[64,512]{1,0:T(8,128)(2,1)S(1)}, bf16[64,512]{1,0:T(8,128)(2,1)S(1)}, u32[]{:S(2)}, u32[]{:S(2)}) collective-permute-start(bf16[64,512]{1,0:T(8,128)(2,1)S(1)} %constant_dynamic-update-slice_fusion.refs_8_), channel_id=1, source_target_pairs={{0,28},{4,0},{8,4},{12,8},{16,12},{20,16},{24,20},{28,24},{1,29},{... | collective-permute-start | bytes 196616 | tf_op jit(solution)/shard_map/ppermute | solution.py:157
  8.2 7.3 %collective-permute-start.1 = (bf16[64,512]{1,0:T(8,128)(2,1)S(1)}, bf16[64,512]{1,0:T(8,128)(2,1)S(1)}, u32[]{:S(2)}, u32[]{:S(2)}) collective-permute-start(bf16[64,512]{1,0:T(8,128)(2,1)S(1)} %constant_dynamic-update-slice_fusion.refs_8_), channel_id=1, source_target_pairs={{0,24},{4,28},{8,0},{12,4},{16,8},{20,12},{24,16},{28,20},{1,25},{... | collective-permute-start | bytes 196616 | tf_op jit(solution)/shard_map/ppermute | solution.py:157
  8.6 18.0 %collective-permute-start.5 = (bf16[64,512]{1,0:T(8,128)(2,1)S(1)}, bf16[64,512]{1,0:T(8,128)(2,1)S(1)}, u32[]{:S(2)}, u32[]{:S(2)}) collective-permute-start(bf16[64,512]{1,0:T(8,128)(2,1)S(1)} %constant_dynamic-update-slice_fusion.refs_8_), channel_id=1, source_target_pairs={{0,16},{4,20},{8,24},{12,28},{16,0},{20,4},{24,8},{28,12},{1,17},{... | collective-permute-start | bytes 196616 | tf_op jit(solution)/shard_map/ppermute | solution.py:157
  8.6 18.0 %collective-permute-start.6 = (bf16[64,512]{1,0:T(8,128)(2,1)S(1)}, bf16[64,512]{1,0:T(8,128)(2,1)S(1)}, u32[]{:S(2)}, u32[]{:S(2)}) collective-permute-start(bf16[64,512]{1,0:T(8,128)(2,1)S(1)} %constant_dynamic-update-slice_fusion.refs_8_), channel_id=1, source_target_pairs={{0,20},{4,24},{8,28},{12,0},{16,4},{20,8},{24,12},{28,16},{1,21},{... | collective-permute-start | bytes 196616 | tf_op jit(solution)/shard_map/ppermute | solution.py:157
  11.7 17.9 %collective-permute-start.2 = (bf16[192,512]{1,0:T(8,128)(2,1)S(1)}, bf16[192,512]{1,0:T(8,128)(2,1)S(1)}, u32[]{:S(2)}, u32[]{:S(2)}) collective-permute-start(bf16[192,512]{1,0:T(8,128)(2,1)S(1)} %maximum_maximum_fusion), channel_id=1, source_target_pairs={{0,4},{4,8},{8,12},{12,16},{16,20},{20,24},{24,28},{28,0},{1,5},{5... | collective-permute-start | bytes 589832 | tf_op jit(solution)/shard_map/ppermute | solution.py:157
  14.1 0.7 %copy-start.3 = (s32[24]{0:T(128)S(1)}, s32[24]{0:T(128)}, u32[]{:S(2)}) copy-start(s32[24]{0:T(128)} %refs_1_.1) | copy-start | bytes 292
  15.4 0.6 %copy-start.5 = (bf16[64,512]{1,0:T(8,128)(2,1)}, bf16[64,512]{1,0:T(8,128)(2,1)S(1)}, u32[]{:S(2)}) copy-start(bf16[64,512]{1,0:T(8,128)(2,1)S(1)} %collective-permute-done.refs_15_) | copy-start | bytes 196612
  15.5 0.6 %copy-start.6 = (bf16[64,512]{1,0:T(8,128)(2,1)}, bf16[64,512]{1,0:T(8,128)(2,1)S(1)}, u32[]{:S(2)}) copy-start(bf16[64,512]{1,0:T(8,128)(2,1)S(1)} %collective-permute-done.1.refs_14_) | copy-start | bytes 196612
  17.1 7.9 %all-to-all-start = ((bf16[2,128,256]{2,0,1:T(2,128)(2,1)}), bf16[2,128,256]{2,0,1:T(2,128)(2,1)S(1)}, u32[]{:S(2)}, u32[]{:S(2)}) async-start(bf16[2,128,256]{2,0,1:T(2,128)(2,1)} %copy.29), calls=%async_computation | async-start | bytes 262144 | tf_op jit(solution)/shard_map/all_to_all | solution.py:215
  21.1 6.7 %collective-permute-start.3 = (bf16[64,512]{1,0:T(8,128)(2,1)S(1)}, bf16[64,512]{1,0:T(8,128)(2,1)S(1)}, u32[]{:S(2)}, u32[]{:S(2)}) collective-permute-start(bf16[64,512]{1,0:T(8,128)(2,1)S(1)} %constant_dynamic-update-slice_fusion.refs_8_), channel_id=1, source_target_pairs={{0,8},{4,12},{8,16},{12,20},{16,24},{20,28},{24,0},{28,4},{1,9},{5... | collective-permute-start | bytes 196616 | tf_op jit(solution)/shard_map/ppermute | solution.py:157
  21.1 8.5 %collective-permute-start.4 = (bf16[64,512]{1,0:T(8,128)(2,1)S(1)}, bf16[64,512]{1,0:T(8,128)(2,1)S(1)}, u32[]{:S(2)}, u32[]{:S(2)}) collective-permute-start(bf16[64,512]{1,0:T(8,128)(2,1)S(1)} %constant_dynamic-update-slice_fusion.refs_8_), channel_id=1, source_target_pairs={{0,12},{4,16},{8,20},{12,24},{16,28},{20,0},{24,4},{28,8},{1,13},{... | collective-permute-start | bytes 196616 | tf_op jit(solution)/shard_map/ppermute | solution.py:157
  26.7 2.9 %copy-start.7 = (bf16[64,512]{1,0:T(8,128)(2,1)}, bf16[64,512]{1,0:T(8,128)(2,1)S(1)}, u32[]{:S(2)}) copy-start(bf16[64,512]{1,0:T(8,128)(2,1)S(1)} %collective-permute-done.5.refs_12_) | copy-start | bytes 196612
  26.7 2.9 %copy-start.8 = (bf16[64,512]{1,0:T(8,128)(2,1)}, bf16[64,512]{1,0:T(8,128)(2,1)S(1)}, u32[]{:S(2)}) copy-start(bf16[64,512]{1,0:T(8,128)(2,1)S(1)} %collective-permute-done.6.refs_13_) | copy-start | bytes 196612
  27.7 1.9 %copy-start.9 = (bf16[64,512]{1,0:T(8,128)(2,1)}, bf16[64,512]{1,0:T(8,128)(2,1)S(1)}, u32[]{:S(2)}) copy-start(bf16[64,512]{1,0:T(8,128)(2,1)S(1)} %collective-permute-done.3.refs_10_) | copy-start | bytes 196612
  29.6 0.6 %copy-start.10 = (bf16[64,512]{1,0:T(8,128)(2,1)}, bf16[64,512]{1,0:T(8,128)(2,1)S(1)}, u32[]{:S(2)}) copy-start(bf16[64,512]{1,0:T(8,128)(2,1)S(1)} %collective-permute-done.4.refs_11_) | copy-start | bytes 196612
  29.6 0.7 %copy-start.4 = (bf16[192,512]{1,0:T(8,128)(2,1)}, bf16[192,512]{1,0:T(8,128)(2,1)S(1)}, u32[]{:S(2)}) copy-start(bf16[192,512]{1,0:T(8,128)(2,1)S(1)} %collective-permute-done.2.refs_9_) | copy-start | bytes 589828

commit v6 on v5

--- a/solution.py
+++ b/solution.py
@@ -33,9 +33,9 @@
 
 def attend_kernel(meta, *refs):
     devices, block_rows, rows, tails, prefix_len, repeat, scale = meta
-    me_ref, lens_ref, rg_ref, bg_ref, freq_ref, q_ref, own_k_ref, own_v_ref = refs[:8]
-    data = refs[8 : 8 + devices]
-    out_ref, kscr, vscr = refs[8 + devices :]
+    me_ref, lens_ref, rg_ref, bg_ref, q_ref, own_k_ref, own_v_ref = refs[:7]
+    data = refs[7 : 7 + devices]
+    out_ref, kscr, vscr = refs[7 + devices :]
     kv_cols = kscr.shape[1]
     count = kscr.shape[0]
     base = devices * block_rows
@@ -57,8 +57,9 @@
             group = jnp.where(after, rg_ref[j], group)
         return request, index - first, group
 
-    freq = freq_ref[...]
     lane = lax.broadcasted_iota(jnp.int32, (1, HD), 1)
+    pair = jnp.where(lane < HD // 2, lane, lane - HD // 2)
+    freq = jnp.exp(pair.astype(jnp.float32) * (-2.0 * math.log(500000.0) / HD))
     sign = jnp.where(lane < HD // 2, -1.0, 1.0).astype(jnp.float32)
 
     def tables(offset):
@@ -71,17 +72,21 @@
     for c in range(devices):
         kscr[c * block_rows : (c + 1) * block_rows, :] = data[c][0:block_rows, 0:kv_cols]
         vscr[c * block_rows : (c + 1) * block_rows, :] = data[c][0:block_rows, kv_cols : 2 * kv_cols]
-    kscr[base : base + rows, :] = own_k_ref[...]
-    vscr[base : base + rows, :] = own_v_ref[...]
-    for b in range(1, tails + 1):
+    for b in range(0, tails + 1):
         low = base + b * rows
         index = (me - b) * rows + lax.broadcasted_iota(jnp.int32, (rows, 1), 0)
         _, offset, _ = info(index)
         cosine, sine = tables(offset)
         for g in range(kv_cols // HD):
-            x = data[b][block_rows : block_rows + rows, g * HD : (g + 1) * HD].astype(jnp.float32)
-            kscr[low : low + rows, g * HD : (g + 1) * HD] = rotated(x, cosine, sine)
-        vscr[low : low + rows, :] = data[b][block_rows : block_rows + rows, kv_cols : 2 * kv_cols]
+            if b == 0:
+                x = own_k_ref[:, g * HD : (g + 1) * HD]
+            else:
+                x = data[b][block_rows : block_rows + rows, g * HD : (g + 1) * HD]
+            kscr[low : low + rows, g * HD : (g + 1) * HD] = rotated(x.astype(jnp.float32), cosine, sine)
+        if b == 0:
+            vscr[low : low + rows, :] = own_v_ref[...]
+        else:
+            vscr[low : low + rows, :] = data[b][block_rows : block_rows + rows, kv_cols : 2 * kv_cols]
 
     token = me * rows + lax.broadcasted_iota(jnp.int32, (rows, 1), 0)
     request, offset, group = info(token)
@@ -99,23 +104,32 @@
         (key_request == request) & (key_index <= token)
     )
     cosine, sine = tables(offset)
-    for h in range(q_heads):
-        g = h // repeat
-        q = rotated(q_ref[:, h * HD : (h + 1) * HD].astype(jnp.float32), cosine, sine)
+    for g in range(q_heads // repeat):
+        heads = range(g * repeat, (g + 1) * repeat)
+        q = jnp.concatenate(
+            [rotated(q_ref[:, h * HD : (h + 1) * HD].astype(jnp.float32), cosine, sine) for h in heads],
+            axis=0,
+        )
         k = kscr[:, g * HD : (g + 1) * HD]
         scores = lax.dot_general(
             q, k, (((1,), (1,)), ((), ())), preferred_element_type=jnp.float32
         ) * scale
-        scores = jnp.where(visible, scores, BIG_NEGATIVE)
-        high = jnp.max(scores, axis=1, keepdims=True)
-        weights = jnp.where(visible, jnp.exp(scores - high), 0.0)
-        total = jnp.sum(weights, axis=1, keepdims=True)
+        weights, totals = [], []
+        for r in range(repeat):
+            part = jnp.where(visible, scores[r * rows : (r + 1) * rows], BIG_NEGATIVE)
+            high = jnp.max(part, axis=1, keepdims=True)
+            part = jnp.exp(part - high)
+            totals.append(jnp.sum(part, axis=1, keepdims=True))
+            weights.append(part.astype(jnp.bfloat16))
         v = vscr[:, g * HD : (g + 1) * HD]
-        summed = jnp.dot(weights.astype(jnp.bfloat16), v, preferred_element_type=jnp.float32)
-        out_ref[:, h * HD : (h + 1) * HD] = (summed / total).astype(out_ref.dtype)
-
-
-def attend(meta, scalars, freq, queries, own_k, own_v, data):
+        summed = jnp.dot(jnp.concatenate(weights, axis=0), v, preferred_element_type=jnp.float32)
+        for r, h in enumerate(heads):
+            out_ref[:, h * HD : (h + 1) * HD] = (summed[r * rows : (r + 1) * rows] / totals[r]).astype(
+                out_ref.dtype
+            )
+
+
+def attend(meta, scalars, queries, own_k, own_v, data):
     devices, block_rows, rows, tails = meta[:4]
     kv_cols = own_k.shape[1]
     q_heads = queries.shape[1] // HD
@@ -128,7 +142,7 @@
     return pl.pallas_call(
         functools.partial(attend_kernel, meta),
         out_shape=jax.ShapeDtypeStruct(queries.shape, jnp.bfloat16),
-        in_specs=[smem] * len(scalars) + [vmem] * (1 + len(arrays)),
+        in_specs=[smem] * len(scalars) + [vmem] * len(arrays),
         out_specs=vmem,
         scratch_shapes=[
             pltpu.VMEM((count, kv_cols), jnp.bfloat16),
@@ -139,7 +153,7 @@
             transcendentals=rows * count * q_heads,
             bytes_accessed=nbytes + queries.size * 2,
         ),
-    )(*scalars, freq, *arrays)
+    )(*scalars, *arrays)
 
 
 def token_info(index, suffix_lengths, request_group):
@@ -215,12 +229,9 @@
         cache = lax.all_to_all(
             jnp.stack([own_k_rot, cache_values_in], axis=0), "tp", split_axis=1, concat_axis=2, tiled=True
         )
-        half = HD // 2
-        freq = jnp.exp(jnp.arange(half, dtype=jnp.float32) * (-2.0 * math.log(500000.0) / HD))
-        freq = jnp.concatenate([freq, freq])[None, :]
         scalars = [me.astype(jnp.int32).reshape(1), suffix_lengths, request_group, block_group]
         meta = (devices, block_rows, rows, min(span, devices - 1), prefix_len, repeat, scale)
-        attended = attend(meta, scalars, freq, queries, own_k_rot, suffix_values, data)
+        attended = attend(meta, scalars, queries, suffix_keys, suffix_values, data)
         return (attended, cache[0], cache[1])
 
     prefix_parts = []

time: 36.2 us -> 37.6 us (1.039)
  starting transfers between devices: 15.8 us -> 18.1 us
  waiting for transfers between devices: 5.57 us -> 7.46 us
  local copies, waits for them, and re-layouts: 6.87 us -> 5.59 us
  Pallas kernels: 5.54 us -> 4.59 us
  other arithmetic: 1.28 us -> 0.63 us
    ppermute x7, waiting for transfers between devices: 2.93 us -> 7.46 us  [shifted(): return lax.ppermute(array, axis, pairs)]
    all_to_all x1, waiting for transfers between devices: 2.64 us -> 0.01 us  [body(): lax.all_to_all(jnp.stack([own_k_rot, cache_values_in], axis=0), 'tp', spl...]
    ppermute x7, starting transfers between devices: 12.5 us -> 14.8 us  [shifted(): return lax.ppermute(array, axis, pairs)]
    pallas_call x1, Pallas kernels: 5.54 us -> 4.59 us  [attend(): pl.pallas_call(functools.partial(attend_kernel, meta), out_shape=jax.Shap...]
    concatenate x1, local copies, waits for them, and re-layouts: 0.76 us -> 0.01 us  [body(): prefix_kv = jnp.concatenate([prefix_keys, prefix_values], axis=1)]
    convert_element_type x1 -> x0, local copies, waits for them, and re-layouts: 0.73 us -> none  [rotate(): return jnp.concatenate([lower * cosine - upper * sine, upper * cosine + l...]
    broadcast_in_dim x1 -> x0, other arithmetic: 0.65 us -> none  [body(): freq = jnp.concatenate([freq, freq])[None, :]]
    unnamed x25 -> x27, local copies, waits for them, and re-layouts: 3.94 us -> 4.15 us
  transfers between devices with their start and end apart: 8 -> 8, of which waited for: 3 -> 3; matrix products, arithmetic and copies ran while one was open for 13% -> 9% of each run, Pallas kernels for 0% -> 0%
where the time goes in v6:
time: 37.6 us; the launch traced here: 37.2 us
  starting transfers between devices  18.1 us (48%)
  waiting for transfers between devices  7.46 us (20%)
  local copies, waits for them, and re-layouts  5.59 us (15%)
  Pallas kernels  4.59 us (12%)
  between operations  0.8 us (2%)
  other arithmetic  0.63 us (2%)
    ppermute x7, starting transfers between devices, shifted(): return lax.ppermute(array, axis, pairs)  14.8 us
    ppermute x7, waiting for transfers between devices, shifted(): return lax.ppermute(array, axis, pairs)  7.46 us
    pallas_call x1, Pallas kernels, attend(): pl.pallas_call(functools.partial(attend_kernel, meta), out_shape=jax.Shap...  4.59 us
    unnamed x27, local copies, waits for them, and re-layouts  4.15 us
    all_to_all x1, starting transfers between devices, body(): lax.all_to_all(jnp.stack([own_k_rot, cache_values_in], axis=0), 'tp', spl...  3.33 us
    another operation x2, local copies, waits for them, and re-layouts, body(): jnp.stack([own_k_rot, cache_values_in], axis=0)  0.9 us
  transfers between devices with their start and end apart: 8, of which 3 were waited for; matrix products, arithmetic and copies ran while one was open for 9% of the time, Pallas kernels for 0%

profile of v6, /device:TPU:0, one launch (start us, length us, event | category | flops | bytes accessed | tf_op | source)
XLA Modules:
  0.0 37.2 jit_solution(14315037740070785056)
XLA Ops:
  0.6 0.8 %constant_dynamic-update-slice_fusion.1 = bf16[64,512]{1,0:T(8,128)(2,1)S(1)} fusion(bf16[64,256]{1,0:T(8,128)(2,1)} %param.11), kind=kLoop, calls=%fused_computation.11 | loop fusion | bytes 65536
  1.4 6.0 %collective-permute-start.1 = (bf16[64,512]{1,0:T(8,128)(2,1)S(1)}, bf16[64,512]{1,0:T(8,128)(2,1)S(1)}, u32[]{:S(2)}, u32[]{:S(2)}) collective-permute-start(bf16[64,512]{1,0:T(8,128)(2,1)S(1)} %constant_dynamic-update-slice_fusion.refs_7_), channel_id=1, source_target_pairs={{0,28},{4,0},{8,4},{12,8},{16,12},{20,16},{24,20},{28,24},{1,29},{... | collective-permute-start | bytes 196616 | tf_op jit(solution)/shard_map/ppermute | solution.py:171
  7.5 0.4 %collective-permute-start.2 = (bf16[64,512]{1,0:T(8,128)(2,1)S(1)}, bf16[64,512]{1,0:T(8,128)(2,1)S(1)}, u32[]{:S(2)}, u32[]{:S(2)}) collective-permute-start(bf16[64,512]{1,0:T(8,128)(2,1)S(1)} %constant_dynamic-update-slice_fusion.refs_7_), channel_id=1, source_target_pairs={{0,24},{4,28},{8,0},{12,4},{16,8},{20,12},{24,16},{28,20},{1,25},{... | collective-permute-start | bytes 196616 | tf_op jit(solution)/shard_map/ppermute | solution.py:171
  7.9 3.0 %collective-permute-start.6 = (bf16[64,512]{1,0:T(8,128)(2,1)S(1)}, bf16[64,512]{1,0:T(8,128)(2,1)S(1)}, u32[]{:S(2)}, u32[]{:S(2)}) collective-permute-start(bf16[64,512]{1,0:T(8,128)(2,1)S(1)} %constant_dynamic-update-slice_fusion.refs_7_), channel_id=1, source_target_pairs={{0,20},{4,24},{8,28},{12,0},{16,4},{20,8},{24,12},{28,16},{1,21},{... | collective-permute-start | bytes 196616 | tf_op jit(solution)/shard_map/ppermute | solution.py:171
  10.9 0.7 %copy-done.4 = s32[24]{0:T(128)S(1)} copy-done((s32[24]{0:T(128)S(1)}, s32[24]{0:T(128)}, u32[]{:S(2)}) %copy-start.4) | copy-done | bytes 120
  11.7 0.1 reduce
  12.0 0.2 multiply_cosine_fusion
  12.3 0.2 collective-permute-done.2.refs_13_
  12.5 0.1 copy.26
  12.6 0.3 copy-done.6
  12.9 0.2 copy-done.7
  13.1 0.2 copy-done
  13.4 0.1 copy.24
  13.5 0.8 %copy.27 = bf16[2,128,256]{2,0,1:T(2,128)(2,1)} copy(bf16[2,128,256]{1,2,0:T(8,128)(2,1)S(1)} %pad_maximum_fusion) | data formatting | bytes 262144 | tf_op jit(solution)/shard_map/stack | solution.py:230
  14.3 3.3 %all-to-all-start = ((bf16[2,128,256]{2,0,1:T(2,128)(2,1)}), bf16[2,128,256]{2,0,1:T(2,128)(2,1)S(1)}, u32[]{:S(2)}, u32[]{:S(2)}) async-start(bf16[2,128,256]{2,0,1:T(2,128)(2,1)} %copy.27), calls=%async_computation | async-start | bytes 262144 | tf_op jit(solution)/shard_map/all_to_all | solution.py:229
  17.7 2.4 %collective-permute-start = (bf16[192,512]{1,0:T(8,128)(2,1)S(1)}, bf16[192,512]{1,0:T(8,128)(2,1)S(1)}, u32[]{:S(2)}, u32[]{:S(2)}) collective-permute-start(bf16[192,512]{1,0:T(8,128)(2,1)S(1)} %maximum_maximum_fusion), channel_id=1, source_target_pairs={{0,4},{4,8},{8,12},{12,16},{16,20},{20,24},{24,28},{28,0},{1,5},{5... | collective-permute-start | bytes 589832 | tf_op jit(solution)/shard_map/ppermute | solution.py:171
  20.0 3.0 %collective-permute-start.4 = (bf16[64,512]{1,0:T(8,128)(2,1)S(1)}, bf16[64,512]{1,0:T(8,128)(2,1)S(1)}, u32[]{:S(2)}, u32[]{:S(2)}) collective-permute-start(bf16[64,512]{1,0:T(8,128)(2,1)S(1)} %constant_dynamic-update-slice_fusion.refs_7_), channel_id=1, source_target_pairs={{0,12},{4,16},{8,20},{12,24},{16,28},{20,0},{24,4},{28,8},{1,13},{... | collective-permute-start | bytes 196616 | tf_op jit(solution)/shard_map/ppermute | solution.py:171
  23.0 0.2 fusion
  23.3 0.6 %copy.30 = bf16[4,8,4,256]{3,1,2,0:T(8,128)(2,1)} copy(bf16[4,8,4,256]{3,2,1,0:T(4,128)(2,1)S(1)} %bitcast.16) | data formatting | bytes 131072
  24.0 0.6 %copy.31 = bf16[4,8,4,256]{3,1,2,0:T(8,128)(2,1)} copy(bf16[4,8,4,256]{3,2,1,0:T(4,128)(2,1)S(1)} %bitcast.17) | data formatting | bytes 131072
  24.7 2.0 %collective-permute-done.3.refs_9_ = bf16[64,512]{1,0:T(8,128)(2,1)S(1)} collective-permute-done((bf16[64,512]{1,0:T(8,128)(2,1)S(1)}, bf16[64,512]{1,0:T(8,128)(2,1)S(1)}, u32[]{:S(2)}, u32[]{:S(2)}) %collective-permute-start.3) | collective-permute-done | bytes 65568 | tf_op jit(solution)/shard_map/ppermute | solution.py:171
  26.7 5.2 %collective-permute-done.4.refs_10_ = bf16[64,512]{1,0:T(8,128)(2,1)S(1)} collective-permute-done((bf16[64,512]{1,0:T(8,128)(2,1)S(1)}, bf16[64,512]{1,0:T(8,128)(2,1)S(1)}, u32[]{:S(2)}, u32[]{:S(2)}) %collective-permute-start.4) | collective-permute-done | bytes 65568 | tf_op jit(solution)/shard_map/ppermute | solution.py:171
  31.9 0.6 %copy-done.11 = bf16[64,512]{1,0:T(8,128)(2,1)} copy-done((bf16[64,512]{1,0:T(8,128)(2,1)}, bf16[64,512]{1,0:T(8,128)(2,1)S(1)}, u32[]{:S(2)}) %copy-start.11) | copy-done | bytes 65560
  32.6 4.6 %shard_map.103 = bf16[128,1024]{1,0:T(8,128)(2,1)} custom-call(s32[1]{0:T(128)} %bitcast.refs_0_, s32[24]{0:T(128)} %refs_1_.1, s32[24]{0:T(128)} %refs_2_.1, s32[8]{0:T(128)} %refs_3_.1, bf16[128,1024]{1,0:T(8,128)(2,1)} %refs_4_.1, bf16[128,256]{1,0:T(8,128)(2,1)} %refs_5_.1, bf16[128,256]{1,0:T(8,128)(2,1)} %refs_6_.1, bf16[64,512]{1,0:T(8,128)(2,1)} %copy-done.2, ...), custom_call_target="tpu_custom_call" | custom-call | flops 402653184 | bytes 1310720 | tf_op jit(solution)/shard_map/pallas_call | solution.py:142
  (41 shorter events, 0.7 us)
Async XLA Ops:
  0.6 0.8 %copy-start.3 = (bf16[64,256]{1,0:T(8,128)(2,1)S(1)}, bf16[64,256]{1,0:T(8,128)(2,1)}, u32[]{:S(2)}) copy-start(bf16[64,256]{1,0:T(8,128)(2,1)} %param.12) | copy-start | bytes 98308
  1.4 18.6 %copy-start.2 = (bf16[64,512]{1,0:T(8,128)(2,1)}, bf16[64,512]{1,0:T(8,128)(2,1)S(1)}, u32[]{:S(2)}) copy-start(bf16[64,512]{1,0:T(8,128)(2,1)S(1)} %constant_dynamic-update-slice_fusion.refs_7_) | copy-start | bytes 196612
  1.4 10.8 %collective-permute-start.1 = (bf16[64,512]{1,0:T(8,128)(2,1)S(1)}, bf16[64,512]{1,0:T(8,128)(2,1)S(1)}, u32[]{:S(2)}, u32[]{:S(2)}) collective-permute-start(bf16[64,512]{1,0:T(8,128)(2,1)S(1)} %constant_dynamic-update-slice_fusion.refs_7_), channel_id=1, source_target_pairs={{0,28},{4,0},{8,4},{12,8},{16,12},{20,16},{24,20},{28,24},{1,29},{... | collective-permute-start | bytes 196616 | tf_op jit(solution)/shard_map/ppermute | solution.py:171
  7.5 5.0 %collective-permute-start.2 = (bf16[64,512]{1,0:T(8,128)(2,1)S(1)}, bf16[64,512]{1,0:T(8,128)(2,1)S(1)}, u32[]{:S(2)}, u32[]{:S(2)}) collective-permute-start(bf16[64,512]{1,0:T(8,128)(2,1)S(1)} %constant_dynamic-update-slice_fusion.refs_7_), channel_id=1, source_target_pairs={{0,24},{4,28},{8,0},{12,4},{16,8},{20,12},{24,16},{28,20},{1,25},{... | collective-permute-start | bytes 196616 | tf_op jit(solution)/shard_map/ppermute | solution.py:171
  7.9 16.8 %collective-permute-start.5 = (bf16[64,512]{1,0:T(8,128)(2,1)S(1)}, bf16[64,512]{1,0:T(8,128)(2,1)S(1)}, u32[]{:S(2)}, u32[]{:S(2)}) collective-permute-start(bf16[64,512]{1,0:T(8,128)(2,1)S(1)} %constant_dynamic-update-slice_fusion.refs_7_), channel_id=1, source_target_pairs={{0,16},{4,20},{8,24},{12,28},{16,0},{20,4},{24,8},{28,12},{1,17},{... | collective-permute-start | bytes 196616 | tf_op jit(solution)/shard_map/ppermute | solution.py:171
  7.9 16.8 %collective-permute-start.6 = (bf16[64,512]{1,0:T(8,128)(2,1)S(1)}, bf16[64,512]{1,0:T(8,128)(2,1)S(1)}, u32[]{:S(2)}, u32[]{:S(2)}) collective-permute-start(bf16[64,512]{1,0:T(8,128)(2,1)S(1)} %constant_dynamic-update-slice_fusion.refs_7_), channel_id=1, source_target_pairs={{0,20},{4,24},{8,28},{12,0},{16,4},{20,8},{24,12},{28,16},{1,21},{... | collective-permute-start | bytes 196616 | tf_op jit(solution)/shard_map/ppermute | solution.py:171
  10.9 0.7 %copy-start.4 = (s32[24]{0:T(128)S(1)}, s32[24]{0:T(128)}, u32[]{:S(2)}) copy-start(s32[24]{0:T(128)} %refs_1_.1) | copy-start | bytes 292
  11.6 0.9 %copy-start.1 = (bf16[128,256]{1,0:T(8,128)(2,1)S(1)}, bf16[128,256]{1,0:T(8,128)(2,1)}, u32[]{:S(2)}) copy-start(bf16[128,256]{1,0:T(8,128)(2,1)} %refs_6_.1) | copy-start | bytes 196612
  12.3 0.6 %copy-start.6 = (bf16[64,512]{1,0:T(8,128)(2,1)}, bf16[64,512]{1,0:T(8,128)(2,1)S(1)}, u32[]{:S(2)}) copy-start(bf16[64,512]{1,0:T(8,128)(2,1)S(1)} %collective-permute-done.1.refs_14_) | copy-start | bytes 196612
  12.5 0.6 %copy-start.7 = (bf16[64,512]{1,0:T(8,128)(2,1)}, bf16[64,512]{1,0:T(8,128)(2,1)S(1)}, u32[]{:S(2)}) copy-start(bf16[64,512]{1,0:T(8,128)(2,1)S(1)} %collective-permute-done.2.refs_13_) | copy-start | bytes 196612
  12.5 0.9 %copy-start = (bf16[128,256]{1,0:T(8,128)(2,1)S(1)}, bf16[128,256]{1,0:T(8,128)(2,1)}, u32[]{:S(2)}) copy-start(bf16[128,256]{1,0:T(8,128)(2,1)} %refs_5_.1) | copy-start | bytes 196612
  14.3 8.7 %all-to-all-start = ((bf16[2,128,256]{2,0,1:T(2,128)(2,1)}), bf16[2,128,256]{2,0,1:T(2,128)(2,1)S(1)}, u32[]{:S(2)}, u32[]{:S(2)}) async-start(bf16[2,128,256]{2,0,1:T(2,128)(2,1)} %copy.27), calls=%async_computation | async-start | bytes 262144 | tf_op jit(solution)/shard_map/all_to_all | solution.py:229
  17.7 14.2 %collective-permute-start = (bf16[192,512]{1,0:T(8,128)(2,1)S(1)}, bf16[192,512]{1,0:T(8,128)(2,1)S(1)}, u32[]{:S(2)}, u32[]{:S(2)}) collective-permute-start(bf16[192,512]{1,0:T(8,128)(2,1)S(1)} %maximum_maximum_fusion), channel_id=1, source_target_pairs={{0,4},{4,8},{8,12},{12,16},{16,20},{20,24},{24,28},{28,0},{1,5},{5... | collective-permute-start | bytes 589832 | tf_op jit(solution)/shard_map/ppermute | solution.py:171
  20.0 6.7 %collective-permute-start.3 = (bf16[64,512]{1,0:T(8,128)(2,1)S(1)}, bf16[64,512]{1,0:T(8,128)(2,1)S(1)}, u32[]{:S(2)}, u32[]{:S(2)}) collective-permute-start(bf16[64,512]{1,0:T(8,128)(2,1)S(1)} %constant_dynamic-update-slice_fusion.refs_7_), channel_id=1, source_target_pairs={{0,8},{4,12},{8,16},{12,20},{16,24},{20,28},{24,0},{28,4},{1,9},{5... | collective-permute-start | bytes 196616 | tf_op jit(solution)/shard_map/ppermute | solution.py:171
  20.0 11.9 %collective-permute-start.4 = (bf16[64,512]{1,0:T(8,128)(2,1)S(1)}, bf16[64,512]{1,0:T(8,128)(2,1)S(1)}, u32[]{:S(2)}, u32[]{:S(2)}) collective-permute-start(bf16[64,512]{1,0:T(8,128)(2,1)S(1)} %constant_dynamic-update-slice_fusion.refs_7_), channel_id=1, source_target_pairs={{0,12},{4,16},{8,20},{12,24},{16,28},{20,0},{24,4},{28,8},{1,13},{... | collective-permute-start | bytes 196616 | tf_op jit(solution)/shard_map/ppermute | solution.py:171
  24.7 7.3 %copy-start.8 = (bf16[64,512]{1,0:T(8,128)(2,1)}, bf16[64,512]{1,0:T(8,128)(2,1)S(1)}, u32[]{:S(2)}) copy-start(bf16[64,512]{1,0:T(8,128)(2,1)S(1)} %collective-permute-done.5.refs_11_) | copy-start | bytes 196612
  24.7 7.3 %copy-start.9 = (bf16[64,512]{1,0:T(8,128)(2,1)}, bf16[64,512]{1,0:T(8,128)(2,1)S(1)}, u32[]{:S(2)}) copy-start(bf16[64,512]{1,0:T(8,128)(2,1)S(1)} %collective-permute-done.6.refs_12_) | copy-start | bytes 196612
  26.7 5.2 %copy-start.10 = (bf16[64,512]{1,0:T(8,128)(2,1)}, bf16[64,512]{1,0:T(8,128)(2,1)S(1)}, u32[]{:S(2)}) copy-start(bf16[64,512]{1,0:T(8,128)(2,1)S(1)} %collective-permute-done.3.refs_9_) | copy-start | bytes 196612
  31.9 0.6 %copy-start.11 = (bf16[64,512]{1,0:T(8,128)(2,1)}, bf16[64,512]{1,0:T(8,128)(2,1)S(1)}, u32[]{:S(2)}) copy-start(bf16[64,512]{1,0:T(8,128)(2,1)S(1)} %collective-permute-done.4.refs_10_) | copy-start | bytes 196612
  31.9 0.7 %copy-start.5 = (bf16[192,512]{1,0:T(8,128)(2,1)}, bf16[192,512]{1,0:T(8,128)(2,1)S(1)}, u32[]{:S(2)}) copy-start(bf16[192,512]{1,0:T(8,128)(2,1)S(1)} %collective-permute-done.refs_8_) | copy-start | bytes 589828

commit v7 on v6

--- a/solution.py
+++ b/solution.py
@@ -205,30 +205,31 @@
         return key_index, key_request, k_rot
 
     if devices <= 16:
+        _, own_offset, _ = token_info(index, suffix_lengths, request_group)
+        own_k_rot = rotate(suffix_keys.reshape(rows, kv_heads, HD), own_offset + prefix_len).reshape(
+            rows, kv_cols
+        )
+        stacked, both, early_kv = lax.optimization_barrier(
+            (
+                jnp.stack([own_k_rot, suffix_values], axis=0),
+                jnp.concatenate([prefix_kv, suffix_kv], axis=0),
+                prefix_kv,
+            )
+        )
+        cache = lax.all_to_all(stacked, "tp", split_axis=1, concat_axis=2, tiled=True)
         received = {}
         late = list(range(span + 1, devices))[: max(0, devices - 1 - 5)]
         for by in range(1, devices):
             if by <= span:
-                received[by] = shifted(jnp.concatenate([prefix_kv, suffix_kv], axis=0), "seq", by, True)
+                received[by] = shifted(both, "seq", by, True)
             elif by not in late:
-                received[by] = shifted(prefix_kv, "seq", by, True)
+                received[by] = shifted(early_kv, "seq", by, True)
         gates = tuple(received[devices - 1 - i] for i in range(len(late)))
-        gates, payload, cache_keys_in, cache_values_in = lax.optimization_barrier(
-            (gates, prefix_kv, suffix_keys, suffix_values)
-        )
+        gates, payload = lax.optimization_barrier((gates, prefix_kv))
         for i, by in enumerate(late):
             received[devices - 1 - i] = gates[i]
             received[by] = shifted(payload, "seq", by, True)
         data = [prefix_kv] + [received[by] for by in range(1, devices)]
-        if not late:
-            cache_keys_in, cache_values_in = suffix_keys, suffix_values
-        _, own_offset, _ = token_info(index, suffix_lengths, request_group)
-        own_k_rot = rotate(cache_keys_in.reshape(rows, kv_heads, HD), own_offset + prefix_len).reshape(
-            rows, kv_cols
-        )
-        cache = lax.all_to_all(
-            jnp.stack([own_k_rot, cache_values_in], axis=0), "tp", split_axis=1, concat_axis=2, tiled=True
-        )
         scalars = [me.astype(jnp.int32).reshape(1), suffix_lengths, request_group, block_group]
         meta = (devices, block_rows, rows, min(span, devices - 1), prefix_len, repeat, scale)
         attended = attend(meta, scalars, queries, suffix_keys, suffix_values, data)

time: 37.6 us -> 37 us (0.984)
  starting transfers between devices: 18.1 us -> 15.8 us
  waiting for transfers between devices: 7.46 us -> 9.3 us
    ppermute x7, starting transfers between devices: 14.8 us -> 11.6 us  [shifted(): return lax.ppermute(array, axis, pairs)]
    ppermute x7, waiting for transfers between devices: 7.46 us -> 9.3 us  [shifted(): return lax.ppermute(array, axis, pairs)]
    all_to_all x1, starting transfers between devices: 3.33 us -> 4.24 us  [body(): lax.all_to_all(stacked, 'tp', split_axis=1, concat_axis=2, tiled=True)]
    optimization_barrier x0 -> x1, local copies, waits for them, and re-layouts: none -> 0.79 us  [body(): lax.optimization_barrier((jnp.stack([own_k_rot, suffix_values], axis=0),...]
    another operation x3 -> x2, local copies, waits for them, and re-layouts: 0.98 us -> 0.2 us  [the longest x1 0.11 us: body(): jnp.stack([own_k_rot, suffix_values], axis=0)]
    unnamed x27 -> x29, local copies, waits for them, and re-layouts: 4.15 us -> 3.98 us
  transfers between devices with their start and end apart: 8 -> 8, of which waited for: 3 -> 2; matrix products, arithmetic and copies ran while one was open for 9% -> 4% of each run, Pallas kernels for 0% -> 0%
where the time goes in v7:
time: 37 us; the launch traced here: 36.6 us
  starting transfers between devices  15.8 us (43%)
  waiting for transfers between devices  9.3 us (25%)
  local copies, waits for them, and re-layouts  5.43 us (15%)
  Pallas kernels  4.59 us (12%)
  between operations  0.85 us (2%)
  other arithmetic  0.62 us (2%)
    ppermute x7, starting transfers between devices, shifted(): return lax.ppermute(array, axis, pairs)  11.6 us
    ppermute x7, waiting for transfers between devices, shifted(): return lax.ppermute(array, axis, pairs)  9.3 us
    pallas_call x1, Pallas kernels, attend(): pl.pallas_call(functools.partial(attend_kernel, meta), out_shape=jax.Shap...  4.59 us
    all_to_all x1, starting transfers between devices, body(): lax.all_to_all(stacked, 'tp', split_axis=1, concat_axis=2, tiled=True)  4.24 us
    unnamed x29, local copies, waits for them, and re-layouts  3.98 us
    optimization_barrier x1, local copies, waits for them, and re-layouts, body(): lax.optimization_barrier((jnp.stack([own_k_rot, suffix_values], axis=0),...  0.79 us
  transfers between devices with their start and end apart: 8, of which 2 were waited for; matrix products, arithmetic and copies ran while one was open for 4% of the time, Pallas kernels for 0%

profile of v7, /device:TPU:0, one launch (start us, length us, event | category | flops | bytes accessed | tf_op | source)
XLA Modules:
  0.0 36.6 jit_solution(12919409743991846444)
XLA Ops:
  0.7 0.6 %copy-done.5 = s32[24]{0:T(128)S(1)} copy-done((s32[24]{0:T(128)S(1)}, s32[24]{0:T(128)}, u32[]{:S(2)}) %copy-start.5) | copy-done | bytes 120
  1.4 0.1 reduce
  1.6 0.1 convert_reduce_fusion
  1.7 0.1 select_reduce_fusion
  1.8 0.1 copy.26
  1.9 0.7 %copy-done = bf16[128,256]{1,0:T(8,128)(2,1)S(1)} copy-done((bf16[128,256]{1,0:T(8,128)(2,1)S(1)}, bf16[128,256]{1,0:T(8,128)(2,1)}, u32[]{:S(2)}) %copy-start) | copy-done | bytes 65560
  2.6 0.1 copy.24
  2.7 0.7 %copy-done.4 = bf16[64,256]{1,0:T(8,128)(2,1)S(1)} copy-done((bf16[64,256]{1,0:T(8,128)(2,1)S(1)}, bf16[64,256]{1,0:T(8,128)(2,1)}, u32[]{:S(2)}) %copy-start.4) | copy-done | bytes 32792
  3.4 0.2 multiply_cosine_fusion
  3.7 0.8 %copy.27 = bf16[2,128,256]{2,0,1:T(2,128)(2,1)} copy(bf16[2,128,256]{1,2,0:T(8,128)(2,1)S(1)} %pad_maximum_fusion) | data formatting | bytes 262144 | tf_op jit(solution)/shard_map/optimization_barrier | solution.py:212
  4.5 4.2 %all-to-all-start = ((bf16[2,128,256]{2,0,1:T(2,128)(2,1)}), bf16[2,128,256]{2,0,1:T(2,128)(2,1)S(1)}, u32[]{:S(2)}, u32[]{:S(2)}) async-start(bf16[2,128,256]{2,0,1:T(2,128)(2,1)} %copy.27), calls=%async_computation | async-start | bytes 262144 | tf_op jit(solution)/shard_map/all_to_all | solution.py:219
  8.7 4.2 %collective-permute-start.2 = (bf16[64,512]{1,0:T(8,128)(2,1)S(1)}, bf16[64,512]{1,0:T(8,128)(2,1)S(1)}, u32[]{:S(2)}, u32[]{:S(2)}) collective-permute-start(bf16[64,512]{1,0:T(8,128)(2,1)S(1)} %constant_dynamic-update-slice_fusion.refs_7_), channel_id=1, source_target_pairs={{0,24},{4,28},{8,0},{12,4},{16,8},{20,12},{24,16},{28,20},{1,25},{... | collective-permute-start | bytes 196616 | tf_op jit(solution)/shard_map/ppermute | solution.py:171
  12.9 1.4 %collective-permute-start.1 = (bf16[64,512]{1,0:T(8,128)(2,1)S(1)}, bf16[64,512]{1,0:T(8,128)(2,1)S(1)}, u32[]{:S(2)}, u32[]{:S(2)}) collective-permute-start(bf16[64,512]{1,0:T(8,128)(2,1)S(1)} %constant_dynamic-update-slice_fusion.refs_7_), channel_id=1, source_target_pairs={{0,28},{4,0},{8,4},{12,8},{16,12},{20,16},{24,20},{28,24},{1,29},{... | collective-permute-start | bytes 196616 | tf_op jit(solution)/shard_map/ppermute | solution.py:171
  14.3 3.0 %collective-permute-start.5 = (bf16[64,512]{1,0:T(8,128)(2,1)S(1)}, bf16[64,512]{1,0:T(8,128)(2,1)S(1)}, u32[]{:S(2)}, u32[]{:S(2)}) collective-permute-start(bf16[64,512]{1,0:T(8,128)(2,1)S(1)} %constant_dynamic-update-slice_fusion.refs_7_), channel_id=1, source_target_pairs={{0,16},{4,20},{8,24},{12,28},{16,0},{20,4},{24,8},{28,12},{1,17},{... | collective-permute-start | bytes 196616 | tf_op jit(solution)/shard_map/ppermute | solution.py:171
  17.3 1.5 %collective-permute-start = (bf16[192,512]{1,0:T(8,128)(2,1)S(1)}, bf16[192,512]{1,0:T(8,128)(2,1)S(1)}, u32[]{:S(2)}, u32[]{:S(2)}) collective-permute-start(bf16[192,512]{1,0:T(8,128)(2,1)S(1)} %maximum_maximum_fusion), channel_id=1, source_target_pairs={{0,4},{4,8},{8,12},{12,16},{16,20},{20,24},{24,28},{28,0},{1,5},{5... | collective-permute-start | bytes 589832 | tf_op jit(solution)/shard_map/ppermute | solution.py:171
  18.9 1.4 %collective-permute-start.3 = (bf16[64,512]{1,0:T(8,128)(2,1)S(1)}, bf16[64,512]{1,0:T(8,128)(2,1)S(1)}, u32[]{:S(2)}, u32[]{:S(2)}) collective-permute-start(bf16[64,512]{1,0:T(8,128)(2,1)S(1)} %constant_dynamic-update-slice_fusion.refs_7_), channel_id=1, source_target_pairs={{0,8},{4,12},{8,16},{12,20},{16,24},{20,28},{24,0},{28,4},{1,9},{5... | collective-permute-start | bytes 196616 | tf_op jit(solution)/shard_map/ppermute | solution.py:171
  20.3 0.2 fusion
  20.5 0.1 copy.29
  20.6 0.6 %copy.31 = bf16[4,8,4,256]{3,1,2,0:T(8,128)(2,1)} copy(bf16[4,8,4,256]{3,2,1,0:T(4,128)(2,1)S(1)} %bitcast.16) | data formatting | bytes 131072
  21.4 0.6 %copy.30 = bf16[4,8,4,256]{3,1,2,0:T(8,128)(2,1)} copy(bf16[4,8,4,256]{3,2,1,0:T(4,128)(2,1)S(1)} %bitcast.17) | data formatting | bytes 131072
  22.0 2.2 %collective-permute-done.5.refs_11_ = bf16[64,512]{1,0:T(8,128)(2,1)S(1)} collective-permute-done((bf16[64,512]{1,0:T(8,128)(2,1)S(1)}, bf16[64,512]{1,0:T(8,128)(2,1)S(1)}, u32[]{:S(2)}, u32[]{:S(2)}) %collective-permute-start.5) | collective-permute-done | bytes 65568 | tf_op jit(solution)/shard_map/ppermute | solution.py:171
  24.2 7.1 %collective-permute-done.4.refs_10_ = bf16[64,512]{1,0:T(8,128)(2,1)S(1)} collective-permute-done((bf16[64,512]{1,0:T(8,128)(2,1)S(1)}, bf16[64,512]{1,0:T(8,128)(2,1)S(1)}, u32[]{:S(2)}, u32[]{:S(2)}) %collective-permute-start.4) | collective-permute-done | bytes 65568 | tf_op jit(solution)/shard_map/ppermute | solution.py:171
  31.3 0.6 %copy-done.11 = bf16[64,512]{1,0:T(8,128)(2,1)} copy-done((bf16[64,512]{1,0:T(8,128)(2,1)}, bf16[64,512]{1,0:T(8,128)(2,1)S(1)}, u32[]{:S(2)}) %copy-start.11) | copy-done | bytes 65560
  32.0 4.6 %shard_map.103 = bf16[128,1024]{1,0:T(8,128)(2,1)} custom-call(s32[1]{0:T(128)} %bitcast.refs_0_, s32[24]{0:T(128)} %refs_1_.1, s32[24]{0:T(128)} %refs_2_.1, s32[8]{0:T(128)} %refs_3_.1, bf16[128,1024]{1,0:T(8,128)(2,1)} %refs_4_.1, bf16[128,256]{1,0:T(8,128)(2,1)} %refs_5_.1, bf16[128,256]{1,0:T(8,128)(2,1)} %refs_6_.1, bf16[64,512]{1,0:T(8,128)(2,1)} %copy-done.2, ...), custom_call_target="tpu_custom_call" | custom-call | flops 402653184 | bytes 1310720 | tf_op jit(solution)/shard_map/pallas_call | solution.py:142
  (43 shorter events, 0.5 us)
Async XLA Ops:
  0.7 0.7 %copy-start.5 = (s32[24]{0:T(128)S(1)}, s32[24]{0:T(128)}, u32[]{:S(2)}) copy-start(s32[24]{0:T(128)} %refs_1_.1) | copy-start | bytes 292
  0.7 1.1 %copy-start.3 = (bf16[64,256]{1,0:T(8,128)(2,1)S(1)}, bf16[64,256]{1,0:T(8,128)(2,1)}, u32[]{:S(2)}) copy-start(bf16[64,256]{1,0:T(8,128)(2,1)} %param.11) | copy-start | bytes 98308
  0.7 1.1 %copy-start.1 = (bf16[128,256]{1,0:T(8,128)(2,1)S(1)}, bf16[128,256]{1,0:T(8,128)(2,1)}, u32[]{:S(2)}) copy-start(bf16[128,256]{1,0:T(8,128)(2,1)} %refs_6_.1) | copy-start | bytes 196612
  1.8 0.8 %copy-start = (bf16[128,256]{1,0:T(8,128)(2,1)S(1)}, bf16[128,256]{1,0:T(8,128)(2,1)}, u32[]{:S(2)}) copy-start(bf16[128,256]{1,0:T(8,128)(2,1)} %refs_5_.1) | copy-start | bytes 196612
  2.6 0.8 %copy-start.4 = (bf16[64,256]{1,0:T(8,128)(2,1)S(1)}, bf16[64,256]{1,0:T(8,128)(2,1)}, u32[]{:S(2)}) copy-start(bf16[64,256]{1,0:T(8,128)(2,1)} %param.12) | copy-start | bytes 98308
  3.4 15.5 %copy-start.2 = (bf16[64,512]{1,0:T(8,128)(2,1)}, bf16[64,512]{1,0:T(8,128)(2,1)S(1)}, u32[]{:S(2)}) copy-start(bf16[64,512]{1,0:T(8,128)(2,1)S(1)} %constant_dynamic-update-slice_fusion.refs_7_) | copy-start | bytes 196612
  4.5 15.9 %all-to-all-start = ((bf16[2,128,256]{2,0,1:T(2,128)(2,1)}), bf16[2,128,256]{2,0,1:T(2,128)(2,1)S(1)}, u32[]{:S(2)}, u32[]{:S(2)}) async-start(bf16[2,128,256]{2,0,1:T(2,128)(2,1)} %copy.27), calls=%async_computation | async-start | bytes 262144 | tf_op jit(solution)/shard_map/all_to_all | solution.py:219
  8.7 10.1 %collective-permute-start.2 = (bf16[64,512]{1,0:T(8,128)(2,1)S(1)}, bf16[64,512]{1,0:T(8,128)(2,1)S(1)}, u32[]{:S(2)}, u32[]{:S(2)}) collective-permute-start(bf16[64,512]{1,0:T(8,128)(2,1)S(1)} %constant_dynamic-update-slice_fusion.refs_7_), channel_id=1, source_target_pairs={{0,24},{4,28},{8,0},{12,4},{16,8},{20,12},{24,16},{28,20},{1,25},{... | collective-permute-start | bytes 196616 | tf_op jit(solution)/shard_map/ppermute | solution.py:171
  12.9 5.9 %collective-permute-start.1 = (bf16[64,512]{1,0:T(8,128)(2,1)S(1)}, bf16[64,512]{1,0:T(8,128)(2,1)S(1)}, u32[]{:S(2)}, u32[]{:S(2)}) collective-permute-start(bf16[64,512]{1,0:T(8,128)(2,1)S(1)} %constant_dynamic-update-slice_fusion.refs_7_), channel_id=1, source_target_pairs={{0,28},{4,0},{8,4},{12,8},{16,12},{20,16},{24,20},{28,24},{1,29},{... | collective-permute-start | bytes 196616 | tf_op jit(solution)/shard_map/ppermute | solution.py:171
  14.3 7.7 %collective-permute-start.6 = (bf16[64,512]{1,0:T(8,128)(2,1)S(1)}, bf16[64,512]{1,0:T(8,128)(2,1)S(1)}, u32[]{:S(2)}, u32[]{:S(2)}) collective-permute-start(bf16[64,512]{1,0:T(8,128)(2,1)S(1)} %constant_dynamic-update-slice_fusion.refs_7_), channel_id=1, source_target_pairs={{0,20},{4,24},{8,28},{12,0},{16,4},{20,8},{24,12},{28,16},{1,21},{... | collective-permute-start | bytes 196616 | tf_op jit(solution)/shard_map/ppermute | solution.py:171
  14.3 9.9 %collective-permute-start.5 = (bf16[64,512]{1,0:T(8,128)(2,1)S(1)}, bf16[64,512]{1,0:T(8,128)(2,1)S(1)}, u32[]{:S(2)}, u32[]{:S(2)}) collective-permute-start(bf16[64,512]{1,0:T(8,128)(2,1)S(1)} %constant_dynamic-update-slice_fusion.refs_7_), channel_id=1, source_target_pairs={{0,16},{4,20},{8,24},{12,28},{16,0},{20,4},{24,8},{28,12},{1,17},{... | collective-permute-start | bytes 196616 | tf_op jit(solution)/shard_map/ppermute | solution.py:171
  17.3 14.0 %collective-permute-start = (bf16[192,512]{1,0:T(8,128)(2,1)S(1)}, bf16[192,512]{1,0:T(8,128)(2,1)S(1)}, u32[]{:S(2)}, u32[]{:S(2)}) collective-permute-start(bf16[192,512]{1,0:T(8,128)(2,1)S(1)} %maximum_maximum_fusion), channel_id=1, source_target_pairs={{0,4},{4,8},{8,12},{12,16},{16,20},{20,24},{24,28},{28,0},{1,5},{5... | collective-permute-start | bytes 589832 | tf_op jit(solution)/shard_map/ppermute | solution.py:171
  18.8 1.7 %copy-start.7 = (bf16[64,512]{1,0:T(8,128)(2,1)}, bf16[64,512]{1,0:T(8,128)(2,1)S(1)}, u32[]{:S(2)}) copy-start(bf16[64,512]{1,0:T(8,128)(2,1)S(1)} %collective-permute-done.2.refs_13_) | copy-start | bytes 196612
  18.8 1.7 %copy-start.8 = (bf16[64,512]{1,0:T(8,128)(2,1)}, bf16[64,512]{1,0:T(8,128)(2,1)S(1)}, u32[]{:S(2)}) copy-start(bf16[64,512]{1,0:T(8,128)(2,1)S(1)} %collective-permute-done.1.refs_14_) | copy-start | bytes 196612
  18.8 12.5 %collective-permute-start.4 = (bf16[64,512]{1,0:T(8,128)(2,1)S(1)}, bf16[64,512]{1,0:T(8,128)(2,1)S(1)}, u32[]{:S(2)}, u32[]{:S(2)}) collective-permute-start(bf16[64,512]{1,0:T(8,128)(2,1)S(1)} %constant_dynamic-update-slice_fusion.refs_7_), channel_id=1, source_target_pairs={{0,12},{4,16},{8,20},{12,24},{16,28},{20,0},{24,4},{28,8},{1,13},{... | collective-permute-start | bytes 196616 | tf_op jit(solution)/shard_map/ppermute | solution.py:171
  18.9 12.4 %collective-permute-start.3 = (bf16[64,512]{1,0:T(8,128)(2,1)S(1)}, bf16[64,512]{1,0:T(8,128)(2,1)S(1)}, u32[]{:S(2)}, u32[]{:S(2)}) collective-permute-start(bf16[64,512]{1,0:T(8,128)(2,1)S(1)} %constant_dynamic-update-slice_fusion.refs_7_), channel_id=1, source_target_pairs={{0,8},{4,12},{8,16},{12,20},{16,24},{20,28},{24,0},{28,4},{1,9},{5... | collective-permute-start | bytes 196616 | tf_op jit(solution)/shard_map/ppermute | solution.py:171
  22.0 9.3 %copy-start.9 = (bf16[64,512]{1,0:T(8,128)(2,1)}, bf16[64,512]{1,0:T(8,128)(2,1)S(1)}, u32[]{:S(2)}) copy-start(bf16[64,512]{1,0:T(8,128)(2,1)S(1)} %collective-permute-done.6.refs_12_) | copy-start | bytes 196612
  24.2 7.2 %copy-start.10 = (bf16[64,512]{1,0:T(8,128)(2,1)}, bf16[64,512]{1,0:T(8,128)(2,1)S(1)}, u32[]{:S(2)}) copy-start(bf16[64,512]{1,0:T(8,128)(2,1)S(1)} %collective-permute-done.5.refs_11_) | copy-start | bytes 196612
  31.3 0.6 %copy-start.11 = (bf16[64,512]{1,0:T(8,128)(2,1)}, bf16[64,512]{1,0:T(8,128)(2,1)S(1)}, u32[]{:S(2)}) copy-start(bf16[64,512]{1,0:T(8,128)(2,1)S(1)} %collective-permute-done.4.refs_10_) | copy-start | bytes 196612
  31.3 0.6 %copy-start.12 = (bf16[64,512]{1,0:T(8,128)(2,1)}, bf16[64,512]{1,0:T(8,128)(2,1)S(1)}, u32[]{:S(2)}) copy-start(bf16[64,512]{1,0:T(8,128)(2,1)S(1)} %collective-permute-done.3.refs_9_) | copy-start | bytes 196612
  31.3 0.7 %copy-start.6 = (bf16[192,512]{1,0:T(8,128)(2,1)}, bf16[192,512]{1,0:T(8,128)(2,1)S(1)}, u32[]{:S(2)}) copy-start(bf16[192,512]{1,0:T(8,128)(2,1)S(1)} %collective-permute-done.refs_8_) | copy-start | bytes 589828

commit v8 on v7

--- a/solution.py
+++ b/solution.py
@@ -32,10 +32,10 @@
 
 
 def attend_kernel(meta, *refs):
-    devices, block_rows, rows, tails, prefix_len, repeat, scale = meta
+    devices, block_rows, rows, tails, prefix_len, repeat, scale, where_block, arrays = meta
     me_ref, lens_ref, rg_ref, bg_ref, q_ref, own_k_ref, own_v_ref = refs[:7]
-    data = refs[7 : 7 + devices]
-    out_ref, kscr, vscr = refs[7 + devices :]
+    data = refs[7 : 7 + arrays]
+    out_ref, kscr, vscr = refs[7 + arrays :]
     kv_cols = kscr.shape[1]
     count = kscr.shape[0]
     base = devices * block_rows
@@ -70,8 +70,9 @@
         return (x * cosine + pltpu.roll(x, HD // 2, 1) * sine).astype(jnp.bfloat16)
 
     for c in range(devices):
-        kscr[c * block_rows : (c + 1) * block_rows, :] = data[c][0:block_rows, 0:kv_cols]
-        vscr[c * block_rows : (c + 1) * block_rows, :] = data[c][0:block_rows, kv_cols : 2 * kv_cols]
+        at, row = where_block[c]
+        kscr[c * block_rows : (c + 1) * block_rows, :] = data[at][row : row + block_rows, 0:kv_cols]
+        vscr[c * block_rows : (c + 1) * block_rows, :] = data[at][row : row + block_rows, kv_cols : 2 * kv_cols]
     for b in range(0, tails + 1):
         low = base + b * rows
         index = (me - b) * rows + lax.broadcasted_iota(jnp.int32, (rows, 1), 0)
@@ -81,12 +82,14 @@
             if b == 0:
                 x = own_k_ref[:, g * HD : (g + 1) * HD]
             else:
-                x = data[b][block_rows : block_rows + rows, g * HD : (g + 1) * HD]
+                at, row = where_block[devices + b - 1]
+                x = data[at][row : row + rows, g * HD : (g + 1) * HD]
             kscr[low : low + rows, g * HD : (g + 1) * HD] = rotated(x.astype(jnp.float32), cosine, sine)
         if b == 0:
             vscr[low : low + rows, :] = own_v_ref[...]
         else:
-            vscr[low : low + rows, :] = data[b][block_rows : block_rows + rows, kv_cols : 2 * kv_cols]
+            at, row = where_block[devices + b - 1]
+            vscr[low : low + rows, :] = data[at][row : row + rows, kv_cols : 2 * kv_cols]
 
     token = me * rows + lax.broadcasted_iota(jnp.int32, (rows, 1), 0)
     request, offset, group = info(token)
@@ -224,14 +227,33 @@
                 received[by] = shifted(both, "seq", by, True)
             elif by not in late:
                 received[by] = shifted(early_kv, "seq", by, True)
-        gates = tuple(received[devices - 1 - i] for i in range(len(late)))
-        gates, payload = lax.optimization_barrier((gates, prefix_kv))
-        for i, by in enumerate(late):
-            received[devices - 1 - i] = gates[i]
-            received[by] = shifted(payload, "seq", by, True)
-        data = [prefix_kv] + [received[by] for by in range(1, devices)]
+        relay = [devices - i for i in range(1, len(late))]
+        if set(relay) & set(late):
+            gates = tuple(received[devices - 1 - i] for i in range(len(late)))
+            gates, payload = lax.optimization_barrier((gates, prefix_kv))
+            for i, by in enumerate(late):
+                received[devices - 1 - i] = gates[i]
+                received[by] = shifted(payload, "seq", by, True)
+            late = []
+        order = [by for by in range(1, devices) if by in received]
+        data = [prefix_kv] + [received[by] for by in order]
+        where_block = {0: (0, 0)}
+        for at, by in enumerate(order):
+            where_block[by] = (at + 1, 0)
+        for back in range(1, min(span, devices - 1) + 1):
+            where_block[devices + back - 1] = (order.index(back) + 1, block_rows)
+        if late:
+            pieces = [prefix_kv] + [received[by] for by in relay]
+            gates = tuple(received[by] for by in relay)
+            gates, payload = lax.optimization_barrier((gates, jnp.concatenate(pieces, axis=0)))
+            data.append(shifted(payload, "seq", late[-1], True))
+            for i, by in enumerate(reversed(late)):
+                where_block[by] = (len(data) - 1, i * block_rows)
+        where_block = tuple(where_block[c] for c in range(devices + min(span, devices - 1)))
         scalars = [me.astype(jnp.int32).reshape(1), suffix_lengths, request_group, block_group]
-        meta = (devices, block_rows, rows, min(span, devices - 1), prefix_len, repeat, scale)
+        meta = (
+            devices, block_rows, rows, min(span, devices - 1), prefix_len, repeat, scale, where_block, len(data)
+        )
         attended = attend(meta, scalars, queries, suffix_keys, suffix_values, data)
         return (attended, cache[0], cache[1])
 

time: 37 us -> 38.6 us (1.043)
  waiting for transfers between devices: 9.3 us -> 11.8 us
  starting transfers between devices: 15.8 us -> 14.4 us
  local copies, waits for them, and re-layouts: 5.43 us -> 6.04 us
    all_to_all x1, waiting for transfers between devices: 0.01 us -> 2.43 us  [body(): lax.all_to_all(stacked, 'tp', split_axis=1, concat_axis=2, tiled=True)]
    all_to_all x1, starting transfers between devices: 4.24 us -> 3.33 us  [body(): lax.all_to_all(stacked, 'tp', split_axis=1, concat_axis=2, tiled=True)]
    unnamed x29 -> x27, local copies, waits for them, and re-layouts: 3.98 us -> 4.59 us
    ppermute x7 -> x6, starting transfers between devices: 11.6 us -> 11 us  [shifted(): return lax.ppermute(array, axis, pairs)]
    ppermute x7 -> x6, waiting for transfers between devices: 9.3 us -> 9.33 us  [shifted(): return lax.ppermute(array, axis, pairs)]
  transfers between devices with their start and end apart: 8 -> 7, of which waited for: 2 -> 2; matrix products, arithmetic and copies ran while one was open for 4% -> 6% of each run, Pallas kernels for 0% -> 0%
where the time goes in v8:
time: 38.6 us; the launch traced here: 38.2 us
  starting transfers between devices  14.4 us (37%)
  waiting for transfers between devices  11.8 us (31%)
  local copies, waits for them, and re-layouts  6.04 us (16%)
  Pallas kernels  4.63 us (12%)
  between operations  0.83 us (2%)
  other arithmetic  0.63 us (2%)
    ppermute x6, starting transfers between devices, shifted(): return lax.ppermute(array, axis, pairs)  11 us
    ppermute x6, waiting for transfers between devices, shifted(): return lax.ppermute(array, axis, pairs)  9.33 us
    pallas_call x1, Pallas kernels, attend(): pl.pallas_call(functools.partial(attend_kernel, meta), out_shape=jax.Shap...  4.63 us
    unnamed x27, local copies, waits for them, and re-layouts  4.59 us
    all_to_all x1, starting transfers between devices, body(): lax.all_to_all(stacked, 'tp', split_axis=1, concat_axis=2, tiled=True)  3.33 us
    all_to_all x1, waiting for transfers between devices, body(): lax.all_to_all(stacked, 'tp', split_axis=1, concat_axis=2, tiled=True)  2.43 us
    optimization_barrier x1, local copies, waits for them, and re-layouts, body(): lax.optimization_barrier((jnp.stack([own_k_rot, suffix_values], axis=0),...  0.79 us
  transfers between devices with their start and end apart: 7, of which 2 were waited for; matrix products, arithmetic and copies ran while one was open for 6% of the time, Pallas kernels for 0%

profile of v8, /device:TPU:0, one launch (start us, length us, event | category | flops | bytes accessed | tf_op | source)
XLA Modules:
  0.0 38.2 jit_solution(18422619652525516522)
XLA Ops:
  0.7 0.6 %copy-done.6 = s32[24]{0:T(128)S(1)} copy-done((s32[24]{0:T(128)S(1)}, s32[24]{0:T(128)}, u32[]{:S(2)}) %copy-start.6) | copy-done | bytes 120
  1.4 0.1 reduce
  1.6 0.1 convert_reduce_fusion
  1.7 0.1 select_reduce_fusion
  1.8 0.1 copy.26
  1.9 0.7 %copy-done.1 = bf16[128,256]{1,0:T(8,128)(2,1)S(1)} copy-done((bf16[128,256]{1,0:T(8,128)(2,1)S(1)}, bf16[128,256]{1,0:T(8,128)(2,1)}, u32[]{:S(2)}) %copy-start.1) | copy-done | bytes 65560
  2.6 0.1 copy.24
  2.7 0.7 %copy-done.5 = bf16[64,256]{1,0:T(8,128)(2,1)S(1)} copy-done((bf16[64,256]{1,0:T(8,128)(2,1)S(1)}, bf16[64,256]{1,0:T(8,128)(2,1)}, u32[]{:S(2)}) %copy-start.5) | copy-done | bytes 32792
  3.4 0.2 multiply_cosine_fusion
  3.7 6.0 %collective-permute-start.4 = (bf16[64,512]{1,0:T(8,128)(2,1)S(1)}, bf16[64,512]{1,0:T(8,128)(2,1)S(1)}, u32[]{:S(2)}, u32[]{:S(2)}) collective-permute-start(bf16[64,512]{1,0:T(8,128)(2,1)S(1)} %constant_dynamic-update-slice_fusion.refs_7_), channel_id=1, source_target_pairs={{0,28},{4,0},{8,4},{12,8},{16,12},{20,16},{24,20},{28,24},{1,29},{... | collective-permute-start | bytes 196616 | tf_op jit(solution)/shard_map/ppermute | solution.py:174
  9.7 0.4 %collective-permute-start.3 = (bf16[64,512]{1,0:T(8,128)(2,1)S(1)}, bf16[64,512]{1,0:T(8,128)(2,1)S(1)}, u32[]{:S(2)}, u32[]{:S(2)}) collective-permute-start(bf16[64,512]{1,0:T(8,128)(2,1)S(1)} %constant_dynamic-update-slice_fusion.refs_7_), channel_id=1, source_target_pairs={{0,24},{4,28},{8,0},{12,4},{16,8},{20,12},{24,16},{28,20},{1,25},{... | collective-permute-start | bytes 196616 | tf_op jit(solution)/shard_map/ppermute | solution.py:174
  10.2 3.0 %collective-permute-start.1 = (bf16[64,512]{1,0:T(8,128)(2,1)S(1)}, bf16[64,512]{1,0:T(8,128)(2,1)S(1)}, u32[]{:S(2)}, u32[]{:S(2)}) collective-permute-start(bf16[64,512]{1,0:T(8,128)(2,1)S(1)} %constant_dynamic-update-slice_fusion.refs_7_), channel_id=1, source_target_pairs={{0,16},{4,20},{8,24},{12,28},{16,0},{20,4},{24,8},{28,12},{1,17},{... | collective-permute-start | bytes 196616 | tf_op jit(solution)/shard_map/ppermute | solution.py:174
  13.2 0.8 %copy.27 = bf16[2,128,256]{2,0,1:T(2,128)(2,1)} copy(bf16[2,128,256]{1,2,0:T(8,128)(2,1)S(1)} %pad_maximum_fusion) | data formatting | bytes 262144 | tf_op jit(solution)/shard_map/optimization_barrier | solution.py:215
  14.0 3.3 %all-to-all-start = ((bf16[2,128,256]{2,0,1:T(2,128)(2,1)}), bf16[2,128,256]{2,0,1:T(2,128)(2,1)S(1)}, u32[]{:S(2)}, u32[]{:S(2)}) async-start(bf16[2,128,256]{2,0,1:T(2,128)(2,1)} %copy.27), calls=%async_computation | async-start | bytes 262144 | tf_op jit(solution)/shard_map/all_to_all | solution.py:222
  17.3 1.5 %collective-permute-start = (bf16[192,512]{1,0:T(8,128)(2,1)S(1)}, bf16[192,512]{1,0:T(8,128)(2,1)S(1)}, u32[]{:S(2)}, u32[]{:S(2)}) collective-permute-start(bf16[192,512]{1,0:T(8,128)(2,1)S(1)} %maximum_maximum_fusion), channel_id=1, source_target_pairs={{0,4},{4,8},{8,12},{12,16},{16,20},{20,24},{24,28},{28,0},{1,5},{5... | collective-permute-start | bytes 589832 | tf_op jit(solution)/shard_map/ppermute | solution.py:174
  18.9 0.6 %copy-done.3 = bf16[64,512]{1,0:T(8,128)(2,1)} copy-done((bf16[64,512]{1,0:T(8,128)(2,1)}, bf16[64,512]{1,0:T(8,128)(2,1)S(1)}, u32[]{:S(2)}) %copy-start.3) | copy-done | bytes 65560
  19.5 2.4 %all-to-all-done = bf16[2,128,256]{2,0,1:T(2,128)(2,1)S(1)} async-done(((bf16[2,128,256]{2,0,1:T(2,128)(2,1)}), bf16[2,128,256]{2,0,1:T(2,128)(2,1)S(1)}, u32[]{:S(2)}, u32[]{:S(2)}) %all-to-all-start) | async-done | bytes 131104 | tf_op jit(solution)/shard_map/all_to_all | solution.py:222
  21.9 0.2 fusion
  22.1 0.1 copy.29
  22.2 0.6 %copy.31 = bf16[4,8,4,256]{3,1,2,0:T(8,128)(2,1)} copy(bf16[4,8,4,256]{3,2,1,0:T(4,128)(2,1)S(1)} %bitcast.16) | data formatting | bytes 131072
  22.9 0.6 %copy.30 = bf16[4,8,4,256]{3,1,2,0:T(8,128)(2,1)} copy(bf16[4,8,4,256]{3,2,1,0:T(4,128)(2,1)S(1)} %bitcast.17) | data formatting | bytes 131072
  23.6 9.3 %collective-permute-done.5.refs_13_ = bf16[128,512]{1,0:T(8,128)(2,1)S(1)} collective-permute-done((bf16[128,512]{1,0:T(8,128)(2,1)S(1)}, bf16[128,512]{1,0:T(8,128)(2,1)S(1)}, u32[]{:S(2)}, u32[]{:S(2)}) %collective-permute-start.5) | collective-permute-done | bytes 131104 | tf_op jit(solution)/shard_map/ppermute | solution.py:174
  32.9 0.6 %copy-done.8 = bf16[128,512]{1,0:T(8,128)(2,1)} copy-done((bf16[128,512]{1,0:T(8,128)(2,1)}, bf16[128,512]{1,0:T(8,128)(2,1)S(1)}, u32[]{:S(2)}) %copy-start.8) | copy-done | bytes 131096
  33.6 4.6 %shard_map.103 = bf16[128,1024]{1,0:T(8,128)(2,1)} custom-call(s32[1]{0:T(128)} %bitcast.refs_0_, s32[24]{0:T(128)} %refs_1_.1, s32[24]{0:T(128)} %refs_2_.1, s32[8]{0:T(128)} %refs_3_.1, bf16[128,1024]{1,0:T(8,128)(2,1)} %refs_4_.1, bf16[128,256]{1,0:T(8,128)(2,1)} %refs_5_.1, bf16[128,256]{1,0:T(8,128)(2,1)} %refs_6_.1, bf16[64,512]{1,0:T(8,128)(2,1)} %copy-done, ...), custom_call_target="tpu_custom_call" | custom-call | flops 402653184 | bytes 1310720 | tf_op jit(solution)/shard_map/pallas_call | solution.py:145
  (40 shorter events, 0.5 us)
Async XLA Ops:
  0.7 0.7 %copy-start.6 = (s32[24]{0:T(128)S(1)}, s32[24]{0:T(128)}, u32[]{:S(2)}) copy-start(s32[24]{0:T(128)} %refs_1_.1) | copy-start | bytes 292
  0.7 1.1 %copy-start.4 = (bf16[64,256]{1,0:T(8,128)(2,1)S(1)}, bf16[64,256]{1,0:T(8,128)(2,1)}, u32[]{:S(2)}) copy-start(bf16[64,256]{1,0:T(8,128)(2,1)} %param.11) | copy-start | bytes 98308
  0.7 1.1 %copy-start.2 = (bf16[128,256]{1,0:T(8,128)(2,1)S(1)}, bf16[128,256]{1,0:T(8,128)(2,1)}, u32[]{:S(2)}) copy-start(bf16[128,256]{1,0:T(8,128)(2,1)} %refs_6_.1) | copy-start | bytes 196612
  1.8 0.8 %copy-start.1 = (bf16[128,256]{1,0:T(8,128)(2,1)S(1)}, bf16[128,256]{1,0:T(8,128)(2,1)}, u32[]{:S(2)}) copy-start(bf16[128,256]{1,0:T(8,128)(2,1)} %refs_5_.1) | copy-start | bytes 196612
  2.6 0.8 %copy-start.5 = (bf16[64,256]{1,0:T(8,128)(2,1)S(1)}, bf16[64,256]{1,0:T(8,128)(2,1)}, u32[]{:S(2)}) copy-start(bf16[64,256]{1,0:T(8,128)(2,1)} %param.12) | copy-start | bytes 98308
  3.4 15.4 %copy-start = (bf16[64,512]{1,0:T(8,128)(2,1)}, bf16[64,512]{1,0:T(8,128)(2,1)S(1)}, u32[]{:S(2)}) copy-start(bf16[64,512]{1,0:T(8,128)(2,1)S(1)} %constant_dynamic-update-slice_fusion.refs_7_) | copy-start | bytes 196612
  3.7 15.2 %collective-permute-start.4 = (bf16[64,512]{1,0:T(8,128)(2,1)S(1)}, bf16[64,512]{1,0:T(8,128)(2,1)S(1)}, u32[]{:S(2)}, u32[]{:S(2)}) collective-permute-start(bf16[64,512]{1,0:T(8,128)(2,1)S(1)} %constant_dynamic-update-slice_fusion.refs_7_), channel_id=1, source_target_pairs={{0,28},{4,0},{8,4},{12,8},{16,12},{20,16},{24,20},{28,24},{1,29},{... | collective-permute-start | bytes 196616 | tf_op jit(solution)/shard_map/ppermute | solution.py:174
  9.7 13.8 %collective-permute-start.3 = (bf16[64,512]{1,0:T(8,128)(2,1)S(1)}, bf16[64,512]{1,0:T(8,128)(2,1)S(1)}, u32[]{:S(2)}, u32[]{:S(2)}) collective-permute-start(bf16[64,512]{1,0:T(8,128)(2,1)S(1)} %constant_dynamic-update-slice_fusion.refs_7_), channel_id=1, source_target_pairs={{0,24},{4,28},{8,0},{12,4},{16,8},{20,12},{24,16},{28,20},{1,25},{... | collective-permute-start | bytes 196616 | tf_op jit(solution)/shard_map/ppermute | solution.py:174
  10.2 13.4 %collective-permute-start.2 = (bf16[64,512]{1,0:T(8,128)(2,1)S(1)}, bf16[64,512]{1,0:T(8,128)(2,1)S(1)}, u32[]{:S(2)}, u32[]{:S(2)}) collective-permute-start(bf16[64,512]{1,0:T(8,128)(2,1)S(1)} %constant_dynamic-update-slice_fusion.refs_7_), channel_id=1, source_target_pairs={{0,20},{4,24},{8,28},{12,0},{16,4},{20,8},{24,12},{28,16},{1,21},{... | collective-permute-start | bytes 196616 | tf_op jit(solution)/shard_map/ppermute | solution.py:174
  10.2 13.4 %collective-permute-start.1 = (bf16[64,512]{1,0:T(8,128)(2,1)S(1)}, bf16[64,512]{1,0:T(8,128)(2,1)S(1)}, u32[]{:S(2)}, u32[]{:S(2)}) collective-permute-start(bf16[64,512]{1,0:T(8,128)(2,1)S(1)} %constant_dynamic-update-slice_fusion.refs_7_), channel_id=1, source_target_pairs={{0,16},{4,20},{8,24},{12,28},{16,0},{20,4},{24,8},{28,12},{1,17},{... | collective-permute-start | bytes 196616 | tf_op jit(solution)/shard_map/ppermute | solution.py:174
  14.0 7.9 %all-to-all-start = ((bf16[2,128,256]{2,0,1:T(2,128)(2,1)}), bf16[2,128,256]{2,0,1:T(2,128)(2,1)S(1)}, u32[]{:S(2)}, u32[]{:S(2)}) async-start(bf16[2,128,256]{2,0,1:T(2,128)(2,1)} %copy.27), calls=%async_computation | async-start | bytes 262144 | tf_op jit(solution)/shard_map/all_to_all | solution.py:222
  17.3 15.6 %collective-permute-start = (bf16[192,512]{1,0:T(8,128)(2,1)S(1)}, bf16[192,512]{1,0:T(8,128)(2,1)S(1)}, u32[]{:S(2)}, u32[]{:S(2)}) collective-permute-start(bf16[192,512]{1,0:T(8,128)(2,1)S(1)} %maximum_maximum_fusion), channel_id=1, source_target_pairs={{0,4},{4,8},{8,12},{12,16},{16,20},{20,24},{24,28},{28,0},{1,5},{5... | collective-permute-start | bytes 589832 | tf_op jit(solution)/shard_map/ppermute | solution.py:174
  18.8 0.6 %copy-start.3 = (bf16[64,512]{1,0:T(8,128)(2,1)}, bf16[64,512]{1,0:T(8,128)(2,1)S(1)}, u32[]{:S(2)}) copy-start(bf16[64,512]{1,0:T(8,128)(2,1)S(1)} %collective-permute-done.4.refs_12_) | copy-start | bytes 196612
  19.5 13.4 %collective-permute-start.5 = (bf16[128,512]{1,0:T(8,128)(2,1)S(1)}, bf16[128,512]{1,0:T(8,128)(2,1)S(1)}, u32[]{:S(2)}, u32[]{:S(2)}) collective-permute-start(bf16[128,512]{1,0:T(8,128)(2,1)S(1)} %pad_maximum_fusion.1), channel_id=1, source_target_pairs={{0,12},{4,16},{8,20},{12,24},{16,28},{20,0},{24,4},{28,8},{1,13},{... | collective-permute-start | bytes 393224 | tf_op jit(solution)/shard_map/ppermute | solution.py:174
  23.5 9.4 %copy-start.9 = (bf16[64,512]{1,0:T(8,128)(2,1)}, bf16[64,512]{1,0:T(8,128)(2,1)S(1)}, u32[]{:S(2)}) copy-start(bf16[64,512]{1,0:T(8,128)(2,1)S(1)} %collective-permute-done.3.refs_11_) | copy-start | bytes 196612
  23.5 9.4 %copy-start.10 = (bf16[64,512]{1,0:T(8,128)(2,1)}, bf16[64,512]{1,0:T(8,128)(2,1)S(1)}, u32[]{:S(2)}) copy-start(bf16[64,512]{1,0:T(8,128)(2,1)S(1)} %collective-permute-done.2.refs_10_) | copy-start | bytes 196612
  23.6 9.3 %copy-start.11 = (bf16[64,512]{1,0:T(8,128)(2,1)}, bf16[64,512]{1,0:T(8,128)(2,1)S(1)}, u32[]{:S(2)}) copy-start(bf16[64,512]{1,0:T(8,128)(2,1)S(1)} %collective-permute-done.1.refs_9_) | copy-start | bytes 196612
  32.9 0.7 %copy-start.8 = (bf16[128,512]{1,0:T(8,128)(2,1)}, bf16[128,512]{1,0:T(8,128)(2,1)S(1)}, u32[]{:S(2)}) copy-start(bf16[128,512]{1,0:T(8,128)(2,1)S(1)} %collective-permute-done.5.refs_13_) | copy-start | bytes 393220
  32.9 0.7 %copy-start.7 = (bf16[192,512]{1,0:T(8,128)(2,1)}, bf16[192,512]{1,0:T(8,128)(2,1)S(1)}, u32[]{:S(2)}) copy-start(bf16[192,512]{1,0:T(8,128)(2,1)S(1)} %collective-permute-done.refs_8_) | copy-start | bytes 589828

commit v9 on v7

--- a/solution.py
+++ b/solution.py
@@ -32,13 +32,20 @@
 
 
 def attend_kernel(meta, *refs):
-    devices, block_rows, rows, tails, prefix_len, repeat, scale = meta
+    devices, block_rows, rows, tails, prefix_len, repeat, scale, shifts, first, last = meta
     me_ref, lens_ref, rg_ref, bg_ref, q_ref, own_k_ref, own_v_ref = refs[:7]
-    data = refs[7 : 7 + devices]
-    out_ref, kscr, vscr = refs[7 + devices :]
+    data = refs[7 : 7 + len(shifts)]
+    rest = refs[7 + len(shifts) :]
+    if not first:
+        acc_in, high_in, total_in = rest[:3]
+        rest = rest[3:]
+    if last:
+        out_ref, kscr, vscr = rest
+    else:
+        acc_out, high_out, total_out, kscr, vscr = rest
     kv_cols = kscr.shape[1]
     count = kscr.shape[0]
-    base = devices * block_rows
+    base = len(shifts) * block_rows
     q_heads = q_ref.shape[1] // HD
     me = me_ref[0]
     starts, at = [], 0
@@ -48,14 +55,14 @@
 
     def info(index):
         request = jnp.full(index.shape, -2, jnp.int32)
-        first = jnp.zeros(index.shape, jnp.int32)
+        first_row = jnp.zeros(index.shape, jnp.int32)
         group = jnp.full(index.shape, -1, jnp.int32)
         for j, start in enumerate(starts):
             after = index >= start
             request = jnp.where(after, j, request)
-            first = jnp.where(after, start, first)
+            first_row = jnp.where(after, start, first_row)
             group = jnp.where(after, rg_ref[j], group)
-        return request, index - first, group
+        return request, index - first_row, group
 
     lane = lax.broadcasted_iota(jnp.int32, (1, HD), 1)
     pair = jnp.where(lane < HD // 2, lane, lane - HD // 2)
@@ -69,10 +76,11 @@
     def rotated(x, cosine, sine):
         return (x * cosine + pltpu.roll(x, HD // 2, 1) * sine).astype(jnp.bfloat16)
 
-    for c in range(devices):
+    for c in range(len(shifts)):
         kscr[c * block_rows : (c + 1) * block_rows, :] = data[c][0:block_rows, 0:kv_cols]
         vscr[c * block_rows : (c + 1) * block_rows, :] = data[c][0:block_rows, kv_cols : 2 * kv_cols]
-    for b in range(0, tails + 1):
+    suffix_blocks = range(tails + 1) if first else range(0)
+    for b in suffix_blocks:
         low = base + b * rows
         index = (me - b) * rows + lax.broadcasted_iota(jnp.int32, (rows, 1), 0)
         _, offset, _ = info(index)
@@ -81,28 +89,28 @@
             if b == 0:
                 x = own_k_ref[:, g * HD : (g + 1) * HD]
             else:
-                x = data[b][block_rows : block_rows + rows, g * HD : (g + 1) * HD]
+                x = data[shifts.index(b)][block_rows : block_rows + rows, g * HD : (g + 1) * HD]
             kscr[low : low + rows, g * HD : (g + 1) * HD] = rotated(x.astype(jnp.float32), cosine, sine)
         if b == 0:
             vscr[low : low + rows, :] = own_v_ref[...]
         else:
-            vscr[low : low + rows, :] = data[b][block_rows : block_rows + rows, kv_cols : 2 * kv_cols]
+            vscr[low : low + rows, :] = data[shifts.index(b)][block_rows : block_rows + rows, kv_cols : 2 * kv_cols]
 
     token = me * rows + lax.broadcasted_iota(jnp.int32, (rows, 1), 0)
     request, offset, group = info(token)
     col = lax.broadcasted_iota(jnp.int32, (1, count), 1)
     key_group = jnp.full((1, count), -1, jnp.int32)
-    for c in range(devices):
-        holder = lax.rem(me - c + devices, devices)
+    for c, by in enumerate(shifts):
+        holder = lax.rem(me - by + devices, devices)
         key_group = jnp.where(col >= c * block_rows, bg_ref[holder], key_group)
-    key_index = jnp.full((1, count), -1, jnp.int32)
-    for b in range(tails + 1):
-        low = base + b * rows
-        key_index = jnp.where(col >= low, (me - b) * rows + col - low, key_index)
-    key_request, _, _ = info(key_index)
-    visible = ((col < base) & (key_group == group)) | (
-        (key_request == request) & (key_index <= token)
-    )
+    visible = (col < base) & (key_group == group)
+    if first:
+        key_index = jnp.full((1, count), -1, jnp.int32)
+        for b in suffix_blocks:
+            low = base + b * rows
+            key_index = jnp.where(col >= low, (me - b) * rows + col - low, key_index)
+        key_request, _, _ = info(key_index)
+        visible = visible | ((key_request == request) & (key_index <= token))
     cosine, sine = tables(offset)
     for g in range(q_heads // repeat):
         heads = range(g * repeat, (g + 1) * repeat)
@@ -114,36 +122,60 @@
         scores = lax.dot_general(
             q, k, (((1,), (1,)), ((), ())), preferred_element_type=jnp.float32
         ) * scale
-        weights, totals = [], []
-        for r in range(repeat):
+        weights, totals, highs, factors = [], [], [], []
+        for r, h in enumerate(heads):
             part = jnp.where(visible, scores[r * rows : (r + 1) * rows], BIG_NEGATIVE)
             high = jnp.max(part, axis=1, keepdims=True)
+            if not first:
+                earlier = high_in[:, h : h + 1]
+                high = jnp.maximum(high, earlier)
+                factors.append(jnp.exp(earlier - high))
             part = jnp.exp(part - high)
+            highs.append(high)
             totals.append(jnp.sum(part, axis=1, keepdims=True))
             weights.append(part.astype(jnp.bfloat16))
         v = vscr[:, g * HD : (g + 1) * HD]
         summed = jnp.dot(jnp.concatenate(weights, axis=0), v, preferred_element_type=jnp.float32)
         for r, h in enumerate(heads):
-            out_ref[:, h * HD : (h + 1) * HD] = (summed[r * rows : (r + 1) * rows] / totals[r]).astype(
-                out_ref.dtype
-            )
-
-
-def attend(meta, scalars, queries, own_k, own_v, data):
+            part = summed[r * rows : (r + 1) * rows]
+            total = totals[r]
+            if not first:
+                part = acc_in[:, h * HD : (h + 1) * HD] * factors[r] + part
+                total = total_in[:, h : h + 1] * factors[r] + total
+            if last:
+                out_ref[:, h * HD : (h + 1) * HD] = (part / total).astype(out_ref.dtype)
+            else:
+                acc_out[:, h * HD : (h + 1) * HD] = part
+                high_out[:, h : h + 1] = highs[r]
+                total_out[:, h : h + 1] = total
+
+
+def attend(meta, scalars, queries, own_k, own_v, data, partial=None):
     devices, block_rows, rows, tails = meta[:4]
+    shifts, first, last = meta[7:]
     kv_cols = own_k.shape[1]
     q_heads = queries.shape[1] // HD
-    count = devices * block_rows + rows * (1 + tails)
+    count = len(shifts) * block_rows + (rows * (1 + tails) if first else 0)
     flops = 4 * rows * count * HD * q_heads
-    arrays = [queries, own_k, own_v, *data]
+    arrays = [queries, own_k, own_v, *data] + (list(partial) if partial is not None else [])
     nbytes = sum(a.size * a.dtype.itemsize for a in arrays)
     smem = pl.BlockSpec(memory_space=pltpu.SMEM)
     vmem = pl.BlockSpec(memory_space=pltpu.VMEM)
+    if last:
+        out_shape = jax.ShapeDtypeStruct(queries.shape, jnp.bfloat16)
+        out_specs = vmem
+    else:
+        out_shape = (
+            jax.ShapeDtypeStruct(queries.shape, jnp.float32),
+            jax.ShapeDtypeStruct((rows, q_heads), jnp.float32),
+            jax.ShapeDtypeStruct((rows, q_heads), jnp.float32),
+        )
+        out_specs = (vmem, vmem, vmem)
     return pl.pallas_call(
         functools.partial(attend_kernel, meta),
-        out_shape=jax.ShapeDtypeStruct(queries.shape, jnp.bfloat16),
+        out_shape=out_shape,
         in_specs=[smem] * len(scalars) + [vmem] * len(arrays),
-        out_specs=vmem,
+        out_specs=out_specs,
         scratch_shapes=[
             pltpu.VMEM((count, kv_cols), jnp.bfloat16),
             pltpu.VMEM((count, kv_cols), jnp.bfloat16),
@@ -229,10 +261,25 @@
         for i, by in enumerate(late):
             received[devices - 1 - i] = gates[i]
             received[by] = shifted(payload, "seq", by, True)
-        data = [prefix_kv] + [received[by] for by in range(1, devices)]
+        received[0] = prefix_kv
         scalars = [me.astype(jnp.int32).reshape(1), suffix_lengths, request_group, block_group]
-        meta = (devices, block_rows, rows, min(span, devices - 1), prefix_len, repeat, scale)
-        attended = attend(meta, scalars, queries, suffix_keys, suffix_values, data)
+        tails = min(span, devices - 1)
+        common = (devices, block_rows, rows, tails, prefix_len, repeat, scale)
+        shifts = tuple(by for by in range(devices) if by not in late)
+        if late:
+            partial = attend(
+                common + (shifts, True, False), scalars, queries, suffix_keys, suffix_values,
+                [received[by] for by in shifts],
+            )
+            attended = attend(
+                common + (tuple(late), False, True), scalars, queries, suffix_keys, suffix_values,
+                [received[by] for by in late], partial,
+            )
+        else:
+            attended = attend(
+                common + (shifts, True, True), scalars, queries, suffix_keys, suffix_values,
+                [received[by] for by in shifts],
+            )
         return (attended, cache[0], cache[1])
 
     prefix_parts = []

time: 37 us -> 39.2 us (1.059)
  Pallas kernels: 4.59 us -> 8.47 us
  waiting for transfers between devices: 9.3 us -> 5.62 us
  local copies, waits for them, and re-layouts: 5.43 us -> 7.36 us
    pallas_call x1 -> x2, Pallas kernels: 4.59 us -> 8.47 us  [attend(): pl.pallas_call(functools.partial(attend_kernel, meta), out_shape=out_shap...]
    ppermute x7, waiting for transfers between devices: 9.3 us -> 5.61 us  [shifted(): return lax.ppermute(array, axis, pairs)]
    unnamed x29, local copies, waits for them, and re-layouts: 3.98 us -> 5.27 us
    another operation x1, local copies, waits for them, and re-layouts: 0.08 us -> 0.74 us
  transfers between devices with their start and end apart: 8 -> 8, of which waited for: 2 -> 2; matrix products, arithmetic and copies ran while one was open for 4% -> 4% of each run, Pallas kernels for 0% -> 11%
where the time goes in v9:
time: 39.2 us; the launch traced here: 38.7 us
  starting transfers between devices  15.8 us (40%)
  Pallas kernels  8.47 us (22%)
  local copies, waits for them, and re-layouts  7.36 us (19%)
  waiting for transfers between devices  5.62 us (14%)
  between operations  0.82 us (2%)
  other arithmetic  0.62 us (2%)
    ppermute x7, starting transfers between devices, shifted(): return lax.ppermute(array, axis, pairs)  11.6 us
    pallas_call x2, Pallas kernels, attend(): pl.pallas_call(functools.partial(attend_kernel, meta), out_shape=out_shap...  8.47 us
    ppermute x7, waiting for transfers between devices, shifted(): return lax.ppermute(array, axis, pairs)  5.61 us
    unnamed x29, local copies, waits for them, and re-layouts  5.27 us
    all_to_all x1, starting transfers between devices, body(): lax.all_to_all(stacked, 'tp', split_axis=1, concat_axis=2, tiled=True)  4.24 us
    optimization_barrier x1, local copies, waits for them, and re-layouts, body(): lax.optimization_barrier((jnp.stack([own_k_rot, suffix_values], axis=0),...  0.79 us
  transfers between devices with their start and end apart: 8, of which 2 were waited for; matrix products, arithmetic and copies ran while one was open for 4% of the time, Pallas kernels for 11%

profile of v9, /device:TPU:0, one launch (start us, length us, event | category | flops | bytes accessed | tf_op | source)
XLA Modules:
  0.0 38.7 jit_solution(5308274951193082197)
XLA Ops:
  0.7 0.7 %copy.25 = s32[24,1]{1,0:T(8,128)S(1)} copy(s32[24,1]{0,1:T(1,128)} %bitcast.22) | data formatting | bytes 192 | tf_op jit(solution)/shard_map/reshape.99
  1.5 0.1 reduce
  1.6 0.5 %copy-done.7 = s32[24]{0:T(128)S(1)} copy-done((s32[24]{0:T(128)S(1)}, s32[24]{0:T(128)}, u32[]{:S(2)}) %copy-start.7) | copy-done | bytes 120
  2.4 0.7 %copy-done.1 = bf16[128,256]{1,0:T(8,128)(2,1)S(1)} copy-done((bf16[128,256]{1,0:T(8,128)(2,1)S(1)}, bf16[128,256]{1,0:T(8,128)(2,1)}, u32[]{:S(2)}) %copy-start.1) | copy-done | bytes 65560
  3.2 0.1 copy.26
  3.3 0.6 %copy-done.5 = bf16[64,256]{1,0:T(8,128)(2,1)S(1)} copy-done((bf16[64,256]{1,0:T(8,128)(2,1)S(1)}, bf16[64,256]{1,0:T(8,128)(2,1)}, u32[]{:S(2)}) %copy-start.5) | copy-done | bytes 32792
  3.9 0.8 %copy-done.6 = bf16[64,256]{1,0:T(8,128)(2,1)S(1)} copy-done((bf16[64,256]{1,0:T(8,128)(2,1)S(1)}, bf16[64,256]{1,0:T(8,128)(2,1)}, u32[]{:S(2)}) %copy-start.6) | copy-done | bytes 32792
  4.7 0.2 multiply_cosine_fusion
  5.0 0.8 %copy.27 = bf16[2,128,256]{2,0,1:T(2,128)(2,1)} copy(bf16[2,128,256]{1,2,0:T(8,128)(2,1)S(1)} %pad_maximum_fusion) | data formatting | bytes 262144 | tf_op jit(solution)/shard_map/optimization_barrier | solution.py:244
  5.7 4.2 %all-to-all-start = ((bf16[2,128,256]{2,0,1:T(2,128)(2,1)}), bf16[2,128,256]{2,0,1:T(2,128)(2,1)S(1)}, u32[]{:S(2)}, u32[]{:S(2)}) async-start(bf16[2,128,256]{2,0,1:T(2,128)(2,1)} %copy.27), calls=%async_computation | async-start | bytes 262144 | tf_op jit(solution)/shard_map/all_to_all | solution.py:251
  10.0 5.1 %collective-permute-start = (bf16[64,512]{1,0:T(8,128)(2,1)S(1)}, bf16[64,512]{1,0:T(8,128)(2,1)S(1)}, u32[]{:S(2)}, u32[]{:S(2)}) collective-permute-start(bf16[64,512]{1,0:T(8,128)(2,1)S(1)} %constant_dynamic-update-slice_fusion.refs_7_), channel_id=1, source_target_pairs={{0,28},{4,0},{8,4},{12,8},{16,12},{20,16},{24,20},{28,24},{1,29},{... | collective-permute-start | bytes 196616 | tf_op jit(solution)/shard_map/ppermute | solution.py:203
  15.1 0.4 %collective-permute-start.1 = (bf16[64,512]{1,0:T(8,128)(2,1)S(1)}, bf16[64,512]{1,0:T(8,128)(2,1)S(1)}, u32[]{:S(2)}, u32[]{:S(2)}) collective-permute-start(bf16[64,512]{1,0:T(8,128)(2,1)S(1)} %constant_dynamic-update-slice_fusion.refs_7_), channel_id=1, source_target_pairs={{0,24},{4,28},{8,0},{12,4},{16,8},{20,12},{24,16},{28,20},{1,25},{... | collective-permute-start | bytes 196616 | tf_op jit(solution)/shard_map/ppermute | solution.py:203
  15.6 3.0 %collective-permute-start.6 = (bf16[64,512]{1,0:T(8,128)(2,1)S(1)}, bf16[64,512]{1,0:T(8,128)(2,1)S(1)}, u32[]{:S(2)}, u32[]{:S(2)}) collective-permute-start(bf16[64,512]{1,0:T(8,128)(2,1)S(1)} %constant_dynamic-update-slice_fusion.refs_7_), channel_id=1, source_target_pairs={{0,20},{4,24},{8,28},{12,0},{16,4},{20,8},{24,12},{28,16},{1,21},{... | collective-permute-start | bytes 196616 | tf_op jit(solution)/shard_map/ppermute | solution.py:203
  18.6 2.4 %collective-permute-start.4 = (bf16[192,512]{1,0:T(8,128)(2,1)S(1)}, bf16[192,512]{1,0:T(8,128)(2,1)S(1)}, u32[]{:S(2)}, u32[]{:S(2)}) collective-permute-start(bf16[192,512]{1,0:T(8,128)(2,1)S(1)} %maximum_maximum_fusion), channel_id=1, source_target_pairs={{0,4},{4,8},{8,12},{12,16},{16,20},{20,24},{24,28},{28,0},{1,5},{5... | collective-permute-start | bytes 589832 | tf_op jit(solution)/shard_map/ppermute | solution.py:203
  21.1 0.5 %collective-permute-start.3 = (bf16[64,512]{1,0:T(8,128)(2,1)S(1)}, bf16[64,512]{1,0:T(8,128)(2,1)S(1)}, u32[]{:S(2)}, u32[]{:S(2)}) collective-permute-start(bf16[64,512]{1,0:T(8,128)(2,1)S(1)} %constant_dynamic-update-slice_fusion.refs_7_), channel_id=1, source_target_pairs={{0,12},{4,16},{8,20},{12,24},{16,28},{20,0},{24,4},{28,8},{1,13},{... | collective-permute-start | bytes 196616 | tf_op jit(solution)/shard_map/ppermute | solution.py:203
  21.6 0.2 fusion
  21.9 0.6 %copy.30 = bf16[4,8,4,256]{3,1,2,0:T(8,128)(2,1)} copy(bf16[4,8,4,256]{3,2,1,0:T(4,128)(2,1)S(1)} %bitcast.17) | data formatting | bytes 131072
  22.6 0.6 %copy.31 = bf16[4,8,4,256]{3,1,2,0:T(8,128)(2,1)} copy(bf16[4,8,4,256]{3,2,1,0:T(4,128)(2,1)S(1)} %bitcast.18) | data formatting | bytes 131072
  23.3 0.6 %collective-permute-done.5.refs_9_ = bf16[64,512]{1,0:T(8,128)(2,1)S(1)} collective-permute-done((bf16[64,512]{1,0:T(8,128)(2,1)S(1)}, bf16[64,512]{1,0:T(8,128)(2,1)S(1)}, u32[]{:S(2)}, u32[]{:S(2)}) %collective-permute-start.5) | collective-permute-done | bytes 65568 | tf_op jit(solution)/shard_map/ppermute | solution.py:203
  23.9 5.0 %collective-permute-done.4.refs_8_ = bf16[192,512]{1,0:T(8,128)(2,1)S(1)} collective-permute-done((bf16[192,512]{1,0:T(8,128)(2,1)S(1)}, bf16[192,512]{1,0:T(8,128)(2,1)S(1)}, u32[]{:S(2)}, u32[]{:S(2)}) %collective-permute-start.4) | collective-permute-done | bytes 196640 | tf_op jit(solution)/shard_map/ppermute | solution.py:203
  28.9 0.7 %copy-done.8 = bf16[192,512]{1,0:T(8,128)(2,1)} copy-done((bf16[192,512]{1,0:T(8,128)(2,1)}, bf16[192,512]{1,0:T(8,128)(2,1)S(1)}, u32[]{:S(2)}) %copy-start.8) | copy-done | bytes 196632
  29.6 4.4 %shard_map.103 = (f32[128,1024]{1,0:T(8,128)}, f32[128,8]{1,0:T(8,128)}, f32[128,8]{1,0:T(8,128)}) custom-call(s32[1]{0:T(128)} %bitcast.refs_0_, s32[24]{0:T(128)} %refs_1_.3, s32[24]{0:T(128)} %refs_2_.3, s32[8]{0:T(128)} %refs_3_.3, bf16[128,1024]{1,0:T(8,128)(2,1)} %refs_4_.3, bf16[128,256]{1,0:T(8,128)(2,1)} %refs_5_.3, bf16[128,256]{1,0:T(8,128)(2,1)} %refs_6_.3, ...), custom_call_target="tpu_custom_call" | custom-call | flops 335544320 | bytes 1179648 | tf_op jit(solution)/shard_map/pallas_call | solution.py:174
  34.0 0.6 %copy-done.3 = bf16[64,512]{1,0:T(8,128)(2,1)} copy-done((bf16[64,512]{1,0:T(8,128)(2,1)}, bf16[64,512]{1,0:T(8,128)(2,1)S(1)}, u32[]{:S(2)}) %copy-start.3) | copy-done | bytes 65560
  34.6 4.1 %shard_map.104 = bf16[128,1024]{1,0:T(8,128)(2,1)} custom-call(s32[1]{0:T(128)} %bitcast.refs_0_, s32[24]{0:T(128)} %refs_1_.3, s32[24]{0:T(128)} %refs_2_.3, s32[8]{0:T(128)} %refs_3_.3, bf16[128,1024]{1,0:T(8,128)(2,1)} %refs_4_.3, bf16[128,256]{1,0:T(8,128)(2,1)} %refs_5_.3, bf16[128,256]{1,0:T(8,128)(2,1)} %refs_6_.3, bf16[64,512]{1,0:T(8,128)(2,1)} %copy-done.3, ...), custom_call_target="tpu_custom_call" | custom-call | flops 67108864 | bytes 1318912 | tf_op jit(solution)/shard_map/pallas_call | solution.py:174
  (44 shorter events, 0.7 us)
Async XLA Ops:
  0.6 1.7 %copy-start = (bf16[128,256]{1,0:T(8,128)(2,1)S(1)}, bf16[128,256]{1,0:T(8,128)(2,1)}, u32[]{:S(2)}) copy-start(bf16[128,256]{1,0:T(8,128)(2,1)} %refs_5_.3) | copy-start | bytes 196612
  1.5 0.7 %copy-start.7 = (s32[24]{0:T(128)S(1)}, s32[24]{0:T(128)}, u32[]{:S(2)}) copy-start(s32[24]{0:T(128)} %refs_1_.3) | copy-start | bytes 292
  2.3 0.8 %copy-start.1 = (bf16[128,256]{1,0:T(8,128)(2,1)S(1)}, bf16[128,256]{1,0:T(8,128)(2,1)}, u32[]{:S(2)}) copy-start(bf16[128,256]{1,0:T(8,128)(2,1)} %refs_6_.3) | copy-start | bytes 196612
  3.1 0.8 %copy-start.5 = (bf16[64,256]{1,0:T(8,128)(2,1)S(1)}, bf16[64,256]{1,0:T(8,128)(2,1)}, u32[]{:S(2)}) copy-start(bf16[64,256]{1,0:T(8,128)(2,1)} %param.11) | copy-start | bytes 98308
  3.9 0.8 %copy-start.6 = (bf16[64,256]{1,0:T(8,128)(2,1)S(1)}, bf16[64,256]{1,0:T(8,128)(2,1)}, u32[]{:S(2)}) copy-start(bf16[64,256]{1,0:T(8,128)(2,1)} %param.12) | copy-start | bytes 98308
  4.7 16.4 %copy-start.2 = (bf16[64,512]{1,0:T(8,128)(2,1)}, bf16[64,512]{1,0:T(8,128)(2,1)S(1)}, u32[]{:S(2)}) copy-start(bf16[64,512]{1,0:T(8,128)(2,1)S(1)} %constant_dynamic-update-slice_fusion.refs_7_) | copy-start | bytes 196612
  5.7 15.9 %all-to-all-start = ((bf16[2,128,256]{2,0,1:T(2,128)(2,1)}), bf16[2,128,256]{2,0,1:T(2,128)(2,1)S(1)}, u32[]{:S(2)}, u32[]{:S(2)}) async-start(bf16[2,128,256]{2,0,1:T(2,128)(2,1)} %copy.27), calls=%async_computation | async-start | bytes 262144 | tf_op jit(solution)/shard_map/all_to_all | solution.py:251
  10.0 11.0 %collective-permute-start = (bf16[64,512]{1,0:T(8,128)(2,1)S(1)}, bf16[64,512]{1,0:T(8,128)(2,1)S(1)}, u32[]{:S(2)}, u32[]{:S(2)}) collective-permute-start(bf16[64,512]{1,0:T(8,128)(2,1)S(1)} %constant_dynamic-update-slice_fusion.refs_7_), channel_id=1, source_target_pairs={{0,28},{4,0},{8,4},{12,8},{16,12},{20,16},{24,20},{28,24},{1,29},{... | collective-permute-start | bytes 196616 | tf_op jit(solution)/shard_map/ppermute | solution.py:203
  15.1 5.9 %collective-permute-start.1 = (bf16[64,512]{1,0:T(8,128)(2,1)S(1)}, bf16[64,512]{1,0:T(8,128)(2,1)S(1)}, u32[]{:S(2)}, u32[]{:S(2)}) collective-permute-start(bf16[64,512]{1,0:T(8,128)(2,1)S(1)} %constant_dynamic-update-slice_fusion.refs_7_), channel_id=1, source_target_pairs={{0,24},{4,28},{8,0},{12,4},{16,8},{20,12},{24,16},{28,20},{1,25},{... | collective-permute-start | bytes 196616 | tf_op jit(solution)/shard_map/ppermute | solution.py:203
  15.6 8.3 %collective-permute-start.5 = (bf16[64,512]{1,0:T(8,128)(2,1)S(1)}, bf16[64,512]{1,0:T(8,128)(2,1)S(1)}, u32[]{:S(2)}, u32[]{:S(2)}) collective-permute-start(bf16[64,512]{1,0:T(8,128)(2,1)S(1)} %constant_dynamic-update-slice_fusion.refs_7_), channel_id=1, source_target_pairs={{0,16},{4,20},{8,24},{12,28},{16,0},{20,4},{24,8},{28,12},{1,17},{... | collective-permute-start | bytes 196616 | tf_op jit(solution)/shard_map/ppermute | solution.py:203
  15.6 8.3 %collective-permute-start.6 = (bf16[64,512]{1,0:T(8,128)(2,1)S(1)}, bf16[64,512]{1,0:T(8,128)(2,1)S(1)}, u32[]{:S(2)}, u32[]{:S(2)}) collective-permute-start(bf16[64,512]{1,0:T(8,128)(2,1)S(1)} %constant_dynamic-update-slice_fusion.refs_7_), channel_id=1, source_target_pairs={{0,20},{4,24},{8,28},{12,0},{16,4},{20,8},{24,12},{28,16},{1,21},{... | collective-permute-start | bytes 196616 | tf_op jit(solution)/shard_map/ppermute | solution.py:203
  18.6 10.3 %collective-permute-start.4 = (bf16[192,512]{1,0:T(8,128)(2,1)S(1)}, bf16[192,512]{1,0:T(8,128)(2,1)S(1)}, u32[]{:S(2)}, u32[]{:S(2)}) collective-permute-start(bf16[192,512]{1,0:T(8,128)(2,1)S(1)} %maximum_maximum_fusion), channel_id=1, source_target_pairs={{0,4},{4,8},{8,12},{12,16},{16,20},{20,24},{24,28},{28,0},{1,5},{5... | collective-permute-start | bytes 589832 | tf_op jit(solution)/shard_map/ppermute | solution.py:203
  21.0 0.8 %copy-start.9 = (bf16[64,512]{1,0:T(8,128)(2,1)}, bf16[64,512]{1,0:T(8,128)(2,1)S(1)}, u32[]{:S(2)}) copy-start(bf16[64,512]{1,0:T(8,128)(2,1)S(1)} %collective-permute-done.refs_12_) | copy-start | bytes 196612
  21.0 0.8 %copy-start.10 = (bf16[64,512]{1,0:T(8,128)(2,1)}, bf16[64,512]{1,0:T(8,128)(2,1)S(1)}, u32[]{:S(2)}) copy-start(bf16[64,512]{1,0:T(8,128)(2,1)S(1)} %collective-permute-done.1.refs_11_) | copy-start | bytes 196612
  21.0 13.0 %collective-permute-start.2 = (bf16[64,512]{1,0:T(8,128)(2,1)S(1)}, bf16[64,512]{1,0:T(8,128)(2,1)S(1)}, u32[]{:S(2)}, u32[]{:S(2)}) collective-permute-start(bf16[64,512]{1,0:T(8,128)(2,1)S(1)} %constant_dynamic-update-slice_fusion.refs_7_), channel_id=1, source_target_pairs={{0,8},{4,12},{8,16},{12,20},{16,24},{20,28},{24,0},{28,4},{1,9},{5... | collective-permute-start | bytes 196616 | tf_op jit(solution)/shard_map/ppermute | solution.py:203
  21.1 12.9 %collective-permute-start.3 = (bf16[64,512]{1,0:T(8,128)(2,1)S(1)}, bf16[64,512]{1,0:T(8,128)(2,1)S(1)}, u32[]{:S(2)}, u32[]{:S(2)}) collective-permute-start(bf16[64,512]{1,0:T(8,128)(2,1)S(1)} %constant_dynamic-update-slice_fusion.refs_7_), channel_id=1, source_target_pairs={{0,12},{4,16},{8,20},{12,24},{16,28},{20,0},{24,4},{28,8},{1,13},{... | collective-permute-start | bytes 196616 | tf_op jit(solution)/shard_map/ppermute | solution.py:203
  23.9 5.0 %copy-start.11 = (bf16[64,512]{1,0:T(8,128)(2,1)}, bf16[64,512]{1,0:T(8,128)(2,1)S(1)}, u32[]{:S(2)}) copy-start(bf16[64,512]{1,0:T(8,128)(2,1)S(1)} %collective-permute-done.5.refs_9_) | copy-start | bytes 196612
  23.9 5.0 %copy-start.12 = (bf16[64,512]{1,0:T(8,128)(2,1)}, bf16[64,512]{1,0:T(8,128)(2,1)S(1)}, u32[]{:S(2)}) copy-start(bf16[64,512]{1,0:T(8,128)(2,1)S(1)} %collective-permute-done.6.refs_10_) | copy-start | bytes 196612
  28.9 0.7 %copy-start.8 = (bf16[192,512]{1,0:T(8,128)(2,1)}, bf16[192,512]{1,0:T(8,128)(2,1)S(1)}, u32[]{:S(2)}) copy-start(bf16[192,512]{1,0:T(8,128)(2,1)S(1)} %collective-permute-done.4.refs_8_) | copy-start | bytes 589828
  34.0 0.6 %copy-start.3 = (bf16[64,512]{1,0:T(8,128)(2,1)}, bf16[64,512]{1,0:T(8,128)(2,1)S(1)}, u32[]{:S(2)}) copy-start(bf16[64,512]{1,0:T(8,128)(2,1)S(1)} %collective-permute-done.2.refs_7_) | copy-start | bytes 196612
  34.0 0.6 %copy-start.4 = (bf16[64,512]{1,0:T(8,128)(2,1)}, bf16[64,512]{1,0:T(8,128)(2,1)S(1)}, u32[]{:S(2)}) copy-start(bf16[64,512]{1,0:T(8,128)(2,1)S(1)} %collective-permute-done.3.refs_8_) | copy-start | bytes 196612

commit v10 on v7

--- a/solution.py
+++ b/solution.py
@@ -41,26 +41,39 @@
     base = devices * block_rows
     q_heads = q_ref.shape[1] // HD
     me = me_ref[0]
-    starts, at = [], 0
-    for j in range(lens_ref.shape[0]):
-        starts.append(at)
+    reqs = lens_ref.shape[0]
+    width = -(-reqs // HD) * HD
+    height = -(-reqs // 8) * 8
+    never = 1 << 30
+    lane = lax.broadcasted_iota(jnp.int32, (1, width), 1)
+    sub = lax.broadcasted_iota(jnp.int32, (height, 1), 0)
+    start_row = jnp.full((1, width), never, jnp.int32)
+    group_row = jnp.zeros((1, width), jnp.int32)
+    start_col = jnp.full((height, 1), never, jnp.int32)
+    at = 0
+    for j in range(reqs):
+        start_row = jnp.where(lane == j, at, start_row)
+        group_row = jnp.where(lane == j, rg_ref[j], group_row)
+        start_col = jnp.where(sub == j, at, start_col)
         at = at + lens_ref[j]
 
     def info(index):
-        request = jnp.full(index.shape, -2, jnp.int32)
-        first = jnp.zeros(index.shape, jnp.int32)
-        group = jnp.full(index.shape, -1, jnp.int32)
-        for j, start in enumerate(starts):
-            after = index >= start
-            request = jnp.where(after, j, request)
-            first = jnp.where(after, start, first)
-            group = jnp.where(after, rg_ref[j], group)
-        return request, index - first, group
-
-    lane = lax.broadcasted_iota(jnp.int32, (1, HD), 1)
-    pair = jnp.where(lane < HD // 2, lane, lane - HD // 2)
+        after = index >= start_row
+        request = jnp.sum(after.astype(jnp.float32), axis=1, keepdims=True).astype(jnp.int32) - 1
+        first = jnp.max(jnp.where(after, start_row, 0).astype(jnp.float32), axis=1, keepdims=True)
+        group = jnp.sum(
+            jnp.where(lane == request, group_row, 0).astype(jnp.float32), axis=1, keepdims=True
+        )
+        return request, index - first.astype(jnp.int32), group.astype(jnp.int32)
+
+    def request_of_row(index):
+        after = index >= start_col
+        return jnp.sum(after.astype(jnp.float32), axis=0, keepdims=True).astype(jnp.int32) - 1
+
+    head_lane = lax.broadcasted_iota(jnp.int32, (1, HD), 1)
+    pair = jnp.where(head_lane < HD // 2, head_lane, head_lane - HD // 2)
     freq = jnp.exp(pair.astype(jnp.float32) * (-2.0 * math.log(500000.0) / HD))
-    sign = jnp.where(lane < HD // 2, -1.0, 1.0).astype(jnp.float32)
+    sign = jnp.where(head_lane < HD // 2, -1.0, 1.0).astype(jnp.float32)
 
     def tables(offset):
         angle = (offset + prefix_len).astype(jnp.float32) * freq
@@ -99,7 +112,7 @@
     for b in range(tails + 1):
         low = base + b * rows
         key_index = jnp.where(col >= low, (me - b) * rows + col - low, key_index)
-    key_request, _, _ = info(key_index)
+    key_request = request_of_row(key_index)
     visible = ((col < base) & (key_group == group)) | (
         (key_request == request) & (key_index <= token)
     )

time: 37 us -> 36.8 us (level)
  transfers between devices with their start and end apart: 8 -> 8, of which waited for: 2 -> 2; matrix products, arithmetic and copies ran while one was open for 4% -> 5% of each run, Pallas kernels for 0% -> 0%
where the time goes in v10:
time: 36.8 us; the launch traced here: 36.4 us
  starting transfers between devices  15.8 us (43%)
  waiting for transfers between devices  9.3 us (25%)
  local copies, waits for them, and re-layouts  5.43 us (15%)
  Pallas kernels  4.4 us (12%)
  between operations  0.85 us (2%)
  other arithmetic  0.62 us (2%)
    ppermute x7, starting transfers between devices, shifted(): return lax.ppermute(array, axis, pairs)  11.6 us
    ppermute x7, waiting for transfers between devices, shifted(): return lax.ppermute(array, axis, pairs)  9.3 us
    pallas_call x1, Pallas kernels, attend(): pl.pallas_call(functools.partial(attend_kernel, meta), out_shape=jax.Shap...  4.4 us
    all_to_all x1, starting transfers between devices, body(): lax.all_to_all(stacked, 'tp', split_axis=1, concat_axis=2, tiled=True)  4.24 us
    unnamed x29, local copies, waits for them, and re-layouts  3.98 us
    optimization_barrier x1, local copies, waits for them, and re-layouts, body(): lax.optimization_barrier((jnp.stack([own_k_rot, suffix_values], axis=0),...  0.79 us
  transfers between devices with their start and end apart: 8, of which 2 were waited for; matrix products, arithmetic and copies ran while one was open for 5% of the time, Pallas kernels for 0%

profile of v10, /device:TPU:0, one launch (start us, length us, event | category | flops | bytes accessed | tf_op | source)
XLA Modules:
  0.0 36.4 jit_solution(5697130737647445774)
XLA Ops:
  0.7 0.6 %copy-done.5 = s32[24]{0:T(128)S(1)} copy-done((s32[24]{0:T(128)S(1)}, s32[24]{0:T(128)}, u32[]{:S(2)}) %copy-start.5) | copy-done | bytes 120
  1.4 0.1 reduce
  1.6 0.1 convert_reduce_fusion
  1.7 0.1 select_reduce_fusion
  1.8 0.1 copy.26
  1.9 0.7 %copy-done = bf16[128,256]{1,0:T(8,128)(2,1)S(1)} copy-done((bf16[128,256]{1,0:T(8,128)(2,1)S(1)}, bf16[128,256]{1,0:T(8,128)(2,1)}, u32[]{:S(2)}) %copy-start) | copy-done | bytes 65560
  2.6 0.1 copy.24
  2.7 0.7 %copy-done.4 = bf16[64,256]{1,0:T(8,128)(2,1)S(1)} copy-done((bf16[64,256]{1,0:T(8,128)(2,1)S(1)}, bf16[64,256]{1,0:T(8,128)(2,1)}, u32[]{:S(2)}) %copy-start.4) | copy-done | bytes 32792
  3.4 0.2 multiply_cosine_fusion
  3.7 0.8 %copy.27 = bf16[2,128,256]{2,0,1:T(2,128)(2,1)} copy(bf16[2,128,256]{1,2,0:T(8,128)(2,1)S(1)} %pad_maximum_fusion) | data formatting | bytes 262144 | tf_op jit(solution)/shard_map/optimization_barrier | solution.py:225
  4.5 4.2 %all-to-all-start = ((bf16[2,128,256]{2,0,1:T(2,128)(2,1)}), bf16[2,128,256]{2,0,1:T(2,128)(2,1)S(1)}, u32[]{:S(2)}, u32[]{:S(2)}) async-start(bf16[2,128,256]{2,0,1:T(2,128)(2,1)} %copy.27), calls=%async_computation | async-start | bytes 262144 | tf_op jit(solution)/shard_map/all_to_all | solution.py:232
  8.7 4.2 %collective-permute-start.2 = (bf16[64,512]{1,0:T(8,128)(2,1)S(1)}, bf16[64,512]{1,0:T(8,128)(2,1)S(1)}, u32[]{:S(2)}, u32[]{:S(2)}) collective-permute-start(bf16[64,512]{1,0:T(8,128)(2,1)S(1)} %constant_dynamic-update-slice_fusion.refs_7_), channel_id=1, source_target_pairs={{0,24},{4,28},{8,0},{12,4},{16,8},{20,12},{24,16},{28,20},{1,25},{... | collective-permute-start | bytes 196616 | tf_op jit(solution)/shard_map/ppermute | solution.py:184
  12.9 1.4 %collective-permute-start.1 = (bf16[64,512]{1,0:T(8,128)(2,1)S(1)}, bf16[64,512]{1,0:T(8,128)(2,1)S(1)}, u32[]{:S(2)}, u32[]{:S(2)}) collective-permute-start(bf16[64,512]{1,0:T(8,128)(2,1)S(1)} %constant_dynamic-update-slice_fusion.refs_7_), channel_id=1, source_target_pairs={{0,28},{4,0},{8,4},{12,8},{16,12},{20,16},{24,20},{28,24},{1,29},{... | collective-permute-start | bytes 196616 | tf_op jit(solution)/shard_map/ppermute | solution.py:184
  14.3 3.0 %collective-permute-start.5 = (bf16[64,512]{1,0:T(8,128)(2,1)S(1)}, bf16[64,512]{1,0:T(8,128)(2,1)S(1)}, u32[]{:S(2)}, u32[]{:S(2)}) collective-permute-start(bf16[64,512]{1,0:T(8,128)(2,1)S(1)} %constant_dynamic-update-slice_fusion.refs_7_), channel_id=1, source_target_pairs={{0,16},{4,20},{8,24},{12,28},{16,0},{20,4},{24,8},{28,12},{1,17},{... | collective-permute-start | bytes 196616 | tf_op jit(solution)/shard_map/ppermute | solution.py:184
  17.3 1.5 %collective-permute-start = (bf16[192,512]{1,0:T(8,128)(2,1)S(1)}, bf16[192,512]{1,0:T(8,128)(2,1)S(1)}, u32[]{:S(2)}, u32[]{:S(2)}) collective-permute-start(bf16[192,512]{1,0:T(8,128)(2,1)S(1)} %maximum_maximum_fusion), channel_id=1, source_target_pairs={{0,4},{4,8},{8,12},{12,16},{16,20},{20,24},{24,28},{28,0},{1,5},{5... | collective-permute-start | bytes 589832 | tf_op jit(solution)/shard_map/ppermute | solution.py:184
  18.9 1.4 %collective-permute-start.3 = (bf16[64,512]{1,0:T(8,128)(2,1)S(1)}, bf16[64,512]{1,0:T(8,128)(2,1)S(1)}, u32[]{:S(2)}, u32[]{:S(2)}) collective-permute-start(bf16[64,512]{1,0:T(8,128)(2,1)S(1)} %constant_dynamic-update-slice_fusion.refs_7_), channel_id=1, source_target_pairs={{0,8},{4,12},{8,16},{12,20},{16,24},{20,28},{24,0},{28,4},{1,9},{5... | collective-permute-start | bytes 196616 | tf_op jit(solution)/shard_map/ppermute | solution.py:184
  20.3 0.2 fusion
  20.5 0.1 copy.29
  20.6 0.6 %copy.31 = bf16[4,8,4,256]{3,1,2,0:T(8,128)(2,1)} copy(bf16[4,8,4,256]{3,2,1,0:T(4,128)(2,1)S(1)} %bitcast.16) | data formatting | bytes 131072
  21.4 0.6 %copy.30 = bf16[4,8,4,256]{3,1,2,0:T(8,128)(2,1)} copy(bf16[4,8,4,256]{3,2,1,0:T(4,128)(2,1)S(1)} %bitcast.17) | data formatting | bytes 131072
  22.0 2.2 %collective-permute-done.5.refs_11_ = bf16[64,512]{1,0:T(8,128)(2,1)S(1)} collective-permute-done((bf16[64,512]{1,0:T(8,128)(2,1)S(1)}, bf16[64,512]{1,0:T(8,128)(2,1)S(1)}, u32[]{:S(2)}, u32[]{:S(2)}) %collective-permute-start.5) | collective-permute-done | bytes 65568 | tf_op jit(solution)/shard_map/ppermute | solution.py:184
  24.2 7.1 %collective-permute-done.4.refs_10_ = bf16[64,512]{1,0:T(8,128)(2,1)S(1)} collective-permute-done((bf16[64,512]{1,0:T(8,128)(2,1)S(1)}, bf16[64,512]{1,0:T(8,128)(2,1)S(1)}, u32[]{:S(2)}, u32[]{:S(2)}) %collective-permute-start.4) | collective-permute-done | bytes 65568 | tf_op jit(solution)/shard_map/ppermute | solution.py:184
  31.3 0.6 %copy-done.11 = bf16[64,512]{1,0:T(8,128)(2,1)} copy-done((bf16[64,512]{1,0:T(8,128)(2,1)}, bf16[64,512]{1,0:T(8,128)(2,1)S(1)}, u32[]{:S(2)}) %copy-start.11) | copy-done | bytes 65560
  32.0 4.4 %shard_map.103 = bf16[128,1024]{1,0:T(8,128)(2,1)} custom-call(s32[1]{0:T(128)} %bitcast.refs_0_, s32[24]{0:T(128)} %refs_1_.1, s32[24]{0:T(128)} %refs_2_.1, s32[8]{0:T(128)} %refs_3_.1, bf16[128,1024]{1,0:T(8,128)(2,1)} %refs_4_.1, bf16[128,256]{1,0:T(8,128)(2,1)} %refs_5_.1, bf16[128,256]{1,0:T(8,128)(2,1)} %refs_6_.1, bf16[64,512]{1,0:T(8,128)(2,1)} %copy-done.2, ...), custom_call_target="tpu_custom_call" | custom-call | flops 402653184 | bytes 1310720 | tf_op jit(solution)/shard_map/pallas_call | solution.py:155
  (43 shorter events, 0.5 us)
Async XLA Ops:
  0.7 0.7 %copy-start.5 = (s32[24]{0:T(128)S(1)}, s32[24]{0:T(128)}, u32[]{:S(2)}) copy-start(s32[24]{0:T(128)} %refs_1_.1) | copy-start | bytes 292
  0.7 1.1 %copy-start.3 = (bf16[64,256]{1,0:T(8,128)(2,1)S(1)}, bf16[64,256]{1,0:T(8,128)(2,1)}, u32[]{:S(2)}) copy-start(bf16[64,256]{1,0:T(8,128)(2,1)} %param.11) | copy-start | bytes 98308
  0.7 1.1 %copy-start.1 = (bf16[128,256]{1,0:T(8,128)(2,1)S(1)}, bf16[128,256]{1,0:T(8,128)(2,1)}, u32[]{:S(2)}) copy-start(bf16[128,256]{1,0:T(8,128)(2,1)} %refs_6_.1) | copy-start | bytes 196612
  1.8 0.8 %copy-start = (bf16[128,256]{1,0:T(8,128)(2,1)S(1)}, bf16[128,256]{1,0:T(8,128)(2,1)}, u32[]{:S(2)}) copy-start(bf16[128,256]{1,0:T(8,128)(2,1)} %refs_5_.1) | copy-start | bytes 196612
  2.6 0.8 %copy-start.4 = (bf16[64,256]{1,0:T(8,128)(2,1)S(1)}, bf16[64,256]{1,0:T(8,128)(2,1)}, u32[]{:S(2)}) copy-start(bf16[64,256]{1,0:T(8,128)(2,1)} %param.12) | copy-start | bytes 98308
  3.4 15.5 %copy-start.2 = (bf16[64,512]{1,0:T(8,128)(2,1)}, bf16[64,512]{1,0:T(8,128)(2,1)S(1)}, u32[]{:S(2)}) copy-start(bf16[64,512]{1,0:T(8,128)(2,1)S(1)} %constant_dynamic-update-slice_fusion.refs_7_) | copy-start | bytes 196612
  4.5 15.9 %all-to-all-start = ((bf16[2,128,256]{2,0,1:T(2,128)(2,1)}), bf16[2,128,256]{2,0,1:T(2,128)(2,1)S(1)}, u32[]{:S(2)}, u32[]{:S(2)}) async-start(bf16[2,128,256]{2,0,1:T(2,128)(2,1)} %copy.27), calls=%async_computation | async-start | bytes 262144 | tf_op jit(solution)/shard_map/all_to_all | solution.py:232
  8.7 10.1 %collective-permute-start.2 = (bf16[64,512]{1,0:T(8,128)(2,1)S(1)}, bf16[64,512]{1,0:T(8,128)(2,1)S(1)}, u32[]{:S(2)}, u32[]{:S(2)}) collective-permute-start(bf16[64,512]{1,0:T(8,128)(2,1)S(1)} %constant_dynamic-update-slice_fusion.refs_7_), channel_id=1, source_target_pairs={{0,24},{4,28},{8,0},{12,4},{16,8},{20,12},{24,16},{28,20},{1,25},{... | collective-permute-start | bytes 196616 | tf_op jit(solution)/shard_map/ppermute | solution.py:184
  12.9 5.9 %collective-permute-start.1 = (bf16[64,512]{1,0:T(8,128)(2,1)S(1)}, bf16[64,512]{1,0:T(8,128)(2,1)S(1)}, u32[]{:S(2)}, u32[]{:S(2)}) collective-permute-start(bf16[64,512]{1,0:T(8,128)(2,1)S(1)} %constant_dynamic-update-slice_fusion.refs_7_), channel_id=1, source_target_pairs={{0,28},{4,0},{8,4},{12,8},{16,12},{20,16},{24,20},{28,24},{1,29},{... | collective-permute-start | bytes 196616 | tf_op jit(solution)/shard_map/ppermute | solution.py:184
  14.3 7.7 %collective-permute-start.6 = (bf16[64,512]{1,0:T(8,128)(2,1)S(1)}, bf16[64,512]{1,0:T(8,128)(2,1)S(1)}, u32[]{:S(2)}, u32[]{:S(2)}) collective-permute-start(bf16[64,512]{1,0:T(8,128)(2,1)S(1)} %constant_dynamic-update-slice_fusion.refs_7_), channel_id=1, source_target_pairs={{0,20},{4,24},{8,28},{12,0},{16,4},{20,8},{24,12},{28,16},{1,21},{... | collective-permute-start | bytes 196616 | tf_op jit(solution)/shard_map/ppermute | solution.py:184
  14.3 9.9 %collective-permute-start.5 = (bf16[64,512]{1,0:T(8,128)(2,1)S(1)}, bf16[64,512]{1,0:T(8,128)(2,1)S(1)}, u32[]{:S(2)}, u32[]{:S(2)}) collective-permute-start(bf16[64,512]{1,0:T(8,128)(2,1)S(1)} %constant_dynamic-update-slice_fusion.refs_7_), channel_id=1, source_target_pairs={{0,16},{4,20},{8,24},{12,28},{16,0},{20,4},{24,8},{28,12},{1,17},{... | collective-permute-start | bytes 196616 | tf_op jit(solution)/shard_map/ppermute | solution.py:184
  17.3 14.0 %collective-permute-start = (bf16[192,512]{1,0:T(8,128)(2,1)S(1)}, bf16[192,512]{1,0:T(8,128)(2,1)S(1)}, u32[]{:S(2)}, u32[]{:S(2)}) collective-permute-start(bf16[192,512]{1,0:T(8,128)(2,1)S(1)} %maximum_maximum_fusion), channel_id=1, source_target_pairs={{0,4},{4,8},{8,12},{12,16},{16,20},{20,24},{24,28},{28,0},{1,5},{5... | collective-permute-start | bytes 589832 | tf_op jit(solution)/shard_map/ppermute | solution.py:184
  18.8 1.7 %copy-start.7 = (bf16[64,512]{1,0:T(8,128)(2,1)}, bf16[64,512]{1,0:T(8,128)(2,1)S(1)}, u32[]{:S(2)}) copy-start(bf16[64,512]{1,0:T(8,128)(2,1)S(1)} %collective-permute-done.2.refs_13_) | copy-start | bytes 196612
  18.8 1.7 %copy-start.8 = (bf16[64,512]{1,0:T(8,128)(2,1)}, bf16[64,512]{1,0:T(8,128)(2,1)S(1)}, u32[]{:S(2)}) copy-start(bf16[64,512]{1,0:T(8,128)(2,1)S(1)} %collective-permute-done.1.refs_14_) | copy-start | bytes 196612
  18.8 12.5 %collective-permute-start.4 = (bf16[64,512]{1,0:T(8,128)(2,1)S(1)}, bf16[64,512]{1,0:T(8,128)(2,1)S(1)}, u32[]{:S(2)}, u32[]{:S(2)}) collective-permute-start(bf16[64,512]{1,0:T(8,128)(2,1)S(1)} %constant_dynamic-update-slice_fusion.refs_7_), channel_id=1, source_target_pairs={{0,12},{4,16},{8,20},{12,24},{16,28},{20,0},{24,4},{28,8},{1,13},{... | collective-permute-start | bytes 196616 | tf_op jit(solution)/shard_map/ppermute | solution.py:184
  18.9 12.4 %collective-permute-start.3 = (bf16[64,512]{1,0:T(8,128)(2,1)S(1)}, bf16[64,512]{1,0:T(8,128)(2,1)S(1)}, u32[]{:S(2)}, u32[]{:S(2)}) collective-permute-start(bf16[64,512]{1,0:T(8,128)(2,1)S(1)} %constant_dynamic-update-slice_fusion.refs_7_), channel_id=1, source_target_pairs={{0,8},{4,12},{8,16},{12,20},{16,24},{20,28},{24,0},{28,4},{1,9},{5... | collective-permute-start | bytes 196616 | tf_op jit(solution)/shard_map/ppermute | solution.py:184
  22.0 9.3 %copy-start.9 = (bf16[64,512]{1,0:T(8,128)(2,1)}, bf16[64,512]{1,0:T(8,128)(2,1)S(1)}, u32[]{:S(2)}) copy-start(bf16[64,512]{1,0:T(8,128)(2,1)S(1)} %collective-permute-done.6.refs_12_) | copy-start | bytes 196612
  24.2 7.2 %copy-start.10 = (bf16[64,512]{1,0:T(8,128)(2,1)}, bf16[64,512]{1,0:T(8,128)(2,1)S(1)}, u32[]{:S(2)}) copy-start(bf16[64,512]{1,0:T(8,128)(2,1)S(1)} %collective-permute-done.5.refs_11_) | copy-start | bytes 196612
  31.3 0.6 %copy-start.11 = (bf16[64,512]{1,0:T(8,128)(2,1)}, bf16[64,512]{1,0:T(8,128)(2,1)S(1)}, u32[]{:S(2)}) copy-start(bf16[64,512]{1,0:T(8,128)(2,1)S(1)} %collective-permute-done.4.refs_10_) | copy-start | bytes 196612
  31.3 0.6 %copy-start.12 = (bf16[64,512]{1,0:T(8,128)(2,1)}, bf16[64,512]{1,0:T(8,128)(2,1)S(1)}, u32[]{:S(2)}) copy-start(bf16[64,512]{1,0:T(8,128)(2,1)S(1)} %collective-permute-done.3.refs_9_) | copy-start | bytes 196612
  31.3 0.7 %copy-start.6 = (bf16[192,512]{1,0:T(8,128)(2,1)}, bf16[192,512]{1,0:T(8,128)(2,1)S(1)}, u32[]{:S(2)}) copy-start(bf16[192,512]{1,0:T(8,128)(2,1)S(1)} %collective-permute-done.refs_8_) | copy-start | bytes 589828

commit v11 on v10

--- a/solution.py
+++ b/solution.py
@@ -126,12 +126,12 @@
         k = kscr[:, g * HD : (g + 1) * HD]
         scores = lax.dot_general(
             q, k, (((1,), (1,)), ((), ())), preferred_element_type=jnp.float32
-        ) * scale
+        )
         weights, totals = [], []
         for r in range(repeat):
             part = jnp.where(visible, scores[r * rows : (r + 1) * rows], BIG_NEGATIVE)
             high = jnp.max(part, axis=1, keepdims=True)
-            part = jnp.exp(part - high)
+            part = jnp.exp2((part - high) * (scale * math.log2(math.e)))
             totals.append(jnp.sum(part, axis=1, keepdims=True))
             weights.append(part.astype(jnp.bfloat16))
         v = vscr[:, g * HD : (g + 1) * HD]

time: 36.8 us -> 36.7 us (level)
  no operation moved by 1% of the time
where the time goes in v11:
time: 36.7 us; the launch traced here: 36.3 us
  starting transfers between devices  15.8 us (43%)
  waiting for transfers between devices  9.3 us (25%)
  local copies, waits for them, and re-layouts  5.43 us (15%)
  Pallas kernels  4.31 us (12%)
  between operations  0.85 us (2%)
  other arithmetic  0.62 us (2%)
    ppermute x7, starting transfers between devices, shifted(): return lax.ppermute(array, axis, pairs)  11.6 us
    ppermute x7, waiting for transfers between devices, shifted(): return lax.ppermute(array, axis, pairs)  9.3 us
    pallas_call x1, Pallas kernels, attend(): pl.pallas_call(functools.partial(attend_kernel, meta), out_shape=jax.Shap...  4.31 us
    all_to_all x1, starting transfers between devices, body(): lax.all_to_all(stacked, 'tp', split_axis=1, concat_axis=2, tiled=True)  4.24 us
    unnamed x29, local copies, waits for them, and re-layouts  3.98 us
    optimization_barrier x1, local copies, waits for them, and re-layouts, body(): lax.optimization_barrier((jnp.stack([own_k_rot, suffix_values], axis=0),...  0.79 us
  transfers between devices with their start and end apart: 8, of which 2 were waited for; matrix products, arithmetic and copies ran while one was open for 5% of the time, Pallas kernels for 0%

profile of v11, /device:TPU:0, one launch (start us, length us, event | category | flops | bytes accessed | tf_op | source)
XLA Modules:
  0.0 36.3 jit_solution(10072729648125515850)
XLA Ops:
  0.7 0.6 %copy-done.5 = s32[24]{0:T(128)S(1)} copy-done((s32[24]{0:T(128)S(1)}, s32[24]{0:T(128)}, u32[]{:S(2)}) %copy-start.5) | copy-done | bytes 120
  1.4 0.1 reduce
  1.6 0.1 convert_reduce_fusion
  1.7 0.1 select_reduce_fusion
  1.8 0.1 copy.26
  1.9 0.7 %copy-done = bf16[128,256]{1,0:T(8,128)(2,1)S(1)} copy-done((bf16[128,256]{1,0:T(8,128)(2,1)S(1)}, bf16[128,256]{1,0:T(8,128)(2,1)}, u32[]{:S(2)}) %copy-start) | copy-done | bytes 65560
  2.6 0.1 copy.24
  2.7 0.7 %copy-done.4 = bf16[64,256]{1,0:T(8,128)(2,1)S(1)} copy-done((bf16[64,256]{1,0:T(8,128)(2,1)S(1)}, bf16[64,256]{1,0:T(8,128)(2,1)}, u32[]{:S(2)}) %copy-start.4) | copy-done | bytes 32792
  3.4 0.2 multiply_cosine_fusion
  3.7 0.8 %copy.27 = bf16[2,128,256]{2,0,1:T(2,128)(2,1)} copy(bf16[2,128,256]{1,2,0:T(8,128)(2,1)S(1)} %pad_maximum_fusion) | data formatting | bytes 262144 | tf_op jit(solution)/shard_map/optimization_barrier | solution.py:225
  4.5 4.2 %all-to-all-start = ((bf16[2,128,256]{2,0,1:T(2,128)(2,1)}), bf16[2,128,256]{2,0,1:T(2,128)(2,1)S(1)}, u32[]{:S(2)}, u32[]{:S(2)}) async-start(bf16[2,128,256]{2,0,1:T(2,128)(2,1)} %copy.27), calls=%async_computation | async-start | bytes 262144 | tf_op jit(solution)/shard_map/all_to_all | solution.py:232
  8.7 4.2 %collective-permute-start.2 = (bf16[64,512]{1,0:T(8,128)(2,1)S(1)}, bf16[64,512]{1,0:T(8,128)(2,1)S(1)}, u32[]{:S(2)}, u32[]{:S(2)}) collective-permute-start(bf16[64,512]{1,0:T(8,128)(2,1)S(1)} %constant_dynamic-update-slice_fusion.refs_7_), channel_id=1, source_target_pairs={{0,24},{4,28},{8,0},{12,4},{16,8},{20,12},{24,16},{28,20},{1,25},{... | collective-permute-start | bytes 196616 | tf_op jit(solution)/shard_map/ppermute | solution.py:184
  12.9 1.4 %collective-permute-start.1 = (bf16[64,512]{1,0:T(8,128)(2,1)S(1)}, bf16[64,512]{1,0:T(8,128)(2,1)S(1)}, u32[]{:S(2)}, u32[]{:S(2)}) collective-permute-start(bf16[64,512]{1,0:T(8,128)(2,1)S(1)} %constant_dynamic-update-slice_fusion.refs_7_), channel_id=1, source_target_pairs={{0,28},{4,0},{8,4},{12,8},{16,12},{20,16},{24,20},{28,24},{1,29},{... | collective-permute-start | bytes 196616 | tf_op jit(solution)/shard_map/ppermute | solution.py:184
  14.3 3.0 %collective-permute-start.5 = (bf16[64,512]{1,0:T(8,128)(2,1)S(1)}, bf16[64,512]{1,0:T(8,128)(2,1)S(1)}, u32[]{:S(2)}, u32[]{:S(2)}) collective-permute-start(bf16[64,512]{1,0:T(8,128)(2,1)S(1)} %constant_dynamic-update-slice_fusion.refs_7_), channel_id=1, source_target_pairs={{0,16},{4,20},{8,24},{12,28},{16,0},{20,4},{24,8},{28,12},{1,17},{... | collective-permute-start | bytes 196616 | tf_op jit(solution)/shard_map/ppermute | solution.py:184
  17.3 1.5 %collective-permute-start = (bf16[192,512]{1,0:T(8,128)(2,1)S(1)}, bf16[192,512]{1,0:T(8,128)(2,1)S(1)}, u32[]{:S(2)}, u32[]{:S(2)}) collective-permute-start(bf16[192,512]{1,0:T(8,128)(2,1)S(1)} %maximum_maximum_fusion), channel_id=1, source_target_pairs={{0,4},{4,8},{8,12},{12,16},{16,20},{20,24},{24,28},{28,0},{1,5},{5... | collective-permute-start | bytes 589832 | tf_op jit(solution)/shard_map/ppermute | solution.py:184
  18.9 1.4 %collective-permute-start.3 = (bf16[64,512]{1,0:T(8,128)(2,1)S(1)}, bf16[64,512]{1,0:T(8,128)(2,1)S(1)}, u32[]{:S(2)}, u32[]{:S(2)}) collective-permute-start(bf16[64,512]{1,0:T(8,128)(2,1)S(1)} %constant_dynamic-update-slice_fusion.refs_7_), channel_id=1, source_target_pairs={{0,8},{4,12},{8,16},{12,20},{16,24},{20,28},{24,0},{28,4},{1,9},{5... | collective-permute-start | bytes 196616 | tf_op jit(solution)/shard_map/ppermute | solution.py:184
  20.3 0.2 fusion
  20.5 0.1 copy.29
  20.6 0.6 %copy.31 = bf16[4,8,4,256]{3,1,2,0:T(8,128)(2,1)} copy(bf16[4,8,4,256]{3,2,1,0:T(4,128)(2,1)S(1)} %bitcast.16) | data formatting | bytes 131072
  21.4 0.6 %copy.30 = bf16[4,8,4,256]{3,1,2,0:T(8,128)(2,1)} copy(bf16[4,8,4,256]{3,2,1,0:T(4,128)(2,1)S(1)} %bitcast.17) | data formatting | bytes 131072
  22.0 2.2 %collective-permute-done.5.refs_11_ = bf16[64,512]{1,0:T(8,128)(2,1)S(1)} collective-permute-done((bf16[64,512]{1,0:T(8,128)(2,1)S(1)}, bf16[64,512]{1,0:T(8,128)(2,1)S(1)}, u32[]{:S(2)}, u32[]{:S(2)}) %collective-permute-start.5) | collective-permute-done | bytes 65568 | tf_op jit(solution)/shard_map/ppermute | solution.py:184
  24.2 7.1 %collective-permute-done.4.refs_10_ = bf16[64,512]{1,0:T(8,128)(2,1)S(1)} collective-permute-done((bf16[64,512]{1,0:T(8,128)(2,1)S(1)}, bf16[64,512]{1,0:T(8,128)(2,1)S(1)}, u32[]{:S(2)}, u32[]{:S(2)}) %collective-permute-start.4) | collective-permute-done | bytes 65568 | tf_op jit(solution)/shard_map/ppermute | solution.py:184
  31.3 0.6 %copy-done.11 = bf16[64,512]{1,0:T(8,128)(2,1)} copy-done((bf16[64,512]{1,0:T(8,128)(2,1)}, bf16[64,512]{1,0:T(8,128)(2,1)S(1)}, u32[]{:S(2)}) %copy-start.11) | copy-done | bytes 65560
  32.0 4.3 %shard_map.103 = bf16[128,1024]{1,0:T(8,128)(2,1)} custom-call(s32[1]{0:T(128)} %bitcast.refs_0_, s32[24]{0:T(128)} %refs_1_.1, s32[24]{0:T(128)} %refs_2_.1, s32[8]{0:T(128)} %refs_3_.1, bf16[128,1024]{1,0:T(8,128)(2,1)} %refs_4_.1, bf16[128,256]{1,0:T(8,128)(2,1)} %refs_5_.1, bf16[128,256]{1,0:T(8,128)(2,1)} %refs_6_.1, bf16[64,512]{1,0:T(8,128)(2,1)} %copy-done.2, ...), custom_call_target="tpu_custom_call" | custom-call | flops 402653184 | bytes 1310720 | tf_op jit(solution)/shard_map/pallas_call | solution.py:155
  (43 shorter events, 0.5 us)
Async XLA Ops:
  0.7 0.7 %copy-start.5 = (s32[24]{0:T(128)S(1)}, s32[24]{0:T(128)}, u32[]{:S(2)}) copy-start(s32[24]{0:T(128)} %refs_1_.1) | copy-start | bytes 292
  0.7 1.1 %copy-start.3 = (bf16[64,256]{1,0:T(8,128)(2,1)S(1)}, bf16[64,256]{1,0:T(8,128)(2,1)}, u32[]{:S(2)}) copy-start(bf16[64,256]{1,0:T(8,128)(2,1)} %param.11) | copy-start | bytes 98308
  0.7 1.1 %copy-start.1 = (bf16[128,256]{1,0:T(8,128)(2,1)S(1)}, bf16[128,256]{1,0:T(8,128)(2,1)}, u32[]{:S(2)}) copy-start(bf16[128,256]{1,0:T(8,128)(2,1)} %refs_6_.1) | copy-start | bytes 196612
  1.8 0.8 %copy-start = (bf16[128,256]{1,0:T(8,128)(2,1)S(1)}, bf16[128,256]{1,0:T(8,128)(2,1)}, u32[]{:S(2)}) copy-start(bf16[128,256]{1,0:T(8,128)(2,1)} %refs_5_.1) | copy-start | bytes 196612
  2.6 0.8 %copy-start.4 = (bf16[64,256]{1,0:T(8,128)(2,1)S(1)}, bf16[64,256]{1,0:T(8,128)(2,1)}, u32[]{:S(2)}) copy-start(bf16[64,256]{1,0:T(8,128)(2,1)} %param.12) | copy-start | bytes 98308
  3.4 15.5 %copy-start.2 = (bf16[64,512]{1,0:T(8,128)(2,1)}, bf16[64,512]{1,0:T(8,128)(2,1)S(1)}, u32[]{:S(2)}) copy-start(bf16[64,512]{1,0:T(8,128)(2,1)S(1)} %constant_dynamic-update-slice_fusion.refs_7_) | copy-start | bytes 196612
  4.5 15.9 %all-to-all-start = ((bf16[2,128,256]{2,0,1:T(2,128)(2,1)}), bf16[2,128,256]{2,0,1:T(2,128)(2,1)S(1)}, u32[]{:S(2)}, u32[]{:S(2)}) async-start(bf16[2,128,256]{2,0,1:T(2,128)(2,1)} %copy.27), calls=%async_computation | async-start | bytes 262144 | tf_op jit(solution)/shard_map/all_to_all | solution.py:232
  8.7 10.1 %collective-permute-start.2 = (bf16[64,512]{1,0:T(8,128)(2,1)S(1)}, bf16[64,512]{1,0:T(8,128)(2,1)S(1)}, u32[]{:S(2)}, u32[]{:S(2)}) collective-permute-start(bf16[64,512]{1,0:T(8,128)(2,1)S(1)} %constant_dynamic-update-slice_fusion.refs_7_), channel_id=1, source_target_pairs={{0,24},{4,28},{8,0},{12,4},{16,8},{20,12},{24,16},{28,20},{1,25},{... | collective-permute-start | bytes 196616 | tf_op jit(solution)/shard_map/ppermute | solution.py:184
  12.9 5.9 %collective-permute-start.1 = (bf16[64,512]{1,0:T(8,128)(2,1)S(1)}, bf16[64,512]{1,0:T(8,128)(2,1)S(1)}, u32[]{:S(2)}, u32[]{:S(2)}) collective-permute-start(bf16[64,512]{1,0:T(8,128)(2,1)S(1)} %constant_dynamic-update-slice_fusion.refs_7_), channel_id=1, source_target_pairs={{0,28},{4,0},{8,4},{12,8},{16,12},{20,16},{24,20},{28,24},{1,29},{... | collective-permute-start | bytes 196616 | tf_op jit(solution)/shard_map/ppermute | solution.py:184
  14.3 7.7 %collective-permute-start.6 = (bf16[64,512]{1,0:T(8,128)(2,1)S(1)}, bf16[64,512]{1,0:T(8,128)(2,1)S(1)}, u32[]{:S(2)}, u32[]{:S(2)}) collective-permute-start(bf16[64,512]{1,0:T(8,128)(2,1)S(1)} %constant_dynamic-update-slice_fusion.refs_7_), channel_id=1, source_target_pairs={{0,20},{4,24},{8,28},{12,0},{16,4},{20,8},{24,12},{28,16},{1,21},{... | collective-permute-start | bytes 196616 | tf_op jit(solution)/shard_map/ppermute | solution.py:184
  14.3 9.9 %collective-permute-start.5 = (bf16[64,512]{1,0:T(8,128)(2,1)S(1)}, bf16[64,512]{1,0:T(8,128)(2,1)S(1)}, u32[]{:S(2)}, u32[]{:S(2)}) collective-permute-start(bf16[64,512]{1,0:T(8,128)(2,1)S(1)} %constant_dynamic-update-slice_fusion.refs_7_), channel_id=1, source_target_pairs={{0,16},{4,20},{8,24},{12,28},{16,0},{20,4},{24,8},{28,12},{1,17},{... | collective-permute-start | bytes 196616 | tf_op jit(solution)/shard_map/ppermute | solution.py:184
  17.3 14.0 %collective-permute-start = (bf16[192,512]{1,0:T(8,128)(2,1)S(1)}, bf16[192,512]{1,0:T(8,128)(2,1)S(1)}, u32[]{:S(2)}, u32[]{:S(2)}) collective-permute-start(bf16[192,512]{1,0:T(8,128)(2,1)S(1)} %maximum_maximum_fusion), channel_id=1, source_target_pairs={{0,4},{4,8},{8,12},{12,16},{16,20},{20,24},{24,28},{28,0},{1,5},{5... | collective-permute-start | bytes 589832 | tf_op jit(solution)/shard_map/ppermute | solution.py:184
  18.8 1.7 %copy-start.7 = (bf16[64,512]{1,0:T(8,128)(2,1)}, bf16[64,512]{1,0:T(8,128)(2,1)S(1)}, u32[]{:S(2)}) copy-start(bf16[64,512]{1,0:T(8,128)(2,1)S(1)} %collective-permute-done.2.refs_13_) | copy-start | bytes 196612
  18.8 1.7 %copy-start.8 = (bf16[64,512]{1,0:T(8,128)(2,1)}, bf16[64,512]{1,0:T(8,128)(2,1)S(1)}, u32[]{:S(2)}) copy-start(bf16[64,512]{1,0:T(8,128)(2,1)S(1)} %collective-permute-done.1.refs_14_) | copy-start | bytes 196612
  18.8 12.5 %collective-permute-start.4 = (bf16[64,512]{1,0:T(8,128)(2,1)S(1)}, bf16[64,512]{1,0:T(8,128)(2,1)S(1)}, u32[]{:S(2)}, u32[]{:S(2)}) collective-permute-start(bf16[64,512]{1,0:T(8,128)(2,1)S(1)} %constant_dynamic-update-slice_fusion.refs_7_), channel_id=1, source_target_pairs={{0,12},{4,16},{8,20},{12,24},{16,28},{20,0},{24,4},{28,8},{1,13},{... | collective-permute-start | bytes 196616 | tf_op jit(solution)/shard_map/ppermute | solution.py:184
  18.9 12.4 %collective-permute-start.3 = (bf16[64,512]{1,0:T(8,128)(2,1)S(1)}, bf16[64,512]{1,0:T(8,128)(2,1)S(1)}, u32[]{:S(2)}, u32[]{:S(2)}) collective-permute-start(bf16[64,512]{1,0:T(8,128)(2,1)S(1)} %constant_dynamic-update-slice_fusion.refs_7_), channel_id=1, source_target_pairs={{0,8},{4,12},{8,16},{12,20},{16,24},{20,28},{24,0},{28,4},{1,9},{5... | collective-permute-start | bytes 196616 | tf_op jit(solution)/shard_map/ppermute | solution.py:184
  22.0 9.3 %copy-start.9 = (bf16[64,512]{1,0:T(8,128)(2,1)}, bf16[64,512]{1,0:T(8,128)(2,1)S(1)}, u32[]{:S(2)}) copy-start(bf16[64,512]{1,0:T(8,128)(2,1)S(1)} %collective-permute-done.6.refs_12_) | copy-start | bytes 196612
  24.2 7.2 %copy-start.10 = (bf16[64,512]{1,0:T(8,128)(2,1)}, bf16[64,512]{1,0:T(8,128)(2,1)S(1)}, u32[]{:S(2)}) copy-start(bf16[64,512]{1,0:T(8,128)(2,1)S(1)} %collective-permute-done.5.refs_11_) | copy-start | bytes 196612
  31.3 0.6 %copy-start.11 = (bf16[64,512]{1,0:T(8,128)(2,1)}, bf16[64,512]{1,0:T(8,128)(2,1)S(1)}, u32[]{:S(2)}) copy-start(bf16[64,512]{1,0:T(8,128)(2,1)S(1)} %collective-permute-done.4.refs_10_) | copy-start | bytes 196612
  31.3 0.6 %copy-start.12 = (bf16[64,512]{1,0:T(8,128)(2,1)}, bf16[64,512]{1,0:T(8,128)(2,1)S(1)}, u32[]{:S(2)}) copy-start(bf16[64,512]{1,0:T(8,128)(2,1)S(1)} %collective-permute-done.3.refs_9_) | copy-start | bytes 196612
  31.3 0.7 %copy-start.6 = (bf16[192,512]{1,0:T(8,128)(2,1)}, bf16[192,512]{1,0:T(8,128)(2,1)S(1)}, u32[]{:S(2)}) copy-start(bf16[192,512]{1,0:T(8,128)(2,1)S(1)} %collective-permute-done.refs_8_) | copy-start | bytes 589828

commit v12 on v11

--- a/solution.py
+++ b/solution.py
@@ -92,10 +92,10 @@
         cosine, sine = tables(offset)
         for g in range(kv_cols // HD):
             if b == 0:
-                x = own_k_ref[:, g * HD : (g + 1) * HD]
+                kscr[low : low + rows, g * HD : (g + 1) * HD] = own_k_ref[:, g * HD : (g + 1) * HD]
             else:
                 x = data[b][block_rows : block_rows + rows, g * HD : (g + 1) * HD]
-            kscr[low : low + rows, g * HD : (g + 1) * HD] = rotated(x.astype(jnp.float32), cosine, sine)
+                kscr[low : low + rows, g * HD : (g + 1) * HD] = rotated(x.astype(jnp.float32), cosine, sine)
         if b == 0:
             vscr[low : low + rows, :] = own_v_ref[...]
         else:
@@ -218,34 +218,36 @@
         return key_index, key_request, k_rot
 
     if devices <= 16:
-        _, own_offset, _ = token_info(index, suffix_lengths, request_group)
-        own_k_rot = rotate(suffix_keys.reshape(rows, kv_heads, HD), own_offset + prefix_len).reshape(
-            rows, kv_cols
-        )
-        stacked, both, early_kv = lax.optimization_barrier(
-            (
-                jnp.stack([own_k_rot, suffix_values], axis=0),
-                jnp.concatenate([prefix_kv, suffix_kv], axis=0),
-                prefix_kv,
-            )
-        )
-        cache = lax.all_to_all(stacked, "tp", split_axis=1, concat_axis=2, tiled=True)
         received = {}
         late = list(range(span + 1, devices))[: max(0, devices - 1 - 5)]
         for by in range(1, devices):
             if by <= span:
-                received[by] = shifted(both, "seq", by, True)
+                received[by] = shifted(jnp.concatenate([prefix_kv, suffix_kv], axis=0), "seq", by, True)
             elif by not in late:
-                received[by] = shifted(early_kv, "seq", by, True)
-        gates = tuple(received[devices - 1 - i] for i in range(len(late)))
-        gates, payload = lax.optimization_barrier((gates, prefix_kv))
-        for i, by in enumerate(late):
-            received[devices - 1 - i] = gates[i]
-            received[by] = shifted(payload, "seq", by, True)
+                received[by] = shifted(prefix_kv, "seq", by, True)
+        cache_keys_in, cache_values_in = suffix_keys, suffix_values
+        if late:
+            first_gate, cache_keys_in, cache_values_in = lax.optimization_barrier(
+                (received[devices - 1], suffix_keys, suffix_values)
+            )
+            received[devices - 1] = first_gate
+            gates = (received[1],) + tuple(received[devices - 1 - i] for i in range(len(late)))
+            gates, payload = lax.optimization_barrier((gates, prefix_kv))
+            received[1] = gates[0]
+            for i, by in enumerate(late):
+                received[devices - 1 - i] = gates[i + 1]
+                received[by] = shifted(payload, "seq", by, True)
         data = [prefix_kv] + [received[by] for by in range(1, devices)]
+        _, own_offset, _ = token_info(index, suffix_lengths, request_group)
+        own_k_rot = rotate(cache_keys_in.reshape(rows, kv_heads, HD), own_offset + prefix_len).reshape(
+            rows, kv_cols
+        )
+        cache = lax.all_to_all(
+            jnp.stack([own_k_rot, cache_values_in], axis=0), "tp", split_axis=1, concat_axis=2, tiled=True
+        )
         scalars = [me.astype(jnp.int32).reshape(1), suffix_lengths, request_group, block_group]
         meta = (devices, block_rows, rows, min(span, devices - 1), prefix_len, repeat, scale)
-        attended = attend(meta, scalars, queries, suffix_keys, suffix_values, data)
+        attended = attend(meta, scalars, queries, own_k_rot, suffix_values, data)
         return (attended, cache[0], cache[1])
 
     prefix_parts = []

time: 36.7 us -> 36.7 us (level)
  waiting for transfers between devices: 9.3 us -> 5.71 us
  starting transfers between devices: 15.8 us -> 18.1 us
  local copies, waits for them, and re-layouts: 5.43 us -> 6.81 us
    ppermute x7, waiting for transfers between devices: 9.3 us -> 5.71 us  [shifted(): return lax.ppermute(array, axis, pairs)]
    ppermute x7, starting transfers between devices: 11.6 us -> 14.7 us  [shifted(): return lax.ppermute(array, axis, pairs)]
    all_to_all x1, starting transfers between devices: 4.24 us -> 3.33 us  [body(): lax.all_to_all(jnp.stack([own_k_rot, cache_values_in], axis=0), 'tp', spl...]
    optimization_barrier x1 -> x0, local copies, waits for them, and re-layouts: 0.79 us -> none  [body(): lax.optimization_barrier((jnp.stack([own_k_rot, suffix_values], axis=0),...]
    another operation x2 -> x3, local copies, waits for them, and re-layouts: 0.2 us -> 0.98 us  [the longest x2 0.9 us: body(): jnp.stack([own_k_rot, cache_values_in], axis=0)]
    concatenate x1, local copies, waits for them, and re-layouts: 0.01 us -> 0.76 us  [body(): prefix_kv = jnp.concatenate([prefix_keys, prefix_values], axis=1)]
    convert_element_type x0 -> x1, local copies, waits for them, and re-layouts: none -> 0.73 us  [rotate(): return jnp.concatenate([lower * cosine - upper * sine, upper * cosine + l...]
    unnamed x29 -> x25, local copies, waits for them, and re-layouts: 3.98 us -> 3.88 us
  transfers between devices with their start and end apart: 8 -> 8, of which waited for: 2 -> 3; matrix products, arithmetic and copies ran while one was open for 5% -> 11% of each run, Pallas kernels for 0% -> 0%
where the time goes in v12:
time: 36.7 us; the launch traced here: 36.3 us
  starting transfers between devices  18.1 us (49%)
  local copies, waits for them, and re-layouts  6.81 us (19%)
  waiting for transfers between devices  5.71 us (16%)
  Pallas kernels  4.3 us (12%)
  between operations  0.83 us (2%)
  other arithmetic  0.63 us (2%)
    ppermute x7, starting transfers between devices, shifted(): return lax.ppermute(array, axis, pairs)  14.7 us
    ppermute x7, waiting for transfers between devices, shifted(): return lax.ppermute(array, axis, pairs)  5.71 us
    pallas_call x1, Pallas kernels, attend(): pl.pallas_call(functools.partial(attend_kernel, meta), out_shape=jax.Shap...  4.3 us
    unnamed x25, local copies, waits for them, and re-layouts  3.88 us
    all_to_all x1, starting transfers between devices, body(): lax.all_to_all(jnp.stack([own_k_rot, cache_values_in], axis=0), 'tp', spl...  3.33 us
    another operation x2, local copies, waits for them, and re-layouts, body(): jnp.stack([own_k_rot, cache_values_in], axis=0)  0.9 us
    concatenate x1, local copies, waits for them, and re-layouts, body(): prefix_kv = jnp.concatenate([prefix_keys, prefix_values], axis=1)  0.76 us
  transfers between devices with their start and end apart: 8, of which 3 were waited for; matrix products, arithmetic and copies ran while one was open for 11% of the time, Pallas kernels for 0%

profile of v12, /device:TPU:0, one launch (start us, length us, event | category | flops | bytes accessed | tf_op | source)
XLA Modules:
  0.0 36.3 jit_solution(15733442723269664583)
XLA Ops:
  0.7 0.8 %constant_dynamic-update-slice_fusion.1 = bf16[64,512]{1,0:T(8,128)(2,1)S(1)} fusion(bf16[64,256]{1,0:T(8,128)(2,1)} %param.11), kind=kLoop, calls=%fused_computation.11 | loop fusion | bytes 65536
  1.4 0.8 %constant_dynamic-update-slice_fusion.refs_7_ = bf16[64,512]{1,0:T(8,128)(2,1)S(1)} fusion(bf16[64,512]{1,0:T(8,128)(2,1)S(1)} %constant_dynamic-update-slice_fusion.1, bf16[64,256]{1,0:T(8,128)(2,1)} %param.12), kind=kLoop, calls=%fused_computation.10 | loop fusion | bytes 65536 | tf_op jit(solution)/shard_map/concatenate | solution.py:211
  2.2 6.0 %collective-permute-start = (bf16[64,512]{1,0:T(8,128)(2,1)S(1)}, bf16[64,512]{1,0:T(8,128)(2,1)S(1)}, u32[]{:S(2)}, u32[]{:S(2)}) collective-permute-start(bf16[64,512]{1,0:T(8,128)(2,1)S(1)} %constant_dynamic-update-slice_fusion.refs_7_), channel_id=1, source_target_pairs={{0,28},{4,0},{8,4},{12,8},{16,12},{20,16},{24,20},{28,24},{1,29},{... | collective-permute-start | bytes 196616 | tf_op jit(solution)/shard_map/ppermute | solution.py:184
  8.3 0.6 %copy-done.3 = s32[24]{0:T(128)S(1)} copy-done((s32[24]{0:T(128)S(1)}, s32[24]{0:T(128)}, u32[]{:S(2)}) %copy-start.3) | copy-done | bytes 120
  9.1 0.1 reduce
  9.3 0.1 select_reduce_fusion
  9.4 0.2 multiply_cosine_fusion
  9.6 0.5 %collective-permute-done.refs_14_ = bf16[64,512]{1,0:T(8,128)(2,1)S(1)} collective-permute-done((bf16[64,512]{1,0:T(8,128)(2,1)S(1)}, bf16[64,512]{1,0:T(8,128)(2,1)S(1)}, u32[]{:S(2)}, u32[]{:S(2)}) %collective-permute-start) | collective-permute-done | bytes 65568 | tf_op jit(solution)/shard_map/ppermute | solution.py:184
  10.1 0.1 copy.25
  10.2 0.5 %copy-done.5 = bf16[64,512]{1,0:T(8,128)(2,1)} copy-done((bf16[64,512]{1,0:T(8,128)(2,1)}, bf16[64,512]{1,0:T(8,128)(2,1)S(1)}, u32[]{:S(2)}) %copy-start.5) | copy-done | bytes 65560
  10.7 0.1 copy.28
  10.9 0.8 %copy.29 = bf16[2,128,256]{2,0,1:T(2,128)(2,1)} copy(bf16[2,128,256]{1,2,0:T(8,128)(2,1)S(1)} %pad_maximum_fusion) | data formatting | bytes 262144 | tf_op jit(solution)/shard_map/stack | solution.py:246
  11.7 3.3 %all-to-all-start = ((bf16[2,128,256]{2,0,1:T(2,128)(2,1)}), bf16[2,128,256]{2,0,1:T(2,128)(2,1)S(1)}, u32[]{:S(2)}, u32[]{:S(2)}) async-start(bf16[2,128,256]{2,0,1:T(2,128)(2,1)} %copy.29), calls=%async_computation | async-start | bytes 262144 | tf_op jit(solution)/shard_map/all_to_all | solution.py:245
  15.0 1.5 %collective-permute-start.2 = (bf16[64,512]{1,0:T(8,128)(2,1)S(1)}, bf16[64,512]{1,0:T(8,128)(2,1)S(1)}, u32[]{:S(2)}, u32[]{:S(2)}) collective-permute-start(bf16[64,512]{1,0:T(8,128)(2,1)S(1)} %constant_dynamic-update-slice_fusion.refs_7_), channel_id=1, source_target_pairs={{0,24},{4,28},{8,0},{12,4},{16,8},{20,12},{24,16},{28,20},{1,25},{... | collective-permute-start | bytes 196616 | tf_op jit(solution)/shard_map/ppermute | solution.py:184
  16.5 6.6 %collective-permute-start.6 = (bf16[64,512]{1,0:T(8,128)(2,1)S(1)}, bf16[64,512]{1,0:T(8,128)(2,1)S(1)}, u32[]{:S(2)}, u32[]{:S(2)}) collective-permute-start(bf16[64,512]{1,0:T(8,128)(2,1)S(1)} %constant_dynamic-update-slice_fusion.refs_7_), channel_id=1, source_target_pairs={{0,20},{4,24},{8,28},{12,0},{16,4},{20,8},{24,12},{28,16},{1,21},{... | collective-permute-start | bytes 196616 | tf_op jit(solution)/shard_map/ppermute | solution.py:184
  23.1 0.7 %copy.32.refs_5_ = bf16[128,256]{1,0:T(8,128)(2,1)} copy(bf16[128,256]{0,1:T(8,128)(2,1)S(1)} %bitcast.17) | data formatting | bytes 131072 | tf_op jit(solution)/shard_map/convert_element_type | solution.py:31
  23.9 0.5 %collective-permute-start.4 = (bf16[64,512]{1,0:T(8,128)(2,1)S(1)}, bf16[64,512]{1,0:T(8,128)(2,1)S(1)}, u32[]{:S(2)}, u32[]{:S(2)}) collective-permute-start(bf16[64,512]{1,0:T(8,128)(2,1)S(1)} %constant_dynamic-update-slice_fusion.refs_7_), channel_id=1, source_target_pairs={{0,12},{4,16},{8,20},{12,24},{16,28},{20,0},{24,4},{28,8},{1,13},{... | collective-permute-start | bytes 196616 | tf_op jit(solution)/shard_map/ppermute | solution.py:184
  24.5 0.2 fusion
  24.8 0.6 %copy.33 = bf16[4,8,4,256]{3,1,2,0:T(8,128)(2,1)} copy(bf16[4,8,4,256]{3,2,1,0:T(4,128)(2,1)S(1)} %bitcast.19) | data formatting | bytes 131072
  25.5 0.6 %copy.34 = bf16[4,8,4,256]{3,1,2,0:T(8,128)(2,1)} copy(bf16[4,8,4,256]{3,2,1,0:T(4,128)(2,1)S(1)} %bitcast.20) | data formatting | bytes 131072
  26.2 3.8 %collective-permute-done.3.refs_9_ = bf16[64,512]{1,0:T(8,128)(2,1)S(1)} collective-permute-done((bf16[64,512]{1,0:T(8,128)(2,1)S(1)}, bf16[64,512]{1,0:T(8,128)(2,1)S(1)}, u32[]{:S(2)}, u32[]{:S(2)}) %collective-permute-start.3) | collective-permute-done | bytes 65568 | tf_op jit(solution)/shard_map/ppermute | solution.py:184
  30.0 1.4 %collective-permute-done.4.refs_10_ = bf16[64,512]{1,0:T(8,128)(2,1)S(1)} collective-permute-done((bf16[64,512]{1,0:T(8,128)(2,1)S(1)}, bf16[64,512]{1,0:T(8,128)(2,1)S(1)}, u32[]{:S(2)}, u32[]{:S(2)}) %collective-permute-start.4) | collective-permute-done | bytes 65568 | tf_op jit(solution)/shard_map/ppermute | solution.py:184
  31.4 0.6 %copy-done.10 = bf16[64,512]{1,0:T(8,128)(2,1)} copy-done((bf16[64,512]{1,0:T(8,128)(2,1)}, bf16[64,512]{1,0:T(8,128)(2,1)S(1)}, u32[]{:S(2)}) %copy-start.10) | copy-done | bytes 65560
  32.0 4.3 %shard_map.103 = bf16[128,1024]{1,0:T(8,128)(2,1)} custom-call(s32[1]{0:T(128)} %bitcast.refs_0_, s32[24]{0:T(128)} %refs_1_.1, s32[24]{0:T(128)} %refs_2_.1, s32[8]{0:T(128)} %refs_3_.1, bf16[128,1024]{1,0:T(8,128)(2,1)} %refs_4_.1, bf16[128,256]{1,0:T(8,128)(2,1)} %copy.32.refs_5_, bf16[128,256]{1,0:T(8,128)(2,1)} %refs_6_.1, bf16[64,512]{1,0:T(8,128)(2,1)} %copy-done.2, ...), custom_call_target="tpu_custom_call" | custom-call | flops 402653184 | bytes 1310720 | tf_op jit(solution)/shard_map/pallas_call | solution.py:155
  (40 shorter events, 0.7 us)
Async XLA Ops:
  0.6 7.6 %copy-start.1 = (bf16[128,256]{1,0:T(8,128)(2,1)S(1)}, bf16[128,256]{1,0:T(8,128)(2,1)}, u32[]{:S(2)}) copy-start(bf16[128,256]{1,0:T(8,128)(2,1)} %refs_6_.1) | copy-start | bytes 196612
  0.6 7.5 %copy-start = (bf16[128,256]{1,0:T(8,128)(2,1)S(1)}, bf16[128,256]{1,0:T(8,128)(2,1)}, u32[]{:S(2)}) copy-start(bf16[128,256]{1,0:T(8,128)(2,1)} %param.9) | copy-start | bytes 196612
  2.2 21.7 %copy-start.2 = (bf16[64,512]{1,0:T(8,128)(2,1)}, bf16[64,512]{1,0:T(8,128)(2,1)S(1)}, u32[]{:S(2)}) copy-start(bf16[64,512]{1,0:T(8,128)(2,1)S(1)} %constant_dynamic-update-slice_fusion.refs_7_) | copy-start | bytes 196612
  2.2 7.9 %collective-permute-start = (bf16[64,512]{1,0:T(8,128)(2,1)S(1)}, bf16[64,512]{1,0:T(8,128)(2,1)S(1)}, u32[]{:S(2)}, u32[]{:S(2)}) collective-permute-start(bf16[64,512]{1,0:T(8,128)(2,1)S(1)} %constant_dynamic-update-slice_fusion.refs_7_), channel_id=1, source_target_pairs={{0,28},{4,0},{8,4},{12,8},{16,12},{20,16},{24,20},{28,24},{1,29},{... | collective-permute-start | bytes 196616 | tf_op jit(solution)/shard_map/ppermute | solution.py:184
  8.2 15.6 %collective-permute-start.1 = (bf16[192,512]{1,0:T(8,128)(2,1)S(1)}, bf16[192,512]{1,0:T(8,128)(2,1)S(1)}, u32[]{:S(2)}, u32[]{:S(2)}) collective-permute-start(bf16[192,512]{1,0:T(8,128)(2,1)S(1)} %maximum_maximum_fusion), channel_id=1, source_target_pairs={{0,4},{4,8},{8,12},{12,16},{16,20},{20,24},{24,28},{28,0},{1,5},{5... | collective-permute-start | bytes 589832 | tf_op jit(solution)/shard_map/ppermute | solution.py:184
  8.3 0.7 %copy-start.3 = (s32[24]{0:T(128)S(1)}, s32[24]{0:T(128)}, u32[]{:S(2)}) copy-start(s32[24]{0:T(128)} %refs_1_.1) | copy-start | bytes 292
  10.1 0.6 %copy-start.5 = (bf16[64,512]{1,0:T(8,128)(2,1)}, bf16[64,512]{1,0:T(8,128)(2,1)S(1)}, u32[]{:S(2)}) copy-start(bf16[64,512]{1,0:T(8,128)(2,1)S(1)} %collective-permute-done.refs_14_) | copy-start | bytes 196612
  11.7 12.8 %all-to-all-start = ((bf16[2,128,256]{2,0,1:T(2,128)(2,1)}), bf16[2,128,256]{2,0,1:T(2,128)(2,1)S(1)}, u32[]{:S(2)}, u32[]{:S(2)}) async-start(bf16[2,128,256]{2,0,1:T(2,128)(2,1)} %copy.29), calls=%async_computation | async-start | bytes 262144 | tf_op jit(solution)/shard_map/all_to_all | solution.py:245
  15.0 8.8 %collective-permute-start.2 = (bf16[64,512]{1,0:T(8,128)(2,1)S(1)}, bf16[64,512]{1,0:T(8,128)(2,1)S(1)}, u32[]{:S(2)}, u32[]{:S(2)}) collective-permute-start(bf16[64,512]{1,0:T(8,128)(2,1)S(1)} %constant_dynamic-update-slice_fusion.refs_7_), channel_id=1, source_target_pairs={{0,24},{4,28},{8,0},{12,4},{16,8},{20,12},{24,16},{28,20},{1,25},{... | collective-permute-start | bytes 196616 | tf_op jit(solution)/shard_map/ppermute | solution.py:184
  16.5 9.7 %collective-permute-start.5 = (bf16[64,512]{1,0:T(8,128)(2,1)S(1)}, bf16[64,512]{1,0:T(8,128)(2,1)S(1)}, u32[]{:S(2)}, u32[]{:S(2)}) collective-permute-start(bf16[64,512]{1,0:T(8,128)(2,1)S(1)} %constant_dynamic-update-slice_fusion.refs_7_), channel_id=1, source_target_pairs={{0,16},{4,20},{8,24},{12,28},{16,0},{20,4},{24,8},{28,12},{1,17},{... | collective-permute-start | bytes 196616 | tf_op jit(solution)/shard_map/ppermute | solution.py:184
  16.5 9.7 %collective-permute-start.6 = (bf16[64,512]{1,0:T(8,128)(2,1)S(1)}, bf16[64,512]{1,0:T(8,128)(2,1)S(1)}, u32[]{:S(2)}, u32[]{:S(2)}) collective-permute-start(bf16[64,512]{1,0:T(8,128)(2,1)S(1)} %constant_dynamic-update-slice_fusion.refs_7_), channel_id=1, source_target_pairs={{0,20},{4,24},{8,28},{12,0},{16,4},{20,8},{24,12},{28,16},{1,21},{... | collective-permute-start | bytes 196616 | tf_op jit(solution)/shard_map/ppermute | solution.py:184
  23.9 0.8 %copy-start.6 = (bf16[64,512]{1,0:T(8,128)(2,1)}, bf16[64,512]{1,0:T(8,128)(2,1)S(1)}, u32[]{:S(2)}) copy-start(bf16[64,512]{1,0:T(8,128)(2,1)S(1)} %collective-permute-done.2.refs_13_) | copy-start | bytes 196612
  23.9 0.8 %copy-start.4 = (bf16[192,512]{1,0:T(8,128)(2,1)}, bf16[192,512]{1,0:T(8,128)(2,1)S(1)}, u32[]{:S(2)}) copy-start(bf16[192,512]{1,0:T(8,128)(2,1)S(1)} %collective-permute-done.1.refs_8_) | copy-start | bytes 589828
  23.9 6.1 %collective-permute-start.3 = (bf16[64,512]{1,0:T(8,128)(2,1)S(1)}, bf16[64,512]{1,0:T(8,128)(2,1)S(1)}, u32[]{:S(2)}, u32[]{:S(2)}) collective-permute-start(bf16[64,512]{1,0:T(8,128)(2,1)S(1)} %constant_dynamic-update-slice_fusion.refs_7_), channel_id=1, source_target_pairs={{0,8},{4,12},{8,16},{12,20},{16,24},{20,28},{24,0},{28,4},{1,9},{5... | collective-permute-start | bytes 196616 | tf_op jit(solution)/shard_map/ppermute | solution.py:184
  23.9 7.5 %collective-permute-start.4 = (bf16[64,512]{1,0:T(8,128)(2,1)S(1)}, bf16[64,512]{1,0:T(8,128)(2,1)S(1)}, u32[]{:S(2)}, u32[]{:S(2)}) collective-permute-start(bf16[64,512]{1,0:T(8,128)(2,1)S(1)} %constant_dynamic-update-slice_fusion.refs_7_), channel_id=1, source_target_pairs={{0,12},{4,16},{8,20},{12,24},{16,28},{20,0},{24,4},{28,8},{1,13},{... | collective-permute-start | bytes 196616 | tf_op jit(solution)/shard_map/ppermute | solution.py:184
  26.2 5.2 %copy-start.7 = (bf16[64,512]{1,0:T(8,128)(2,1)}, bf16[64,512]{1,0:T(8,128)(2,1)S(1)}, u32[]{:S(2)}) copy-start(bf16[64,512]{1,0:T(8,128)(2,1)S(1)} %collective-permute-done.5.refs_11_) | copy-start | bytes 196612
  26.2 5.2 %copy-start.8 = (bf16[64,512]{1,0:T(8,128)(2,1)}, bf16[64,512]{1,0:T(8,128)(2,1)S(1)}, u32[]{:S(2)}) copy-start(bf16[64,512]{1,0:T(8,128)(2,1)S(1)} %collective-permute-done.6.refs_12_) | copy-start | bytes 196612
  30.0 1.4 %copy-start.9 = (bf16[64,512]{1,0:T(8,128)(2,1)}, bf16[64,512]{1,0:T(8,128)(2,1)S(1)}, u32[]{:S(2)}) copy-start(bf16[64,512]{1,0:T(8,128)(2,1)S(1)} %collective-permute-done.3.refs_9_) | copy-start | bytes 196612
  31.4 0.6 %copy-start.10 = (bf16[64,512]{1,0:T(8,128)(2,1)}, bf16[64,512]{1,0:T(8,128)(2,1)S(1)}, u32[]{:S(2)}) copy-start(bf16[64,512]{1,0:T(8,128)(2,1)S(1)} %collective-permute-done.4.refs_10_) | copy-start | bytes 196612

commit v13 on v12

--- a/solution.py
+++ b/solution.py
@@ -33,9 +33,9 @@
 
 def attend_kernel(meta, *refs):
     devices, block_rows, rows, tails, prefix_len, repeat, scale = meta
-    me_ref, lens_ref, rg_ref, bg_ref, q_ref, own_k_ref, own_v_ref = refs[:7]
-    data = refs[7 : 7 + devices]
-    out_ref, kscr, vscr = refs[7 + devices :]
+    me_ref, lens_ref, rg_ref, bg_ref, freq_ref, q_ref, own_k_ref, own_v_ref = refs[:8]
+    data = refs[8 : 8 + devices]
+    out_ref, kscr, vscr = refs[8 + devices :]
     kv_cols = kscr.shape[1]
     count = kscr.shape[0]
     base = devices * block_rows
@@ -71,8 +71,7 @@
         return jnp.sum(after.astype(jnp.float32), axis=0, keepdims=True).astype(jnp.int32) - 1
 
     head_lane = lax.broadcasted_iota(jnp.int32, (1, HD), 1)
-    pair = jnp.where(head_lane < HD // 2, head_lane, head_lane - HD // 2)
-    freq = jnp.exp(pair.astype(jnp.float32) * (-2.0 * math.log(500000.0) / HD))
+    freq = freq_ref[...]
     sign = jnp.where(head_lane < HD // 2, -1.0, 1.0).astype(jnp.float32)
 
     def tables(offset):
@@ -142,7 +141,7 @@
             )
 
 
-def attend(meta, scalars, queries, own_k, own_v, data):
+def attend(meta, scalars, freq, queries, own_k, own_v, data):
     devices, block_rows, rows, tails = meta[:4]
     kv_cols = own_k.shape[1]
     q_heads = queries.shape[1] // HD
@@ -155,7 +154,7 @@
     return pl.pallas_call(
         functools.partial(attend_kernel, meta),
         out_shape=jax.ShapeDtypeStruct(queries.shape, jnp.bfloat16),
-        in_specs=[smem] * len(scalars) + [vmem] * len(arrays),
+        in_specs=[smem] * len(scalars) + [vmem] * (1 + len(arrays)),
         out_specs=vmem,
         scratch_shapes=[
             pltpu.VMEM((count, kv_cols), jnp.bfloat16),
@@ -166,7 +165,7 @@
             transcendentals=rows * count * q_heads,
             bytes_accessed=nbytes + queries.size * 2,
         ),
-    )(*scalars, *arrays)
+    )(*scalars, freq, *arrays)
 
 
 def token_info(index, suffix_lengths, request_group):
@@ -225,19 +224,16 @@
                 received[by] = shifted(jnp.concatenate([prefix_kv, suffix_kv], axis=0), "seq", by, True)
             elif by not in late:
                 received[by] = shifted(prefix_kv, "seq", by, True)
-        cache_keys_in, cache_values_in = suffix_keys, suffix_values
-        if late:
-            first_gate, cache_keys_in, cache_values_in = lax.optimization_barrier(
-                (received[devices - 1], suffix_keys, suffix_values)
-            )
-            received[devices - 1] = first_gate
-            gates = (received[1],) + tuple(received[devices - 1 - i] for i in range(len(late)))
-            gates, payload = lax.optimization_barrier((gates, prefix_kv))
-            received[1] = gates[0]
-            for i, by in enumerate(late):
-                received[devices - 1 - i] = gates[i + 1]
-                received[by] = shifted(payload, "seq", by, True)
+        gates = tuple(received[devices - 1 - i] for i in range(len(late)))
+        gates, payload, cache_keys_in, cache_values_in = lax.optimization_barrier(
+            (gates, prefix_kv, suffix_keys, suffix_values)
+        )
+        for i, by in enumerate(late):
+            received[devices - 1 - i] = gates[i]
+            received[by] = shifted(payload, "seq", by, True)
         data = [prefix_kv] + [received[by] for by in range(1, devices)]
+        if not late:
+            cache_keys_in, cache_values_in = suffix_keys, suffix_values
         _, own_offset, _ = token_info(index, suffix_lengths, request_group)
         own_k_rot = rotate(cache_keys_in.reshape(rows, kv_heads, HD), own_offset + prefix_len).reshape(
             rows, kv_cols
@@ -245,9 +241,12 @@
         cache = lax.all_to_all(
             jnp.stack([own_k_rot, cache_values_in], axis=0), "tp", split_axis=1, concat_axis=2, tiled=True
         )
+        half = HD // 2
+        freq = jnp.exp(jnp.arange(half, dtype=jnp.float32) * (-2.0 * math.log(500000.0) / HD))
+        freq = jnp.concatenate([freq, freq])[None, :]
         scalars = [me.astype(jnp.int32).reshape(1), suffix_lengths, request_group, block_group]
         meta = (devices, block_rows, rows, min(span, devices - 1), prefix_len, repeat, scale)
-        attended = attend(meta, scalars, queries, own_k_rot, suffix_values, data)
+        attended = attend(meta, scalars, freq, queries, own_k_rot, suffix_values, data)
         return (attended, cache[0], cache[1])
 
     prefix_parts = []

time: 36.7 us -> 34.9 us (0.951)
  starting transfers between devices: 18.1 us -> 15.8 us
  other arithmetic: 0.63 us -> 1.28 us
    ppermute x7, waiting for transfers between devices: 5.71 us -> 2.93 us  [shifted(): return lax.ppermute(array, axis, pairs)]
    all_to_all x1, waiting for transfers between devices: 0.01 us -> 2.64 us  [body(): lax.all_to_all(jnp.stack([own_k_rot, cache_values_in], axis=0), 'tp', spl...]
    ppermute x7, starting transfers between devices: 14.7 us -> 12.5 us  [shifted(): return lax.ppermute(array, axis, pairs)]
    broadcast_in_dim x0 -> x1, other arithmetic: none -> 0.65 us  [body(): freq = jnp.concatenate([freq, freq])[None, :]]
  transfers between devices with their start and end apart: 8 -> 8, of which waited for: 3 -> 3; matrix products, arithmetic and copies ran while one was open for 11% -> 14% of each run, Pallas kernels for 0% -> 0%
where the time goes in v13:
time: 34.9 us; the launch traced here: 34.6 us
  starting transfers between devices  15.8 us (45%)
  local copies, waits for them, and re-layouts  6.87 us (20%)
  waiting for transfers between devices  5.57 us (16%)
  Pallas kernels  4.28 us (12%)
  other arithmetic  1.28 us (4%)
  between operations  0.81 us (2%)
    ppermute x7, starting transfers between devices, shifted(): return lax.ppermute(array, axis, pairs)  12.5 us
    pallas_call x1, Pallas kernels, attend(): pl.pallas_call(functools.partial(attend_kernel, meta), out_shape=jax.Shap...  4.28 us
    unnamed x25, local copies, waits for them, and re-layouts  3.94 us
    all_to_all x1, starting transfers between devices, body(): lax.all_to_all(jnp.stack([own_k_rot, cache_values_in], axis=0), 'tp', spl...  3.33 us
    ppermute x7, waiting for transfers between devices, shifted(): return lax.ppermute(array, axis, pairs)  2.93 us
    all_to_all x1, waiting for transfers between devices, body(): lax.all_to_all(jnp.stack([own_k_rot, cache_values_in], axis=0), 'tp', spl...  2.64 us
    another operation x2, local copies, waits for them, and re-layouts, body(): jnp.stack([own_k_rot, cache_values_in], axis=0)  0.9 us
    concatenate x1, local copies, waits for them, and re-layouts, body(): prefix_kv = jnp.concatenate([prefix_keys, prefix_values], axis=1)  0.76 us
  transfers between devices with their start and end apart: 8, of which 3 were waited for; matrix products, arithmetic and copies ran while one was open for 14% of the time, Pallas kernels for 0%

profile of v13, /device:TPU:0, one launch (start us, length us, event | category | flops | bytes accessed | tf_op | source)
XLA Modules:
  0.0 34.6 jit_solution(11866125716646720399)
XLA Ops:
  0.7 0.8 %constant_dynamic-update-slice_fusion.1 = bf16[64,512]{1,0:T(8,128)(2,1)S(1)} fusion(bf16[64,256]{1,0:T(8,128)(2,1)} %param.11), kind=kLoop, calls=%fused_computation.11 | loop fusion | bytes 65536
  1.4 0.8 %constant_dynamic-update-slice_fusion.refs_8_ = bf16[64,512]{1,0:T(8,128)(2,1)S(1)} fusion(bf16[64,512]{1,0:T(8,128)(2,1)S(1)} %constant_dynamic-update-slice_fusion.1, bf16[64,256]{1,0:T(8,128)(2,1)} %param.12), kind=kLoop, calls=%fused_computation.10 | loop fusion | bytes 65536 | tf_op jit(solution)/shard_map/concatenate | solution.py:210
  2.2 6.0 %collective-permute-start = (bf16[64,512]{1,0:T(8,128)(2,1)S(1)}, bf16[64,512]{1,0:T(8,128)(2,1)S(1)}, u32[]{:S(2)}, u32[]{:S(2)}) collective-permute-start(bf16[64,512]{1,0:T(8,128)(2,1)S(1)} %constant_dynamic-update-slice_fusion.refs_8_), channel_id=1, source_target_pairs={{0,28},{4,0},{8,4},{12,8},{16,12},{20,16},{24,20},{28,24},{1,29},{... | collective-permute-start | bytes 196616 | tf_op jit(solution)/shard_map/ppermute | solution.py:183
  8.2 0.4 %collective-permute-start.1 = (bf16[64,512]{1,0:T(8,128)(2,1)S(1)}, bf16[64,512]{1,0:T(8,128)(2,1)S(1)}, u32[]{:S(2)}, u32[]{:S(2)}) collective-permute-start(bf16[64,512]{1,0:T(8,128)(2,1)S(1)} %constant_dynamic-update-slice_fusion.refs_8_), channel_id=1, source_target_pairs={{0,24},{4,28},{8,0},{12,4},{16,8},{20,12},{24,16},{28,20},{1,25},{... | collective-permute-start | bytes 196616 | tf_op jit(solution)/shard_map/ppermute | solution.py:183
  8.6 3.0 %collective-permute-start.6 = (bf16[64,512]{1,0:T(8,128)(2,1)S(1)}, bf16[64,512]{1,0:T(8,128)(2,1)S(1)}, u32[]{:S(2)}, u32[]{:S(2)}) collective-permute-start(bf16[64,512]{1,0:T(8,128)(2,1)S(1)} %constant_dynamic-update-slice_fusion.refs_8_), channel_id=1, source_target_pairs={{0,20},{4,24},{8,28},{12,0},{16,4},{20,8},{24,12},{28,16},{1,21},{... | collective-permute-start | bytes 196616 | tf_op jit(solution)/shard_map/ppermute | solution.py:183
  11.7 2.4 %collective-permute-start.2 = (bf16[192,512]{1,0:T(8,128)(2,1)S(1)}, bf16[192,512]{1,0:T(8,128)(2,1)S(1)}, u32[]{:S(2)}, u32[]{:S(2)}) collective-permute-start(bf16[192,512]{1,0:T(8,128)(2,1)S(1)} %maximum_maximum_fusion), channel_id=1, source_target_pairs={{0,4},{4,8},{8,12},{12,16},{16,20},{20,24},{24,28},{28,0},{1,5},{5... | collective-permute-start | bytes 589832 | tf_op jit(solution)/shard_map/ppermute | solution.py:183
  14.1 0.6 %copy-done.3 = s32[24]{0:T(128)S(1)} copy-done((s32[24]{0:T(128)S(1)}, s32[24]{0:T(128)}, u32[]{:S(2)}) %copy-start.3) | copy-done | bytes 120
  14.9 0.1 reduce
  15.2 0.2 multiply_cosine_fusion
  15.6 0.5 %copy-done.5 = bf16[64,512]{1,0:T(8,128)(2,1)} copy-done((bf16[64,512]{1,0:T(8,128)(2,1)}, bf16[64,512]{1,0:T(8,128)(2,1)S(1)}, u32[]{:S(2)}) %copy-start.5) | copy-done | bytes 65560
  16.1 0.1 copy.28
  16.3 0.8 %copy.29 = bf16[2,128,256]{2,0,1:T(2,128)(2,1)} copy(bf16[2,128,256]{1,2,0:T(8,128)(2,1)S(1)} %pad_maximum_fusion) | data formatting | bytes 262144 | tf_op jit(solution)/shard_map/stack | solution.py:242
  17.1 3.3 %all-to-all-start = ((bf16[2,128,256]{2,0,1:T(2,128)(2,1)}), bf16[2,128,256]{2,0,1:T(2,128)(2,1)S(1)}, u32[]{:S(2)}, u32[]{:S(2)}) async-start(bf16[2,128,256]{2,0,1:T(2,128)(2,1)} %copy.29), calls=%async_computation | async-start | bytes 262144 | tf_op jit(solution)/shard_map/all_to_all | solution.py:241
  20.4 0.6 %maximum_bitcast_fusion.refs_4_ = f32[1,128]{1,0:T(1,128)} fusion(f32[64]{0:T(128)S(1)} %multiply_exponential_fusion), kind=kLoop, calls=%fused_computation.12 | loop fusion | flops 128 | bytes 768 | tf_op jit(solution)/shard_map/broadcast_in_dim | solution.py:246
  21.1 0.6 %collective-permute-start.4 = (bf16[64,512]{1,0:T(8,128)(2,1)S(1)}, bf16[64,512]{1,0:T(8,128)(2,1)S(1)}, u32[]{:S(2)}, u32[]{:S(2)}) collective-permute-start(bf16[64,512]{1,0:T(8,128)(2,1)S(1)} %constant_dynamic-update-slice_fusion.refs_8_), channel_id=1, source_target_pairs={{0,12},{4,16},{8,20},{12,24},{16,28},{20,0},{24,4},{28,8},{1,13},{... | collective-permute-start | bytes 196616 | tf_op jit(solution)/shard_map/ppermute | solution.py:183
  21.6 0.7 %copy.32.refs_6_ = bf16[128,256]{1,0:T(8,128)(2,1)} copy(bf16[128,256]{0,1:T(8,128)(2,1)S(1)} %bitcast.19) | data formatting | bytes 131072 | tf_op jit(solution)/shard_map/convert_element_type | solution.py:31
  22.4 2.6 %all-to-all-done = bf16[2,128,256]{2,0,1:T(2,128)(2,1)S(1)} async-done(((bf16[2,128,256]{2,0,1:T(2,128)(2,1)}), bf16[2,128,256]{2,0,1:T(2,128)(2,1)S(1)}, u32[]{:S(2)}, u32[]{:S(2)}) %all-to-all-start) | async-done | bytes 131104 | tf_op jit(solution)/shard_map/all_to_all | solution.py:241
  25.0 0.2 fusion
  25.3 0.6 %copy.33 = bf16[4,8,4,256]{3,1,2,0:T(8,128)(2,1)} copy(bf16[4,8,4,256]{3,2,1,0:T(4,128)(2,1)S(1)} %bitcast.21) | data formatting | bytes 131072
  26.0 0.6 %copy.34 = bf16[4,8,4,256]{3,1,2,0:T(8,128)(2,1)} copy(bf16[4,8,4,256]{3,2,1,0:T(4,128)(2,1)S(1)} %bitcast.22) | data formatting | bytes 131072
  26.7 1.1 %collective-permute-done.3.refs_10_ = bf16[64,512]{1,0:T(8,128)(2,1)S(1)} collective-permute-done((bf16[64,512]{1,0:T(8,128)(2,1)S(1)}, bf16[64,512]{1,0:T(8,128)(2,1)S(1)}, u32[]{:S(2)}, u32[]{:S(2)}) %collective-permute-start.3) | collective-permute-done | bytes 65568 | tf_op jit(solution)/shard_map/ppermute | solution.py:183
  27.8 1.8 %collective-permute-done.4.refs_11_ = bf16[64,512]{1,0:T(8,128)(2,1)S(1)} collective-permute-done((bf16[64,512]{1,0:T(8,128)(2,1)S(1)}, bf16[64,512]{1,0:T(8,128)(2,1)S(1)}, u32[]{:S(2)}, u32[]{:S(2)}) %collective-permute-start.4) | collective-permute-done | bytes 65568 | tf_op jit(solution)/shard_map/ppermute | solution.py:183
  29.6 0.6 %copy-done.10 = bf16[64,512]{1,0:T(8,128)(2,1)} copy-done((bf16[64,512]{1,0:T(8,128)(2,1)}, bf16[64,512]{1,0:T(8,128)(2,1)S(1)}, u32[]{:S(2)}) %copy-start.10) | copy-done | bytes 65560
  30.3 4.3 %shard_map.103 = bf16[128,1024]{1,0:T(8,128)(2,1)} custom-call(s32[1]{0:T(128)} %bitcast.refs_0_, s32[24]{0:T(128)} %refs_1_.1, s32[24]{0:T(128)} %refs_2_.1, s32[8]{0:T(128)} %refs_3_.1, f32[1,128]{1,0:T(1,128)} %maximum_bitcast_fusion.refs_4_, bf16[128,1024]{1,0:T(8,128)(2,1)} %refs_5_.1, bf16[128,256]{1,0:T(8,128)(2,1)} %copy.32.refs_6_, ...), custom_call_target="tpu_custom_call" | custom-call | flops 402653184 | bytes 1310720 | tf_op jit(solution)/shard_map/pallas_call | solution.py:154
  (41 shorter events, 0.8 us)
Async XLA Ops:
  0.6 11.0 %copy-start.1 = (bf16[128,256]{1,0:T(8,128)(2,1)S(1)}, bf16[128,256]{1,0:T(8,128)(2,1)}, u32[]{:S(2)}) copy-start(bf16[128,256]{1,0:T(8,128)(2,1)} %refs_7_.1) | copy-start | bytes 196612
  0.6 11.0 %copy-start = (bf16[128,256]{1,0:T(8,128)(2,1)S(1)}, bf16[128,256]{1,0:T(8,128)(2,1)}, u32[]{:S(2)}) copy-start(bf16[128,256]{1,0:T(8,128)(2,1)} %param.9) | copy-start | bytes 196612
  2.2 18.9 %copy-start.2 = (bf16[64,512]{1,0:T(8,128)(2,1)}, bf16[64,512]{1,0:T(8,128)(2,1)S(1)}, u32[]{:S(2)}) copy-start(bf16[64,512]{1,0:T(8,128)(2,1)S(1)} %constant_dynamic-update-slice_fusion.refs_8_) | copy-start | bytes 196612
  2.2 13.2 %collective-permute-start = (bf16[64,512]{1,0:T(8,128)(2,1)S(1)}, bf16[64,512]{1,0:T(8,128)(2,1)S(1)}, u32[]{:S(2)}, u32[]{:S(2)}) collective-permute-start(bf16[64,512]{1,0:T(8,128)(2,1)S(1)} %constant_dynamic-update-slice_fusion.refs_8_), channel_id=1, source_target_pairs={{0,28},{4,0},{8,4},{12,8},{16,12},{20,16},{24,20},{28,24},{1,29},{... | collective-permute-start | bytes 196616 | tf_op jit(solution)/shard_map/ppermute | solution.py:183
  8.2 7.3 %collective-permute-start.1 = (bf16[64,512]{1,0:T(8,128)(2,1)S(1)}, bf16[64,512]{1,0:T(8,128)(2,1)S(1)}, u32[]{:S(2)}, u32[]{:S(2)}) collective-permute-start(bf16[64,512]{1,0:T(8,128)(2,1)S(1)} %constant_dynamic-update-slice_fusion.refs_8_), channel_id=1, source_target_pairs={{0,24},{4,28},{8,0},{12,4},{16,8},{20,12},{24,16},{28,20},{1,25},{... | collective-permute-start | bytes 196616 | tf_op jit(solution)/shard_map/ppermute | solution.py:183
  8.6 18.0 %collective-permute-start.5 = (bf16[64,512]{1,0:T(8,128)(2,1)S(1)}, bf16[64,512]{1,0:T(8,128)(2,1)S(1)}, u32[]{:S(2)}, u32[]{:S(2)}) collective-permute-start(bf16[64,512]{1,0:T(8,128)(2,1)S(1)} %constant_dynamic-update-slice_fusion.refs_8_), channel_id=1, source_target_pairs={{0,16},{4,20},{8,24},{12,28},{16,0},{20,4},{24,8},{28,12},{1,17},{... | collective-permute-start | bytes 196616 | tf_op jit(solution)/shard_map/ppermute | solution.py:183
  8.6 18.0 %collective-permute-start.6 = (bf16[64,512]{1,0:T(8,128)(2,1)S(1)}, bf16[64,512]{1,0:T(8,128)(2,1)S(1)}, u32[]{:S(2)}, u32[]{:S(2)}) collective-permute-start(bf16[64,512]{1,0:T(8,128)(2,1)S(1)} %constant_dynamic-update-slice_fusion.refs_8_), channel_id=1, source_target_pairs={{0,20},{4,24},{8,28},{12,0},{16,4},{20,8},{24,12},{28,16},{1,21},{... | collective-permute-start | bytes 196616 | tf_op jit(solution)/shard_map/ppermute | solution.py:183
  11.7 17.9 %collective-permute-start.2 = (bf16[192,512]{1,0:T(8,128)(2,1)S(1)}, bf16[192,512]{1,0:T(8,128)(2,1)S(1)}, u32[]{:S(2)}, u32[]{:S(2)}) collective-permute-start(bf16[192,512]{1,0:T(8,128)(2,1)S(1)} %maximum_maximum_fusion), channel_id=1, source_target_pairs={{0,4},{4,8},{8,12},{12,16},{16,20},{20,24},{24,28},{28,0},{1,5},{5... | collective-permute-start | bytes 589832 | tf_op jit(solution)/shard_map/ppermute | solution.py:183
  14.1 0.7 %copy-start.3 = (s32[24]{0:T(128)S(1)}, s32[24]{0:T(128)}, u32[]{:S(2)}) copy-start(s32[24]{0:T(128)} %refs_1_.1) | copy-start | bytes 292
  15.4 0.6 %copy-start.5 = (bf16[64,512]{1,0:T(8,128)(2,1)}, bf16[64,512]{1,0:T(8,128)(2,1)S(1)}, u32[]{:S(2)}) copy-start(bf16[64,512]{1,0:T(8,128)(2,1)S(1)} %collective-permute-done.refs_15_) | copy-start | bytes 196612
  15.5 0.6 %copy-start.6 = (bf16[64,512]{1,0:T(8,128)(2,1)}, bf16[64,512]{1,0:T(8,128)(2,1)S(1)}, u32[]{:S(2)}) copy-start(bf16[64,512]{1,0:T(8,128)(2,1)S(1)} %collective-permute-done.1.refs_14_) | copy-start | bytes 196612
  17.1 7.9 %all-to-all-start = ((bf16[2,128,256]{2,0,1:T(2,128)(2,1)}), bf16[2,128,256]{2,0,1:T(2,128)(2,1)S(1)}, u32[]{:S(2)}, u32[]{:S(2)}) async-start(bf16[2,128,256]{2,0,1:T(2,128)(2,1)} %copy.29), calls=%async_computation | async-start | bytes 262144 | tf_op jit(solution)/shard_map/all_to_all | solution.py:241
  21.1 6.7 %collective-permute-start.3 = (bf16[64,512]{1,0:T(8,128)(2,1)S(1)}, bf16[64,512]{1,0:T(8,128)(2,1)S(1)}, u32[]{:S(2)}, u32[]{:S(2)}) collective-permute-start(bf16[64,512]{1,0:T(8,128)(2,1)S(1)} %constant_dynamic-update-slice_fusion.refs_8_), channel_id=1, source_target_pairs={{0,8},{4,12},{8,16},{12,20},{16,24},{20,28},{24,0},{28,4},{1,9},{5... | collective-permute-start | bytes 196616 | tf_op jit(solution)/shard_map/ppermute | solution.py:183
  21.1 8.5 %collective-permute-start.4 = (bf16[64,512]{1,0:T(8,128)(2,1)S(1)}, bf16[64,512]{1,0:T(8,128)(2,1)S(1)}, u32[]{:S(2)}, u32[]{:S(2)}) collective-permute-start(bf16[64,512]{1,0:T(8,128)(2,1)S(1)} %constant_dynamic-update-slice_fusion.refs_8_), channel_id=1, source_target_pairs={{0,12},{4,16},{8,20},{12,24},{16,28},{20,0},{24,4},{28,8},{1,13},{... | collective-permute-start | bytes 196616 | tf_op jit(solution)/shard_map/ppermute | solution.py:183
  26.7 2.9 %copy-start.7 = (bf16[64,512]{1,0:T(8,128)(2,1)}, bf16[64,512]{1,0:T(8,128)(2,1)S(1)}, u32[]{:S(2)}) copy-start(bf16[64,512]{1,0:T(8,128)(2,1)S(1)} %collective-permute-done.5.refs_12_) | copy-start | bytes 196612
  26.7 2.9 %copy-start.8 = (bf16[64,512]{1,0:T(8,128)(2,1)}, bf16[64,512]{1,0:T(8,128)(2,1)S(1)}, u32[]{:S(2)}) copy-start(bf16[64,512]{1,0:T(8,128)(2,1)S(1)} %collective-permute-done.6.refs_13_) | copy-start | bytes 196612
  27.7 1.9 %copy-start.9 = (bf16[64,512]{1,0:T(8,128)(2,1)}, bf16[64,512]{1,0:T(8,128)(2,1)S(1)}, u32[]{:S(2)}) copy-start(bf16[64,512]{1,0:T(8,128)(2,1)S(1)} %collective-permute-done.3.refs_10_) | copy-start | bytes 196612
  29.6 0.6 %copy-start.10 = (bf16[64,512]{1,0:T(8,128)(2,1)}, bf16[64,512]{1,0:T(8,128)(2,1)S(1)}, u32[]{:S(2)}) copy-start(bf16[64,512]{1,0:T(8,128)(2,1)S(1)} %collective-permute-done.4.refs_11_) | copy-start | bytes 196612
  29.6 0.7 %copy-start.4 = (bf16[192,512]{1,0:T(8,128)(2,1)}, bf16[192,512]{1,0:T(8,128)(2,1)S(1)}, u32[]{:S(2)}) copy-start(bf16[192,512]{1,0:T(8,128)(2,1)S(1)} %collective-permute-done.2.refs_9_) | copy-start | bytes 589828

commit v14 on v13

--- a/solution.py
+++ b/solution.py
@@ -35,7 +35,7 @@
     devices, block_rows, rows, tails, prefix_len, repeat, scale = meta
     me_ref, lens_ref, rg_ref, bg_ref, freq_ref, q_ref, own_k_ref, own_v_ref = refs[:8]
     data = refs[8 : 8 + devices]
-    out_ref, kscr, vscr = refs[8 + devices :]
+    out_ref, kscr, vscr, raw, sems = refs[8 + devices :]
     kv_cols = kscr.shape[1]
     count = kscr.shape[0]
     base = devices * block_rows
@@ -81,9 +81,28 @@
     def rotated(x, cosine, sine):
         return (x * cosine + pltpu.roll(x, HD // 2, 1) * sine).astype(jnp.bfloat16)
 
+    copies = []
     for c in range(devices):
-        kscr[c * block_rows : (c + 1) * block_rows, :] = data[c][0:block_rows, 0:kv_cols]
-        vscr[c * block_rows : (c + 1) * block_rows, :] = data[c][0:block_rows, kv_cols : 2 * kv_cols]
+        rows_c = pl.ds(c * block_rows, block_rows)
+        copies.append(pltpu.make_async_copy(
+            data[c].at[pl.ds(0, block_rows), pl.ds(0, kv_cols)], kscr.at[rows_c, :], sems.at[len(copies)]
+        ))
+        copies.append(pltpu.make_async_copy(
+            data[c].at[pl.ds(0, block_rows), pl.ds(kv_cols, kv_cols)], vscr.at[rows_c, :], sems.at[len(copies)]
+        ))
+    for b in range(1, tails + 1):
+        low = base + b * rows
+        copies.append(pltpu.make_async_copy(
+            data[b].at[pl.ds(block_rows, rows), pl.ds(0, kv_cols)], raw.at[b - 1], sems.at[len(copies)]
+        ))
+        copies.append(pltpu.make_async_copy(
+            data[b].at[pl.ds(block_rows, rows), pl.ds(kv_cols, kv_cols)], vscr.at[pl.ds(low, rows), :],
+            sems.at[len(copies)],
+        ))
+    for copy in copies:
+        copy.start()
+    for copy in copies:
+        copy.wait()
     for b in range(0, tails + 1):
         low = base + b * rows
         index = (me - b) * rows + lax.broadcasted_iota(jnp.int32, (rows, 1), 0)
@@ -93,12 +112,10 @@
             if b == 0:
                 kscr[low : low + rows, g * HD : (g + 1) * HD] = own_k_ref[:, g * HD : (g + 1) * HD]
             else:
-                x = data[b][block_rows : block_rows + rows, g * HD : (g + 1) * HD]
+                x = raw[b - 1, :, g * HD : (g + 1) * HD]
                 kscr[low : low + rows, g * HD : (g + 1) * HD] = rotated(x.astype(jnp.float32), cosine, sine)
         if b == 0:
             vscr[low : low + rows, :] = own_v_ref[...]
-        else:
-            vscr[low : low + rows, :] = data[b][block_rows : block_rows + rows, kv_cols : 2 * kv_cols]
 
     token = me * rows + lax.broadcasted_iota(jnp.int32, (rows, 1), 0)
     request, offset, group = info(token)
@@ -154,11 +171,13 @@
     return pl.pallas_call(
         functools.partial(attend_kernel, meta),
         out_shape=jax.ShapeDtypeStruct(queries.shape, jnp.bfloat16),
-        in_specs=[smem] * len(scalars) + [vmem] * (1 + len(arrays)),
+        in_specs=[smem] * len(scalars) + [vmem] * 4 + [pl.BlockSpec(memory_space=pl.ANY)] * len(data),
         out_specs=vmem,
         scratch_shapes=[
             pltpu.VMEM((count, kv_cols), jnp.bfloat16),
             pltpu.VMEM((count, kv_cols), jnp.bfloat16),
+            pltpu.VMEM((max(tails, 1), rows, kv_cols), jnp.bfloat16),
+            pltpu.SemaphoreType.DMA((2 * devices + 2 * tails,)),
         ],
         cost_estimate=pl.CostEstimate(
             flops=flops,

time: 34.9 us -> 36 us (1.032)
  Pallas kernels: 4.28 us -> 5.26 us
    pallas_call x1, Pallas kernels: 4.28 us -> 5.26 us  [attend(): pl.pallas_call(functools.partial(attend_kernel, meta), out_shape=jax.Shap...]
  transfers between devices with their start and end apart: 8 -> 8, of which waited for: 3 -> 3; matrix products, arithmetic and copies ran while one was open for 14% -> 13% of each run, Pallas kernels for 0% -> 0%
where the time goes in v14:
time: 36 us; the launch traced here: 35.6 us
  starting transfers between devices  15.8 us (44%)
  local copies, waits for them, and re-layouts  6.87 us (19%)
  waiting for transfers between devices  5.57 us (15%)
  Pallas kernels  5.26 us (15%)
  other arithmetic  1.28 us (4%)
  between operations  0.81 us (2%)
    ppermute x7, starting transfers between devices, shifted(): return lax.ppermute(array, axis, pairs)  12.5 us
    pallas_call x1, Pallas kernels, attend(): pl.pallas_call(functools.partial(attend_kernel, meta), out_shape=jax.Shap...  5.26 us
    unnamed x25, local copies, waits for them, and re-layouts  3.94 us
    all_to_all x1, starting transfers between devices, body(): lax.all_to_all(jnp.stack([own_k_rot, cache_values_in], axis=0), 'tp', spl...  3.33 us
    ppermute x7, waiting for transfers between devices, shifted(): return lax.ppermute(array, axis, pairs)  2.93 us
    all_to_all x1, waiting for transfers between devices, body(): lax.all_to_all(jnp.stack([own_k_rot, cache_values_in], axis=0), 'tp', spl...  2.64 us
    another operation x2, local copies, waits for them, and re-layouts, body(): jnp.stack([own_k_rot, cache_values_in], axis=0)  0.9 us
    concatenate x1, local copies, waits for them, and re-layouts, body(): prefix_kv = jnp.concatenate([prefix_keys, prefix_values], axis=1)  0.76 us
  transfers between devices with their start and end apart: 8, of which 3 were waited for; matrix products, arithmetic and copies ran while one was open for 13% of the time, Pallas kernels for 0%

profile of v14, /device:TPU:0, one launch (start us, length us, event | category | flops | bytes accessed | tf_op | source)
XLA Modules:
  0.0 35.6 jit_solution(1384210630132754756)
XLA Ops:
  0.7 0.8 %constant_dynamic-update-slice_fusion.1 = bf16[64,512]{1,0:T(8,128)(2,1)S(1)} fusion(bf16[64,256]{1,0:T(8,128)(2,1)} %param.11), kind=kLoop, calls=%fused_computation.11 | loop fusion | bytes 65536
  1.4 0.8 %constant_dynamic-update-slice_fusion.refs_8_ = bf16[64,512]{1,0:T(8,128)(2,1)S(1)} fusion(bf16[64,512]{1,0:T(8,128)(2,1)S(1)} %constant_dynamic-update-slice_fusion.1, bf16[64,256]{1,0:T(8,128)(2,1)} %param.12), kind=kLoop, calls=%fused_computation.10 | loop fusion | bytes 65536 | tf_op jit(solution)/shard_map/concatenate | solution.py:229
  2.2 6.0 %collective-permute-start = (bf16[64,512]{1,0:T(8,128)(2,1)S(1)}, bf16[64,512]{1,0:T(8,128)(2,1)S(1)}, u32[]{:S(2)}, u32[]{:S(2)}) collective-permute-start(bf16[64,512]{1,0:T(8,128)(2,1)S(1)} %constant_dynamic-update-slice_fusion.refs_8_), channel_id=1, source_target_pairs={{0,28},{4,0},{8,4},{12,8},{16,12},{20,16},{24,20},{28,24},{1,29},{... | collective-permute-start | bytes 196616 | tf_op jit(solution)/shard_map/ppermute | solution.py:202
  8.2 0.4 %collective-permute-start.1 = (bf16[64,512]{1,0:T(8,128)(2,1)S(1)}, bf16[64,512]{1,0:T(8,128)(2,1)S(1)}, u32[]{:S(2)}, u32[]{:S(2)}) collective-permute-start(bf16[64,512]{1,0:T(8,128)(2,1)S(1)} %constant_dynamic-update-slice_fusion.refs_8_), channel_id=1, source_target_pairs={{0,24},{4,28},{8,0},{12,4},{16,8},{20,12},{24,16},{28,20},{1,25},{... | collective-permute-start | bytes 196616 | tf_op jit(solution)/shard_map/ppermute | solution.py:202
  8.6 3.0 %collective-permute-start.6 = (bf16[64,512]{1,0:T(8,128)(2,1)S(1)}, bf16[64,512]{1,0:T(8,128)(2,1)S(1)}, u32[]{:S(2)}, u32[]{:S(2)}) collective-permute-start(bf16[64,512]{1,0:T(8,128)(2,1)S(1)} %constant_dynamic-update-slice_fusion.refs_8_), channel_id=1, source_target_pairs={{0,20},{4,24},{8,28},{12,0},{16,4},{20,8},{24,12},{28,16},{1,21},{... | collective-permute-start | bytes 196616 | tf_op jit(solution)/shard_map/ppermute | solution.py:202
  11.7 2.4 %collective-permute-start.2 = (bf16[192,512]{1,0:T(8,128)(2,1)S(1)}, bf16[192,512]{1,0:T(8,128)(2,1)S(1)}, u32[]{:S(2)}, u32[]{:S(2)}) collective-permute-start(bf16[192,512]{1,0:T(8,128)(2,1)S(1)} %maximum_maximum_fusion), channel_id=1, source_target_pairs={{0,4},{4,8},{8,12},{12,16},{16,20},{20,24},{24,28},{28,0},{1,5},{5... | collective-permute-start | bytes 589832 | tf_op jit(solution)/shard_map/ppermute | solution.py:202
  14.1 0.6 %copy-done.3 = s32[24]{0:T(128)S(1)} copy-done((s32[24]{0:T(128)S(1)}, s32[24]{0:T(128)}, u32[]{:S(2)}) %copy-start.3) | copy-done | bytes 120
  14.9 0.1 reduce
  15.2 0.2 multiply_cosine_fusion
  15.6 0.5 %copy-done.5 = bf16[64,512]{1,0:T(8,128)(2,1)} copy-done((bf16[64,512]{1,0:T(8,128)(2,1)}, bf16[64,512]{1,0:T(8,128)(2,1)S(1)}, u32[]{:S(2)}) %copy-start.5) | copy-done | bytes 65560
  16.1 0.1 copy.28
  16.3 0.8 %copy.29 = bf16[2,128,256]{2,0,1:T(2,128)(2,1)} copy(bf16[2,128,256]{1,2,0:T(8,128)(2,1)S(1)} %pad_maximum_fusion) | data formatting | bytes 262144 | tf_op jit(solution)/shard_map/stack | solution.py:261
  17.1 3.3 %all-to-all-start = ((bf16[2,128,256]{2,0,1:T(2,128)(2,1)}), bf16[2,128,256]{2,0,1:T(2,128)(2,1)S(1)}, u32[]{:S(2)}, u32[]{:S(2)}) async-start(bf16[2,128,256]{2,0,1:T(2,128)(2,1)} %copy.29), calls=%async_computation | async-start | bytes 262144 | tf_op jit(solution)/shard_map/all_to_all | solution.py:260
  20.4 0.6 %maximum_bitcast_fusion.refs_4_ = f32[1,128]{1,0:T(1,128)} fusion(f32[64]{0:T(128)S(1)} %multiply_exponential_fusion), kind=kLoop, calls=%fused_computation.12 | loop fusion | flops 128 | bytes 768 | tf_op jit(solution)/shard_map/broadcast_in_dim | solution.py:265
  21.1 0.6 %collective-permute-start.4 = (bf16[64,512]{1,0:T(8,128)(2,1)S(1)}, bf16[64,512]{1,0:T(8,128)(2,1)S(1)}, u32[]{:S(2)}, u32[]{:S(2)}) collective-permute-start(bf16[64,512]{1,0:T(8,128)(2,1)S(1)} %constant_dynamic-update-slice_fusion.refs_8_), channel_id=1, source_target_pairs={{0,12},{4,16},{8,20},{12,24},{16,28},{20,0},{24,4},{28,8},{1,13},{... | collective-permute-start | bytes 196616 | tf_op jit(solution)/shard_map/ppermute | solution.py:202
  21.6 0.7 %copy.32.refs_6_ = bf16[128,256]{1,0:T(8,128)(2,1)} copy(bf16[128,256]{0,1:T(8,128)(2,1)S(1)} %bitcast.19) | data formatting | bytes 131072 | tf_op jit(solution)/shard_map/convert_element_type | solution.py:31
  22.4 2.6 %all-to-all-done = bf16[2,128,256]{2,0,1:T(2,128)(2,1)S(1)} async-done(((bf16[2,128,256]{2,0,1:T(2,128)(2,1)}), bf16[2,128,256]{2,0,1:T(2,128)(2,1)S(1)}, u32[]{:S(2)}, u32[]{:S(2)}) %all-to-all-start) | async-done | bytes 131104 | tf_op jit(solution)/shard_map/all_to_all | solution.py:260
  25.0 0.2 fusion
  25.3 0.6 %copy.33 = bf16[4,8,4,256]{3,1,2,0:T(8,128)(2,1)} copy(bf16[4,8,4,256]{3,2,1,0:T(4,128)(2,1)S(1)} %bitcast.21) | data formatting | bytes 131072
  26.0 0.6 %copy.34 = bf16[4,8,4,256]{3,1,2,0:T(8,128)(2,1)} copy(bf16[4,8,4,256]{3,2,1,0:T(4,128)(2,1)S(1)} %bitcast.22) | data formatting | bytes 131072
  26.7 1.1 %collective-permute-done.3.refs_10_ = bf16[64,512]{1,0:T(8,128)(2,1)S(1)} collective-permute-done((bf16[64,512]{1,0:T(8,128)(2,1)S(1)}, bf16[64,512]{1,0:T(8,128)(2,1)S(1)}, u32[]{:S(2)}, u32[]{:S(2)}) %collective-permute-start.3) | collective-permute-done | bytes 65568 | tf_op jit(solution)/shard_map/ppermute | solution.py:202
  27.8 1.8 %collective-permute-done.4.refs_11_ = bf16[64,512]{1,0:T(8,128)(2,1)S(1)} collective-permute-done((bf16[64,512]{1,0:T(8,128)(2,1)S(1)}, bf16[64,512]{1,0:T(8,128)(2,1)S(1)}, u32[]{:S(2)}, u32[]{:S(2)}) %collective-permute-start.4) | collective-permute-done | bytes 65568 | tf_op jit(solution)/shard_map/ppermute | solution.py:202
  29.6 0.6 %copy-done.10 = bf16[64,512]{1,0:T(8,128)(2,1)} copy-done((bf16[64,512]{1,0:T(8,128)(2,1)}, bf16[64,512]{1,0:T(8,128)(2,1)S(1)}, u32[]{:S(2)}) %copy-start.10) | copy-done | bytes 65560
  30.3 5.3 %shard_map.103 = bf16[128,1024]{1,0:T(8,128)(2,1)} custom-call(s32[1]{0:T(128)} %bitcast.refs_0_, s32[24]{0:T(128)} %refs_1_.1, s32[24]{0:T(128)} %refs_2_.1, s32[8]{0:T(128)} %refs_3_.1, f32[1,128]{1,0:T(1,128)} %maximum_bitcast_fusion.refs_4_, bf16[128,1024]{1,0:T(8,128)(2,1)} %refs_5_.1, bf16[128,256]{1,0:T(8,128)(2,1)} %copy.32.refs_6_, ...), custom_call_target="tpu_custom_call" | custom-call | flops 402653184 | bytes 1310720 | tf_op jit(solution)/shard_map/pallas_call | solution.py:171
  (41 shorter events, 0.8 us)
Async XLA Ops:
  0.6 11.0 %copy-start.1 = (bf16[128,256]{1,0:T(8,128)(2,1)S(1)}, bf16[128,256]{1,0:T(8,128)(2,1)}, u32[]{:S(2)}) copy-start(bf16[128,256]{1,0:T(8,128)(2,1)} %refs_7_.1) | copy-start | bytes 196612
  0.6 11.0 %copy-start = (bf16[128,256]{1,0:T(8,128)(2,1)S(1)}, bf16[128,256]{1,0:T(8,128)(2,1)}, u32[]{:S(2)}) copy-start(bf16[128,256]{1,0:T(8,128)(2,1)} %param.9) | copy-start | bytes 196612
  2.2 18.9 %copy-start.2 = (bf16[64,512]{1,0:T(8,128)(2,1)}, bf16[64,512]{1,0:T(8,128)(2,1)S(1)}, u32[]{:S(2)}) copy-start(bf16[64,512]{1,0:T(8,128)(2,1)S(1)} %constant_dynamic-update-slice_fusion.refs_8_) | copy-start | bytes 196612
  2.2 13.2 %collective-permute-start = (bf16[64,512]{1,0:T(8,128)(2,1)S(1)}, bf16[64,512]{1,0:T(8,128)(2,1)S(1)}, u32[]{:S(2)}, u32[]{:S(2)}) collective-permute-start(bf16[64,512]{1,0:T(8,128)(2,1)S(1)} %constant_dynamic-update-slice_fusion.refs_8_), channel_id=1, source_target_pairs={{0,28},{4,0},{8,4},{12,8},{16,12},{20,16},{24,20},{28,24},{1,29},{... | collective-permute-start | bytes 196616 | tf_op jit(solution)/shard_map/ppermute | solution.py:202
  8.2 7.3 %collective-permute-start.1 = (bf16[64,512]{1,0:T(8,128)(2,1)S(1)}, bf16[64,512]{1,0:T(8,128)(2,1)S(1)}, u32[]{:S(2)}, u32[]{:S(2)}) collective-permute-start(bf16[64,512]{1,0:T(8,128)(2,1)S(1)} %constant_dynamic-update-slice_fusion.refs_8_), channel_id=1, source_target_pairs={{0,24},{4,28},{8,0},{12,4},{16,8},{20,12},{24,16},{28,20},{1,25},{... | collective-permute-start | bytes 196616 | tf_op jit(solution)/shard_map/ppermute | solution.py:202
  8.6 18.0 %collective-permute-start.5 = (bf16[64,512]{1,0:T(8,128)(2,1)S(1)}, bf16[64,512]{1,0:T(8,128)(2,1)S(1)}, u32[]{:S(2)}, u32[]{:S(2)}) collective-permute-start(bf16[64,512]{1,0:T(8,128)(2,1)S(1)} %constant_dynamic-update-slice_fusion.refs_8_), channel_id=1, source_target_pairs={{0,16},{4,20},{8,24},{12,28},{16,0},{20,4},{24,8},{28,12},{1,17},{... | collective-permute-start | bytes 196616 | tf_op jit(solution)/shard_map/ppermute | solution.py:202
  8.6 18.0 %collective-permute-start.6 = (bf16[64,512]{1,0:T(8,128)(2,1)S(1)}, bf16[64,512]{1,0:T(8,128)(2,1)S(1)}, u32[]{:S(2)}, u32[]{:S(2)}) collective-permute-start(bf16[64,512]{1,0:T(8,128)(2,1)S(1)} %constant_dynamic-update-slice_fusion.refs_8_), channel_id=1, source_target_pairs={{0,20},{4,24},{8,28},{12,0},{16,4},{20,8},{24,12},{28,16},{1,21},{... | collective-permute-start | bytes 196616 | tf_op jit(solution)/shard_map/ppermute | solution.py:202
  11.7 17.9 %collective-permute-start.2 = (bf16[192,512]{1,0:T(8,128)(2,1)S(1)}, bf16[192,512]{1,0:T(8,128)(2,1)S(1)}, u32[]{:S(2)}, u32[]{:S(2)}) collective-permute-start(bf16[192,512]{1,0:T(8,128)(2,1)S(1)} %maximum_maximum_fusion), channel_id=1, source_target_pairs={{0,4},{4,8},{8,12},{12,16},{16,20},{20,24},{24,28},{28,0},{1,5},{5... | collective-permute-start | bytes 589832 | tf_op jit(solution)/shard_map/ppermute | solution.py:202
  14.1 0.7 %copy-start.3 = (s32[24]{0:T(128)S(1)}, s32[24]{0:T(128)}, u32[]{:S(2)}) copy-start(s32[24]{0:T(128)} %refs_1_.1) | copy-start | bytes 292
  15.4 0.6 %copy-start.5 = (bf16[64,512]{1,0:T(8,128)(2,1)}, bf16[64,512]{1,0:T(8,128)(2,1)S(1)}, u32[]{:S(2)}) copy-start(bf16[64,512]{1,0:T(8,128)(2,1)S(1)} %collective-permute-done.refs_15_) | copy-start | bytes 196612
  15.5 0.6 %copy-start.6 = (bf16[64,512]{1,0:T(8,128)(2,1)}, bf16[64,512]{1,0:T(8,128)(2,1)S(1)}, u32[]{:S(2)}) copy-start(bf16[64,512]{1,0:T(8,128)(2,1)S(1)} %collective-permute-done.1.refs_14_) | copy-start | bytes 196612
  17.1 7.9 %all-to-all-start = ((bf16[2,128,256]{2,0,1:T(2,128)(2,1)}), bf16[2,128,256]{2,0,1:T(2,128)(2,1)S(1)}, u32[]{:S(2)}, u32[]{:S(2)}) async-start(bf16[2,128,256]{2,0,1:T(2,128)(2,1)} %copy.29), calls=%async_computation | async-start | bytes 262144 | tf_op jit(solution)/shard_map/all_to_all | solution.py:260
  21.1 6.7 %collective-permute-start.3 = (bf16[64,512]{1,0:T(8,128)(2,1)S(1)}, bf16[64,512]{1,0:T(8,128)(2,1)S(1)}, u32[]{:S(2)}, u32[]{:S(2)}) collective-permute-start(bf16[64,512]{1,0:T(8,128)(2,1)S(1)} %constant_dynamic-update-slice_fusion.refs_8_), channel_id=1, source_target_pairs={{0,8},{4,12},{8,16},{12,20},{16,24},{20,28},{24,0},{28,4},{1,9},{5... | collective-permute-start | bytes 196616 | tf_op jit(solution)/shard_map/ppermute | solution.py:202
  21.1 8.5 %collective-permute-start.4 = (bf16[64,512]{1,0:T(8,128)(2,1)S(1)}, bf16[64,512]{1,0:T(8,128)(2,1)S(1)}, u32[]{:S(2)}, u32[]{:S(2)}) collective-permute-start(bf16[64,512]{1,0:T(8,128)(2,1)S(1)} %constant_dynamic-update-slice_fusion.refs_8_), channel_id=1, source_target_pairs={{0,12},{4,16},{8,20},{12,24},{16,28},{20,0},{24,4},{28,8},{1,13},{... | collective-permute-start | bytes 196616 | tf_op jit(solution)/shard_map/ppermute | solution.py:202
  26.7 2.9 %copy-start.7 = (bf16[64,512]{1,0:T(8,128)(2,1)}, bf16[64,512]{1,0:T(8,128)(2,1)S(1)}, u32[]{:S(2)}) copy-start(bf16[64,512]{1,0:T(8,128)(2,1)S(1)} %collective-permute-done.5.refs_12_) | copy-start | bytes 196612
  26.7 2.9 %copy-start.8 = (bf16[64,512]{1,0:T(8,128)(2,1)}, bf16[64,512]{1,0:T(8,128)(2,1)S(1)}, u32[]{:S(2)}) copy-start(bf16[64,512]{1,0:T(8,128)(2,1)S(1)} %collective-permute-done.6.refs_13_) | copy-start | bytes 196612
  27.7 1.9 %copy-start.9 = (bf16[64,512]{1,0:T(8,128)(2,1)}, bf16[64,512]{1,0:T(8,128)(2,1)S(1)}, u32[]{:S(2)}) copy-start(bf16[64,512]{1,0:T(8,128)(2,1)S(1)} %collective-permute-done.3.refs_10_) | copy-start | bytes 196612
  29.6 0.6 %copy-start.10 = (bf16[64,512]{1,0:T(8,128)(2,1)}, bf16[64,512]{1,0:T(8,128)(2,1)S(1)}, u32[]{:S(2)}) copy-start(bf16[64,512]{1,0:T(8,128)(2,1)S(1)} %collective-permute-done.4.refs_11_) | copy-start | bytes 196612
  29.6 0.7 %copy-start.4 = (bf16[192,512]{1,0:T(8,128)(2,1)}, bf16[192,512]{1,0:T(8,128)(2,1)S(1)}, u32[]{:S(2)}) copy-start(bf16[192,512]{1,0:T(8,128)(2,1)S(1)} %collective-permute-done.2.refs_9_) | copy-start | bytes 589828

commit v15 on v14

--- a/solution.py
+++ b/solution.py
@@ -101,7 +101,7 @@
         ))
     for copy in copies:
         copy.start()
-    for copy in copies:
+    for copy in copies[2 * devices :]:
         copy.wait()
     for b in range(0, tails + 1):
         low = base + b * rows
@@ -133,6 +133,8 @@
         (key_request == request) & (key_index <= token)
     )
     cosine, sine = tables(offset)
+    for copy in copies[: 2 * devices]:
+        copy.wait()
     for g in range(q_heads // repeat):
         heads = range(g * repeat, (g + 1) * repeat)
         q = jnp.concatenate(

time: 36 us -> 36.2 us (level)
  no operation moved by 1% of the time
where the time goes in v15:
time: 36.2 us; the launch traced here: 35.8 us
  starting transfers between devices  15.8 us (44%)
  local copies, waits for them, and re-layouts  6.87 us (19%)
  waiting for transfers between devices  5.57 us (15%)
  Pallas kernels  5.49 us (15%)
  other arithmetic  1.28 us (4%)
  between operations  0.81 us (2%)
    ppermute x7, starting transfers between devices, shifted(): return lax.ppermute(array, axis, pairs)  12.5 us
    pallas_call x1, Pallas kernels, attend(): pl.pallas_call(functools.partial(attend_kernel, meta), out_shape=jax.Shap...  5.49 us
    unnamed x25, local copies, waits for them, and re-layouts  3.94 us
    all_to_all x1, starting transfers between devices, body(): lax.all_to_all(jnp.stack([own_k_rot, cache_values_in], axis=0), 'tp', spl...  3.33 us
    ppermute x7, waiting for transfers between devices, shifted(): return lax.ppermute(array, axis, pairs)  2.93 us
    all_to_all x1, waiting for transfers between devices, body(): lax.all_to_all(jnp.stack([own_k_rot, cache_values_in], axis=0), 'tp', spl...  2.64 us
    another operation x2, local copies, waits for them, and re-layouts, body(): jnp.stack([own_k_rot, cache_values_in], axis=0)  0.9 us
    concatenate x1, local copies, waits for them, and re-layouts, body(): prefix_kv = jnp.concatenate([prefix_keys, prefix_values], axis=1)  0.76 us
  transfers between devices with their start and end apart: 8, of which 3 were waited for; matrix products, arithmetic and copies ran while one was open for 13% of the time, Pallas kernels for 0%

profile of v15, /device:TPU:0, one launch (start us, length us, event | category | flops | bytes accessed | tf_op | source)
XLA Modules:
  0.0 35.8 jit_solution(8869464009329523033)
XLA Ops:
  0.7 0.8 %constant_dynamic-update-slice_fusion.1 = bf16[64,512]{1,0:T(8,128)(2,1)S(1)} fusion(bf16[64,256]{1,0:T(8,128)(2,1)} %param.11), kind=kLoop, calls=%fused_computation.11 | loop fusion | bytes 65536
  1.4 0.8 %constant_dynamic-update-slice_fusion.refs_8_ = bf16[64,512]{1,0:T(8,128)(2,1)S(1)} fusion(bf16[64,512]{1,0:T(8,128)(2,1)S(1)} %constant_dynamic-update-slice_fusion.1, bf16[64,256]{1,0:T(8,128)(2,1)} %param.12), kind=kLoop, calls=%fused_computation.10 | loop fusion | bytes 65536 | tf_op jit(solution)/shard_map/concatenate | solution.py:231
  2.2 6.0 %collective-permute-start = (bf16[64,512]{1,0:T(8,128)(2,1)S(1)}, bf16[64,512]{1,0:T(8,128)(2,1)S(1)}, u32[]{:S(2)}, u32[]{:S(2)}) collective-permute-start(bf16[64,512]{1,0:T(8,128)(2,1)S(1)} %constant_dynamic-update-slice_fusion.refs_8_), channel_id=1, source_target_pairs={{0,28},{4,0},{8,4},{12,8},{16,12},{20,16},{24,20},{28,24},{1,29},{... | collective-permute-start | bytes 196616 | tf_op jit(solution)/shard_map/ppermute | solution.py:204
  8.2 0.4 %collective-permute-start.1 = (bf16[64,512]{1,0:T(8,128)(2,1)S(1)}, bf16[64,512]{1,0:T(8,128)(2,1)S(1)}, u32[]{:S(2)}, u32[]{:S(2)}) collective-permute-start(bf16[64,512]{1,0:T(8,128)(2,1)S(1)} %constant_dynamic-update-slice_fusion.refs_8_), channel_id=1, source_target_pairs={{0,24},{4,28},{8,0},{12,4},{16,8},{20,12},{24,16},{28,20},{1,25},{... | collective-permute-start | bytes 196616 | tf_op jit(solution)/shard_map/ppermute | solution.py:204
  8.6 3.0 %collective-permute-start.6 = (bf16[64,512]{1,0:T(8,128)(2,1)S(1)}, bf16[64,512]{1,0:T(8,128)(2,1)S(1)}, u32[]{:S(2)}, u32[]{:S(2)}) collective-permute-start(bf16[64,512]{1,0:T(8,128)(2,1)S(1)} %constant_dynamic-update-slice_fusion.refs_8_), channel_id=1, source_target_pairs={{0,20},{4,24},{8,28},{12,0},{16,4},{20,8},{24,12},{28,16},{1,21},{... | collective-permute-start | bytes 196616 | tf_op jit(solution)/shard_map/ppermute | solution.py:204
  11.7 2.4 %collective-permute-start.2 = (bf16[192,512]{1,0:T(8,128)(2,1)S(1)}, bf16[192,512]{1,0:T(8,128)(2,1)S(1)}, u32[]{:S(2)}, u32[]{:S(2)}) collective-permute-start(bf16[192,512]{1,0:T(8,128)(2,1)S(1)} %maximum_maximum_fusion), channel_id=1, source_target_pairs={{0,4},{4,8},{8,12},{12,16},{16,20},{20,24},{24,28},{28,0},{1,5},{5... | collective-permute-start | bytes 589832 | tf_op jit(solution)/shard_map/ppermute | solution.py:204
  14.1 0.6 %copy-done.3 = s32[24]{0:T(128)S(1)} copy-done((s32[24]{0:T(128)S(1)}, s32[24]{0:T(128)}, u32[]{:S(2)}) %copy-start.3) | copy-done | bytes 120
  14.9 0.1 reduce
  15.2 0.2 multiply_cosine_fusion
  15.6 0.5 %copy-done.5 = bf16[64,512]{1,0:T(8,128)(2,1)} copy-done((bf16[64,512]{1,0:T(8,128)(2,1)}, bf16[64,512]{1,0:T(8,128)(2,1)S(1)}, u32[]{:S(2)}) %copy-start.5) | copy-done | bytes 65560
  16.1 0.1 copy.28
  16.3 0.8 %copy.29 = bf16[2,128,256]{2,0,1:T(2,128)(2,1)} copy(bf16[2,128,256]{1,2,0:T(8,128)(2,1)S(1)} %pad_maximum_fusion) | data formatting | bytes 262144 | tf_op jit(solution)/shard_map/stack | solution.py:263
  17.1 3.3 %all-to-all-start = ((bf16[2,128,256]{2,0,1:T(2,128)(2,1)}), bf16[2,128,256]{2,0,1:T(2,128)(2,1)S(1)}, u32[]{:S(2)}, u32[]{:S(2)}) async-start(bf16[2,128,256]{2,0,1:T(2,128)(2,1)} %copy.29), calls=%async_computation | async-start | bytes 262144 | tf_op jit(solution)/shard_map/all_to_all | solution.py:262
  20.4 0.6 %maximum_bitcast_fusion.refs_4_ = f32[1,128]{1,0:T(1,128)} fusion(f32[64]{0:T(128)S(1)} %multiply_exponential_fusion), kind=kLoop, calls=%fused_computation.12 | loop fusion | flops 128 | bytes 768 | tf_op jit(solution)/shard_map/broadcast_in_dim | solution.py:267
  21.1 0.6 %collective-permute-start.4 = (bf16[64,512]{1,0:T(8,128)(2,1)S(1)}, bf16[64,512]{1,0:T(8,128)(2,1)S(1)}, u32[]{:S(2)}, u32[]{:S(2)}) collective-permute-start(bf16[64,512]{1,0:T(8,128)(2,1)S(1)} %constant_dynamic-update-slice_fusion.refs_8_), channel_id=1, source_target_pairs={{0,12},{4,16},{8,20},{12,24},{16,28},{20,0},{24,4},{28,8},{1,13},{... | collective-permute-start | bytes 196616 | tf_op jit(solution)/shard_map/ppermute | solution.py:204
  21.6 0.7 %copy.32.refs_6_ = bf16[128,256]{1,0:T(8,128)(2,1)} copy(bf16[128,256]{0,1:T(8,128)(2,1)S(1)} %bitcast.19) | data formatting | bytes 131072 | tf_op jit(solution)/shard_map/convert_element_type | solution.py:31
  22.4 2.6 %all-to-all-done = bf16[2,128,256]{2,0,1:T(2,128)(2,1)S(1)} async-done(((bf16[2,128,256]{2,0,1:T(2,128)(2,1)}), bf16[2,128,256]{2,0,1:T(2,128)(2,1)S(1)}, u32[]{:S(2)}, u32[]{:S(2)}) %all-to-all-start) | async-done | bytes 131104 | tf_op jit(solution)/shard_map/all_to_all | solution.py:262
  25.0 0.2 fusion
  25.3 0.6 %copy.33 = bf16[4,8,4,256]{3,1,2,0:T(8,128)(2,1)} copy(bf16[4,8,4,256]{3,2,1,0:T(4,128)(2,1)S(1)} %bitcast.21) | data formatting | bytes 131072
  26.0 0.6 %copy.34 = bf16[4,8,4,256]{3,1,2,0:T(8,128)(2,1)} copy(bf16[4,8,4,256]{3,2,1,0:T(4,128)(2,1)S(1)} %bitcast.22) | data formatting | bytes 131072
  26.7 1.1 %collective-permute-done.3.refs_10_ = bf16[64,512]{1,0:T(8,128)(2,1)S(1)} collective-permute-done((bf16[64,512]{1,0:T(8,128)(2,1)S(1)}, bf16[64,512]{1,0:T(8,128)(2,1)S(1)}, u32[]{:S(2)}, u32[]{:S(2)}) %collective-permute-start.3) | collective-permute-done | bytes 65568 | tf_op jit(solution)/shard_map/ppermute | solution.py:204
  27.8 1.8 %collective-permute-done.4.refs_11_ = bf16[64,512]{1,0:T(8,128)(2,1)S(1)} collective-permute-done((bf16[64,512]{1,0:T(8,128)(2,1)S(1)}, bf16[64,512]{1,0:T(8,128)(2,1)S(1)}, u32[]{:S(2)}, u32[]{:S(2)}) %collective-permute-start.4) | collective-permute-done | bytes 65568 | tf_op jit(solution)/shard_map/ppermute | solution.py:204
  29.6 0.6 %copy-done.10 = bf16[64,512]{1,0:T(8,128)(2,1)} copy-done((bf16[64,512]{1,0:T(8,128)(2,1)}, bf16[64,512]{1,0:T(8,128)(2,1)S(1)}, u32[]{:S(2)}) %copy-start.10) | copy-done | bytes 65560
  30.3 5.5 %shard_map.103 = bf16[128,1024]{1,0:T(8,128)(2,1)} custom-call(s32[1]{0:T(128)} %bitcast.refs_0_, s32[24]{0:T(128)} %refs_1_.1, s32[24]{0:T(128)} %refs_2_.1, s32[8]{0:T(128)} %refs_3_.1, f32[1,128]{1,0:T(1,128)} %maximum_bitcast_fusion.refs_4_, bf16[128,1024]{1,0:T(8,128)(2,1)} %refs_5_.1, bf16[128,256]{1,0:T(8,128)(2,1)} %copy.32.refs_6_, ...), custom_call_target="tpu_custom_call" | custom-call | flops 402653184 | bytes 1310720 | tf_op jit(solution)/shard_map/pallas_call | solution.py:173
  (41 shorter events, 0.8 us)
Async XLA Ops:
  0.6 11.0 %copy-start.1 = (bf16[128,256]{1,0:T(8,128)(2,1)S(1)}, bf16[128,256]{1,0:T(8,128)(2,1)}, u32[]{:S(2)}) copy-start(bf16[128,256]{1,0:T(8,128)(2,1)} %refs_7_.1) | copy-start | bytes 196612
  0.6 11.0 %copy-start = (bf16[128,256]{1,0:T(8,128)(2,1)S(1)}, bf16[128,256]{1,0:T(8,128)(2,1)}, u32[]{:S(2)}) copy-start(bf16[128,256]{1,0:T(8,128)(2,1)} %param.9) | copy-start | bytes 196612
  2.2 18.9 %copy-start.2 = (bf16[64,512]{1,0:T(8,128)(2,1)}, bf16[64,512]{1,0:T(8,128)(2,1)S(1)}, u32[]{:S(2)}) copy-start(bf16[64,512]{1,0:T(8,128)(2,1)S(1)} %constant_dynamic-update-slice_fusion.refs_8_) | copy-start | bytes 196612
  2.2 13.2 %collective-permute-start = (bf16[64,512]{1,0:T(8,128)(2,1)S(1)}, bf16[64,512]{1,0:T(8,128)(2,1)S(1)}, u32[]{:S(2)}, u32[]{:S(2)}) collective-permute-start(bf16[64,512]{1,0:T(8,128)(2,1)S(1)} %constant_dynamic-update-slice_fusion.refs_8_), channel_id=1, source_target_pairs={{0,28},{4,0},{8,4},{12,8},{16,12},{20,16},{24,20},{28,24},{1,29},{... | collective-permute-start | bytes 196616 | tf_op jit(solution)/shard_map/ppermute | solution.py:204
  8.2 7.3 %collective-permute-start.1 = (bf16[64,512]{1,0:T(8,128)(2,1)S(1)}, bf16[64,512]{1,0:T(8,128)(2,1)S(1)}, u32[]{:S(2)}, u32[]{:S(2)}) collective-permute-start(bf16[64,512]{1,0:T(8,128)(2,1)S(1)} %constant_dynamic-update-slice_fusion.refs_8_), channel_id=1, source_target_pairs={{0,24},{4,28},{8,0},{12,4},{16,8},{20,12},{24,16},{28,20},{1,25},{... | collective-permute-start | bytes 196616 | tf_op jit(solution)/shard_map/ppermute | solution.py:204
  8.6 18.0 %collective-permute-start.5 = (bf16[64,512]{1,0:T(8,128)(2,1)S(1)}, bf16[64,512]{1,0:T(8,128)(2,1)S(1)}, u32[]{:S(2)}, u32[]{:S(2)}) collective-permute-start(bf16[64,512]{1,0:T(8,128)(2,1)S(1)} %constant_dynamic-update-slice_fusion.refs_8_), channel_id=1, source_target_pairs={{0,16},{4,20},{8,24},{12,28},{16,0},{20,4},{24,8},{28,12},{1,17},{... | collective-permute-start | bytes 196616 | tf_op jit(solution)/shard_map/ppermute | solution.py:204
  8.6 18.0 %collective-permute-start.6 = (bf16[64,512]{1,0:T(8,128)(2,1)S(1)}, bf16[64,512]{1,0:T(8,128)(2,1)S(1)}, u32[]{:S(2)}, u32[]{:S(2)}) collective-permute-start(bf16[64,512]{1,0:T(8,128)(2,1)S(1)} %constant_dynamic-update-slice_fusion.refs_8_), channel_id=1, source_target_pairs={{0,20},{4,24},{8,28},{12,0},{16,4},{20,8},{24,12},{28,16},{1,21},{... | collective-permute-start | bytes 196616 | tf_op jit(solution)/shard_map/ppermute | solution.py:204
  11.7 17.9 %collective-permute-start.2 = (bf16[192,512]{1,0:T(8,128)(2,1)S(1)}, bf16[192,512]{1,0:T(8,128)(2,1)S(1)}, u32[]{:S(2)}, u32[]{:S(2)}) collective-permute-start(bf16[192,512]{1,0:T(8,128)(2,1)S(1)} %maximum_maximum_fusion), channel_id=1, source_target_pairs={{0,4},{4,8},{8,12},{12,16},{16,20},{20,24},{24,28},{28,0},{1,5},{5... | collective-permute-start | bytes 589832 | tf_op jit(solution)/shard_map/ppermute | solution.py:204
  14.1 0.7 %copy-start.3 = (s32[24]{0:T(128)S(1)}, s32[24]{0:T(128)}, u32[]{:S(2)}) copy-start(s32[24]{0:T(128)} %refs_1_.1) | copy-start | bytes 292
  15.4 0.6 %copy-start.5 = (bf16[64,512]{1,0:T(8,128)(2,1)}, bf16[64,512]{1,0:T(8,128)(2,1)S(1)}, u32[]{:S(2)}) copy-start(bf16[64,512]{1,0:T(8,128)(2,1)S(1)} %collective-permute-done.refs_15_) | copy-start | bytes 196612
  15.5 0.6 %copy-start.6 = (bf16[64,512]{1,0:T(8,128)(2,1)}, bf16[64,512]{1,0:T(8,128)(2,1)S(1)}, u32[]{:S(2)}) copy-start(bf16[64,512]{1,0:T(8,128)(2,1)S(1)} %collective-permute-done.1.refs_14_) | copy-start | bytes 196612
  17.1 7.9 %all-to-all-start = ((bf16[2,128,256]{2,0,1:T(2,128)(2,1)}), bf16[2,128,256]{2,0,1:T(2,128)(2,1)S(1)}, u32[]{:S(2)}, u32[]{:S(2)}) async-start(bf16[2,128,256]{2,0,1:T(2,128)(2,1)} %copy.29), calls=%async_computation | async-start | bytes 262144 | tf_op jit(solution)/shard_map/all_to_all | solution.py:262
  21.1 6.7 %collective-permute-start.3 = (bf16[64,512]{1,0:T(8,128)(2,1)S(1)}, bf16[64,512]{1,0:T(8,128)(2,1)S(1)}, u32[]{:S(2)}, u32[]{:S(2)}) collective-permute-start(bf16[64,512]{1,0:T(8,128)(2,1)S(1)} %constant_dynamic-update-slice_fusion.refs_8_), channel_id=1, source_target_pairs={{0,8},{4,12},{8,16},{12,20},{16,24},{20,28},{24,0},{28,4},{1,9},{5... | collective-permute-start | bytes 196616 | tf_op jit(solution)/shard_map/ppermute | solution.py:204
  21.1 8.5 %collective-permute-start.4 = (bf16[64,512]{1,0:T(8,128)(2,1)S(1)}, bf16[64,512]{1,0:T(8,128)(2,1)S(1)}, u32[]{:S(2)}, u32[]{:S(2)}) collective-permute-start(bf16[64,512]{1,0:T(8,128)(2,1)S(1)} %constant_dynamic-update-slice_fusion.refs_8_), channel_id=1, source_target_pairs={{0,12},{4,16},{8,20},{12,24},{16,28},{20,0},{24,4},{28,8},{1,13},{... | collective-permute-start | bytes 196616 | tf_op jit(solution)/shard_map/ppermute | solution.py:204
  26.7 2.9 %copy-start.7 = (bf16[64,512]{1,0:T(8,128)(2,1)}, bf16[64,512]{1,0:T(8,128)(2,1)S(1)}, u32[]{:S(2)}) copy-start(bf16[64,512]{1,0:T(8,128)(2,1)S(1)} %collective-permute-done.5.refs_12_) | copy-start | bytes 196612
  26.7 2.9 %copy-start.8 = (bf16[64,512]{1,0:T(8,128)(2,1)}, bf16[64,512]{1,0:T(8,128)(2,1)S(1)}, u32[]{:S(2)}) copy-start(bf16[64,512]{1,0:T(8,128)(2,1)S(1)} %collective-permute-done.6.refs_13_) | copy-start | bytes 196612
  27.7 1.9 %copy-start.9 = (bf16[64,512]{1,0:T(8,128)(2,1)}, bf16[64,512]{1,0:T(8,128)(2,1)S(1)}, u32[]{:S(2)}) copy-start(bf16[64,512]{1,0:T(8,128)(2,1)S(1)} %collective-permute-done.3.refs_10_) | copy-start | bytes 196612
  29.6 0.6 %copy-start.10 = (bf16[64,512]{1,0:T(8,128)(2,1)}, bf16[64,512]{1,0:T(8,128)(2,1)S(1)}, u32[]{:S(2)}) copy-start(bf16[64,512]{1,0:T(8,128)(2,1)S(1)} %collective-permute-done.4.refs_11_) | copy-start | bytes 196612
  29.6 0.7 %copy-start.4 = (bf16[192,512]{1,0:T(8,128)(2,1)}, bf16[192,512]{1,0:T(8,128)(2,1)S(1)}, u32[]{:S(2)}) copy-start(bf16[192,512]{1,0:T(8,128)(2,1)S(1)} %collective-permute-done.2.refs_9_) | copy-start | bytes 589828

commit v16 on v13

--- a/solution.py
+++ b/solution.py
@@ -165,6 +165,7 @@
             transcendentals=rows * count * q_heads,
             bytes_accessed=nbytes + queries.size * 2,
         ),
+        compiler_params=pltpu.CompilerParams(vmem_limit_bytes=16 * 1024 * 1024),
     )(*scalars, freq, *arrays)
 
 

time: 34.9 us -> 32.5 us (0.931)
  local copies, waits for them, and re-layouts: 6.87 us -> 5.06 us
  Pallas kernels: 4.28 us -> 3.66 us
  waiting for transfers between devices: 5.57 us -> 6.19 us
  other arithmetic: 1.28 us -> 0.7 us
    all_to_all x1, waiting for transfers between devices: 2.64 us -> 3.83 us  [body(): lax.all_to_all(jnp.stack([own_k_rot, cache_values_in], axis=0), 'tp', spl...]
    unnamed x25 -> x15, local copies, waits for them, and re-layouts: 3.94 us -> 2.75 us
    convert_element_type x1, local copies, waits for them, and re-layouts: 0.73 us -> 0.11 us  [rotate(): return jnp.concatenate([lower * cosine - upper * sine, upper * cosine + l...]
    pallas_call x1, Pallas kernels: 4.28 us -> 3.66 us  [attend(): pl.pallas_call(functools.partial(attend_kernel, meta), out_shape=jax.Shap...]
    ppermute x7, waiting for transfers between devices: 2.93 us -> 2.35 us  [shifted(): return lax.ppermute(array, axis, pairs)]
    broadcast_in_dim x1, other arithmetic: 0.65 us -> 0.08 us  [body(): freq = jnp.concatenate([freq, freq])[None, :]]
  transfers between devices with their start and end apart: 8 -> 8, of which waited for: 3 -> 3; matrix products, arithmetic and copies ran while one was open for 14% -> 11% of each run, Pallas kernels for 0% -> 0%
where the time goes in v16:
time: 32.5 us; the launch traced here: 32.2 us
  starting transfers between devices  15.8 us (49%)
  waiting for transfers between devices  6.19 us (19%)
  local copies, waits for them, and re-layouts  5.06 us (16%)
  Pallas kernels  3.66 us (11%)
  between operations  0.79 us (2%)
  other arithmetic  0.7 us (2%)
    ppermute x7, starting transfers between devices, shifted(): return lax.ppermute(array, axis, pairs)  12.4 us
    all_to_all x1, waiting for transfers between devices, body(): lax.all_to_all(jnp.stack([own_k_rot, cache_values_in], axis=0), 'tp', spl...  3.83 us
    pallas_call x1, Pallas kernels, attend(): pl.pallas_call(functools.partial(attend_kernel, meta), out_shape=jax.Shap...  3.66 us
    all_to_all x1, starting transfers between devices, body(): lax.all_to_all(jnp.stack([own_k_rot, cache_values_in], axis=0), 'tp', spl...  3.33 us
    unnamed x15, local copies, waits for them, and re-layouts  2.75 us
    ppermute x7, waiting for transfers between devices, shifted(): return lax.ppermute(array, axis, pairs)  2.35 us
    another operation x2, local copies, waits for them, and re-layouts, body(): jnp.stack([own_k_rot, cache_values_in], axis=0)  0.9 us
    concatenate x1, local copies, waits for them, and re-layouts, body(): prefix_kv = jnp.concatenate([prefix_keys, prefix_values], axis=1)  0.76 us
  transfers between devices with their start and end apart: 8, of which 3 were waited for; matrix products, arithmetic and copies ran while one was open for 11% of the time, Pallas kernels for 0%

profile of v16, /device:TPU:0, one launch (start us, length us, event | category | flops | bytes accessed | tf_op | source)
XLA Modules:
  0.0 32.2 jit_solution(16618693926187576322)
XLA Ops:
  0.7 0.8 %constant_dynamic-update-slice_fusion.1 = bf16[64,512]{1,0:T(8,128)(2,1)S(1)} fusion(bf16[64,256]{1,0:T(8,128)(2,1)} %param.11), kind=kLoop, calls=%fused_computation.11 | loop fusion | bytes 65536
  1.4 0.8 %constant_dynamic-update-slice_fusion.refs_8_ = bf16[64,512]{1,0:T(8,128)(2,1)S(1)} fusion(bf16[64,512]{1,0:T(8,128)(2,1)S(1)} %constant_dynamic-update-slice_fusion.1, bf16[64,256]{1,0:T(8,128)(2,1)} %param.12), kind=kLoop, calls=%fused_computation.10 | loop fusion | bytes 65536 | tf_op jit(solution)/shard_map/concatenate | solution.py:211
  2.2 6.0 %collective-permute-start = (bf16[64,512]{1,0:T(8,128)(2,1)S(1)}, bf16[64,512]{1,0:T(8,128)(2,1)S(1)}, u32[]{:S(2)}, u32[]{:S(2)}) collective-permute-start(bf16[64,512]{1,0:T(8,128)(2,1)S(1)} %constant_dynamic-update-slice_fusion.refs_8_), channel_id=1, source_target_pairs={{0,28},{4,0},{8,4},{12,8},{16,12},{20,16},{24,20},{28,24},{1,29},{... | collective-permute-start | bytes 196616 | tf_op jit(solution)/shard_map/ppermute | solution.py:184
  8.2 0.4 %collective-permute-start.1 = (bf16[64,512]{1,0:T(8,128)(2,1)S(1)}, bf16[64,512]{1,0:T(8,128)(2,1)S(1)}, u32[]{:S(2)}, u32[]{:S(2)}) collective-permute-start(bf16[64,512]{1,0:T(8,128)(2,1)S(1)} %constant_dynamic-update-slice_fusion.refs_8_), channel_id=1, source_target_pairs={{0,24},{4,28},{8,0},{12,4},{16,8},{20,12},{24,16},{28,20},{1,25},{... | collective-permute-start | bytes 196616 | tf_op jit(solution)/shard_map/ppermute | solution.py:184
  8.6 3.0 %collective-permute-start.6 = (bf16[64,512]{1,0:T(8,128)(2,1)S(1)}, bf16[64,512]{1,0:T(8,128)(2,1)S(1)}, u32[]{:S(2)}, u32[]{:S(2)}) collective-permute-start(bf16[64,512]{1,0:T(8,128)(2,1)S(1)} %constant_dynamic-update-slice_fusion.refs_8_), channel_id=1, source_target_pairs={{0,20},{4,24},{8,28},{12,0},{16,4},{20,8},{24,12},{28,16},{1,21},{... | collective-permute-start | bytes 196616 | tf_op jit(solution)/shard_map/ppermute | solution.py:184
  11.7 2.4 %collective-permute-start.2 = (bf16[192,512]{1,0:T(8,128)(2,1)S(1)}, bf16[192,512]{1,0:T(8,128)(2,1)S(1)}, u32[]{:S(2)}, u32[]{:S(2)}) collective-permute-start(bf16[192,512]{1,0:T(8,128)(2,1)S(1)} %maximum_maximum_fusion), channel_id=1, source_target_pairs={{0,4},{4,8},{8,12},{12,16},{16,20},{20,24},{24,28},{28,0},{1,5},{5... | collective-permute-start | bytes 589832 | tf_op jit(solution)/shard_map/ppermute | solution.py:184
  14.1 0.6 %copy-done.1 = s32[24]{0:T(128)S(1)} copy-done((s32[24]{0:T(128)S(1)}, s32[24]{0:T(128)}, u32[]{:S(2)}) %copy-start.1) | copy-done | bytes 120
  14.9 0.1 reduce
  15.1 0.1 select_reduce_fusion
  15.2 0.2 multiply_cosine_fusion
  15.5 0.1 copy.25
  15.6 0.1 copy.28
  15.7 0.8 %copy.29 = bf16[2,128,256]{2,0,1:T(2,128)(2,1)} copy(bf16[2,128,256]{1,2,0:T(8,128)(2,1)S(1)} %pad_maximum_fusion) | data formatting | bytes 262144 | tf_op jit(solution)/shard_map/stack | solution.py:243
  16.5 3.3 %all-to-all-start = ((bf16[2,128,256]{2,0,1:T(2,128)(2,1)}), bf16[2,128,256]{2,0,1:T(2,128)(2,1)S(1)}, u32[]{:S(2)}, u32[]{:S(2)}) async-start(bf16[2,128,256]{2,0,1:T(2,128)(2,1)} %copy.29), calls=%async_computation | async-start | bytes 262144 | tf_op jit(solution)/shard_map/all_to_all | solution.py:242
  20.0 0.6 %collective-permute-start.4 = (bf16[64,512]{1,0:T(8,128)(2,1)S(1)}, bf16[64,512]{1,0:T(8,128)(2,1)S(1)}, u32[]{:S(2)}, u32[]{:S(2)}) collective-permute-start(bf16[64,512]{1,0:T(8,128)(2,1)S(1)} %constant_dynamic-update-slice_fusion.refs_8_), channel_id=1, source_target_pairs={{0,12},{4,16},{8,20},{12,24},{16,28},{20,0},{24,4},{28,8},{1,13},{... | collective-permute-start | bytes 196616 | tf_op jit(solution)/shard_map/ppermute | solution.py:184
  20.5 0.1 copy.32.refs_6_
  20.6 3.8 %all-to-all-done = bf16[2,128,256]{2,0,1:T(2,128)(2,1)S(1)} async-done(((bf16[2,128,256]{2,0,1:T(2,128)(2,1)}), bf16[2,128,256]{2,0,1:T(2,128)(2,1)S(1)}, u32[]{:S(2)}, u32[]{:S(2)}) %all-to-all-start) | async-done | bytes 131104 | tf_op jit(solution)/shard_map/all_to_all | solution.py:242
  24.5 0.2 fusion
  24.7 0.1 copy.30
  24.8 0.6 %copy.33 = bf16[4,8,4,256]{3,1,2,0:T(8,128)(2,1)} copy(bf16[4,8,4,256]{3,2,1,0:T(4,128)(2,1)S(1)} %bitcast.23) | data formatting | bytes 131072
  25.5 0.6 %copy.34 = bf16[4,8,4,256]{3,1,2,0:T(8,128)(2,1)} copy(bf16[4,8,4,256]{3,2,1,0:T(4,128)(2,1)S(1)} %bitcast.24) | data formatting | bytes 131072
  26.1 0.5 %collective-permute-done.3.refs_10_ = bf16[64,512]{1,0:T(8,128)(2,1)S(1)} collective-permute-done((bf16[64,512]{1,0:T(8,128)(2,1)S(1)}, bf16[64,512]{1,0:T(8,128)(2,1)S(1)}, u32[]{:S(2)}, u32[]{:S(2)}) %collective-permute-start.3) | collective-permute-done | bytes 65568 | tf_op jit(solution)/shard_map/ppermute | solution.py:184
  26.6 1.8 %collective-permute-done.4.refs_11_ = bf16[64,512]{1,0:T(8,128)(2,1)S(1)} collective-permute-done((bf16[64,512]{1,0:T(8,128)(2,1)S(1)}, bf16[64,512]{1,0:T(8,128)(2,1)S(1)}, u32[]{:S(2)}, u32[]{:S(2)}) %collective-permute-start.4) | collective-permute-done | bytes 65568 | tf_op jit(solution)/shard_map/ppermute | solution.py:184
  28.5 3.7 %shard_map.103 = bf16[128,1024]{1,0:T(8,128)(2,1)} custom-call(s32[1]{0:T(128)} %bitcast.refs_0_, s32[24]{0:T(128)S(1)} %copy-done.1, s32[24]{0:T(128)S(1)} %copy-done.3, s32[8]{0:T(128)S(1)} %copy-done.4, f32[1,128]{1,0:T(1,128)S(1)} %maximum_bitcast_fusion.refs_4_, bf16[128,1024]{1,0:T(8,128)(2,1)S(1)} %copy-done.2, bf16[128,256]{1,0:T(8,128)(2,1)S(1)} %copy.32.refs_6_, ...), custom_call_target="tpu_custom_call" | custom-call | flops 402653184 | bytes 1310720 | tf_op jit(solution)/shard_map/pallas_call | solution.py:154
  (31 shorter events, 0.5 us)
Async XLA Ops:
  0.6 11.0 %copy-start = (bf16[128,256]{1,0:T(8,128)(2,1)S(1)}, bf16[128,256]{1,0:T(8,128)(2,1)}, u32[]{:S(2)}) copy-start(bf16[128,256]{1,0:T(8,128)(2,1)} %refs_7_.1) | copy-start | bytes 196612
  0.6 11.0 %copy-start.5 = (bf16[128,256]{1,0:T(8,128)(2,1)S(1)}, bf16[128,256]{1,0:T(8,128)(2,1)}, u32[]{:S(2)}) copy-start(bf16[128,256]{1,0:T(8,128)(2,1)} %param.9) | copy-start | bytes 196612
  2.2 13.2 %collective-permute-start = (bf16[64,512]{1,0:T(8,128)(2,1)S(1)}, bf16[64,512]{1,0:T(8,128)(2,1)S(1)}, u32[]{:S(2)}, u32[]{:S(2)}) collective-permute-start(bf16[64,512]{1,0:T(8,128)(2,1)S(1)} %constant_dynamic-update-slice_fusion.refs_8_), channel_id=1, source_target_pairs={{0,28},{4,0},{8,4},{12,8},{16,12},{20,16},{24,20},{28,24},{1,29},{... | collective-permute-start | bytes 196616 | tf_op jit(solution)/shard_map/ppermute | solution.py:184
  8.2 7.3 %collective-permute-start.1 = (bf16[64,512]{1,0:T(8,128)(2,1)S(1)}, bf16[64,512]{1,0:T(8,128)(2,1)S(1)}, u32[]{:S(2)}, u32[]{:S(2)}) collective-permute-start(bf16[64,512]{1,0:T(8,128)(2,1)S(1)} %constant_dynamic-update-slice_fusion.refs_8_), channel_id=1, source_target_pairs={{0,24},{4,28},{8,0},{12,4},{16,8},{20,12},{24,16},{28,20},{1,25},{... | collective-permute-start | bytes 196616 | tf_op jit(solution)/shard_map/ppermute | solution.py:184
  8.6 17.5 %collective-permute-start.5 = (bf16[64,512]{1,0:T(8,128)(2,1)S(1)}, bf16[64,512]{1,0:T(8,128)(2,1)S(1)}, u32[]{:S(2)}, u32[]{:S(2)}) collective-permute-start(bf16[64,512]{1,0:T(8,128)(2,1)S(1)} %constant_dynamic-update-slice_fusion.refs_8_), channel_id=1, source_target_pairs={{0,16},{4,20},{8,24},{12,28},{16,0},{20,4},{24,8},{28,12},{1,17},{... | collective-permute-start | bytes 196616 | tf_op jit(solution)/shard_map/ppermute | solution.py:184
  8.6 17.5 %collective-permute-start.6 = (bf16[64,512]{1,0:T(8,128)(2,1)S(1)}, bf16[64,512]{1,0:T(8,128)(2,1)S(1)}, u32[]{:S(2)}, u32[]{:S(2)}) collective-permute-start(bf16[64,512]{1,0:T(8,128)(2,1)S(1)} %constant_dynamic-update-slice_fusion.refs_8_), channel_id=1, source_target_pairs={{0,20},{4,24},{8,28},{12,0},{16,4},{20,8},{24,12},{28,16},{1,21},{... | collective-permute-start | bytes 196616 | tf_op jit(solution)/shard_map/ppermute | solution.py:184
  11.7 16.8 %collective-permute-start.2 = (bf16[192,512]{1,0:T(8,128)(2,1)S(1)}, bf16[192,512]{1,0:T(8,128)(2,1)S(1)}, u32[]{:S(2)}, u32[]{:S(2)}) collective-permute-start(bf16[192,512]{1,0:T(8,128)(2,1)S(1)} %maximum_maximum_fusion), channel_id=1, source_target_pairs={{0,4},{4,8},{8,12},{12,16},{16,20},{20,24},{24,28},{28,0},{1,5},{5... | collective-permute-start | bytes 589832 | tf_op jit(solution)/shard_map/ppermute | solution.py:184
  14.1 0.7 %copy-start.1 = (s32[24]{0:T(128)S(1)}, s32[24]{0:T(128)}, u32[]{:S(2)}) copy-start(s32[24]{0:T(128)} %refs_1_.1) | copy-start | bytes 292
  16.5 7.9 %all-to-all-start = ((bf16[2,128,256]{2,0,1:T(2,128)(2,1)}), bf16[2,128,256]{2,0,1:T(2,128)(2,1)S(1)}, u32[]{:S(2)}, u32[]{:S(2)}) async-start(bf16[2,128,256]{2,0,1:T(2,128)(2,1)} %copy.29), calls=%async_computation | async-start | bytes 262144 | tf_op jit(solution)/shard_map/all_to_all | solution.py:242
  19.9 6.7 %collective-permute-start.3 = (bf16[64,512]{1,0:T(8,128)(2,1)S(1)}, bf16[64,512]{1,0:T(8,128)(2,1)S(1)}, u32[]{:S(2)}, u32[]{:S(2)}) collective-permute-start(bf16[64,512]{1,0:T(8,128)(2,1)S(1)} %constant_dynamic-update-slice_fusion.refs_8_), channel_id=1, source_target_pairs={{0,8},{4,12},{8,16},{12,20},{16,24},{20,28},{24,0},{28,4},{1,9},{5... | collective-permute-start | bytes 196616 | tf_op jit(solution)/shard_map/ppermute | solution.py:184
  20.0 8.5 %collective-permute-start.4 = (bf16[64,512]{1,0:T(8,128)(2,1)S(1)}, bf16[64,512]{1,0:T(8,128)(2,1)S(1)}, u32[]{:S(2)}, u32[]{:S(2)}) collective-permute-start(bf16[64,512]{1,0:T(8,128)(2,1)S(1)} %constant_dynamic-update-slice_fusion.refs_8_), channel_id=1, source_target_pairs={{0,12},{4,16},{8,20},{12,24},{16,28},{20,0},{24,4},{28,8},{1,13},{... | collective-permute-start | bytes 196616 | tf_op jit(solution)/shard_map/ppermute | solution.py:184
  24.8 3.7 %copy-start.2 = (bf16[128,1024]{1,0:T(8,128)(2,1)S(1)}, bf16[128,1024]{1,0:T(8,128)(2,1)}, u32[]{:S(2)}) copy-start(bf16[128,1024]{1,0:T(8,128)(2,1)} %refs_5_.1) | copy-start | bytes 786436
  26.1 2.4 %copy-start.3 = (s32[24]{0:T(128)S(1)}, s32[24]{0:T(128)}, u32[]{:S(2)}) copy-start(s32[24]{0:T(128)} %refs_2_.1) | copy-start | bytes 292
  26.1 2.4 %copy-start.4 = (s32[8]{0:T(128)S(1)}, s32[8]{0:T(128)}, u32[]{:S(2)}) copy-start(s32[8]{0:T(128)} %refs_3_.1) | copy-start | bytes 100
